TPU v7x, 256 devices: a whole 4x4x8 slice. The times are simulated.
256 devices in a mesh: dom: 32 (over x, z), head: 8 (over y, core).
Axes of the slice: x: 4, y: 4, z: 8, core: 2. Of those that a mesh axis runs over, the one named last changes fastest.
Arguments:
- features: bfloat16 [131072, 512], P(('dom', 'head')), may hold values from -6 to 6
- norm_gain: float32 [512], replicated, may hold values from 0.5 to 1.5
- w_qkv: bfloat16 [512, 1536], replicated, may hold values from -8 to 8
- w_out: bfloat16 [512, 512], replicated, may hold values from -0.25 to 0.25
- grad_y: bfloat16 [131072, 512], P(('dom', 'head')), may hold values from -6 to 6
- local_keys: int32 [1024, 4], P('dom'), may hold values from 0 to 31, as said below
- remote_keys: int32 [1024, 4], P('dom'), may hold values from 0 to 95
- boundary_blocks: int32 [32, 32, 3], P('dom'), may hold values from 0 to 31
- boundary_count: int32 [32, 32], P(None, 'dom'), may hold values from 1 to 3
Outputs:
- mixed_out: bfloat16 [131072, 512], P(('dom', 'head'))
- grad_x: bfloat16 [131072, 512], P(('dom', 'head'))
Inputs may be any that keep to these rules, and one draw needn't show every extreme that they name: `local_keys`: column 0 of row b is b % 32, the query block itself.
All inputs are finite; a program needn't handle non-finite values.
Results may differ from a plain program's by a relative error of at most 0.012.
The roundings to bfloat16 on the way count: a program that leaves them out, or rounds other values in their place, can miss the bound.
Values may be sent and summed in bfloat16 or wider, within the bound.
No kernel may reach another device: no remote copies, remote signals or barrier semaphores. Data moves between devices by JAX's collectives and lax.ppermute only.
A program may use at most 128 MiB of HBM per device.

v0:
```python
import math

import jax
import jax.numpy as jnp
from jax import lax
from jax.sharding import PartitionSpec as P

HEADS = 8


EPS = 1e-05
STEP_BLOCKS = 4


def probabilities(queries, keys, alive, score_scale):
    scores = (
        jnp.einsum("qbpe,qkcpe->qbpkc", queries, keys, preferred_element_type=jnp.float32)
        * score_scale
    )
    masked = jnp.where(alive[:, None, None, :, None], scores, -jnp.inf)
    top = jnp.max(masked, axis=(3, 4), keepdims=True)
    expo = jnp.exp(masked - top)
    total = jnp.sum(expo, axis=(3, 4), keepdims=True)
    return lax.optimization_barrier((expo / total).astype(jnp.bfloat16))


def fetch_keys(kv_blocks, pool, slot_alive, local_ids, remote_ids, per, depth):
    near = jnp.take(kv_blocks, local_ids, axis=0)
    far = jnp.take(pool, remote_ids, axis=0)
    both = jnp.concatenate([near, far], axis=1)
    both = both.reshape(both.shape[:3] + (2, per, depth))
    alive = jnp.concatenate(
        [jnp.ones(local_ids.shape, jnp.bool_), jnp.take(slot_alive, remote_ids, axis=0)], axis=1
    )
    return (both[:, :, :, 0], both[:, :, :, 1], alive)


def local(
    features,
    norm_gain,
    w_qkv,
    w_out,
    grad_y,
    local_keys,
    remote_keys,
    boundary_blocks,
    boundary_count,
):
    f32 = jnp.float32
    bf16 = jnp.bfloat16
    nhead = lax.axis_size("head")
    mine = lax.axis_index("head")
    rows, width = features.shape
    per = HEADS // nhead
    depth = width // HEADS
    hwide = per * depth
    nblk, near_count = local_keys.shape
    far_count = remote_keys.shape[1]
    ndom = boundary_blocks.shape[1]
    pair_slots = boundary_blocks.shape[2]
    slots = ndom * pair_slots
    bsize = rows * nhead // nblk
    steps = nblk // STEP_BLOCKS
    flat = bsize * 2 * hwide
    score_scale = 1.0 / math.sqrt(depth)
    xf = features.astype(f32)
    inv = lax.rsqrt(jnp.mean(xf * xf, axis=1, keepdims=True) + EPS)
    normed = xf * inv
    hidden = (normed * norm_gain).astype(bf16)
    w_heads = (
        w_qkv.reshape(width, 3, nhead, hwide).transpose(2, 0, 1, 3).reshape(nhead, width, 3 * hwide)
    )
    w_out_heads = w_out.reshape(nhead, hwide, width)
    w_mine = lax.dynamic_index_in_dim(w_heads, mine, 0, keepdims=False)
    qkv = jnp.dot(
        lax.all_gather(hidden, "head", axis=0, tiled=True), w_mine, preferred_element_type=f32
    ).astype(bf16)
    qkv = qkv.reshape(nblk, bsize, 3, hwide)
    queries = qkv[:, :, 0].reshape(steps, STEP_BLOCKS, bsize, per, depth)
    kv_blocks = qkv[:, :, 1:].reshape(nblk, bsize, 2 * hwide)
    send_ids = boundary_blocks[0]
    outgoing = jnp.take(kv_blocks, send_ids, axis=0)
    pool = lax.all_to_all(outgoing, "dom", split_axis=0, concat_axis=0, tiled=True).reshape(
        slots, bsize, 2 * hwide
    )
    slot_alive = (jnp.arange(pair_slots, dtype=jnp.int32)[None, :] < boundary_count).reshape(slots)
    local_steps = local_keys.reshape(steps, STEP_BLOCKS, near_count)
    remote_steps = remote_keys.reshape(steps, STEP_BLOCKS, far_count)

    def attend(item):
        query_part, local_ids, remote_ids = item
        keys, values, alive = fetch_keys(
            kv_blocks, pool, slot_alive, local_ids, remote_ids, per, depth
        )
        weights = probabilities(query_part, keys, alive, score_scale)
        out = jnp.einsum("qbpkc,qkcpe->qbpe", weights, values, preferred_element_type=f32).astype(
            bf16
        )
        return (out, weights)

    def attend_only(item):
        return attend(item)[0]

    items = (queries, local_steps, remote_steps)
    outs = lax.map(attend_only, items)
    attn = lax.all_to_all(
        outs.reshape(nhead, rows, hwide), "head", split_axis=0, concat_axis=0, tiled=True
    )
    mixed_out = (
        xf + jnp.einsum("hre,hef->rf", attn, w_out_heads, preferred_element_type=f32)
    ).astype(bf16)
    d_attn = jnp.einsum("rf,hef->hre", grad_y, w_out_heads, preferred_element_type=f32).astype(bf16)
    d_group = lax.all_to_all(d_attn, "head", split_axis=0, concat_axis=1, tiled=True)
    d_group = d_group.reshape(steps, STEP_BLOCKS, bsize, per, depth)

    def backward(carry, item):
        near_sum, far_sum = carry
        query_part, local_ids, remote_ids, d_out, out_part, stored = item
        keys, values, alive = fetch_keys(
            kv_blocks, pool, slot_alive, local_ids, remote_ids, per, depth
        )
        weights = probabilities(query_part, keys, alive, score_scale)
        delta = jnp.sum(d_out.astype(f32) * out_part.astype(f32), axis=-1)
        d_weights = jnp.einsum("qbpe,qkcpe->qbpkc", d_out, values, preferred_element_type=f32)
        d_scores = (
            weights.astype(f32) * (d_weights - delta[:, :, :, None, None]) * score_scale
        ).astype(bf16)
        d_query = jnp.einsum("qbpkc,qkcpe->qbpe", d_scores, keys, preferred_element_type=f32)
        left = jnp.stack([d_scores, weights], axis=0)
        right = jnp.stack([query_part, d_out], axis=0)
        d_pair = jnp.einsum("tqbpkc,tqbpe->qkctpe", left, right, preferred_element_type=f32)
        d_pair = d_pair.reshape(STEP_BLOCKS, near_count + far_count, flat)
        near_sum = near_sum.at[local_ids.reshape(-1)].add(d_pair[:, :near_count].reshape(-1, flat))
        far_sum = far_sum.at[remote_ids.reshape(-1)].add(d_pair[:, near_count:].reshape(-1, flat))
        return ((near_sum, far_sum), d_query)

    start = (jnp.zeros((nblk, flat), f32), jnp.zeros((slots, flat), f32))
    back_items = (queries, local_steps, remote_steps, d_group, outs, outs)
    (near_sum, far_sum), d_queries = lax.scan(backward, start, back_items)
    returned = lax.all_to_all(
        far_sum.astype(bf16).reshape(ndom, pair_slots, flat),
        "dom",
        split_axis=0,
        concat_axis=0,
        tiled=True,
    )
    near_sum = near_sum.at[send_ids.reshape(-1)].add(returned.reshape(slots, flat).astype(f32))
    d_kv = near_sum.reshape(nblk, bsize, 2, hwide)
    d_q = d_queries.reshape(nblk, bsize, 1, hwide)
    d_qkv = jnp.concatenate([d_q, d_kv], axis=2).astype(bf16).reshape(nhead, rows, 3 * hwide)
    d_rows = lax.all_to_all(d_qkv, "head", split_axis=0, concat_axis=0, tiled=True)
    d_hidden = jnp.einsum("hrc,hdc->rd", d_rows, w_heads, preferred_element_type=f32)
    d_normed = d_hidden * norm_gain
    d_input = inv * (d_normed - normed * jnp.mean(d_normed * normed, axis=1, keepdims=True))
    grad_x = (grad_y.astype(f32) + d_input).astype(bf16)
    return (mixed_out, grad_x)


def solution(mesh):
    return jax.shard_map(
        local,
        mesh=mesh,
        in_specs=(
            P(("dom", "head"), None),
            P(),
            P(),
            P(),
            P(("dom", "head"), None),
            P("dom", None),
            P("dom", None),
            P("dom", None, None),
            P(None, "dom"),
        ),
        out_specs=(P(("dom", "head"), None), P(("dom", "head"), None)),
        check_vma=False,
    )
```

profile of v0, /device:TPU:1, one launch (start us, length us, event | category | flops | bytes accessed | tf_op | source)
XLA Modules:
  0.0 854.1 jit_solution(9502199738507399854)
XLA Ops:
  12.6 6.6 all-to-all-start.2
  22.7 27.6 %all-gather.2.cloned.1.call-done = bf16[4096,512]{1,0:T(8,128)(2,1)} async-done(((bf16[512,512]{1,0:T(8,128)(2,1)}), bf16[4096,512]{1,0:T(8,128)(2,1)}) %all-gather.2.cloned.1.call-update) | async-done | bytes 4194320 | tf_op jit(solution)/shard_map/all_gather | solution.py:76
  50.3 3.7 fusion.36
  55.5 2.7 gather_fusion.6
  58.2 3.9 broadcast_select_fusion.6
  62.1 9.8 %all-to-all-start = ((bf16[32,3,128,128]{2,3,1,0:T(8,128)(2,1)}), bf16[32,3,128,128]{2,3,1,0:T(8,128)(2,1)}, u32[]{:S(2)}, u32[]{:S(2)}) async-start(bf16[32,3,128,128]{2,3,1,0:T(8,128)(2,1)} %broadcast_select_fusion.6), calls=%async_computation | async-start | bytes 6291456 | tf_op jit(solution)/shard_map/all_to_all | solution.py:83
  76.1 67.7 %all-to-all-done = bf16[32,3,128,128]{2,3,1,0:T(8,128)(2,1)} async-done(((bf16[32,3,128,128]{2,3,1,0:T(8,128)(2,1)}), bf16[32,3,128,128]{2,3,1,0:T(8,128)(2,1)}, u32[]{:S(2)}, u32[]{:S(2)}) %all-to-all-start) | async-done | bytes 3145760 | tf_op jit(solution)/shard_map/all_to_all | solution.py:83
  143.8 4.7 copy.152
  148.5 70.8 %while.26 = (s32[]{:T(128)}, bf16[8,4,128,1,64]{2,4,1,3,0:T(8,128)(2,1)}, s32[8,4,4]{2,1,0:T(4,128)S(1)}, bf16[32,128,128]{2,1,0:T(8,128)(2,1)S(1)}, s32[8,4,4]{...) while((s32[]{:T(128)}, ...), condition=%wide.region_4.8_spmd.clone, body=%wide.region_1.7_spmd.clone.sunk | while | flops 141591904 | bytes 17977520 | solution.py:105
  220.4 3.3 broadcast_in_dim.90
  223.7 435.7 %while.27 = (s32[]{:T(128)}, f32[32,16384]{1,0:T(8,128)S(1)}, f32[96,16384]{1,0:T(8,128)}, bf16[8,4,128,1,64]{2,4,1,3,0:T(8,128)(2,1)}, s32[8,4,4]{2,1,0:T(4,128...) while((s32[]{:T(128)}, f32[32,16384]{1,0:T(8,128)S(1)}, ...), condition=%wide.region_11.15_spmd.clone, body=%wide.region_5.14_spmd.clone.sunk | while | flops 347472896 | bytes 48653336 | solution.py:139
  244.8 6.7 copy.228
  251.5 6.5 reshape.558
  258.0 3.9 fusion.85
  264.6 3.2 scatter_fusion
  270.3 7.8 scatter_fusion.1
  299.2 6.7 copy.228
  306.0 6.5 reshape.558
  312.5 3.9 fusion.85
  319.1 3.2 scatter_fusion
  324.8 7.8 scatter_fusion.1
  353.7 6.7 copy.228
  360.4 6.5 reshape.558
  366.9 3.9 fusion.85
  373.5 3.2 scatter_fusion
  379.3 7.8 scatter_fusion.1
  408.2 6.7 copy.228
  414.9 6.5 reshape.558
  421.4 3.9 fusion.85
  428.0 3.2 scatter_fusion
  433.7 7.8 scatter_fusion.1
  462.6 6.7 copy.228
  469.4 6.5 reshape.558
  475.9 3.9 fusion.85
  482.5 3.2 scatter_fusion
  488.2 7.8 scatter_fusion.1
  517.1 6.7 copy.228
  523.8 6.5 reshape.558
  530.4 3.9 fusion.85
  536.9 3.2 scatter_fusion
  542.7 7.8 scatter_fusion.1
  571.6 6.7 copy.228
  578.3 6.5 reshape.558
  584.8 3.9 fusion.85
  591.4 3.2 scatter_fusion
  597.1 7.8 scatter_fusion.1
  626.0 6.7 copy.228
  632.8 6.5 reshape.558
  639.3 3.9 fusion.85
  645.9 3.2 scatter_fusion
  651.6 7.8 scatter_fusion.1
  659.4 4.8 convert_element_type.90
  664.3 5.2 reshape.354
  669.5 8.1 all-to-all-start.3
  680.3 5.3 copy.167
  685.6 84.1 %all-to-all-done.3 = bf16[32,3,16384]{2,1,0:T(4,128)(2,1)} async-done(((bf16[32,3,16384]{2,1,0:T(4,128)(2,1)}), bf16[32,3,16384]{2,1,0:T(4,128)(2,1)}, u32[]{:S(2)}, u32[]{:S(2)}) %all-to-all-start.3) | async-done | bytes 3145760 | tf_op jit(solution)/shard_map/all_to_all | solution.py:140
  769.6 9.0 %all-to-all-start.1 = ((bf16[8,512,64]{1,2,0:T(8,128)(2,1)}), bf16[8,512,64]{1,2,0:T(8,128)(2,1)S(1)}, u32[]{:S(2)}, u32[]{:S(2)}) async-start(bf16[8,512,64]{1,2,0:T(8,128)(2,1)} %reshape.350), calls=%async_computation.1 | async-start | bytes 1048576 | tf_op jit(solution)/shard_map/all_to_all | solution.py:106
  778.6 6.3 reshape.433
  785.0 10.4 %scatter_fusion.2 = f32[32,16384]{1,0:T(8,128)S(1)} fusion(f32[32,16384]{1,0:T(8,128)S(1)} %get-tuple-element.113, s32[96]{0:T(128)S(1)} %fusion.53, f32[96,16384]{1,0:T(8,128)} %reshape.433), kind=kCustom, calls=%fused_computation.9 | custom fusion | flops 1572864 | bytes 18874752 | tf_op jit(solution)/shard_map/scatter-add | solution.py:147
  796.6 4.2 reshape.355
  800.8 7.6 pad_maximum_fusion.2
  808.3 7.2 reshape.507
  817.9 5.0 all-to-all-start.4
  824.2 19.4 %all-to-all-done.4 = bf16[8,512,192]{1,2,0:T(8,128)(2,1)} async-done(((bf16[8,512,192]{1,2,0:T(8,128)(2,1)}), bf16[8,512,192]{1,2,0:T(8,128)(2,1)}, u32[]{:S(2)}, u32[]{:S(2)}) %all-to-all-start.4) | async-done | bytes 1572896 | tf_op jit(solution)/shard_map/all_to_all | solution.py:151
  (535 shorter events, 306.7 us)
Async XLA Ops:
  7.2 4.2 copy-start
  7.2 4.1 copy-start.9
  7.2 43.1 %all-gather.2.cloned.1.call-start = ((), (), s32[]{:S(2)}) async-start(), calls=%async_computation.5 | async-start | bytes 4718592 | tf_op jit(solution)/shard_map/all_gather | solution.py:76
  8.5 0.6 copy-start.12
  9.1 10.1 %copy-start.16 = (s32[1,32,3]{1,0,2:T(1,128)S(1)}, s32[1,32,3]{1,0,2:T(1,128)}, u32[]{:S(2)}) copy-start(s32[1,32,3]{1,0,2:T(1,128)} %param.26) | copy-start | bytes 1156
  9.1 10.4 %copy-start.11 = (bf16[512,1536]{1,0:T(8,128)(2,1)S(1)}, bf16[512,1536]{1,0:T(8,128)(2,1)}, u32[]{:S(2)}) copy-start(bf16[512,1536]{1,0:T(8,128)(2,1)} %param.21) | copy-start | bytes 4718596
  12.6 49.5 %all-to-all-start.2 = ((bf16[8,512,64]{1,2,0:T(8,128)(2,1)}), bf16[8,512,64]{1,2,0:T(8,128)(2,1)S(1)}, u32[]{:S(2)}, u32[]{:S(2)}) async-start(bf16[8,512,64]{1,2,0:T(8,128)(2,1)} %fusion.42), calls=%async_computation.2 | async-start | bytes 1048576 | tf_op jit(solution)/shard_map/all_to_all | solution.py:113
  22.7 31.3 %copy-start.6 = (bf16[8,512,3,64]{1,3,2,0:T(8,128)(2,1)}, bf16[8,512,3,64]{1,3,2,0:T(8,128)(2,1)S(1)}, u32[]{:S(2)}) copy-start(bf16[8,512,3,64]{1,3,2,0:T(8,128)(2,1)S(1)} %copy.148) | copy-start | bytes 4718596
  54.3 1.1 copy-start.8
  54.4 3.8 copy-start.2
  62.1 9.8 %copy-start.18 = (s32[32,4]{0,1:T(4,128)S(1)}, s32[32,4]{0,1:T(4,128)}, u32[]{:S(2)}) copy-start(s32[32,4]{0,1:T(4,128)} %param.24) | copy-start | bytes 1540
  62.1 9.9 %copy-start.19 = (s32[32,4]{0,1:T(4,128)S(1)}, s32[32,4]{0,1:T(4,128)}, u32[]{:S(2)}) copy-start(s32[32,4]{0,1:T(4,128)} %param.25) | copy-start | bytes 1540
  62.1 81.7 %all-to-all-start = ((bf16[32,3,128,128]{2,3,1,0:T(8,128)(2,1)}), bf16[32,3,128,128]{2,3,1,0:T(8,128)(2,1)}, u32[]{:S(2)}, u32[]{:S(2)}) async-start(bf16[32,3,128,128]{2,3,1,0:T(8,128)(2,1)} %broadcast_select_fusion.6), calls=%async_computation | async-start | bytes 6291456 | tf_op jit(solution)/shard_map/all_to_all | solution.py:83
  71.9 3.2 copy-start.3
  76.1 72.4 %copy-start.15 = (s32[32,1]{0,1:T(1,128)S(1)}, s32[32,1]{0,1:T(1,128)}, u32[]{:S(2)}) copy-start(s32[32,1]{0,1:T(1,128)} %param.27) | copy-start | bytes 388
  219.3 1.0 copy-start.1
  669.5 8.2 copy-start.17
  669.5 100.2 %all-to-all-start.3 = ((bf16[32,3,16384]{2,1,0:T(4,128)(2,1)}), bf16[32,3,16384]{2,1,0:T(4,128)(2,1)}, u32[]{:S(2)}, u32[]{:S(2)}) async-start(bf16[32,3,16384]{2,1,0:T(4,128)(2,1)} %reshape.354), calls=%async_computation.3 | async-start | bytes 8388608 | tf_op jit(solution)/shard_map/all_to_all | solution.py:140
  769.6 48.3 %all-to-all-start.1 = ((bf16[8,512,64]{1,2,0:T(8,128)(2,1)}), bf16[8,512,64]{1,2,0:T(8,128)(2,1)S(1)}, u32[]{:S(2)}, u32[]{:S(2)}) async-start(bf16[8,512,64]{1,2,0:T(8,128)(2,1)} %reshape.350), calls=%async_computation.1 | async-start | bytes 1048576 | tf_op jit(solution)/shard_map/all_to_all | solution.py:106
  796.6 4.2 copy-start.5
  817.9 5.0 copy-start.4
  817.9 25.6 %all-to-all-start.4 = ((bf16[8,512,192]{1,2,0:T(8,128)(2,1)}), bf16[8,512,192]{1,2,0:T(8,128)(2,1)}, u32[]{:S(2)}, u32[]{:S(2)}) async-start(bf16[8,512,192]{1,2,0:T(8,128)(2,1)} %copy.169), calls=%async_computation.4 | async-start | bytes 3145728 | tf_op jit(solution)/shard_map/all_to_all | solution.py:151
  822.9 20.7 %copy-start.7 = (bf16[8,512,3,64]{1,3,2,0:T(8,128)(2,1)S(1)}, bf16[8,512,3,64]{1,3,2,0:T(8,128)(2,1)}, u32[]{:S(2)}) copy-start(bf16[8,512,3,64]{1,3,2,0:T(8,128)(2,1)} %copy-done.6) | copy-start | bytes 4718596
  822.9 20.7 %copy-start.13 = (f32[512]{0:T(512)S(1)}, f32[512]{0:T(512)}, u32[]{:S(2)}) copy-start(f32[512]{0:T(512)} %copy-done.12) | copy-start | bytes 6148
  822.9 20.7 %copy-start.14 = (f32[512]{0:T(512)S(1)}, f32[512]{0:T(512)}, u32[]{:S(2)}) copy-start(f32[512]{0:T(512)} %param.20) | copy-start | bytes 6148
  824.2 21.9 %copy-start.10 = (bf16[512,512]{1,0:T(8,128)(2,1)S(1)}, bf16[512,512]{1,0:T(8,128)(2,1)}, u32[]{:S(2)}) copy-start(bf16[512,512]{1,0:T(8,128)(2,1)} %param.23) | copy-start | bytes 1572868
Sparse Core Ops, SparseCore 0:
  11.4 38.8 all-gather.1
where the time goes:
time: 862 us; the launch traced here: 854 us
  local copies, waits for them, and re-layouts  348 us (40%)
  waiting for transfers between devices  199 us (23%)
  other arithmetic  184 us (21%)
  matrix products  69.7 us (8%)
  starting transfers between devices  38.5 us (4%)
  between operations  14.3 us (2%)
    all_to_all x1, waiting for transfers between devices, local(): lax.all_to_all(far_sum.astype(bf16).reshape(ndom, pair_slots, flat), 'dom...  84.1 us
    all_to_all x1, waiting for transfers between devices, local(): lax.all_to_all(outgoing, 'dom', split_axis=0, concat_axis=0, tiled=True)  67.7 us
    scatter-add x8, other arithmetic, backward(): far_sum.at[remote_ids.reshape(-1)]  62.5 us
    transpose x8, local copies, waits for them, and re-layouts, backward(): jnp.einsum('tqbpkc,tqbpe->qkctpe', left, right, preferred_element_type=f32)  53.7 us
    reshape x8, local copies, waits for them, and re-layouts, backward(): d_pair = d_pair.reshape(STEP_BLOCKS, near_count + far_count, flat)  52.2 us
    gather x32, local copies, waits for them, and re-layouts, fetch_keys(): far = jnp.take(pool, remote_ids, axis=0)  50.9 us
    slice x8, local copies, waits for them, and re-layouts, backward(): d_pair[:, near_count:].reshape(-1, flat)  31.4 us
    gather x32, local copies, waits for them, and re-layouts, fetch_keys(): near = jnp.take(kv_blocks, local_ids, axis=0)  30.5 us
  transfers between devices with their start and end apart: 6, of which 4 were waited for; matrix products, arithmetic and copies ran while one was open for 8% of the time, Pallas kernels for 0%

commit v1 on v0

v1 whole, which is shorter than its diff:
```python
import math

import jax
import jax.numpy as jnp
from jax import lax
from jax.experimental import pallas as pl
from jax.experimental.pallas import tpu as pltpu
from jax.sharding import PartitionSpec as P

HEADS = 8
EPS = 1e-05


def attention_kernel(
    lk_ref, rk_ref, q_ref, do_ref, kl_ref, vl_ref, kp_ref, vp_ref, bias_ref,
    o_ref, dq_ref, dkl_ref, dvl_ref, dkp_ref, dvp_ref, *, near, far, bsize, scale
):
    f32 = jnp.float32
    bf16 = jnp.bfloat16
    nq = q_ref.shape[0]
    dkl_ref[...] = jnp.zeros(dkl_ref.shape, f32)
    dvl_ref[...] = jnp.zeros(dvl_ref.shape, f32)
    dkp_ref[...] = jnp.zeros(dkp_ref.shape, f32)
    dvp_ref[...] = jnp.zeros(dvp_ref.shape, f32)

    def body(b, carry):
        q = q_ref[b]
        do = do_ref[b]
        ids_l = [lk_ref[b * near + i] for i in range(near)]
        ids_r = [rk_ref[b * far + i] for i in range(far)]
        keys = jnp.concatenate([kl_ref[i] for i in ids_l] + [kp_ref[i] for i in ids_r], axis=0)
        vals = jnp.concatenate([vl_ref[i] for i in ids_l] + [vp_ref[i] for i in ids_r], axis=0)
        s = lax.dot_general(q, keys, (((1,), (1,)), ((), ())), preferred_element_type=f32) * scale
        s = s + bias_ref[b]
        top = jnp.max(s, axis=1, keepdims=True)
        expo = jnp.exp(s - top)
        total = jnp.sum(expo, axis=1, keepdims=True)
        w = (expo / total).astype(bf16)
        o = jnp.dot(w, vals, preferred_element_type=f32).astype(bf16)
        o_ref[b] = o
        delta = jnp.sum(do.astype(f32) * o.astype(f32), axis=1, keepdims=True)
        dw = lax.dot_general(do, vals, (((1,), (1,)), ((), ())), preferred_element_type=f32)
        ds = (w.astype(f32) * (dw - delta) * scale).astype(bf16)
        dq_ref[b] = jnp.dot(ds, keys, preferred_element_type=f32)
        dk = lax.dot_general(ds, q, (((0,), (0,)), ((), ())), preferred_element_type=f32)
        dv = lax.dot_general(w, do, (((0,), (0,)), ((), ())), preferred_element_type=f32)
        for i in range(near):
            part = slice(i * bsize, (i + 1) * bsize)
            dkl_ref[ids_l[i]] = dkl_ref[ids_l[i]] + dk[part]
            dvl_ref[ids_l[i]] = dvl_ref[ids_l[i]] + dv[part]
        for i in range(far):
            part = slice((near + i) * bsize, (near + i + 1) * bsize)
            dkp_ref[ids_r[i]] = dkp_ref[ids_r[i]] + dk[part]
            dvp_ref[ids_r[i]] = dvp_ref[ids_r[i]] + dv[part]
        return carry

    lax.fori_loop(0, nq, body, 0)


def fused_attention(local_ids, remote_ids, q, d_out, k_loc, v_loc, k_pool, v_pool, bias, scale):
    nq, bsize, depth = q.shape
    near = local_ids.size // nq
    far = remote_ids.size // nq
    nloc = k_loc.shape[0]
    npool = k_pool.shape[0]
    f32 = jnp.float32
    smem = pl.BlockSpec(memory_space=pltpu.SMEM)
    vmem = pl.BlockSpec(memory_space=pltpu.VMEM)
    kernel = lambda *refs: attention_kernel(
        *refs, near=near, far=far, bsize=bsize, scale=scale
    )
    return pl.pallas_call(
        kernel,
        out_shape=(
            jax.ShapeDtypeStruct((nq, bsize, depth), jnp.bfloat16),
            jax.ShapeDtypeStruct((nq, bsize, depth), f32),
            jax.ShapeDtypeStruct((nloc, bsize, depth), f32),
            jax.ShapeDtypeStruct((nloc, bsize, depth), f32),
            jax.ShapeDtypeStruct((npool, bsize, depth), f32),
            jax.ShapeDtypeStruct((npool, bsize, depth), f32),
        ),
        in_specs=[smem, smem] + [vmem] * 7,
        out_specs=tuple([vmem] * 6),
        compiler_params=pltpu.CompilerParams(vmem_limit_bytes=60 * 1024 * 1024),
    )(local_ids, remote_ids, q, d_out, k_loc, v_loc, k_pool, v_pool, bias)


def local(
    features,
    norm_gain,
    w_qkv,
    w_out,
    grad_y,
    local_keys,
    remote_keys,
    boundary_blocks,
    boundary_count,
):
    f32 = jnp.float32
    bf16 = jnp.bfloat16
    nhead = lax.axis_size("head")
    rows, width = features.shape
    per = HEADS // nhead
    depth = width // HEADS
    hwide = per * depth
    nblk, near_count = local_keys.shape
    far_count = remote_keys.shape[1]
    ndom = boundary_blocks.shape[1]
    pair_slots = boundary_blocks.shape[2]
    slots = ndom * pair_slots
    grows = rows * nhead
    bsize = grows // nblk
    score_scale = 1.0 / math.sqrt(depth)

    xf = features.astype(f32)
    inv = lax.rsqrt(jnp.mean(xf * xf, axis=1, keepdims=True) + EPS)
    normed = xf * inv
    hidden = (normed * norm_gain).astype(bf16)
    w_heads = (
        w_qkv.reshape(width, 3, nhead, hwide).transpose(0, 2, 1, 3).reshape(width, 3 * width)
    )
    qkv_own = jnp.dot(hidden, w_heads, preferred_element_type=f32).astype(bf16)
    qkv = lax.all_to_all(
        qkv_own.reshape(rows, nhead, 3 * hwide), "head", split_axis=1, concat_axis=0, tiled=True
    ).reshape(nblk, bsize, 3, hwide)
    queries = qkv[:, :, 0]
    kv_blocks = qkv[:, :, 1:]

    d_attn = jnp.dot(grad_y, w_out.T, preferred_element_type=f32).astype(bf16)
    d_group = lax.all_to_all(
        d_attn.reshape(rows, nhead, hwide), "head", split_axis=1, concat_axis=0, tiled=True
    ).reshape(nblk, bsize, hwide)

    send_ids = boundary_blocks[0]
    outgoing = jnp.take(kv_blocks, send_ids.reshape(-1), axis=0)
    pool = lax.all_to_all(
        outgoing.reshape(ndom, pair_slots, bsize, 2, hwide),
        "dom",
        split_axis=0,
        concat_axis=0,
        tiled=True,
    ).reshape(slots, bsize, 2, hwide)
    slot_alive = (jnp.arange(pair_slots, dtype=jnp.int32)[None, :] < boundary_count).reshape(slots)
    remote_alive = jnp.take(slot_alive, remote_keys, axis=0)
    bias_far = jnp.where(remote_alive, 0.0, -jnp.inf).astype(f32)
    bias = jnp.concatenate(
        [jnp.zeros((nblk, near_count), f32), bias_far], axis=1
    )
    bias = jnp.repeat(bias, bsize, axis=1).reshape(nblk, 1, (near_count + far_count) * bsize)

    o, d_q, dk_loc, dv_loc, dk_pool, dv_pool = fused_attention(
        local_keys.reshape(-1),
        remote_keys.reshape(-1),
        queries,
        d_group,
        kv_blocks[:, :, 0],
        kv_blocks[:, :, 1],
        pool[:, :, 0],
        pool[:, :, 1],
        bias,
        score_scale,
    )

    attn = lax.all_to_all(
        o.reshape(grows, hwide), "head", split_axis=0, concat_axis=1, tiled=True
    )
    mixed_out = (xf + jnp.dot(attn, w_out, preferred_element_type=f32)).astype(bf16)

    slot_grads = jnp.stack([dk_pool, dv_pool], axis=2).astype(bf16)
    returned = lax.all_to_all(
        slot_grads.reshape(ndom, pair_slots, bsize * 2 * hwide),
        "dom",
        split_axis=0,
        concat_axis=0,
        tiled=True,
    ).reshape(slots, bsize * 2 * hwide)
    onehot = (
        send_ids.reshape(1, slots) == jnp.arange(nblk, dtype=jnp.int32)[:, None]
    ).astype(bf16)
    d_kv = jnp.stack([dk_loc, dv_loc], axis=2).reshape(nblk, bsize * 2 * hwide) + jnp.dot(
        onehot, returned, preferred_element_type=f32
    )
    d_qkv = jnp.concatenate(
        [d_q.reshape(nblk, bsize, 1, hwide), d_kv.reshape(nblk, bsize, 2, hwide)], axis=2
    ).astype(bf16)
    d_rows = lax.all_to_all(
        d_qkv.reshape(grows, 3 * hwide), "head", split_axis=0, concat_axis=1, tiled=True
    )
    d_hidden = jnp.dot(d_rows, w_heads.T, preferred_element_type=f32)
    d_normed = d_hidden * norm_gain
    d_input = inv * (d_normed - normed * jnp.mean(d_normed * normed, axis=1, keepdims=True))
    grad_x = (grad_y.astype(f32) + d_input).astype(bf16)
    return (mixed_out, grad_x)


def solution(mesh):
    return jax.shard_map(
        local,
        mesh=mesh,
        in_specs=(
            P(("dom", "head"), None),
            P(),
            P(),
            P(),
            P(("dom", "head"), None),
            P("dom", None),
            P("dom", None),
            P("dom", None, None),
            P(None, "dom"),
        ),
        out_specs=(P(("dom", "head"), None), P(("dom", "head"), None)),
        check_vma=False,
    )
```

time: 862 us -> 394 us (0.46)
  local copies, waits for them, and re-layouts: 348 us -> 97.3 us
  other arithmetic: 184 us -> 22.2 us
  matrix products: 69.7 us -> 10.6 us
  Pallas kernels: 0 us -> 44.4 us
  waiting for transfers between devices: 199 us -> 171 us
  between operations: 14.3 us -> 0.92 us
    scatter-add x17 -> x0, other arithmetic: 98.4 us -> none  [the longest x8 62.5 us: backward(): far_sum.at[remote_ids.reshape(-1)]]
    gather x97 -> x4, local copies, waits for them, and re-layouts: 96.1 us -> 4.15 us  [the longest x1 2.72 us: local(): outgoing = jnp.take(kv_blocks, send_ids.reshape(-1), axis=0)]
    reshape x45 -> x7, local copies, waits for them, and re-layouts: 112 us -> 22.8 us  [the longest x1 5.71 us: local(): returned = lax.all_to_all(slot_grads.reshape(ndom, pair_slots, bsize * 2...]
    dot_general x52 -> x5, matrix products: 69.7 us -> 10.6 us  [the longest x1 3.44 us: local(): jnp.dot(onehot, returned, preferred_element_type=f32)]
    transpose x9 -> x1, local copies, waits for them, and re-layouts: 55.2 us -> 0.15 us  [local(): w_qkv.reshape(width, 3, nhead, hwide).transpose(0, 2, 1, 3)]
    pallas_call x0 -> x1, Pallas kernels: none -> 44.4 us  [fused_attention(): pl.pallas_call(kernel, out_shape=(jax.ShapeDtypeStruct((nq, bsize, depth)...]
    slice x10 -> x2, local copies, waits for them, and re-layouts: 32.5 us -> 1.18 us  [the longest x1 1.11 us: local(): kv_blocks[:, :, 1]]
    all_gather x1 -> x0, waiting for transfers between devices: 27.6 us -> none  [local(): lax.all_gather(hidden, 'head', axis=0, tiled=True)]
  transfers between devices with their start and end apart: 6 -> 6, of which waited for: 4 -> 4; matrix products, arithmetic and copies ran while one was open for 8% -> 19% of each run, Pallas kernels for 0% -> 0%
where the time goes in v1:
time: 394 us; the launch traced here: 392 us
  waiting for transfers between devices  171 us (43%)
  local copies, waits for them, and re-layouts  97.3 us (25%)
  starting transfers between devices  45.4 us (12%)
  Pallas kernels  44.4 us (11%)
  other arithmetic  22.2 us (6%)
  matrix products  10.6 us (3%)
    all_to_all x1, waiting for transfers between devices, local(): lax.all_to_all(slot_grads.reshape(ndom, pair_slots, bsize * 2 * hwide), '...  76.3 us
    all_to_all x1, waiting for transfers between devices, local(): lax.all_to_all(outgoing.reshape(ndom, pair_slots, bsize, 2, hwide), 'dom'...  57.8 us
    pallas_call x1, Pallas kernels, fused_attention(): pl.pallas_call(kernel, out_shape=(jax.ShapeDtypeStruct((nq, bsize, depth)...  44.4 us
    all_to_all x1, waiting for transfers between devices, local(): lax.all_to_all(qkv_own.reshape(rows, nhead, 3 * hwide), 'head', split_axi...  19 us
    all_to_all x1, waiting for transfers between devices, local(): lax.all_to_all(d_qkv.reshape(grows, 3 * hwide), 'head', split_axis=0, con...  18.3 us
    convert_element_type x1, local copies, waits for them, and re-layouts, local(): slot_grads = jnp.stack([dk_pool, dv_pool], axis=2).astype(bf16)  13.8 us
    all_to_all x1, starting transfers between devices, local(): lax.all_to_all(outgoing.reshape(ndom, pair_slots, bsize, 2, hwide), 'dom'...  10.7 us
    unnamed x41, local copies, waits for them, and re-layouts  9.68 us
  transfers between devices with their start and end apart: 6, of which 4 were waited for; matrix products, arithmetic and copies ran while one was open for 19% of the time, Pallas kernels for 0%

profile of v1, /device:TPU:1, one launch (start us, length us, event | category | flops | bytes accessed | tf_op | source)
XLA Modules:
  0.0 392.4 jit_solution(27199448546601467)
XLA Ops:
  0.6 1.3 fusion.11
  2.0 1.8 copy.135
  3.7 0.2 copy.136
  3.9 1.2 copy-done.2
  5.1 1.0 convolution_convert_fusion
  6.2 1.6 copy.137
  7.8 6.7 %all-to-all-start = ((bf16[512,8,192]{0,2,1:T(8,128)(2,1)}), bf16[512,8,192]{0,2,1:T(8,128)(2,1)S(1)}, u32[]{:S(2)}, u32[]{:S(2)}) async-start(bf16[512,8,192]{0,2,1:T(8,128)(2,1)} %bitcast.60), calls=%async_computation | async-start | bytes 3145728 | tf_op jit(solution)/shard_map/all_to_all | solution.py:123
  14.5 0.1 copy.145
  14.6 0.1 copy.143
  14.7 0.1 reshape_squeeze.9
  14.8 1.3 convolution_convert_fusion.1
  16.1 19.0 %all-to-all-done = bf16[512,8,192]{0,2,1:T(8,128)(2,1)S(1)} async-done(((bf16[512,8,192]{0,2,1:T(8,128)(2,1)}), bf16[512,8,192]{0,2,1:T(8,128)(2,1)S(1)}, u32[]{:S(2)}, u32[]{:S(2)}) %all-to-all-start) | async-done | bytes 1572896 | tf_op jit(solution)/shard_map/all_to_all | solution.py:123
  35.1 5.0 %all-to-all-start.1 = ((bf16[512,8,64]{0,2,1:T(8,128)(2,1)}), bf16[512,8,64]{0,2,1:T(8,128)(2,1)}, u32[]{:S(2)}, u32[]{:S(2)}) async-start(bf16[512,8,64]{0,2,1:T(8,128)(2,1)} %bitcast.7), calls=%async_computation.1 | async-start | bytes 1048576 | tf_op jit(solution)/shard_map/all_to_all | solution.py:130
  40.1 2.0 copy.138
  42.1 2.7 reshape.128
  44.9 0.4 copy.165
  45.4 2.7 gather_fusion
  48.1 3.9 broadcast_select_fusion
  52.0 10.7 %all-to-all-start.2 = ((bf16[32,3,128,2,64]{2,4,3,1,0:T(8,128)(2,1)}), bf16[32,3,128,2,64]{2,4,3,1,0:T(8,128)(2,1)}, u32[]{:S(2)}, u32[]{:S(2)}) async-start(bf16[32,3,128,2,64]{2,4,3,1,0:T(8,128)(2,1)} %broadcast_select_fusion), calls=%async_computation.2 | async-start | bytes 6291456 | tf_op jit(solution)/shard_map/all_to_all | solution.py:136
  62.8 0.1 lt.59
  62.9 0.1 copy.134
  63.0 0.1 copy.147
  63.1 0.1 reshape.146
  63.2 1.2 gather_fusion.1
  64.5 0.1 reshape.145
  64.6 0.1 copy.148
  64.7 0.1 copy.166
  64.9 0.6 reshape.123.refs_0_
  65.5 0.6 reshape.124.refs_1_
  66.2 2.4 copy.140
  68.6 1.1 fusion.17
  69.7 2.6 copy.164
  72.3 1.7 copy.163
  73.9 1.6 copy.162
  75.5 57.8 %all-to-all-done.2 = bf16[32,3,128,2,64]{2,4,3,1,0:T(8,128)(2,1)} async-done(((bf16[32,3,128,2,64]{2,4,3,1,0:T(8,128)(2,1)}), bf16[32,3,128,2,64]{2,4,3,1,0:T(8,128)(2,1)}, u32[]{:S(2)}, u32[]{:S(2)}) %all-to-all-start.2) | async-done | bytes 3145760 | tf_op jit(solution)/shard_map/all_to_all | solution.py:136
  133.3 6.6 %copy.146 = bf16[32,3,128,2,64]{4,2,1,0,3:T(8,128)(2,1)} copy(bf16[32,3,128,2,64]{2,4,3,1,0:T(8,128)(2,1)} %all-to-all-done.2) | data formatting | bytes 6291456 | tf_op jit(solution)/shard_map/all_to_all | solution.py:136
  139.9 8.1 %slice_bitcast_fusion = (bf16[96,128,64]{2,1,0:T(8,128)(2,1)}, bf16[96,128,64]{2,1,0:T(8,128)(2,1)}) fusion(bf16[96,128,2,64]{3,1,0,2:T(8,128)(2,1)} %bitcast.58), kind=kLoop, calls=%fused_computation.7 | loop fusion | bytes 6291456 | tf_op jit(solution)/shard_map/squeeze | solution.py:159
  148.0 0.8 broadcast_in_dim.42
  148.7 44.4 %shard_map.104 = (bf16[32,128,64]{2,1,0:T(8,128)(2,1)}, f32[32,128,64]{2,1,0:T(8,128)}, f32[32,128,64]{2,1,0:T(8,128)}, f32[32,128,64]{2,1,0:T(8,128)}, f32[96,128,64]{2,1,0:T(8,128)}, /*index=5*/f32[96,128,64]{2,1,0:T(8,128)}) custom-call(s32[128]{0:T(128)} %reshape.123.refs_0_, s32[128]{0:T(128)} %reshape.124.refs_1_, bf16[32,128,64]{2,1,0:T(8,128)(2,1)} %bitcast.67, ...), custom_call_target="tpu_custom_call" | custom-call | tf_op jit(solution)/shard_map/pallas_call | solution.py:72
  193.2 6.2 %convert_bitcast_fusion = (bf16[96,128,1,64]{3,1,0,2:T(8,128)(2,1)S(1)}, bf16[96,128,1,64]{3,1,0,2:T(8,128)(2,1)S(1)}) fusion(f32[96,128,64]{2,1,0:T(8,128)} %get-tuple-element.13, f32[96,128,64]{2,1,0:T(8,128)} %get-tuple-element.12), kind=kLoop, calls=%fused_computation.9 | loop fusion | flops 1572864 | bytes 9437184 | tf_op jit(solution)/shard_map/stack | solution.py:169
  199.4 1.4 pad_maximum_fusion
  200.8 6.1 %copy.153 = bf16[96,128,2,64]{3,2,1,0:T(2,128)(2,1)} copy(bf16[96,128,2,64]{3,1,0,2:T(8,128)(2,1)S(1)} %pad_maximum_fusion) | data formatting | bytes 6291456 | tf_op jit(solution)/shard_map/stack | solution.py:169
  206.9 13.8 %convert_element_type.39 = bf16[32,3,16384]{2,1,0:T(4,128)(2,1)} reshape(bf16[96,128,2,64]{3,2,1,0:T(2,128)(2,1)} %copy.153) | data formatting | bytes 6291456 | tf_op jit(solution)/shard_map/convert_element_type | solution.py:169
  220.8 8.9 %all-to-all-start.4 = ((bf16[32,3,16384]{2,1,0:T(4,128)(2,1)}), bf16[32,3,16384]{2,1,0:T(4,128)(2,1)}, u32[]{:S(2)}, u32[]{:S(2)}) async-start(bf16[32,3,16384]{2,1,0:T(4,128)(2,1)} %convert_element_type.39), calls=%async_computation.4 | async-start | bytes 8388608 | tf_op jit(solution)/shard_map/all_to_all | solution.py:170
  229.7 0.1 reshape_squeeze.10
  229.8 2.3 copy.150
  232.2 0.2 convert_bitcast_fusion.2
  232.4 3.4 copy.154
  235.8 0.5 pad_maximum_fusion.1
  236.3 5.3 %copy.151 = f32[32,128,2,64]{3,2,1,0:T(2,128)} copy(f32[32,128,2,64]{3,1,0,2:T(8,128)S(1)} %pad_maximum_fusion.1) | data formatting | bytes 4194304 | tf_op jit(solution)/shard_map/stack | solution.py:180
  241.7 5.5 %reshape.133 = f32[32,16384]{1,0:T(8,128)S(1)} reshape(f32[32,128,2,64]{3,2,1,0:T(2,128)} %copy.151) | data formatting | bytes 4194304 | tf_op jit(solution)/shard_map/reshape | solution.py:180
  247.2 76.3 %all-to-all-done.4 = bf16[32,3,16384]{2,1,0:T(4,128)(2,1)} async-done(((bf16[32,3,16384]{2,1,0:T(4,128)(2,1)}), bf16[32,3,16384]{2,1,0:T(4,128)(2,1)}, u32[]{:S(2)}, u32[]{:S(2)}) %all-to-all-start.4) | async-done | bytes 3145760 | tf_op jit(solution)/shard_map/all_to_all | solution.py:170
  323.5 9.2 %all-to-all-start.3 = ((bf16[8,512,64]{1,2,0:T(8,128)(2,1)}), bf16[8,512,64]{1,2,0:T(8,128)(2,1)}, u32[]{:S(2)}, u32[]{:S(2)}) async-start(bf16[8,512,64]{1,2,0:T(8,128)(2,1)} %copy.150), calls=%async_computation.3 | async-start | bytes 1048576 | tf_op jit(solution)/shard_map/all_to_all | solution.py:164
  332.7 5.7 %reshape.134 = bf16[96,16384]{1,0:T(8,128)(2,1)} reshape(bf16[32,3,16384]{2,1,0:T(4,128)(2,1)} %all-to-all-done.4) | data formatting | bytes 6291456 | tf_op jit(solution)/shard_map/reshape | solution.py:176
  338.4 3.4 fusion
  341.9 4.2 %reshape.135 = bf16[32,128,2,64]{3,2,1,0:T(2,128)(2,1)} reshape(bf16[32,16384]{1,0:T(8,128)(2,1)} %fusion) | data formatting | bytes 2097152 | tf_op jit(solution)/shard_map/reshape | solution.py:184
  346.0 7.5 %pad_maximum_fusion.2 = bf16[32,128,3,64]{3,2,1,0:T(4,128)(2,1)} fusion(bf16[32,128,2,64]{3,2,1,0:T(2,128)(2,1)} %reshape.135, bf16[32,128,1,64]{3,2,1,0:T(2,128)(2,1)S(1)} %copy-done.1), kind=kLoop, calls=%fused_computation.6 | loop fusion | flops 3145728 | bytes 3145728 | tf_op jit(solution)/shard_map/concatenate | solution.py:183
  353.5 7.2 %reshape.154 = bf16[8,512,192]{2,1,0:T(8,128)(2,1)S(1)} reshape(bf16[32,128,3,64]{3,2,1,0:T(4,128)(2,1)} %pad_maximum_fusion.2) | data formatting | bytes 3145728 | tf_op jit(solution)/shard_map/convert_element_type | solution.py:185
  360.8 2.3 copy.156
  363.1 4.9 %all-to-all-start.5 = ((bf16[8,512,192]{1,2,0:T(8,128)(2,1)}), bf16[8,512,192]{1,2,0:T(8,128)(2,1)}, u32[]{:S(2)}, u32[]{:S(2)}) async-start(bf16[8,512,192]{1,2,0:T(8,128)(2,1)} %copy.156), calls=%async_computation.5 | async-start | bytes 3145728 | tf_op jit(solution)/shard_map/all_to_all | solution.py:186
  368.0 2.4 fusion.4
  370.4 18.3 %all-to-all-done.5 = bf16[8,512,192]{1,2,0:T(8,128)(2,1)} async-done(((bf16[8,512,192]{1,2,0:T(8,128)(2,1)}), bf16[8,512,192]{1,2,0:T(8,128)(2,1)}, u32[]{:S(2)}, u32[]{:S(2)}) %all-to-all-start.5) | async-done | bytes 1572896 | tf_op jit(solution)/shard_map/all_to_all | solution.py:186
  388.7 2.5 fusion.6
  391.2 1.1 fusion.10
  (45 shorter events, 0.4 us)
Async XLA Ops:
  0.6 14.2 %copy-start = (bf16[512,512]{1,0:T(8,128)(2,1)S(1)}, bf16[512,512]{1,0:T(8,128)(2,1)}, u32[]{:S(2)}) copy-start(bf16[512,512]{1,0:T(8,128)(2,1)} %param.12) | copy-start | bytes 1572868
  1.9 3.2 copy-start.4
  1.9 3.2 copy-start.11
  3.9 1.2 copy-start.2
  6.2 8.3 %copy-start.13 = (s32[1,32,3]{1,0,2:T(1,128)S(1)}, s32[1,32,3]{1,0,2:T(1,128)}, u32[]{:S(2)}) copy-start(s32[1,32,3]{1,0,2:T(1,128)} %param.16) | copy-start | bytes 1156
  6.2 8.6 %copy-start.6 = (bf16[512,512]{1,0:T(8,128)(2,1)S(1)}, bf16[512,512]{1,0:T(8,128)(2,1)}, u32[]{:S(2)}) copy-start(bf16[512,512]{1,0:T(8,128)(2,1)} %param.13) | copy-start | bytes 1572868
  7.8 27.3 %all-to-all-start = ((bf16[512,8,192]{0,2,1:T(8,128)(2,1)}), bf16[512,8,192]{0,2,1:T(8,128)(2,1)S(1)}, u32[]{:S(2)}, u32[]{:S(2)}) async-start(bf16[512,8,192]{0,2,1:T(8,128)(2,1)} %bitcast.60), calls=%async_computation | async-start | bytes 3145728 | tf_op jit(solution)/shard_map/all_to_all | solution.py:123
  35.1 16.9 %all-to-all-start.1 = ((bf16[512,8,64]{0,2,1:T(8,128)(2,1)}), bf16[512,8,64]{0,2,1:T(8,128)(2,1)}, u32[]{:S(2)}, u32[]{:S(2)}) async-start(bf16[512,8,64]{0,2,1:T(8,128)(2,1)} %bitcast.7), calls=%async_computation.1 | async-start | bytes 1048576 | tf_op jit(solution)/shard_map/all_to_all | solution.py:130
  52.0 10.8 %copy-start.15 = (s32[32,1]{0,1:T(1,128)S(1)}, s32[32,1]{0,1:T(1,128)}, u32[]{:S(2)}) copy-start(s32[32,1]{0,1:T(1,128)} %param.17) | copy-start | bytes 388
  52.0 10.9 %copy-start.12 = (s32[32,4]{0,1:T(4,128)S(1)}, s32[32,4]{0,1:T(4,128)}, u32[]{:S(2)}) copy-start(s32[32,4]{0,1:T(4,128)} %param.15) | copy-start | bytes 1540
  52.0 81.4 %all-to-all-start.2 = ((bf16[32,3,128,2,64]{2,4,3,1,0:T(8,128)(2,1)}), bf16[32,3,128,2,64]{2,4,3,1,0:T(8,128)(2,1)}, u32[]{:S(2)}, u32[]{:S(2)}) async-start(bf16[32,3,128,2,64]{2,4,3,1,0:T(8,128)(2,1)} %broadcast_select_fusion), calls=%async_computation.2 | async-start | bytes 6291456 | tf_op jit(solution)/shard_map/all_to_all | solution.py:136
  62.7 2.1 copy-start.14
  220.8 11.4 %copy-start.8 = (f32[32,128,64]{2,1,0:T(8,128)S(1)}, f32[32,128,64]{2,1,0:T(8,128)}, u32[]{:S(2)}) copy-start(f32[32,128,64]{2,1,0:T(8,128)} %get-tuple-element.9) | copy-start | bytes 3145732
  220.8 102.7 %all-to-all-start.4 = ((bf16[32,3,16384]{2,1,0:T(4,128)(2,1)}), bf16[32,3,16384]{2,1,0:T(4,128)(2,1)}, u32[]{:S(2)}, u32[]{:S(2)}) async-start(bf16[32,3,16384]{2,1,0:T(4,128)(2,1)} %convert_element_type.39), calls=%async_computation.4 | async-start | bytes 8388608 | tf_op jit(solution)/shard_map/all_to_all | solution.py:170
  232.2 3.6 copy-start.9
  232.2 3.6 copy-start.10
  323.5 39.6 %all-to-all-start.3 = ((bf16[8,512,64]{1,2,0:T(8,128)(2,1)}), bf16[8,512,64]{1,2,0:T(8,128)(2,1)}, u32[]{:S(2)}, u32[]{:S(2)}) async-start(bf16[8,512,64]{1,2,0:T(8,128)(2,1)} %copy.150), calls=%async_computation.3 | async-start | bytes 1048576 | tf_op jit(solution)/shard_map/all_to_all | solution.py:164
  341.9 4.2 %copy-start.1 = (bf16[32,128,1,64]{3,2,1,0:T(2,128)(2,1)S(1)}, bf16[32,128,1,64]{3,2,1,0:T(2,128)(2,1)}, u32[]{:S(2)}) copy-start(bf16[32,128,1,64]{3,2,1,0:T(2,128)(2,1)} %copy.154) | copy-start | bytes 1572868
  360.8 7.2 %copy-start.5 = (bf16[512,512]{1,0:T(8,128)(2,1)S(1)}, bf16[512,512]{1,0:T(8,128)(2,1)}, u32[]{:S(2)}) copy-start(bf16[512,512]{1,0:T(8,128)(2,1)} %param.9) | copy-start | bytes 1572868
  363.1 25.6 %copy-start.3 = (bf16[512,8,3,64]{0,3,2,1:T(8,128)(2,1)S(1)}, bf16[512,8,3,64]{0,3,2,1:T(8,128)(2,1)}, u32[]{:S(2)}) copy-start(bf16[512,8,3,64]{0,3,2,1:T(8,128)(2,1)} %copy-done.2) | copy-start | bytes 4718596
  363.1 25.6 %all-to-all-start.5 = ((bf16[8,512,192]{1,2,0:T(8,128)(2,1)}), bf16[8,512,192]{1,2,0:T(8,128)(2,1)}, u32[]{:S(2)}, u32[]{:S(2)}) async-start(bf16[8,512,192]{1,2,0:T(8,128)(2,1)} %copy.156), calls=%async_computation.5 | async-start | bytes 3145728 | tf_op jit(solution)/shard_map/all_to_all | solution.py:186
  368.0 23.2 %copy-start.7 = (bf16[512,512]{1,0:T(8,128)(2,1)S(1)}, bf16[512,512]{1,0:T(8,128)(2,1)}, u32[]{:S(2)}) copy-start(bf16[512,512]{1,0:T(8,128)(2,1)} %param.13) | copy-start | bytes 1572868

commit v2 on v1

v2 whole, which is shorter than its diff:
```python
import math

import jax
import jax.numpy as jnp
from jax import lax
from jax.experimental import pallas as pl
from jax.experimental.pallas import tpu as pltpu
from jax.sharding import PartitionSpec as P

HEADS = 8
EPS = 1e-05


def attention_kernel(
    lk_ref, rk_ref, qkv_ref, do_ref, pool_ref, bias_ref, o_ref, acc_ref, slot_ref, slot_acc,
    *, near, far, bsize, depth, scale
):
    f32 = jnp.float32
    bf16 = jnp.bfloat16
    nq = qkv_ref.shape[0]
    acc_ref[...] = jnp.zeros(acc_ref.shape, f32)
    slot_acc[...] = jnp.zeros(slot_acc.shape, f32)
    kcols = pl.ds(depth, depth)
    vcols = pl.ds(2 * depth, depth)
    pk = pl.ds(0, depth)
    pv = pl.ds(depth, depth)

    def body(b, carry):
        q = qkv_ref[b, :, pl.ds(0, depth)]
        do = do_ref[b]
        ids_l = [lk_ref[b * near + i] for i in range(near)]
        ids_r = [rk_ref[b * far + i] for i in range(far)]
        keys = jnp.concatenate(
            [qkv_ref[i, :, kcols] for i in ids_l] + [pool_ref[i, :, pk] for i in ids_r], axis=0
        )
        vals = jnp.concatenate(
            [qkv_ref[i, :, vcols] for i in ids_l] + [pool_ref[i, :, pv] for i in ids_r], axis=0
        )
        s = lax.dot_general(q, keys, (((1,), (1,)), ((), ())), preferred_element_type=f32) * scale
        s = s + bias_ref[b]
        top = jnp.max(s, axis=1, keepdims=True)
        expo = jnp.exp(s - top)
        total = jnp.sum(expo, axis=1, keepdims=True)
        w = (expo / total).astype(bf16)
        o = jnp.dot(w, vals, preferred_element_type=f32).astype(bf16)
        o_ref[b] = o
        delta = jnp.sum(do.astype(f32) * o.astype(f32), axis=1, keepdims=True)
        dw = lax.dot_general(do, vals, (((1,), (1,)), ((), ())), preferred_element_type=f32)
        ds = (w.astype(f32) * (dw - delta) * scale).astype(bf16)
        acc_ref[b, :, pl.ds(0, depth)] = jnp.dot(ds, keys, preferred_element_type=f32)
        dk = lax.dot_general(ds, q, (((0,), (0,)), ((), ())), preferred_element_type=f32)
        dv = lax.dot_general(w, do, (((0,), (0,)), ((), ())), preferred_element_type=f32)
        for i in range(near):
            part = slice(i * bsize, (i + 1) * bsize)
            acc_ref[ids_l[i], :, kcols] = acc_ref[ids_l[i], :, kcols] + dk[part]
            acc_ref[ids_l[i], :, vcols] = acc_ref[ids_l[i], :, vcols] + dv[part]
        for i in range(far):
            part = slice((near + i) * bsize, (near + i + 1) * bsize)
            slot_acc[ids_r[i], :, pk] = slot_acc[ids_r[i], :, pk] + dk[part]
            slot_acc[ids_r[i], :, pv] = slot_acc[ids_r[i], :, pv] + dv[part]
        return carry

    lax.fori_loop(0, nq, body, 0)
    slot_ref[...] = slot_acc[...].astype(bf16)


def fused_attention(local_ids, remote_ids, qkv, d_out, pool, bias, scale):
    nq, bsize, depth = d_out.shape
    near = local_ids.size // nq
    far = remote_ids.size // nq
    npool = pool.shape[0]
    f32 = jnp.float32
    smem = pl.BlockSpec(memory_space=pltpu.SMEM)
    vmem = pl.BlockSpec(memory_space=pltpu.VMEM)
    kernel = lambda *refs: attention_kernel(
        *refs, near=near, far=far, bsize=bsize, depth=depth, scale=scale
    )
    return pl.pallas_call(
        kernel,
        out_shape=(
            jax.ShapeDtypeStruct((nq, bsize, depth), jnp.bfloat16),
            jax.ShapeDtypeStruct(qkv.shape, f32),
            jax.ShapeDtypeStruct(pool.shape, jnp.bfloat16),
        ),
        in_specs=[smem, smem] + [vmem] * 4,
        out_specs=(vmem, vmem, vmem),
        scratch_shapes=[pltpu.VMEM(pool.shape, f32)],
        compiler_params=pltpu.CompilerParams(vmem_limit_bytes=60 * 1024 * 1024),
    )(local_ids, remote_ids, qkv, d_out, pool, bias)


def finish_kernel(ids_ref, acc_ref, ret_ref, out_ref, total_ref, *, depth):
    width = ret_ref.shape[2]
    total_ref[...] = acc_ref[...]

    def body(j, carry):
        i = ids_ref[j]
        cols = pl.ds(depth, width)
        total_ref[i, :, cols] = total_ref[i, :, cols] + ret_ref[j].astype(jnp.float32)
        return carry

    lax.fori_loop(0, ret_ref.shape[0], body, 0)
    out_ref[...] = total_ref[...].astype(jnp.bfloat16)


def finish_grads(send_ids, acc, returned, depth):
    smem = pl.BlockSpec(memory_space=pltpu.SMEM)
    vmem = pl.BlockSpec(memory_space=pltpu.VMEM)
    return pl.pallas_call(
        lambda *refs: finish_kernel(*refs, depth=depth),
        out_shape=jax.ShapeDtypeStruct(acc.shape, jnp.bfloat16),
        in_specs=[smem, vmem, vmem],
        out_specs=vmem,
        scratch_shapes=[pltpu.VMEM(acc.shape, jnp.float32)],
        compiler_params=pltpu.CompilerParams(vmem_limit_bytes=60 * 1024 * 1024),
    )(send_ids, acc, returned)


def local(
    features,
    norm_gain,
    w_qkv,
    w_out,
    grad_y,
    local_keys,
    remote_keys,
    boundary_blocks,
    boundary_count,
):
    f32 = jnp.float32
    bf16 = jnp.bfloat16
    nhead = lax.axis_size("head")
    rows, width = features.shape
    per = HEADS // nhead
    depth = width // HEADS
    hwide = per * depth
    nblk, near_count = local_keys.shape
    far_count = remote_keys.shape[1]
    ndom = boundary_blocks.shape[1]
    pair_slots = boundary_blocks.shape[2]
    slots = ndom * pair_slots
    grows = rows * nhead
    bsize = grows // nblk
    score_scale = 1.0 / math.sqrt(depth)

    xf = features.astype(f32)
    inv = lax.rsqrt(jnp.mean(xf * xf, axis=1, keepdims=True) + EPS)
    normed = xf * inv
    hidden = (normed * norm_gain).astype(bf16)
    w_heads = (
        w_qkv.reshape(width, 3, nhead, hwide).transpose(2, 0, 1, 3).reshape(nhead, width, 3 * hwide)
    )
    w_out_heads = w_out.reshape(nhead, hwide, width)
    qkv_own = jnp.einsum("rd,hdc->hrc", hidden, w_heads, preferred_element_type=f32).astype(bf16)
    qkv = lax.all_to_all(qkv_own, "head", split_axis=0, concat_axis=0, tiled=True).reshape(
        nblk, bsize, 3 * hwide
    )

    d_attn = jnp.einsum("rf,hef->hre", grad_y, w_out_heads, preferred_element_type=f32).astype(bf16)
    d_group = lax.all_to_all(d_attn, "head", split_axis=0, concat_axis=0, tiled=True).reshape(
        nblk, bsize, hwide
    )

    send_ids = boundary_blocks[0].reshape(slots)
    outgoing = jnp.take(qkv[:, :, hwide:], send_ids, axis=0)
    pool = lax.all_to_all(
        outgoing.reshape(ndom, pair_slots * bsize, 2 * hwide),
        "dom",
        split_axis=0,
        concat_axis=0,
        tiled=True,
    ).reshape(slots, bsize, 2 * hwide)
    slot_alive = (jnp.arange(pair_slots, dtype=jnp.int32)[None, :] < boundary_count).reshape(slots)
    remote_alive = jnp.take(slot_alive, remote_keys, axis=0)
    bias_far = jnp.where(remote_alive, 0.0, -jnp.inf).astype(f32)
    bias = jnp.concatenate([jnp.zeros((nblk, near_count), f32), bias_far], axis=1)
    bias = jnp.repeat(bias, bsize, axis=1).reshape(nblk, 1, (near_count + far_count) * bsize)

    o, acc, slot_grads = fused_attention(
        local_keys.reshape(-1), remote_keys.reshape(-1), qkv, d_group, pool, bias, score_scale
    )

    attn = lax.all_to_all(
        o.reshape(nhead, rows, hwide), "head", split_axis=0, concat_axis=0, tiled=True
    )
    mixed_out = (
        xf + jnp.einsum("hre,hef->rf", attn, w_out_heads, preferred_element_type=f32)
    ).astype(bf16)

    returned = lax.all_to_all(
        slot_grads.reshape(ndom, pair_slots * bsize, 2 * hwide),
        "dom",
        split_axis=0,
        concat_axis=0,
        tiled=True,
    ).reshape(slots, bsize, 2 * hwide)
    d_qkv = finish_grads(send_ids, acc, returned, hwide)
    d_rows = lax.all_to_all(
        d_qkv.reshape(nhead, rows, 3 * hwide), "head", split_axis=0, concat_axis=0, tiled=True
    )
    d_hidden = jnp.einsum("hrc,hdc->rd", d_rows, w_heads, preferred_element_type=f32)
    d_normed = d_hidden * norm_gain
    d_input = inv * (d_normed - normed * jnp.mean(d_normed * normed, axis=1, keepdims=True))
    grad_x = (grad_y.astype(f32) + d_input).astype(bf16)
    return (mixed_out, grad_x)


def solution(mesh):
    return jax.shard_map(
        local,
        mesh=mesh,
        in_specs=(
            P(("dom", "head"), None),
            P(),
            P(),
            P(),
            P(("dom", "head"), None),
            P("dom", None),
            P("dom", None),
            P("dom", None, None),
            P(None, "dom"),
        ),
        out_specs=(P(("dom", "head"), None), P(("dom", "head"), None)),
        check_vma=False,
    )
```

time: 394 us -> 322 us (0.82)
  local copies, waits for them, and re-layouts: 97.3 us -> 25.3 us
  Pallas kernels: 44.4 us -> 58.6 us
  other arithmetic: 22.2 us -> 11.1 us
  matrix products: 10.6 us -> 6.22 us
    convert_element_type x4 -> x0, local copies, waits for them, and re-layouts: 25 us -> none  [the longest x1 13.8 us: local(): slot_grads = jnp.stack([dk_pool, dv_pool], axis=2).astype(bf16)]
    reshape x5 -> x2, local copies, waits for them, and re-layouts: 21.6 us -> 4.97 us  [the longest x1 3.84 us: local(): d_qkv.reshape(nhead, rows, 3 * hwide)]
    pallas_call x0 -> x1, Pallas kernels: none -> 12.8 us  [finish_grads(): pl.pallas_call(lambda *refs: finish_kernel(*refs, depth=depth), out_shape...]
    another operation x4 -> x2, local copies, waits for them, and re-layouts: 11.7 us -> 0.72 us  [local(): send_ids = boundary_blocks[0].reshape(slots)]
    another operation x3 -> x0, other arithmetic: 8.14 us -> none  [the longest x2 7.62 us: local(): slot_grads = jnp.stack([dk_pool, dv_pool], axis=2).astype(bf16)]
    squeeze x1 -> x0, local copies, waits for them, and re-layouts: 8.07 us -> none  [local(): pool[:, :, 1]]
    concatenate x1 -> x0, other arithmetic: 7.51 us -> none  [local(): jnp.concatenate([d_q.reshape(nblk, bsize, 1, hwide), d_kv.reshape(nblk, b...]
    all_to_all x4 -> x2, local copies, waits for them, and re-layouts: 13.3 us -> 6.13 us  [the longest x1 3.72 us: local(): lax.all_to_all(qkv_own, 'head', split_axis=0, concat_axis=0, tiled=True)]
  transfers between devices with their start and end apart: 6 -> 6, of which waited for: 4 -> 4; matrix products, arithmetic and copies ran while one was open for 19% -> 9% of each run, Pallas kernels for 0% -> 4%
where the time goes in v2:
time: 322 us; the launch traced here: 321 us
  waiting for transfers between devices  174 us (54%)
  Pallas kernels  58.6 us (18%)
  starting transfers between devices  45.1 us (14%)
  local copies, waits for them, and re-layouts  25.3 us (8%)
  other arithmetic  11.1 us (3%)
  matrix products  6.22 us (2%)
    all_to_all x1, waiting for transfers between devices, local(): lax.all_to_all(slot_grads.reshape(ndom, pair_slots * bsize, 2 * hwide), '...  70.6 us
    all_to_all x1, waiting for transfers between devices, local(): lax.all_to_all(outgoing.reshape(ndom, pair_slots * bsize, 2 * hwide), 'do...  64.9 us
    pallas_call x1, Pallas kernels, fused_attention(): pl.pallas_call(kernel, out_shape=(jax.ShapeDtypeStruct((nq, bsize, depth)...  45.8 us
    all_to_all x1, waiting for transfers between devices, local(): lax.all_to_all(d_qkv.reshape(nhead, rows, 3 * hwide), 'head', split_axis=...  19.4 us
    all_to_all x1, waiting for transfers between devices, local(): lax.all_to_all(qkv_own, 'head', split_axis=0, concat_axis=0, tiled=True)  19 us
    pallas_call x1, Pallas kernels, finish_grads(): pl.pallas_call(lambda *refs: finish_kernel(*refs, depth=depth), out_shape...  12.8 us
    all_to_all x1, starting transfers between devices, local(): lax.all_to_all(outgoing.reshape(ndom, pair_slots * bsize, 2 * hwide), 'do...  9.86 us
    all_to_all x1, starting transfers between devices, local(): lax.all_to_all(slot_grads.reshape(ndom, pair_slots * bsize, 2 * hwide), '...  8.93 us
  transfers between devices with their start and end apart: 6, of which 4 were waited for; matrix products, arithmetic and copies ran while one was open for 9% of the time, Pallas kernels for 4%

profile of v2, /device:TPU:1, one launch (start us, length us, event | category | flops | bytes accessed | tf_op | source)
XLA Modules:
  0.0 321.1 jit_solution(333865190572614001)
XLA Ops:
  0.6 0.0 copy-start
  0.6 1.3 fusion.12
  1.9 2.6 copy.62
  4.5 0.0 copy-start.1
  4.6 0.0 copy-start.6
  4.6 1.6 copy.63
  6.2 0.0 copy-done.1
  6.2 0.0 copy-done.6
  6.2 1.1 fusion.13
  7.3 1.3 convert_bitcast_fusion
  8.7 7.5 %all-to-all-start = ((bf16[8,512,192]{1,2,0:T(8,128)(2,1)}), bf16[8,512,192]{1,2,0:T(8,128)(2,1)}, u32[]{:S(2)}, u32[]{:S(2)}) async-start(bf16[8,512,192]{1,2,0:T(8,128)(2,1)} %convert_bitcast_fusion), calls=%async_computation | async-start | bytes 3145728 | tf_op jit(solution)/shard_map/all_to_all | solution.py:155
  16.2 0.0 copy-done.8
  16.2 0.1 copy.67
  16.3 0.1 copy.66
  16.4 0.1 broadcast_in_dim.39
  16.5 0.1 reshape_squeeze.8
  16.6 0.0 copy-done
  16.6 0.0 copy-done.3
  16.6 1.3 fusion.5
  17.9 19.0 %all-to-all-done = bf16[8,512,192]{1,2,0:T(8,128)(2,1)} async-done(((bf16[8,512,192]{1,2,0:T(8,128)(2,1)}), bf16[8,512,192]{1,2,0:T(8,128)(2,1)}, u32[]{:S(2)}, u32[]{:S(2)}) %all-to-all-start) | async-done | bytes 1572896 | tf_op jit(solution)/shard_map/all_to_all | solution.py:155
  36.9 5.0 %all-to-all-start.1 = ((bf16[8,512,64]{1,2,0:T(8,128)(2,1)}), bf16[8,512,64]{1,2,0:T(8,128)(2,1)}, u32[]{:S(2)}, u32[]{:S(2)}) async-start(bf16[8,512,64]{1,2,0:T(8,128)(2,1)} %fusion.5), calls=%async_computation.1 | async-start | bytes 1048576 | tf_op jit(solution)/shard_map/all_to_all | solution.py:160
  41.9 3.7 %copy.64 = bf16[8,512,192]{2,1,0:T(8,128)(2,1)} copy(bf16[8,512,192]{1,2,0:T(8,128)(2,1)} %all-to-all-done) | data formatting | bytes 3145728 | tf_op jit(solution)/shard_map/all_to_all | solution.py:155
  45.6 2.0 slice.8
  47.6 2.7 gather_fusion
  50.3 7.2 %bitcast_select_fusion = bf16[32,384,128]{2,1,0:T(8,128)(2,1)} fusion(pred[32,384]{1,0:T(8,128)(4,1)S(1)} %bitcast.70, bf16[32,384,128]{2,1,0:T(8,128)(2,1)} %bitcast.62), kind=kLoop, calls=%fused_computation.2 | loop fusion | flops 1572864 | bytes 6303744 | tf_op jit(solution)/shard_map/jit(_take)/select_n | solution.py:165
  57.5 0.0 all-to-all-done.1
  57.5 9.9 %all-to-all-start.2 = ((bf16[32,384,128]{2,1,0:T(8,128)(2,1)}), bf16[32,384,128]{2,1,0:T(8,128)(2,1)}, u32[]{:S(2)}, u32[]{:S(2)}) async-start(bf16[32,384,128]{2,1,0:T(8,128)(2,1)} %bitcast_select_fusion), calls=%async_computation.2 | async-start | bytes 6291456 | tf_op jit(solution)/shard_map/all_to_all | solution.py:166
  67.4 0.0 copy-done.10
  67.4 0.1 iota_compare_fusion
  67.5 0.1 lt.59
  67.6 0.0 copy-done.7
  67.6 0.1 copy.61
  67.7 0.1 copy.68
  67.8 0.1 reshape.124
  67.9 0.0 copy-start.9
  67.9 1.2 gather_fusion.1
  69.2 0.1 reshape.123
  69.3 0.1 copy.69
  69.4 0.1 copy.78
  69.5 0.0 copy-done.9
  69.5 0.1 copy.60
  69.6 0.6 reshape.102.refs_0_
  70.2 0.7 reshape.103.refs_1_
  70.9 0.1 concatenate.3.clone
  71.0 2.4 copy.65
  73.4 64.9 %all-to-all-done.2 = bf16[32,384,128]{2,1,0:T(8,128)(2,1)} async-done(((bf16[32,384,128]{2,1,0:T(8,128)(2,1)}), bf16[32,384,128]{2,1,0:T(8,128)(2,1)}, u32[]{:S(2)}, u32[]{:S(2)}) %all-to-all-start.2) | async-done | bytes 3145760 | tf_op jit(solution)/shard_map/all_to_all | solution.py:166
  138.2 0.8 broadcast_in_dim.47
  139.0 45.8 %shard_map.104 = (bf16[32,128,64]{2,1,0:T(8,128)(2,1)}, f32[32,128,192]{2,1,0:T(8,128)}, bf16[96,128,128]{2,1,0:T(8,128)(2,1)}) custom-call(s32[128]{0:T(128)} %reshape.102.refs_0_, s32[128]{0:T(128)} %reshape.103.refs_1_, bf16[32,128,192]{2,1,0:T(8,128)(2,1)} %bitcast.60, bf16[32,128,64]{2,1,0:T(8,128)(2,1)} %bitcast.65, ...), custom_call_target="tpu_custom_call" | custom-call | tf_op jit(solution)/shard_map/pallas_call | solution.py:78
  184.8 8.9 %all-to-all-start.4 = ((bf16[32,384,128]{2,1,0:T(8,128)(2,1)}), bf16[32,384,128]{2,1,0:T(8,128)(2,1)}, u32[]{:S(2)}, u32[]{:S(2)}) async-start(bf16[32,384,128]{2,1,0:T(8,128)(2,1)} %bitcast.66), calls=%async_computation.4 | async-start | bytes 6291456 | tf_op jit(solution)/shard_map/all_to_all | solution.py:190
  193.8 0.0 copy-done.5
  193.8 1.1 copy.71
  194.9 70.6 %all-to-all-done.4 = bf16[32,384,128]{2,1,0:T(8,128)(2,1)} async-done(((bf16[32,384,128]{2,1,0:T(8,128)(2,1)}), bf16[32,384,128]{2,1,0:T(8,128)(2,1)}, u32[]{:S(2)}, u32[]{:S(2)}) %all-to-all-start.4) | async-done | bytes 3145760 | tf_op jit(solution)/shard_map/all_to_all | solution.py:190
  265.5 8.9 %all-to-all-start.3 = ((bf16[8,512,64]{1,2,0:T(8,128)(2,1)}), bf16[8,512,64]{1,2,0:T(8,128)(2,1)S(1)}, u32[]{:S(2)}, u32[]{:S(2)}) async-start(bf16[8,512,64]{1,2,0:T(8,128)(2,1)} %copy.71), calls=%async_computation.3 | async-start | bytes 1048576 | tf_op jit(solution)/shard_map/all_to_all | solution.py:183
  274.4 0.6 reshape_squeeze.9.refs_0_
  275.1 12.8 %shard_map.105 = bf16[32,128,192]{2,1,0:T(8,128)(2,1)} custom-call(s32[96]{0:T(128)} %reshape_squeeze.9.refs_0_, f32[32,128,192]{2,1,0:T(8,128)} %get-tuple-element.6.refs_1_, bf16[96,128,128]{2,1,0:T(8,128)(2,1)} %bitcast.20.refs_2_), custom_call_target="tpu_custom_call" | custom-call | tf_op jit(solution)/shard_map/pallas_call | solution.py:109
  287.9 3.8 %copy.73 = bf16[8,512,192]{1,2,0:T(8,128)(2,1)} copy(bf16[8,512,192]{2,1,0:T(8,128)(2,1)} %bitcast.63) | data formatting | bytes 3145728 | tf_op jit(solution)/shard_map/reshape | solution.py:199
  291.7 0.0 all-to-all-done.3
  291.7 4.9 %all-to-all-start.5 = ((bf16[8,512,192]{1,2,0:T(8,128)(2,1)}), bf16[8,512,192]{1,2,0:T(8,128)(2,1)}, u32[]{:S(2)}, u32[]{:S(2)}) async-start(bf16[8,512,192]{1,2,0:T(8,128)(2,1)} %copy.73), calls=%async_computation.5 | async-start | bytes 3145728 | tf_op jit(solution)/shard_map/all_to_all | solution.py:198
  296.7 0.0 copy-done.2
  296.7 1.3 fusion.4
  297.9 19.4 %all-to-all-done.5 = bf16[8,512,192]{1,2,0:T(8,128)(2,1)} async-done(((bf16[8,512,192]{1,2,0:T(8,128)(2,1)}), bf16[8,512,192]{1,2,0:T(8,128)(2,1)}, u32[]{:S(2)}, u32[]{:S(2)}) %all-to-all-start.5) | async-done | bytes 1572896 | tf_op jit(solution)/shard_map/all_to_all | solution.py:198
  317.4 2.6 fusion.7
  319.9 0.0 copy-done.4
  319.9 1.1 fusion.11
  (16 shorter events, 0.1 us)
Async XLA Ops:
  0.6 16.0 %copy-start = (bf16[512,512]{1,0:T(8,128)(2,1)S(1)}, bf16[512,512]{1,0:T(8,128)(2,1)}, u32[]{:S(2)}) copy-start(bf16[512,512]{1,0:T(8,128)(2,1)} %param.12) | copy-start | bytes 1572868
  4.5 1.6 copy-start.1
  4.6 1.6 copy-start.6
  8.7 7.5 %copy-start.8 = (s32[1,32,3]{1,0,2:T(1,128)S(1)}, s32[1,32,3]{1,0,2:T(1,128)}, u32[]{:S(2)}) copy-start(s32[1,32,3]{1,0,2:T(1,128)} %param.16) | copy-start | bytes 1156
  8.7 8.0 %copy-start.3 = (bf16[512,512]{1,0:T(8,128)(2,1)S(1)}, bf16[512,512]{1,0:T(8,128)(2,1)}, u32[]{:S(2)}) copy-start(bf16[512,512]{1,0:T(8,128)(2,1)} %param.13) | copy-start | bytes 1572868
  8.7 28.2 %all-to-all-start = ((bf16[8,512,192]{1,2,0:T(8,128)(2,1)}), bf16[8,512,192]{1,2,0:T(8,128)(2,1)}, u32[]{:S(2)}, u32[]{:S(2)}) async-start(bf16[8,512,192]{1,2,0:T(8,128)(2,1)} %convert_bitcast_fusion), calls=%async_computation | async-start | bytes 3145728 | tf_op jit(solution)/shard_map/all_to_all | solution.py:155
  36.9 20.7 %all-to-all-start.1 = ((bf16[8,512,64]{1,2,0:T(8,128)(2,1)}), bf16[8,512,64]{1,2,0:T(8,128)(2,1)}, u32[]{:S(2)}, u32[]{:S(2)}) async-start(bf16[8,512,64]{1,2,0:T(8,128)(2,1)} %fusion.5), calls=%async_computation.1 | async-start | bytes 1048576 | tf_op jit(solution)/shard_map/all_to_all | solution.py:160
  57.5 9.9 %copy-start.10 = (s32[32,1]{0,1:T(1,128)S(1)}, s32[32,1]{0,1:T(1,128)}, u32[]{:S(2)}) copy-start(s32[32,1]{0,1:T(1,128)} %param.17) | copy-start | bytes 388
  57.5 10.1 %copy-start.7 = (s32[32,4]{0,1:T(4,128)S(1)}, s32[32,4]{0,1:T(4,128)}, u32[]{:S(2)}) copy-start(s32[32,4]{0,1:T(4,128)} %param.15) | copy-start | bytes 1540
  57.5 80.7 %all-to-all-start.2 = ((bf16[32,384,128]{2,1,0:T(8,128)(2,1)}), bf16[32,384,128]{2,1,0:T(8,128)(2,1)}, u32[]{:S(2)}, u32[]{:S(2)}) async-start(bf16[32,384,128]{2,1,0:T(8,128)(2,1)} %bitcast_select_fusion), calls=%async_computation.2 | async-start | bytes 6291456 | tf_op jit(solution)/shard_map/all_to_all | solution.py:166
  67.9 1.6 copy-start.9
  184.8 8.9 %copy-start.5 = (bf16[32,128,64]{2,1,0:T(8,128)(2,1)S(1)}, bf16[32,128,64]{2,1,0:T(8,128)(2,1)}, u32[]{:S(2)}) copy-start(bf16[32,128,64]{2,1,0:T(8,128)(2,1)} %get-tuple-element.5) | copy-start | bytes 1572868
  184.8 80.7 %all-to-all-start.4 = ((bf16[32,384,128]{2,1,0:T(8,128)(2,1)}), bf16[32,384,128]{2,1,0:T(8,128)(2,1)}, u32[]{:S(2)}, u32[]{:S(2)}) async-start(bf16[32,384,128]{2,1,0:T(8,128)(2,1)} %bitcast.66), calls=%async_computation.4 | async-start | bytes 6291456 | tf_op jit(solution)/shard_map/all_to_all | solution.py:190
  265.5 26.2 %all-to-all-start.3 = ((bf16[8,512,64]{1,2,0:T(8,128)(2,1)}), bf16[8,512,64]{1,2,0:T(8,128)(2,1)S(1)}, u32[]{:S(2)}, u32[]{:S(2)}) async-start(bf16[8,512,64]{1,2,0:T(8,128)(2,1)} %copy.71), calls=%async_computation.3 | async-start | bytes 1048576 | tf_op jit(solution)/shard_map/all_to_all | solution.py:183
  291.7 4.9 %copy-start.2 = (bf16[512,512]{1,0:T(8,128)(2,1)S(1)}, bf16[512,512]{1,0:T(8,128)(2,1)}, u32[]{:S(2)}) copy-start(bf16[512,512]{1,0:T(8,128)(2,1)} %param.9) | copy-start | bytes 1572868
  291.7 25.6 %all-to-all-start.5 = ((bf16[8,512,192]{1,2,0:T(8,128)(2,1)}), bf16[8,512,192]{1,2,0:T(8,128)(2,1)}, u32[]{:S(2)}, u32[]{:S(2)}) async-start(bf16[8,512,192]{1,2,0:T(8,128)(2,1)} %copy.73), calls=%async_computation.5 | async-start | bytes 3145728 | tf_op jit(solution)/shard_map/all_to_all | solution.py:198
  317.4 2.6 copy-start.4

commit v3 on v2

v3 whole, which is shorter than its diff:
```python
import math

import jax
import jax.numpy as jnp
from jax import lax
from jax.experimental import pallas as pl
from jax.experimental.pallas import tpu as pltpu
from jax.sharding import PartitionSpec as P

HEADS = 8
EPS = 1e-05


def attention_kernel(
    lk_ref, rk_ref, qkv_ref, do_ref, pool_ref, bias_ref, o_ref, dq_ref, acc_ref, slot_ref, slot_acc,
    *, near, far, bsize, depth, scale
):
    f32 = jnp.float32
    bf16 = jnp.bfloat16
    nq = qkv_ref.shape[0]
    acc_ref[...] = jnp.zeros(acc_ref.shape, f32)
    slot_acc[...] = jnp.zeros(slot_acc.shape, f32)
    kcols = pl.ds(0, depth)
    vcols = pl.ds(depth, depth)
    qcols = pl.ds(2 * depth, depth)
    nt = (((1,), (1,)), ((), ()))

    def body(b, carry):
        q = qkv_ref[b, :, qcols]
        do = do_ref[b]
        ids_l = [lk_ref[b * near + i] for i in range(near)]
        ids_r = [rk_ref[b * far + i] for i in range(far)]
        keys = jnp.concatenate(
            [qkv_ref[i, :, kcols] for i in ids_l] + [pool_ref[i, :, kcols] for i in ids_r], axis=0
        )
        vals = jnp.concatenate(
            [qkv_ref[i, :, vcols] for i in ids_l] + [pool_ref[i, :, vcols] for i in ids_r], axis=0
        )
        q_s = q * scale
        do_s = do * scale
        s = lax.dot_general(q_s, keys, nt, preferred_element_type=f32)
        s = s + bias_ref[pl.ds(b, 1), :]
        top = jnp.max(s, axis=1, keepdims=True)
        expo = jnp.exp(s - top)
        total = jnp.sum(expo, axis=1, keepdims=True)
        w = (expo * (1.0 / total)).astype(bf16)
        o = jnp.dot(w, vals, preferred_element_type=f32).astype(bf16)
        o_ref[b] = o
        delta = jnp.sum(do_s.astype(f32) * o.astype(f32), axis=1, keepdims=True)
        dw = lax.dot_general(do_s, vals, nt, preferred_element_type=f32)
        ds = (w.astype(f32) * (dw - delta)).astype(bf16)
        dq_ref[b] = jnp.dot(ds, keys, preferred_element_type=f32)
        dk_t = jnp.dot(q.T, ds, preferred_element_type=f32)
        dv_t = jnp.dot(do.T, w, preferred_element_type=f32)
        dkv_t = jnp.concatenate([dk_t, dv_t], axis=0)
        for i in range(near):
            part = dkv_t[:, i * bsize:(i + 1) * bsize]
            acc_ref[ids_l[i]] = acc_ref[ids_l[i]] + part
        for i in range(far):
            part = dkv_t[:, (near + i) * bsize:(near + i + 1) * bsize]
            slot_acc[ids_r[i]] = slot_acc[ids_r[i]] + part
        return carry

    lax.fori_loop(0, nq, body, 0)
    slot_ref[...] = slot_acc[...].astype(bf16)


def fused_attention(local_ids, remote_ids, qkv, d_out, pool, bias, scale):
    nq, bsize, depth = d_out.shape
    near = local_ids.size // nq
    far = remote_ids.size // nq
    npool = pool.shape[0]
    f32 = jnp.float32
    smem = pl.BlockSpec(memory_space=pltpu.SMEM)
    vmem = pl.BlockSpec(memory_space=pltpu.VMEM)
    kernel = lambda *refs: attention_kernel(
        *refs, near=near, far=far, bsize=bsize, depth=depth, scale=scale
    )
    kv_t = (2 * depth, bsize)
    return pl.pallas_call(
        kernel,
        out_shape=(
            jax.ShapeDtypeStruct((nq, bsize, depth), jnp.bfloat16),
            jax.ShapeDtypeStruct((nq, bsize, depth), f32),
            jax.ShapeDtypeStruct((nq,) + kv_t, f32),
            jax.ShapeDtypeStruct((npool,) + kv_t, jnp.bfloat16),
        ),
        in_specs=[smem, smem] + [vmem] * 4,
        out_specs=(vmem, vmem, vmem, vmem),
        scratch_shapes=[pltpu.VMEM((npool,) + kv_t, f32)],
        compiler_params=pltpu.CompilerParams(vmem_limit_bytes=60 * 1024 * 1024),
    )(local_ids, remote_ids, qkv, d_out, pool, bias)


def finish_kernel(ids_ref, dq_ref, acc_ref, ret_ref, out_ref, total_ref):
    kvw = acc_ref.shape[1]
    qw = dq_ref.shape[2]
    total_ref[...] = acc_ref[...]

    def add_slot(j, carry):
        i = ids_ref[j]
        total_ref[i] = total_ref[i] + ret_ref[j].astype(jnp.float32)
        return carry

    lax.fori_loop(0, ret_ref.shape[0], add_slot, 0, unroll=8)

    def emit(b, carry):
        out_ref[b, :, pl.ds(0, kvw)] = total_ref[b].T.astype(jnp.bfloat16)
        out_ref[b, :, pl.ds(kvw, qw)] = dq_ref[b].astype(jnp.bfloat16)
        return carry

    lax.fori_loop(0, acc_ref.shape[0], emit, 0, unroll=4)


def finish_grads(send_ids, d_q, acc, returned):
    nq, bsize, depth = d_q.shape
    smem = pl.BlockSpec(memory_space=pltpu.SMEM)
    vmem = pl.BlockSpec(memory_space=pltpu.VMEM)
    return pl.pallas_call(
        finish_kernel,
        out_shape=jax.ShapeDtypeStruct((nq, bsize, acc.shape[1] + depth), jnp.bfloat16),
        in_specs=[smem, vmem, vmem, vmem],
        out_specs=vmem,
        scratch_shapes=[pltpu.VMEM(acc.shape, jnp.float32)],
        compiler_params=pltpu.CompilerParams(vmem_limit_bytes=60 * 1024 * 1024),
    )(send_ids, d_q, acc, returned)


def local(
    features,
    norm_gain,
    w_qkv,
    w_out,
    grad_y,
    local_keys,
    remote_keys,
    boundary_blocks,
    boundary_count,
):
    f32 = jnp.float32
    bf16 = jnp.bfloat16
    nhead = lax.axis_size("head")
    rows, width = features.shape
    per = HEADS // nhead
    depth = width // HEADS
    hwide = per * depth
    nblk, near_count = local_keys.shape
    far_count = remote_keys.shape[1]
    ndom = boundary_blocks.shape[1]
    pair_slots = boundary_blocks.shape[2]
    slots = ndom * pair_slots
    grows = rows * nhead
    bsize = grows // nblk
    score_scale = 1.0 / math.sqrt(depth)

    xf = features.astype(f32)
    inv = lax.rsqrt(jnp.mean(xf * xf, axis=1, keepdims=True) + EPS)
    normed = xf * inv
    hidden = (normed * norm_gain).astype(bf16)
    w_heads = (
        w_qkv.reshape(width, 3, nhead, hwide)[:, jnp.array([1, 2, 0])]
        .transpose(2, 0, 1, 3)
        .reshape(nhead, width, 3 * hwide)
    )
    w_out_heads = w_out.reshape(nhead, hwide, width)
    qkv_own = jnp.einsum("rd,hdc->hrc", hidden, w_heads, preferred_element_type=f32).astype(bf16)
    qkv = lax.all_to_all(qkv_own, "head", split_axis=0, concat_axis=0, tiled=True).reshape(
        nblk, bsize, 3 * hwide
    )

    d_attn = jnp.einsum("rf,hef->hre", grad_y, w_out_heads, preferred_element_type=f32).astype(bf16)
    d_group = lax.all_to_all(d_attn, "head", split_axis=0, concat_axis=0, tiled=True).reshape(
        nblk, bsize, hwide
    )

    send_ids = boundary_blocks[0].reshape(slots)
    outgoing = jnp.take(qkv[:, :, : 2 * hwide], send_ids, axis=0, mode="clip")
    pool = lax.all_to_all(
        outgoing.reshape(ndom, pair_slots * bsize, 2 * hwide),
        "dom",
        split_axis=0,
        concat_axis=0,
        tiled=True,
    ).reshape(slots, bsize, 2 * hwide)
    slot_alive = (jnp.arange(pair_slots, dtype=jnp.int32)[None, :] < boundary_count).reshape(slots)
    remote_alive = jnp.take(slot_alive, remote_keys, axis=0, mode="clip")
    bias_far = jnp.where(remote_alive, 0.0, -jnp.inf).astype(f32)
    bias = jnp.concatenate([jnp.zeros((nblk, near_count), f32), bias_far], axis=1)
    bias = jnp.repeat(bias, bsize, axis=1)

    o, d_q, acc, slot_grads = fused_attention(
        local_keys.reshape(-1), remote_keys.reshape(-1), qkv, d_group, pool, bias, score_scale
    )

    attn = lax.all_to_all(
        o.reshape(nhead, rows, hwide), "head", split_axis=0, concat_axis=0, tiled=True
    )
    mixed_out = (
        xf + jnp.einsum("hre,hef->rf", attn, w_out_heads, preferred_element_type=f32)
    ).astype(bf16)

    returned = lax.all_to_all(
        slot_grads.reshape(ndom, pair_slots * 2 * hwide, bsize),
        "dom",
        split_axis=0,
        concat_axis=0,
        tiled=True,
    ).reshape(slots, 2 * hwide, bsize)
    d_qkv = finish_grads(send_ids, d_q, acc, returned)
    d_rows = lax.all_to_all(
        d_qkv.reshape(nhead, rows, 3 * hwide), "head", split_axis=0, concat_axis=0, tiled=True
    )
    d_hidden = jnp.einsum("hrc,hdc->rd", d_rows, w_heads, preferred_element_type=f32)
    d_normed = d_hidden * norm_gain
    d_input = inv * (d_normed - normed * jnp.mean(d_normed * normed, axis=1, keepdims=True))
    grad_x = (grad_y.astype(f32) + d_input).astype(bf16)
    return (mixed_out, grad_x)


def solution(mesh):
    return jax.shard_map(
        local,
        mesh=mesh,
        in_specs=(
            P(("dom", "head"), None),
            P(),
            P(),
            P(),
            P(("dom", "head"), None),
            P("dom", None),
            P("dom", None),
            P("dom", None, None),
            P(None, "dom"),
        ),
        out_specs=(P(("dom", "head"), None), P(("dom", "head"), None)),
        check_vma=False,
    )
```

time: 322 us -> 302 us (0.938)
  Pallas kernels: 58.6 us -> 45.3 us
  other arithmetic: 11.1 us -> 3.19 us
    select_n x3 -> x0, other arithmetic: 7.21 us -> none  [the longest x2 7.21 us: local(): outgoing = jnp.take(qkv[:, :, hwide:], send_ids, axis=0)]
    pallas_call x1, Pallas kernels: 45.8 us -> 39 us  [fused_attention(): pl.pallas_call(kernel, out_shape=(jax.ShapeDtypeStruct((nq, bsize, depth)...]
    pallas_call x1, Pallas kernels: 12.8 us -> 6.28 us  [finish_grads(): pl.pallas_call(finish_kernel, out_shape=jax.ShapeDtypeStruct((nq, bsize,...]
  transfers between devices with their start and end apart: 6 -> 6, of which waited for: 4 -> 5; matrix products, arithmetic and copies ran while one was open for 9% -> 7% of each run, Pallas kernels for 4% -> 2%
where the time goes in v3:
time: 302 us
  waiting for transfers between devices  176 us (58%)
  Pallas kernels  45.3 us (15%)
  starting transfers between devices  44 us (15%)
  local copies, waits for them, and re-layouts  24 us (8%)
  matrix products  8.49 us (3%)
  other arithmetic  3.19 us (1%)
    all_to_all x1, waiting for transfers between devices, local(): lax.all_to_all(slot_grads.reshape(ndom, pair_slots * 2 * hwide, bsize), '...  70.1 us
    all_to_all x1, waiting for transfers between devices, local(): lax.all_to_all(outgoing.reshape(ndom, pair_slots * bsize, 2 * hwide), 'do...  65.4 us
    pallas_call x1, Pallas kernels, fused_attention(): pl.pallas_call(kernel, out_shape=(jax.ShapeDtypeStruct((nq, bsize, depth)...  39 us
    all_to_all x1, waiting for transfers between devices, local(): lax.all_to_all(qkv_own, 'head', split_axis=0, concat_axis=0, tiled=True)  19.3 us
    all_to_all x1, waiting for transfers between devices, local(): lax.all_to_all(d_qkv.reshape(nhead, rows, 3 * hwide), 'head', split_axis=...  18.3 us
    all_to_all x1, starting transfers between devices, local(): lax.all_to_all(outgoing.reshape(ndom, pair_slots * bsize, 2 * hwide), 'do...  10.5 us
    all_to_all x1, starting transfers between devices, local(): lax.all_to_all(slot_grads.reshape(ndom, pair_slots * 2 * hwide, bsize), '...  9.03 us
    all_to_all x1, starting transfers between devices, local(): lax.all_to_all(o.reshape(nhead, rows, hwide), 'head', split_axis=0, conca...  7.76 us
  transfers between devices with their start and end apart: 6, of which 5 were waited for; matrix products, arithmetic and copies ran while one was open for 7% of the time, Pallas kernels for 2%

profile of v3, /device:TPU:1, one launch (start us, length us, event | category | flops | bytes accessed | tf_op | source)
XLA Modules:
  0.0 301.7 jit_solution(4347988117670827294)
XLA Ops:
  0.6 0.0 copy-start
  0.6 1.3 fusion.13
  1.9 0.7 pad_clamp_fusion.2
  2.6 2.6 copy.32
  5.2 2.1 gather_fusion
  7.3 0.0 copy-start.3
  7.3 0.0 copy-start.7
  7.3 0.1 copy.33
  7.4 0.0 copy-start.1
  7.4 1.2 copy-done.1
  8.6 0.0 copy-done.3
  8.6 0.0 copy-done.7
  8.6 2.3 fusion
  10.9 0.0 copy-start.4
  10.9 6.8 %all-to-all-start = ((bf16[8,512,192]{1,2,0:T(8,128)(2,1)}), bf16[8,512,192]{1,2,0:T(8,128)(2,1)S(1)}, u32[]{:S(2)}, u32[]{:S(2)}) async-start(bf16[8,512,192]{1,2,0:T(8,128)(2,1)} %fusion), calls=%async_computation | async-start | bytes 3145728 | tf_op jit(solution)/shard_map/all_to_all | solution.py:167
  17.7 0.0 copy-done
  17.7 0.0 copy-done.4
  17.7 1.3 fusion.6
  19.0 19.3 %all-to-all-done = bf16[8,512,192]{1,2,0:T(8,128)(2,1)S(1)} async-done(((bf16[8,512,192]{1,2,0:T(8,128)(2,1)}), bf16[8,512,192]{1,2,0:T(8,128)(2,1)S(1)}, u32[]{:S(2)}, u32[]{:S(2)}) %all-to-all-start) | async-done | bytes 1572896 | tf_op jit(solution)/shard_map/all_to_all | solution.py:167
  38.3 5.0 %all-to-all-start.1 = ((bf16[8,512,64]{1,2,0:T(8,128)(2,1)}), bf16[8,512,64]{1,2,0:T(8,128)(2,1)}, u32[]{:S(2)}, u32[]{:S(2)}) async-start(bf16[8,512,64]{1,2,0:T(8,128)(2,1)} %fusion.6), calls=%async_computation.1 | async-start | bytes 1048576 | tf_op jit(solution)/shard_map/all_to_all | solution.py:172
  43.3 0.0 copy-done.12
  43.3 0.1 copy.36
  43.4 0.1 reshape.88.ids_ref
  43.5 0.0 copy-start.8
  43.5 2.5 copy.34
  46.0 0.0 copy-done.8
  46.0 1.3 slice.10
  47.3 2.7 gather_fusion.1
  50.1 2.7 all-to-all-done.1
  52.8 10.5 %all-to-all-start.2 = ((bf16[32,384,128]{2,1,0:T(8,128)(2,1)}), bf16[32,384,128]{2,1,0:T(8,128)(2,1)}, u32[]{:S(2)}, u32[]{:S(2)}) async-start(bf16[32,384,128]{2,1,0:T(8,128)(2,1)} %bitcast.49), calls=%async_computation.2 | async-start | bytes 6291456 | tf_op jit(solution)/shard_map/all_to_all | solution.py:178
  63.4 0.0 copy-done.13
  63.4 0.1 iota_compare_fusion
  63.4 0.1 lt.27
  63.5 0.0 copy-done.10
  63.6 0.1 copy.30
  63.6 0.6 reshape.64.refs_0_
  64.3 0.0 copy-done.11
  64.3 0.1 copy.31
  64.4 0.1 reshape.65.refs_1_
  64.5 0.0 copy-start.9
  64.5 1.2 gather_fusion.2
  65.7 0.0 copy-done.9
  65.8 0.1 reshape.107
  65.9 0.1 concatenate.3
  65.9 0.1 broadcast_in_dim.33
  66.0 0.7 copy.44
  66.7 2.4 copy.35
  69.1 65.4 %all-to-all-done.2 = bf16[32,384,128]{2,1,0:T(8,128)(2,1)} async-done(((bf16[32,384,128]{2,1,0:T(8,128)(2,1)}), bf16[32,384,128]{2,1,0:T(8,128)(2,1)}, u32[]{:S(2)}, u32[]{:S(2)}) %all-to-all-start.2) | async-done | bytes 3145760 | tf_op jit(solution)/shard_map/all_to_all | solution.py:178
  134.5 39.0 %shard_map.113 = (bf16[32,128,64]{2,1,0:T(8,128)(2,1)}, f32[32,128,64]{2,1,0:T(8,128)}, f32[32,128,128]{2,1,0:T(8,128)}, bf16[96,128,128]{2,1,0:T(8,128)(2,1)}) custom-call(s32[128]{0:T(128)} %reshape.64.refs_0_, s32[128]{0:T(128)} %copy-done.9, bf16[32,128,192]{2,1,0:T(8,128)(2,1)} %bitcast.48, bf16[32,128,64]{2,1,0:T(8,128)(2,1)} %bitcast.53, ...), custom_call_target="tpu_custom_call" | custom-call | tf_op jit(solution)/shard_map/pallas_call | solution.py:80
  173.6 9.0 %all-to-all-start.4 = ((bf16[32,384,128]{2,1,0:T(8,128)(2,1)}), bf16[32,384,128]{2,1,0:T(8,128)(2,1)}, u32[]{:S(2)}, u32[]{:S(2)}) async-start(bf16[32,384,128]{2,1,0:T(8,128)(2,1)} %bitcast.54), calls=%async_computation.4 | async-start | bytes 6291456 | tf_op jit(solution)/shard_map/all_to_all | solution.py:202
  182.6 0.0 copy-done.5
  182.6 1.1 copy.37
  183.7 70.1 %all-to-all-done.4 = bf16[32,384,128]{2,1,0:T(8,128)(2,1)} async-done(((bf16[32,384,128]{2,1,0:T(8,128)(2,1)}), bf16[32,384,128]{2,1,0:T(8,128)(2,1)}, u32[]{:S(2)}, u32[]{:S(2)}) %all-to-all-start.4) | async-done | bytes 3145760 | tf_op jit(solution)/shard_map/all_to_all | solution.py:202
  253.8 7.8 %all-to-all-start.3 = ((bf16[8,512,64]{1,2,0:T(8,128)(2,1)}), bf16[8,512,64]{1,2,0:T(8,128)(2,1)S(1)}, u32[]{:S(2)}, u32[]{:S(2)}) async-start(bf16[8,512,64]{1,2,0:T(8,128)(2,1)} %copy.37), calls=%async_computation.3 | async-start | bytes 1048576 | tf_op jit(solution)/shard_map/all_to_all | solution.py:195
  261.6 6.3 %shard_map.114 = bf16[32,128,192]{2,1,0:T(8,128)(2,1)} custom-call(s32[96]{0:T(128)} %copy-done.8, f32[32,128,64]{2,1,0:T(8,128)} %get-tuple-element.7.dq_ref, f32[32,128,128]{2,1,0:T(8,128)} %get-tuple-element.8.acc_ref, bf16[96,128,128]{2,1,0:T(8,128)(2,1)} %bitcast.16.ret_ref), custom_call_target="tpu_custom_call" | custom-call | tf_op jit(solution)/shard_map/pallas_call | solution.py:119
  267.9 3.8 %copy.38 = bf16[8,512,192]{1,2,0:T(8,128)(2,1)} copy(bf16[8,512,192]{2,1,0:T(8,128)(2,1)} %bitcast.50) | data formatting | bytes 3145728 | tf_op jit(solution)/shard_map/reshape | solution.py:211
  271.7 0.0 all-to-all-done.3
  271.7 0.8 copy-done.6
  272.5 4.8 %all-to-all-start.5 = ((bf16[8,512,192]{1,2,0:T(8,128)(2,1)}), bf16[8,512,192]{1,2,0:T(8,128)(2,1)}, u32[]{:S(2)}, u32[]{:S(2)}) async-start(bf16[8,512,192]{1,2,0:T(8,128)(2,1)} %copy.38), calls=%async_computation.5 | async-start | bytes 3145728 | tf_op jit(solution)/shard_map/all_to_all | solution.py:210
  277.3 2.4 fusion.5
  279.7 18.3 %all-to-all-done.5 = bf16[8,512,192]{1,2,0:T(8,128)(2,1)} async-done(((bf16[8,512,192]{1,2,0:T(8,128)(2,1)}), bf16[8,512,192]{1,2,0:T(8,128)(2,1)}, u32[]{:S(2)}, u32[]{:S(2)}) %all-to-all-start.5) | async-done | bytes 1572896 | tf_op jit(solution)/shard_map/all_to_all | solution.py:210
  298.0 0.0 copy-done.2
  298.0 2.5 fusion.8
  300.5 1.1 fusion.12
  (12 shorter events, 0.0 us)
Async XLA Ops:
  0.6 17.1 %copy-start = (bf16[512,512]{1,0:T(8,128)(2,1)S(1)}, bf16[512,512]{1,0:T(8,128)(2,1)}, u32[]{:S(2)}) copy-start(bf16[512,512]{1,0:T(8,128)(2,1)} %param.13) | copy-start | bytes 1572868
  7.3 1.3 copy-start.3
  7.3 1.3 copy-start.7
  7.4 1.2 copy-start.1
  10.9 6.8 %copy-start.4 = (bf16[512,512]{1,0:T(8,128)(2,1)S(1)}, bf16[512,512]{1,0:T(8,128)(2,1)}, u32[]{:S(2)}) copy-start(bf16[512,512]{1,0:T(8,128)(2,1)} %param.14) | copy-start | bytes 1572868
  10.9 27.4 %all-to-all-start = ((bf16[8,512,192]{1,2,0:T(8,128)(2,1)}), bf16[8,512,192]{1,2,0:T(8,128)(2,1)S(1)}, u32[]{:S(2)}, u32[]{:S(2)}) async-start(bf16[8,512,192]{1,2,0:T(8,128)(2,1)} %fusion), calls=%async_computation | async-start | bytes 3145728 | tf_op jit(solution)/shard_map/all_to_all | solution.py:167
  17.7 25.6 %copy-start.12 = (s32[1,32,3]{1,0,2:T(1,128)S(1)}, s32[1,32,3]{1,0,2:T(1,128)}, u32[]{:S(2)}) copy-start(s32[1,32,3]{1,0,2:T(1,128)} %param.17) | copy-start | bytes 1156
  38.3 14.5 %all-to-all-start.1 = ((bf16[8,512,64]{1,2,0:T(8,128)(2,1)}), bf16[8,512,64]{1,2,0:T(8,128)(2,1)}, u32[]{:S(2)}, u32[]{:S(2)}) async-start(bf16[8,512,64]{1,2,0:T(8,128)(2,1)} %fusion.6), calls=%async_computation.1 | async-start | bytes 1048576 | tf_op jit(solution)/shard_map/all_to_all | solution.py:172
  43.5 2.5 copy-start.8
  52.8 10.5 %copy-start.13 = (s32[32,1]{0,1:T(1,128)S(1)}, s32[32,1]{0,1:T(1,128)}, u32[]{:S(2)}) copy-start(s32[32,1]{0,1:T(1,128)} %param.18) | copy-start | bytes 388
  52.8 10.7 %copy-start.10 = (s32[32,4]{0,1:T(4,128)S(1)}, s32[32,4]{0,1:T(4,128)}, u32[]{:S(2)}) copy-start(s32[32,4]{0,1:T(4,128)} %param.15) | copy-start | bytes 1540
  52.8 11.5 %copy-start.11 = (s32[32,4]{0,1:T(4,128)S(1)}, s32[32,4]{0,1:T(4,128)}, u32[]{:S(2)}) copy-start(s32[32,4]{0,1:T(4,128)} %param.16) | copy-start | bytes 1540
  52.8 81.7 %all-to-all-start.2 = ((bf16[32,384,128]{2,1,0:T(8,128)(2,1)}), bf16[32,384,128]{2,1,0:T(8,128)(2,1)}, u32[]{:S(2)}, u32[]{:S(2)}) async-start(bf16[32,384,128]{2,1,0:T(8,128)(2,1)} %bitcast.49), calls=%async_computation.2 | async-start | bytes 6291456 | tf_op jit(solution)/shard_map/all_to_all | solution.py:178
  64.5 1.3 copy-start.9
  173.6 9.0 %copy-start.5 = (bf16[32,128,64]{2,1,0:T(8,128)(2,1)S(1)}, bf16[32,128,64]{2,1,0:T(8,128)(2,1)}, u32[]{:S(2)}) copy-start(bf16[32,128,64]{2,1,0:T(8,128)(2,1)} %get-tuple-element.6) | copy-start | bytes 1572868
  173.6 80.2 %all-to-all-start.4 = ((bf16[32,384,128]{2,1,0:T(8,128)(2,1)}), bf16[32,384,128]{2,1,0:T(8,128)(2,1)}, u32[]{:S(2)}, u32[]{:S(2)}) async-start(bf16[32,384,128]{2,1,0:T(8,128)(2,1)} %bitcast.54), calls=%async_computation.4 | async-start | bytes 6291456 | tf_op jit(solution)/shard_map/all_to_all | solution.py:202
  253.8 17.9 %all-to-all-start.3 = ((bf16[8,512,64]{1,2,0:T(8,128)(2,1)}), bf16[8,512,64]{1,2,0:T(8,128)(2,1)S(1)}, u32[]{:S(2)}, u32[]{:S(2)}) async-start(bf16[8,512,64]{1,2,0:T(8,128)(2,1)} %copy.37), calls=%async_computation.3 | async-start | bytes 1048576 | tf_op jit(solution)/shard_map/all_to_all | solution.py:195
  271.7 0.8 copy-start.6
  272.5 25.5 %all-to-all-start.5 = ((bf16[8,512,192]{1,2,0:T(8,128)(2,1)}), bf16[8,512,192]{1,2,0:T(8,128)(2,1)}, u32[]{:S(2)}, u32[]{:S(2)}) async-start(bf16[8,512,192]{1,2,0:T(8,128)(2,1)} %copy.38), calls=%async_computation.5 | async-start | bytes 3145728 | tf_op jit(solution)/shard_map/all_to_all | solution.py:210
  277.3 20.7 %copy-start.2 = (bf16[8,512,3,64]{1,3,2,0:T(8,128)(2,1)S(1)}, bf16[8,512,3,64]{1,3,2,0:T(8,128)(2,1)}, u32[]{:S(2)}) copy-start(bf16[8,512,3,64]{1,3,2,0:T(8,128)(2,1)} %copy-done.1) | copy-start | bytes 4718596

commit v4 on v3

--- a/solution.py
+++ b/solution.py
@@ -12,29 +12,28 @@
 
 
 def attention_kernel(
-    lk_ref, rk_ref, qkv_ref, do_ref, pool_ref, bias_ref, o_ref, dq_ref, acc_ref, slot_ref, slot_acc,
+    lk_ref, rk_ref, q_ref, kv_ref, do_ref, pool_ref, bias_ref, o_ref, dq_ref, acc_ref, slot_ref, slot_acc,
     *, near, far, bsize, depth, scale
 ):
     f32 = jnp.float32
     bf16 = jnp.bfloat16
-    nq = qkv_ref.shape[0]
+    nq = q_ref.shape[0]
     acc_ref[...] = jnp.zeros(acc_ref.shape, f32)
     slot_acc[...] = jnp.zeros(slot_acc.shape, f32)
     kcols = pl.ds(0, depth)
     vcols = pl.ds(depth, depth)
-    qcols = pl.ds(2 * depth, depth)
     nt = (((1,), (1,)), ((), ()))
 
     def body(b, carry):
-        q = qkv_ref[b, :, qcols]
+        q = q_ref[b]
         do = do_ref[b]
         ids_l = [lk_ref[b * near + i] for i in range(near)]
         ids_r = [rk_ref[b * far + i] for i in range(far)]
         keys = jnp.concatenate(
-            [qkv_ref[i, :, kcols] for i in ids_l] + [pool_ref[i, :, kcols] for i in ids_r], axis=0
+            [kv_ref[i, :, kcols] for i in ids_l] + [pool_ref[i, :, kcols] for i in ids_r], axis=0
         )
         vals = jnp.concatenate(
-            [qkv_ref[i, :, vcols] for i in ids_l] + [pool_ref[i, :, vcols] for i in ids_r], axis=0
+            [kv_ref[i, :, vcols] for i in ids_l] + [pool_ref[i, :, vcols] for i in ids_r], axis=0
         )
         q_s = q * scale
         do_s = do * scale
@@ -49,7 +48,7 @@
         delta = jnp.sum(do_s.astype(f32) * o.astype(f32), axis=1, keepdims=True)
         dw = lax.dot_general(do_s, vals, nt, preferred_element_type=f32)
         ds = (w.astype(f32) * (dw - delta)).astype(bf16)
-        dq_ref[b] = jnp.dot(ds, keys, preferred_element_type=f32)
+        dq_ref[b] = jnp.dot(ds, keys, preferred_element_type=f32).astype(bf16)
         dk_t = jnp.dot(q.T, ds, preferred_element_type=f32)
         dv_t = jnp.dot(do.T, w, preferred_element_type=f32)
         dkv_t = jnp.concatenate([dk_t, dv_t], axis=0)
@@ -61,11 +60,11 @@
             slot_acc[ids_r[i]] = slot_acc[ids_r[i]] + part
         return carry
 
-    lax.fori_loop(0, nq, body, 0)
+    lax.fori_loop(0, nq, body, 0, unroll=2)
     slot_ref[...] = slot_acc[...].astype(bf16)
 
 
-def fused_attention(local_ids, remote_ids, qkv, d_out, pool, bias, scale):
+def fused_attention(local_ids, remote_ids, q, kv, d_out, pool, bias, scale):
     nq, bsize, depth = d_out.shape
     near = local_ids.size // nq
     far = remote_ids.size // nq
@@ -81,20 +80,18 @@
         kernel,
         out_shape=(
             jax.ShapeDtypeStruct((nq, bsize, depth), jnp.bfloat16),
-            jax.ShapeDtypeStruct((nq, bsize, depth), f32),
+            jax.ShapeDtypeStruct((nq, bsize, depth), jnp.bfloat16),
             jax.ShapeDtypeStruct((nq,) + kv_t, f32),
             jax.ShapeDtypeStruct((npool,) + kv_t, jnp.bfloat16),
         ),
-        in_specs=[smem, smem] + [vmem] * 4,
+        in_specs=[smem, smem] + [vmem] * 5,
         out_specs=(vmem, vmem, vmem, vmem),
         scratch_shapes=[pltpu.VMEM((npool,) + kv_t, f32)],
         compiler_params=pltpu.CompilerParams(vmem_limit_bytes=60 * 1024 * 1024),
-    )(local_ids, remote_ids, qkv, d_out, pool, bias)
-
-
-def finish_kernel(ids_ref, dq_ref, acc_ref, ret_ref, out_ref, total_ref):
-    kvw = acc_ref.shape[1]
-    qw = dq_ref.shape[2]
+    )(local_ids, remote_ids, q, kv, d_out, pool, bias)
+
+
+def finish_kernel(ids_ref, acc_ref, ret_ref, out_ref, total_ref):
     total_ref[...] = acc_ref[...]
 
     def add_slot(j, carry):
@@ -105,25 +102,38 @@
     lax.fori_loop(0, ret_ref.shape[0], add_slot, 0, unroll=8)
 
     def emit(b, carry):
-        out_ref[b, :, pl.ds(0, kvw)] = total_ref[b].T.astype(jnp.bfloat16)
-        out_ref[b, :, pl.ds(kvw, qw)] = dq_ref[b].astype(jnp.bfloat16)
+        out_ref[b] = total_ref[b].T.astype(jnp.bfloat16)
         return carry
 
     lax.fori_loop(0, acc_ref.shape[0], emit, 0, unroll=4)
 
 
-def finish_grads(send_ids, d_q, acc, returned):
-    nq, bsize, depth = d_q.shape
+def finish_grads(send_ids, acc, returned):
+    nq, kvw, bsize = acc.shape
     smem = pl.BlockSpec(memory_space=pltpu.SMEM)
     vmem = pl.BlockSpec(memory_space=pltpu.VMEM)
     return pl.pallas_call(
         finish_kernel,
-        out_shape=jax.ShapeDtypeStruct((nq, bsize, acc.shape[1] + depth), jnp.bfloat16),
-        in_specs=[smem, vmem, vmem, vmem],
+        out_shape=jax.ShapeDtypeStruct((nq, bsize, kvw), jnp.bfloat16),
+        in_specs=[smem, vmem, vmem],
         out_specs=vmem,
         scratch_shapes=[pltpu.VMEM(acc.shape, jnp.float32)],
         compiler_params=pltpu.CompilerParams(vmem_limit_bytes=60 * 1024 * 1024),
-    )(send_ids, d_q, acc, returned)
+    )(send_ids, acc, returned)
+
+
+def head_exchange(x, axis):
+    n = x.shape[0]
+    me = lax.axis_index(axis)
+    twice = jnp.concatenate([x, x], axis=0)
+    rot = lax.dynamic_slice_in_dim(twice, me, n, axis=0)
+    recv = [rot[0]]
+    for k in range(1, n):
+        perm = [(i, (i + k) % n) for i in range(n)]
+        recv.append(lax.ppermute(rot[k], axis, perm))
+    back = jnp.stack([recv[0]] + recv[1:][::-1], axis=0)
+    twice = jnp.concatenate([back, back], axis=0)
+    return lax.dynamic_slice_in_dim(twice, (n - me) % n, n, axis=0)
 
 
 def local(
@@ -157,24 +167,22 @@
     inv = lax.rsqrt(jnp.mean(xf * xf, axis=1, keepdims=True) + EPS)
     normed = xf * inv
     hidden = (normed * norm_gain).astype(bf16)
-    w_heads = (
-        w_qkv.reshape(width, 3, nhead, hwide)[:, jnp.array([1, 2, 0])]
-        .transpose(2, 0, 1, 3)
-        .reshape(nhead, width, 3 * hwide)
-    )
+    w_split = w_qkv.reshape(width, 3, nhead, hwide).transpose(2, 0, 1, 3)
+    w_q = w_split[:, :, 0]
+    w_kv = w_split[:, :, 1:].reshape(nhead, width, 2 * hwide)
     w_out_heads = w_out.reshape(nhead, hwide, width)
-    qkv_own = jnp.einsum("rd,hdc->hrc", hidden, w_heads, preferred_element_type=f32).astype(bf16)
-    qkv = lax.all_to_all(qkv_own, "head", split_axis=0, concat_axis=0, tiled=True).reshape(
-        nblk, bsize, 3 * hwide
-    )
+    kv_own = jnp.einsum("rd,hdc->hrc", hidden, w_kv, preferred_element_type=f32).astype(bf16)
+    kv = lax.all_to_all(kv_own, "head", split_axis=0, concat_axis=0, tiled=True).reshape(
+        nblk, bsize, 2 * hwide
+    )
+    q_own = jnp.einsum("rd,hdc->hrc", hidden, w_q, preferred_element_type=f32).astype(bf16)
+    queries = head_exchange(q_own, "head").reshape(nblk, bsize, hwide)
 
     d_attn = jnp.einsum("rf,hef->hre", grad_y, w_out_heads, preferred_element_type=f32).astype(bf16)
-    d_group = lax.all_to_all(d_attn, "head", split_axis=0, concat_axis=0, tiled=True).reshape(
-        nblk, bsize, hwide
-    )
+    d_group = head_exchange(d_attn, "head").reshape(nblk, bsize, hwide)
 
     send_ids = boundary_blocks[0].reshape(slots)
-    outgoing = jnp.take(qkv[:, :, : 2 * hwide], send_ids, axis=0, mode="clip")
+    outgoing = jnp.take(kv, send_ids, axis=0, mode="clip")
     pool = lax.all_to_all(
         outgoing.reshape(ndom, pair_slots * bsize, 2 * hwide),
         "dom",
@@ -189,15 +197,16 @@
     bias = jnp.repeat(bias, bsize, axis=1)
 
     o, d_q, acc, slot_grads = fused_attention(
-        local_keys.reshape(-1), remote_keys.reshape(-1), qkv, d_group, pool, bias, score_scale
-    )
-
-    attn = lax.all_to_all(
-        o.reshape(nhead, rows, hwide), "head", split_axis=0, concat_axis=0, tiled=True
-    )
+        local_keys.reshape(-1), remote_keys.reshape(-1), queries, kv, d_group, pool, bias,
+        score_scale,
+    )
+
+    attn = head_exchange(o.reshape(nhead, rows, hwide), "head")
     mixed_out = (
         xf + jnp.einsum("hre,hef->rf", attn, w_out_heads, preferred_element_type=f32)
     ).astype(bf16)
+    d_rows_q = head_exchange(d_q.reshape(nhead, rows, hwide), "head")
+    d_hidden_q = jnp.einsum("hrc,hdc->rd", d_rows_q, w_q, preferred_element_type=f32)
 
     returned = lax.all_to_all(
         slot_grads.reshape(ndom, pair_slots * 2 * hwide, bsize),
@@ -206,11 +215,11 @@
         concat_axis=0,
         tiled=True,
     ).reshape(slots, 2 * hwide, bsize)
-    d_qkv = finish_grads(send_ids, d_q, acc, returned)
+    d_kv = finish_grads(send_ids, acc, returned)
     d_rows = lax.all_to_all(
-        d_qkv.reshape(nhead, rows, 3 * hwide), "head", split_axis=0, concat_axis=0, tiled=True
-    )
-    d_hidden = jnp.einsum("hrc,hdc->rd", d_rows, w_heads, preferred_element_type=f32)
+        d_kv.reshape(nhead, rows, 2 * hwide), "head", split_axis=0, concat_axis=0, tiled=True
+    )
+    d_hidden = d_hidden_q + jnp.einsum("hrc,hdc->rd", d_rows, w_kv, preferred_element_type=f32)
     d_normed = d_hidden * norm_gain
     d_input = inv * (d_normed - normed * jnp.mean(d_normed * normed, axis=1, keepdims=True))
     grad_x = (grad_y.astype(f32) + d_input).astype(bf16)

time: 302 us -> 289 us (0.957)
  waiting for transfers between devices: 176 us -> 89.1 us
  starting transfers between devices: 44 us -> 81.9 us
  local copies, waits for them, and re-layouts: 24 us -> 60.6 us
  Pallas kernels: 45.3 us -> 41.8 us
    ppermute x0 -> x28, starting transfers between devices: none -> 47.9 us  [head_exchange(): recv.append(lax.ppermute(rot[k], axis, perm))]
    all_to_all x1, waiting for transfers between devices: 70.1 us -> 24.6 us  [local(): lax.all_to_all(slot_grads.reshape(ndom, pair_slots * 2 * hwide, bsize), '...]
    unnamed x33 -> x113, local copies, waits for them, and re-layouts: 5.58 us -> 38.1 us
    all_to_all x1, waiting for transfers between devices: 65.4 us -> 33 us  [local(): lax.all_to_all(outgoing.reshape(ndom, pair_slots * bsize, 2 * hwide), 'do...]
    all_to_all x4 -> x2, waiting for transfers between devices: 40.4 us -> 10.9 us  [the longest x1 10.9 us: local(): lax.all_to_all(d_kv.reshape(nhead, rows, 2 * hwide), 'head', split_axis=0...]
    ppermute x0 -> x28, waiting for transfers between devices: none -> 20.7 us  [head_exchange(): recv.append(lax.ppermute(rot[k], axis, perm))]
    all_to_all x4 -> x2, starting transfers between devices: 24.4 us -> 15.2 us  [the longest x1 9.92 us: local(): lax.all_to_all(d_kv.reshape(nhead, rows, 2 * hwide), 'head', split_axis=0...]
    dynamic_slice x0 -> x4, local copies, waits for them, and re-layouts: none -> 4.88 us  [head_exchange(): return lax.dynamic_slice_in_dim(twice, (n - me) % n, n, axis=0)]
  transfers between devices with their start and end apart: 6 -> 32, of which waited for: 5 -> 13; matrix products, arithmetic and copies ran while one was open for 7% -> 21% of each run, Pallas kernels for 2% -> 0%
where the time goes in v4:
time: 289 us; the launch traced here: 288 us
  waiting for transfers between devices  89.1 us (31%)
  starting transfers between devices  81.9 us (28%)
  local copies, waits for them, and re-layouts  60.6 us (21%)
  Pallas kernels  41.8 us (14%)
  matrix products  10.4 us (4%)
    ppermute x28, starting transfers between devices, head_exchange(): recv.append(lax.ppermute(rot[k], axis, perm))  47.9 us
    unnamed x113, local copies, waits for them, and re-layouts  38.1 us
    pallas_call x1, Pallas kernels, fused_attention(): pl.pallas_call(kernel, out_shape=(jax.ShapeDtypeStruct((nq, bsize, depth)...  36.6 us
    all_to_all x1, waiting for transfers between devices, local(): lax.all_to_all(outgoing.reshape(ndom, pair_slots * bsize, 2 * hwide), 'do...  33 us
    all_to_all x1, waiting for transfers between devices, local(): lax.all_to_all(slot_grads.reshape(ndom, pair_slots * 2 * hwide, bsize), '...  24.6 us
    ppermute x28, waiting for transfers between devices, head_exchange(): recv.append(lax.ppermute(rot[k], axis, perm))  20.7 us
    all_to_all x1, waiting for transfers between devices, local(): lax.all_to_all(d_kv.reshape(nhead, rows, 2 * hwide), 'head', split_axis=0...  10.9 us
    all_to_all x1, starting transfers between devices, local(): lax.all_to_all(d_kv.reshape(nhead, rows, 2 * hwide), 'head', split_axis=0...  9.92 us
  transfers between devices with their start and end apart: 32, of which 13 were waited for; matrix products, arithmetic and copies ran while one was open for 21% of the time, Pallas kernels for 0%

profile of v4, /device:TPU:1, one launch (start us, length us, event | category | flops | bytes accessed | tf_op | source)
XLA Modules:
  0.0 287.7 jit_solution(16723715915175353300)
XLA Ops:
  0.7 1.0 copy-done
  1.7 1.5 fusion.7
  3.4 0.8 slice_bitcast_fusion.14
  4.3 2.7 collective-permute-start.13
  6.9 1.3 collective-permute-start.12
  8.2 1.6 collective-permute-start.11
  9.8 1.4 collective-permute-start.10
  12.1 1.7 copy.25
  14.0 0.9 copy-done.7
  15.0 1.8 fusion.3
  16.8 5.2 %all-to-all-start = ((bf16[8,512,128]{2,1,0:T(8,128)(2,1)}), bf16[8,512,128]{2,1,0:T(8,128)(2,1)S(1)}, u32[]{:S(2)}, u32[]{:S(2)}) async-start(bf16[8,512,128]{2,1,0:T(8,128)(2,1)} %fusion.3), calls=%async_computation | async-start | bytes 2097152 | tf_op jit(solution)/shard_map/all_to_all | solution.py:175
  22.1 0.8 slice.140
  23.8 0.8 reshape.71.refs_1_
  25.2 1.2 gather_fusion.1
  26.9 1.4 copy.30
  28.3 0.8 reshape.88.ids_ref
  29.1 1.8 fusion.25
  32.0 0.8 slice_bitcast_fusion.21
  33.5 1.4 reshape.70.refs_0_
  34.9 1.3 reshape.107
  37.8 2.6 collective-permute-start.8
  41.0 1.0 collective-permute-done.8
  42.0 4.3 %collective-permute-start.9 = (bf16[512,64]{0,1:T(8,128)(2,1)S(1)}, bf16[512,64]{0,1:T(8,128)(2,1)S(1)}, u32[]{:S(2)}, u32[]{:S(2)}) collective-permute-start(bf16[512,64]{0,1:T(8,128)(2,1)S(1)} %get-tuple-element.31), channel_id=1, source_target_pairs={{0,5},{1,6},{2,7},{3,0},{4,1},{5,2},{6,3},{7,4},{8,13},{9,14},{10,... | collective-permute-start | bytes 196616 | tf_op jit(solution)/shard_map/ppermute | solution.py:133
  48.3 1.2 collective-permute-start.5
  50.1 2.7 gather_fusion
  52.9 9.6 %all-to-all-start.1 = ((bf16[32,384,128]{2,1,0:T(8,128)(2,1)}), bf16[32,384,128]{2,1,0:T(8,128)(2,1)}, u32[]{:S(2)}, u32[]{:S(2)}) async-start(bf16[32,384,128]{2,1,0:T(8,128)(2,1)} %bitcast.206), calls=%async_computation.1 | async-start | bytes 6291456 | tf_op jit(solution)/shard_map/all_to_all | solution.py:186
  62.6 4.3 %collective-permute-start.4 = (bf16[512,64]{0,1:T(8,128)(2,1)S(1)}, bf16[512,64]{0,1:T(8,128)(2,1)S(1)}, u32[]{:S(2)}, u32[]{:S(2)}) collective-permute-start(bf16[512,64]{0,1:T(8,128)(2,1)S(1)} %copy-done.12), channel_id=1, source_target_pairs={{0,3},{1,4},{2,5},{3,6},{4,7},{5,0},{6,1},{7,2},{8,11},{9,12},{10,... | collective-permute-start | bytes 196616 | tf_op jit(solution)/shard_map/ppermute | solution.py:133
  69.2 1.5 constant_dynamic-update-slice_fusion.23
  75.1 1.8 collective-permute-start.1
  77.5 1.1 collective-permute-done.1
  78.6 5.1 %collective-permute-start.2 = (bf16[512,64]{0,1:T(8,128)(2,1)S(1)}, bf16[512,64]{0,1:T(8,128)(2,1)S(1)}, u32[]{:S(2)}, u32[]{:S(2)}) collective-permute-start(bf16[512,64]{0,1:T(8,128)(2,1)S(1)} %copy-done.14), channel_id=1, source_target_pairs={{0,5},{1,6},{2,7},{3,0},{4,1},{5,2},{6,3},{7,4},{8,13},{9,14},{10,... | collective-permute-start | bytes 196616 | tf_op jit(solution)/shard_map/ppermute | solution.py:133
  86.9 1.5 constant_dynamic-update-slice_fusion.9
  88.3 1.1 constant_dynamic-slice_fusion
  89.4 1.3 copy.29
  91.4 1.5 constant_dynamic-update-slice_fusion.7
  95.9 1.5 constant_dynamic-update-slice_fusion.1
  98.0 1.1 constant_dynamic-slice_fusion.1
  99.1 1.4 copy.26
  100.5 33.0 %all-to-all-done.1 = bf16[32,384,128]{2,1,0:T(8,128)(2,1)} async-done(((bf16[32,384,128]{2,1,0:T(8,128)(2,1)}), bf16[32,384,128]{2,1,0:T(8,128)(2,1)}, u32[]{:S(2)}, u32[]{:S(2)}) %all-to-all-start.1) | async-done | bytes 3145760 | tf_op jit(solution)/shard_map/all_to_all | solution.py:186
  133.5 36.6 %shard_map.104 = (bf16[32,128,64]{2,1,0:T(8,128)(2,1)}, bf16[32,128,64]{2,1,0:T(8,128)(2,1)}, f32[32,128,128]{2,1,0:T(8,128)}, bf16[96,128,128]{2,1,0:T(8,128)(2,1)}) custom-call(s32[128]{0:T(128)} %reshape.70.refs_0_, s32[128]{0:T(128)} %copy-done.18, bf16[32,128,64]{2,1,0:T(8,128)(2,1)} %bitcast.213, bf16[32,128,128]{2,1,0:T(8,128)(2,1)} %bitcast.205, ...), custom_call_target="tpu_custom_call" | custom-call | tf_op jit(solution)/shard_map/pallas_call | solution.py:79
  170.1 1.5 copy.31
  171.6 1.5 copy.33
  173.2 9.2 %all-to-all-start.2 = ((bf16[32,384,128]{2,1,0:T(8,128)(2,1)}), bf16[32,384,128]{2,1,0:T(8,128)(2,1)}, u32[]{:S(2)}, u32[]{:S(2)}) async-start(bf16[32,384,128]{2,1,0:T(8,128)(2,1)} %bitcast.214), calls=%async_computation.2 | async-start | bytes 6291456 | tf_op jit(solution)/shard_map/all_to_all | solution.py:211
  182.9 1.5 collective-permute-start.27
  184.4 2.6 collective-permute-start.26
  188.0 1.0 collective-permute-start.21
  189.6 4.3 %collective-permute-done.21 = bf16[512,64]{0,1:T(8,128)(2,1)S(1)} collective-permute-done((bf16[512,64]{0,1:T(8,128)(2,1)S(1)}, bf16[512,64]{0,1:T(8,128)(2,1)S(1)}, u32[]{:S(2)}, u32[]{:S(2)}) %collective-permute-start.21) | collective-permute-done | bytes 65568 | tf_op jit(solution)/shard_map/ppermute | solution.py:133
  193.9 2.3 collective-permute-start.22
  196.2 1.6 collective-permute-done.22
  197.8 1.1 collective-permute-start.23
  198.8 4.5 %collective-permute-done.23 = bf16[512,64]{0,1:T(8,128)(2,1)S(1)} collective-permute-done((bf16[512,64]{0,1:T(8,128)(2,1)S(1)}, bf16[512,64]{0,1:T(8,128)(2,1)S(1)}, u32[]{:S(2)}, u32[]{:S(2)}) %collective-permute-start.23) | collective-permute-done | bytes 65568 | tf_op jit(solution)/shard_map/ppermute | solution.py:133
  203.7 0.9 collective-permute-start.19
  204.6 3.9 %collective-permute-start.18 = (bf16[512,64]{0,1:T(8,128)(2,1)S(1)}, bf16[512,64]{0,1:T(8,128)(2,1)S(1)}, u32[]{:S(2)}, u32[]{:S(2)}) collective-permute-start(bf16[512,64]{0,1:T(8,128)(2,1)S(1)} %get-tuple-element.21), channel_id=1, source_target_pairs={{0,3},{1,4},{2,5},{3,6},{4,7},{5,0},{6,1},{7,2},{8,11},{9,12},{10,... | collective-permute-start | bytes 196616 | tf_op jit(solution)/shard_map/ppermute | solution.py:133
  209.1 3.7 %collective-permute-done.14 = bf16[512,64]{0,1:T(8,128)(2,1)S(1)} collective-permute-done((bf16[512,64]{0,1:T(8,128)(2,1)S(1)}, bf16[512,64]{0,1:T(8,128)(2,1)S(1)}, u32[]{:S(2)}, u32[]{:S(2)}) %collective-permute-start.14) | collective-permute-done | bytes 65568 | tf_op jit(solution)/shard_map/ppermute | solution.py:133
  212.8 2.7 collective-permute-start.15
  216.8 2.7 collective-permute-start.16
  220.2 2.2 collective-permute-done.16
  228.8 24.6 %all-to-all-done.2 = bf16[32,384,128]{2,1,0:T(8,128)(2,1)} async-done(((bf16[32,384,128]{2,1,0:T(8,128)(2,1)}), bf16[32,384,128]{2,1,0:T(8,128)(2,1)}, u32[]{:S(2)}, u32[]{:S(2)}) %all-to-all-start.2) | async-done | bytes 3145760 | tf_op jit(solution)/shard_map/all_to_all | solution.py:211
  253.4 5.2 %shard_map.105 = bf16[32,128,128]{2,1,0:T(8,128)(2,1)} custom-call(s32[96]{0:T(128)} %copy-done.17, f32[32,128,128]{2,1,0:T(8,128)} %get-tuple-element.8.acc_ref, bf16[96,128,128]{2,1,0:T(8,128)(2,1)} %bitcast.81.ret_ref), custom_call_target="tpu_custom_call" | custom-call | tf_op jit(solution)/shard_map/pallas_call | solution.py:115
  258.6 9.9 %all-to-all-start.3 = ((bf16[8,512,128]{2,1,0:T(8,128)(2,1)}), bf16[8,512,128]{2,1,0:T(8,128)(2,1)}, u32[]{:S(2)}, u32[]{:S(2)}) async-start(bf16[8,512,128]{2,1,0:T(8,128)(2,1)} %bitcast.210), calls=%async_computation.3 | async-start | bytes 2097152 | tf_op jit(solution)/shard_map/all_to_all | solution.py:219
  270.4 2.3 fusion.6
  272.7 10.9 %all-to-all-done.3 = bf16[8,512,128]{2,1,0:T(8,128)(2,1)} async-done(((bf16[8,512,128]{2,1,0:T(8,128)(2,1)}), bf16[8,512,128]{2,1,0:T(8,128)(2,1)}, u32[]{:S(2)}, u32[]{:S(2)}) %all-to-all-start.3) | async-done | bytes 1048608 | tf_op jit(solution)/shard_map/all_to_all | solution.py:219
  283.6 2.3 convolution_bitcast_fusion
  286.6 1.1 fusion.13
  (159 shorter events, 38.3 us)
Async XLA Ops:
  0.6 1.0 copy-start
  0.6 11.2 %copy-start.2 = (bf16[512,512]{1,0:T(8,128)(2,1)S(1)}, bf16[512,512]{1,0:T(8,128)(2,1)}, u32[]{:S(2)}) copy-start(bf16[512,512]{1,0:T(8,128)(2,1)} %param.9) | copy-start | bytes 1572868
  3.4 8.7 %copy-start.5 = (bf16[8,512,64]{1,2,0:T(8,128)(2,1)}, bf16[8,512,64]{1,2,0:T(8,128)(2,1)S(1)}, u32[]{:S(2)}) copy-start(bf16[8,512,64]{1,2,0:T(8,128)(2,1)S(1)} %fusion.17) | copy-start | bytes 1572868
  4.3 63.9 %collective-permute-start.13 = (bf16[512,64]{0,1:T(8,128)(2,1)}, bf16[512,64]{0,1:T(8,128)(2,1)S(1)}, u32[]{:S(2)}, u32[]{:S(2)}) collective-permute-start(bf16[512,64]{0,1:T(8,128)(2,1)} %get-tuple-element.26), channel_id=1, source_target_pairs={{0,1},{1,2},{2,3},{3,4},{4,5},{5,6},{6,7},{7,0},{8,9},{9,10},{10,1... | collective-permute-start | bytes 196616 | tf_op jit(solution)/shard_map/ppermute | solution.py:133
  6.9 60.6 %collective-permute-start.12 = (bf16[512,64]{0,1:T(8,128)(2,1)}, bf16[512,64]{0,1:T(8,128)(2,1)S(1)}, u32[]{:S(2)}, u32[]{:S(2)}) collective-permute-start(bf16[512,64]{0,1:T(8,128)(2,1)} %get-tuple-element.28), channel_id=1, source_target_pairs={{0,2},{1,3},{2,4},{3,5},{4,6},{5,7},{6,0},{7,1},{8,10},{9,11},{10,... | collective-permute-start | bytes 196616 | tf_op jit(solution)/shard_map/ppermute | solution.py:133
  8.2 54.3 %collective-permute-start.11 = (bf16[512,64]{0,1:T(8,128)(2,1)}, bf16[512,64]{0,1:T(8,128)(2,1)S(1)}, u32[]{:S(2)}, u32[]{:S(2)}) collective-permute-start(bf16[512,64]{0,1:T(8,128)(2,1)} %get-tuple-element.29), channel_id=1, source_target_pairs={{0,3},{1,4},{2,5},{3,6},{4,7},{5,0},{6,1},{7,2},{8,11},{9,12},{10,... | collective-permute-start | bytes 196616 | tf_op jit(solution)/shard_map/ppermute | solution.py:133
  9.8 38.5 %collective-permute-start.10 = (bf16[512,64]{0,1:T(8,128)(2,1)}, bf16[512,64]{0,1:T(8,128)(2,1)S(1)}, u32[]{:S(2)}, u32[]{:S(2)}) collective-permute-start(bf16[512,64]{0,1:T(8,128)(2,1)} %get-tuple-element.30), channel_id=1, source_target_pairs={{0,4},{1,5},{2,6},{3,7},{4,0},{5,1},{6,2},{7,3},{8,12},{9,13},{10,... | collective-permute-start | bytes 196616 | tf_op jit(solution)/shard_map/ppermute | solution.py:133
  11.2 26.6 %collective-permute-start.7 = (bf16[512,64]{0,1:T(8,128)(2,1)}, bf16[512,64]{0,1:T(8,128)(2,1)S(1)}, u32[]{:S(2)}, u32[]{:S(2)}) collective-permute-start(bf16[512,64]{0,1:T(8,128)(2,1)} %get-tuple-element.33), channel_id=1, source_target_pairs={{0,7},{1,0},{2,1},{3,2},{4,3},{5,4},{6,5},{7,6},{8,15},{9,8},{10,9... | collective-permute-start | bytes 196616 | tf_op jit(solution)/shard_map/ppermute | solution.py:133
  12.1 2.9 %copy-start.23 = (f32[512]{0:T(512)S(1)}, f32[512]{0:T(512)}, u32[]{:S(2)}) copy-start(f32[512]{0:T(512)} %param.10) | copy-start | bytes 6148
  14.0 1.0 copy-start.7
  14.0 8.9 %copy-start.25 = (s32[32,1]{0,1:T(1,128)S(1)}, s32[32,1]{0,1:T(1,128)}, u32[]{:S(2)}) copy-start(s32[32,1]{0,1:T(1,128)} %param.17) | copy-start | bytes 388
  14.0 9.1 %copy-start.21 = (s32[32,4]{0,1:T(4,128)S(1)}, s32[32,4]{0,1:T(4,128)}, u32[]{:S(2)}) copy-start(s32[32,4]{0,1:T(4,128)} %param.15) | copy-start | bytes 1540
  16.8 33.3 %all-to-all-start = ((bf16[8,512,128]{2,1,0:T(8,128)(2,1)}), bf16[8,512,128]{2,1,0:T(8,128)(2,1)S(1)}, u32[]{:S(2)}, u32[]{:S(2)}) async-start(bf16[8,512,128]{2,1,0:T(8,128)(2,1)} %fusion.3), calls=%async_computation | async-start | bytes 2097152 | tf_op jit(solution)/shard_map/all_to_all | solution.py:175
  24.6 0.5 copy-start.18
  26.4 6.5 %copy-start.22 = (s32[32,4]{0,1:T(4,128)S(1)}, s32[32,4]{0,1:T(4,128)}, u32[]{:S(2)}) copy-start(s32[32,4]{0,1:T(4,128)} %param.14) | copy-start | bytes 1540
  29.1 8.7 %copy-start.17 = (s32[96]{0:T(128)}, s32[96]{0:T(128)S(1)}, u32[]{:S(2)}) copy-start(s32[96]{0:T(128)S(1)} %reshape.88.ids_ref) | copy-start | bytes 1156
  31.2 0.8 copy-start.4
  37.8 4.2 %collective-permute-start.8 = (bf16[512,64]{0,1:T(8,128)(2,1)}, bf16[512,64]{0,1:T(8,128)(2,1)S(1)}, u32[]{:S(2)}, u32[]{:S(2)}) collective-permute-start(bf16[512,64]{0,1:T(8,128)(2,1)} %get-tuple-element.32), channel_id=1, source_target_pairs={{0,6},{1,7},{2,0},{3,1},{4,2},{5,3},{6,4},{7,5},{8,14},{9,15},{10,... | collective-permute-start | bytes 196616 | tf_op jit(solution)/shard_map/ppermute | solution.py:133
  42.0 7.5 %copy-start.8 = (bf16[512,64]{0,1:T(8,128)(2,1)}, bf16[512,64]{0,1:T(8,128)(2,1)S(1)}, u32[]{:S(2)}) copy-start(bf16[512,64]{0,1:T(8,128)(2,1)S(1)} %collective-permute-done.8) | copy-start | bytes 196612
  42.0 5.7 %collective-permute-start.9 = (bf16[512,64]{0,1:T(8,128)(2,1)S(1)}, bf16[512,64]{0,1:T(8,128)(2,1)S(1)}, u32[]{:S(2)}, u32[]{:S(2)}) collective-permute-start(bf16[512,64]{0,1:T(8,128)(2,1)S(1)} %get-tuple-element.31), channel_id=1, source_target_pairs={{0,5},{1,6},{2,7},{3,0},{4,1},{5,2},{6,3},{7,4},{8,13},{9,14},{10,... | collective-permute-start | bytes 196616 | tf_op jit(solution)/shard_map/ppermute | solution.py:133
  47.7 1.8 copy-start.10
  47.7 43.0 %collective-permute-start.6 = (bf16[512,64]{0,1:T(8,128)(2,1)}, bf16[512,64]{0,1:T(8,128)(2,1)S(1)}, u32[]{:S(2)}, u32[]{:S(2)}) collective-permute-start(bf16[512,64]{0,1:T(8,128)(2,1)} %get-tuple-element.34), channel_id=1, source_target_pairs={{0,1},{1,2},{2,3},{3,4},{4,5},{5,6},{6,7},{7,0},{8,9},{9,10},{10,1... | collective-permute-start | bytes 196616 | tf_op jit(solution)/shard_map/ppermute | solution.py:133
  48.3 38.5 %collective-permute-start.5 = (bf16[512,64]{0,1:T(8,128)(2,1)}, bf16[512,64]{0,1:T(8,128)(2,1)}, u32[]{:S(2)}, u32[]{:S(2)}) collective-permute-start(bf16[512,64]{0,1:T(8,128)(2,1)} %get-tuple-element.36), channel_id=1, source_target_pairs={{0,2},{1,3},{2,4},{3,5},{4,6},{5,7},{6,0},{7,1},{8,10},{9,11},{10,... | collective-permute-start | bytes 196616 | tf_op jit(solution)/shard_map/ppermute | solution.py:133
  50.1 2.7 copy-start.1
  52.9 9.7 %copy-start.12 = (bf16[512,64]{0,1:T(8,128)(2,1)S(1)}, bf16[512,64]{0,1:T(8,128)(2,1)}, u32[]{:S(2)}) copy-start(bf16[512,64]{0,1:T(8,128)(2,1)} %get-tuple-element.37) | copy-start | bytes 196612
  52.9 14.7 %copy-start.13 = (bf16[512,64]{0,1:T(8,128)(2,1)S(1)}, bf16[512,64]{0,1:T(8,128)(2,1)}, u32[]{:S(2)}) copy-start(bf16[512,64]{0,1:T(8,128)(2,1)} %get-tuple-element.38) | copy-start | bytes 196612
  52.9 15.3 %copy-start.16 = (bf16[512,64]{0,1:T(8,128)(2,1)S(1)}, bf16[512,64]{0,1:T(8,128)(2,1)}, u32[]{:S(2)}) copy-start(bf16[512,64]{0,1:T(8,128)(2,1)} %get-tuple-element.41) | copy-start | bytes 196612
  52.9 18.4 %copy-start.9 = (bf16[512,64]{0,1:T(8,128)(2,1)S(1)}, bf16[512,64]{0,1:T(8,128)(2,1)}, u32[]{:S(2)}) copy-start(bf16[512,64]{0,1:T(8,128)(2,1)} %copy-done.8) | copy-start | bytes 196612
  52.9 19.0 %copy-start.11 = (bf16[512,64]{0,1:T(8,128)(2,1)S(1)}, bf16[512,64]{0,1:T(8,128)(2,1)}, u32[]{:S(2)}) copy-start(bf16[512,64]{0,1:T(8,128)(2,1)} %copy-done.10) | copy-start | bytes 196612
  52.9 22.2 %copy-start.15 = (bf16[512,64]{0,1:T(8,128)(2,1)S(1)}, bf16[512,64]{0,1:T(8,128)(2,1)}, u32[]{:S(2)}) copy-start(bf16[512,64]{0,1:T(8,128)(2,1)} %get-tuple-element.40) | copy-start | bytes 196612
  52.9 25.7 %copy-start.14 = (bf16[512,64]{0,1:T(8,128)(2,1)S(1)}, bf16[512,64]{0,1:T(8,128)(2,1)}, u32[]{:S(2)}) copy-start(bf16[512,64]{0,1:T(8,128)(2,1)} %get-tuple-element.39) | copy-start | bytes 196612
  52.9 80.6 %all-to-all-start.1 = ((bf16[32,384,128]{2,1,0:T(8,128)(2,1)}), bf16[32,384,128]{2,1,0:T(8,128)(2,1)}, u32[]{:S(2)}, u32[]{:S(2)}) async-start(bf16[32,384,128]{2,1,0:T(8,128)(2,1)} %bitcast.206), calls=%async_computation.1 | async-start | bytes 6291456 | tf_op jit(solution)/shard_map/all_to_all | solution.py:186
  62.6 23.7 %collective-permute-start.4 = (bf16[512,64]{0,1:T(8,128)(2,1)S(1)}, bf16[512,64]{0,1:T(8,128)(2,1)S(1)}, u32[]{:S(2)}, u32[]{:S(2)}) collective-permute-start(bf16[512,64]{0,1:T(8,128)(2,1)S(1)} %copy-done.12), channel_id=1, source_target_pairs={{0,3},{1,4},{2,5},{3,6},{4,7},{5,0},{6,1},{7,2},{8,11},{9,12},{10,... | collective-permute-start | bytes 196616 | tf_op jit(solution)/shard_map/ppermute | solution.py:133
  67.6 18.1 %collective-permute-start.3 = (bf16[512,64]{0,1:T(8,128)(2,1)S(1)}, bf16[512,64]{0,1:T(8,128)(2,1)S(1)}, u32[]{:S(2)}, u32[]{:S(2)}) collective-permute-start(bf16[512,64]{0,1:T(8,128)(2,1)S(1)} %copy-done.13), channel_id=1, source_target_pairs={{0,4},{1,5},{2,6},{3,7},{4,0},{5,1},{6,2},{7,3},{8,12},{9,13},{10,... | collective-permute-start | bytes 196616 | tf_op jit(solution)/shard_map/ppermute | solution.py:133
  68.2 6.9 %collective-permute-start = (bf16[512,64]{0,1:T(8,128)(2,1)S(1)}, bf16[512,64]{0,1:T(8,128)(2,1)S(1)}, u32[]{:S(2)}, u32[]{:S(2)}) collective-permute-start(bf16[512,64]{0,1:T(8,128)(2,1)S(1)} %copy-done.16), channel_id=1, source_target_pairs={{0,7},{1,0},{2,1},{3,2},{4,3},{5,4},{6,5},{7,6},{8,15},{9,8},{10,9... | collective-permute-start | bytes 196616 | tf_op jit(solution)/shard_map/ppermute | solution.py:133
  75.1 3.5 %collective-permute-start.1 = (bf16[512,64]{0,1:T(8,128)(2,1)S(1)}, bf16[512,64]{0,1:T(8,128)(2,1)S(1)}, u32[]{:S(2)}, u32[]{:S(2)}) collective-permute-start(bf16[512,64]{0,1:T(8,128)(2,1)S(1)} %copy-done.15), channel_id=1, source_target_pairs={{0,6},{1,7},{2,0},{3,1},{4,2},{5,3},{6,4},{7,5},{8,14},{9,15},{10,... | collective-permute-start | bytes 196616 | tf_op jit(solution)/shard_map/ppermute | solution.py:133
  78.6 6.4 %collective-permute-start.2 = (bf16[512,64]{0,1:T(8,128)(2,1)S(1)}, bf16[512,64]{0,1:T(8,128)(2,1)S(1)}, u32[]{:S(2)}, u32[]{:S(2)}) collective-permute-start(bf16[512,64]{0,1:T(8,128)(2,1)S(1)} %copy-done.14), channel_id=1, source_target_pairs={{0,5},{1,6},{2,7},{3,0},{4,1},{5,2},{6,3},{7,4},{8,13},{9,14},{10,... | collective-permute-start | bytes 196616 | tf_op jit(solution)/shard_map/ppermute | solution.py:133
  173.2 80.2 %all-to-all-start.2 = ((bf16[32,384,128]{2,1,0:T(8,128)(2,1)}), bf16[32,384,128]{2,1,0:T(8,128)(2,1)}, u32[]{:S(2)}, u32[]{:S(2)}) async-start(bf16[32,384,128]{2,1,0:T(8,128)(2,1)} %bitcast.214), calls=%async_computation.2 | async-start | bytes 6291456 | tf_op jit(solution)/shard_map/all_to_all | solution.py:211
  182.9 25.8 %collective-permute-start.27 = (bf16[512,64]{0,1:T(8,128)(2,1)S(1)}, bf16[512,64]{0,1:T(8,128)(2,1)S(1)}, u32[]{:S(2)}, u32[]{:S(2)}) collective-permute-start(bf16[512,64]{0,1:T(8,128)(2,1)S(1)} %get-tuple-element.10), channel_id=1, source_target_pairs={{0,1},{1,2},{2,3},{3,4},{4,5},{5,6},{6,7},{7,0},{8,9},{9,10},{10,1... | collective-permute-start | bytes 196616 | tf_op jit(solution)/shard_map/ppermute | solution.py:133
  184.4 24.2 %collective-permute-start.26 = (bf16[512,64]{0,1:T(8,128)(2,1)S(1)}, bf16[512,64]{0,1:T(8,128)(2,1)S(1)}, u32[]{:S(2)}, u32[]{:S(2)}) collective-permute-start(bf16[512,64]{0,1:T(8,128)(2,1)S(1)} %get-tuple-element.12), channel_id=1, source_target_pairs={{0,2},{1,3},{2,4},{3,5},{4,6},{5,7},{6,0},{7,1},{8,10},{9,11},{10,... | collective-permute-start | bytes 196616 | tf_op jit(solution)/shard_map/ppermute | solution.py:133
  187.0 17.6 %collective-permute-start.25 = (bf16[512,64]{0,1:T(8,128)(2,1)S(1)}, bf16[512,64]{0,1:T(8,128)(2,1)S(1)}, u32[]{:S(2)}, u32[]{:S(2)}) collective-permute-start(bf16[512,64]{0,1:T(8,128)(2,1)S(1)} %get-tuple-element.13), channel_id=1, source_target_pairs={{0,3},{1,4},{2,5},{3,6},{4,7},{5,0},{6,1},{7,2},{8,11},{9,12},{10,... | collective-permute-start | bytes 196616 | tf_op jit(solution)/shard_map/ppermute | solution.py:133
  187.5 16.2 %collective-permute-start.24 = (bf16[512,64]{0,1:T(8,128)(2,1)S(1)}, bf16[512,64]{0,1:T(8,128)(2,1)S(1)}, u32[]{:S(2)}, u32[]{:S(2)}) collective-permute-start(bf16[512,64]{0,1:T(8,128)(2,1)S(1)} %get-tuple-element.14), channel_id=1, source_target_pairs={{0,4},{1,5},{2,6},{3,7},{4,0},{5,1},{6,2},{7,3},{8,12},{9,13},{10,... | collective-permute-start | bytes 196616 | tf_op jit(solution)/shard_map/ppermute | solution.py:133
  188.0 5.9 %collective-permute-start.21 = (bf16[512,64]{0,1:T(8,128)(2,1)S(1)}, bf16[512,64]{0,1:T(8,128)(2,1)S(1)}, u32[]{:S(2)}, u32[]{:S(2)}) collective-permute-start(bf16[512,64]{0,1:T(8,128)(2,1)S(1)} %get-tuple-element.17), channel_id=1, source_target_pairs={{0,7},{1,0},{2,1},{3,2},{4,3},{5,4},{6,5},{7,6},{8,15},{9,8},{10,9... | collective-permute-start | bytes 196616 | tf_op jit(solution)/shard_map/ppermute | solution.py:133
  193.9 3.9 %collective-permute-start.22 = (bf16[512,64]{0,1:T(8,128)(2,1)S(1)}, bf16[512,64]{0,1:T(8,128)(2,1)S(1)}, u32[]{:S(2)}, u32[]{:S(2)}) collective-permute-start(bf16[512,64]{0,1:T(8,128)(2,1)S(1)} %get-tuple-element.16), channel_id=1, source_target_pairs={{0,6},{1,7},{2,0},{3,1},{4,2},{5,3},{6,4},{7,5},{8,14},{9,15},{10,... | collective-permute-start | bytes 196616 | tf_op jit(solution)/shard_map/ppermute | solution.py:133
  197.8 5.6 %collective-permute-start.23 = (bf16[512,64]{0,1:T(8,128)(2,1)S(1)}, bf16[512,64]{0,1:T(8,128)(2,1)S(1)}, u32[]{:S(2)}, u32[]{:S(2)}) collective-permute-start(bf16[512,64]{0,1:T(8,128)(2,1)S(1)} %get-tuple-element.15), channel_id=1, source_target_pairs={{0,5},{1,6},{2,7},{3,0},{4,1},{5,2},{6,3},{7,4},{8,13},{9,14},{10,... | collective-permute-start | bytes 196616 | tf_op jit(solution)/shard_map/ppermute | solution.py:133
  203.4 21.6 %collective-permute-start.20 = (bf16[512,64]{0,1:T(8,128)(2,1)S(1)}, bf16[512,64]{0,1:T(8,128)(2,1)S(1)}, u32[]{:S(2)}, u32[]{:S(2)}) collective-permute-start(bf16[512,64]{0,1:T(8,128)(2,1)S(1)} %get-tuple-element.18), channel_id=1, source_target_pairs={{0,1},{1,2},{2,3},{3,4},{4,5},{5,6},{6,7},{7,0},{8,9},{9,10},{10,1... | collective-permute-start | bytes 196616 | tf_op jit(solution)/shard_map/ppermute | solution.py:133
  203.7 20.6 %collective-permute-start.19 = (bf16[512,64]{0,1:T(8,128)(2,1)S(1)}, bf16[512,64]{0,1:T(8,128)(2,1)S(1)}, u32[]{:S(2)}, u32[]{:S(2)}) collective-permute-start(bf16[512,64]{0,1:T(8,128)(2,1)S(1)} %get-tuple-element.20), channel_id=1, source_target_pairs={{0,2},{1,3},{2,4},{3,5},{4,6},{5,7},{6,0},{7,1},{8,10},{9,11},{10,... | collective-permute-start | bytes 196616 | tf_op jit(solution)/shard_map/ppermute | solution.py:133
  204.6 19.0 %collective-permute-start.18 = (bf16[512,64]{0,1:T(8,128)(2,1)S(1)}, bf16[512,64]{0,1:T(8,128)(2,1)S(1)}, u32[]{:S(2)}, u32[]{:S(2)}) collective-permute-start(bf16[512,64]{0,1:T(8,128)(2,1)S(1)} %get-tuple-element.21), channel_id=1, source_target_pairs={{0,3},{1,4},{2,5},{3,6},{4,7},{5,0},{6,1},{7,2},{8,11},{9,12},{10,... | collective-permute-start | bytes 196616 | tf_op jit(solution)/shard_map/ppermute | solution.py:133
  208.6 14.5 %collective-permute-start.17 = (bf16[512,64]{0,1:T(8,128)(2,1)S(1)}, bf16[512,64]{0,1:T(8,128)(2,1)S(1)}, u32[]{:S(2)}, u32[]{:S(2)}) collective-permute-start(bf16[512,64]{0,1:T(8,128)(2,1)S(1)} %get-tuple-element.22), channel_id=1, source_target_pairs={{0,4},{1,5},{2,6},{3,7},{4,0},{5,1},{6,2},{7,3},{8,12},{9,13},{10,... | collective-permute-start | bytes 196616 | tf_op jit(solution)/shard_map/ppermute | solution.py:133
  208.7 4.1 %collective-permute-start.14 = (bf16[512,64]{0,1:T(8,128)(2,1)S(1)}, bf16[512,64]{0,1:T(8,128)(2,1)S(1)}, u32[]{:S(2)}, u32[]{:S(2)}) collective-permute-start(bf16[512,64]{0,1:T(8,128)(2,1)S(1)} %get-tuple-element.25), channel_id=1, source_target_pairs={{0,7},{1,0},{2,1},{3,2},{4,3},{5,4},{6,5},{7,6},{8,15},{9,8},{10,9... | collective-permute-start | bytes 196616 | tf_op jit(solution)/shard_map/ppermute | solution.py:133
  212.8 4.1 %collective-permute-start.15 = (bf16[512,64]{0,1:T(8,128)(2,1)S(1)}, bf16[512,64]{0,1:T(8,128)(2,1)S(1)}, u32[]{:S(2)}, u32[]{:S(2)}) collective-permute-start(bf16[512,64]{0,1:T(8,128)(2,1)S(1)} %get-tuple-element.24), channel_id=1, source_target_pairs={{0,6},{1,7},{2,0},{3,1},{4,2},{5,3},{6,4},{7,5},{8,14},{9,15},{10,... | collective-permute-start | bytes 196616 | tf_op jit(solution)/shard_map/ppermute | solution.py:133
  216.8 5.6 %collective-permute-start.16 = (bf16[512,64]{0,1:T(8,128)(2,1)S(1)}, bf16[512,64]{0,1:T(8,128)(2,1)S(1)}, u32[]{:S(2)}, u32[]{:S(2)}) collective-permute-start(bf16[512,64]{0,1:T(8,128)(2,1)S(1)} %get-tuple-element.23), channel_id=1, source_target_pairs={{0,5},{1,6},{2,7},{3,0},{4,1},{5,2},{6,3},{7,4},{8,13},{9,14},{10,... | collective-permute-start | bytes 196616 | tf_op jit(solution)/shard_map/ppermute | solution.py:133
  226.3 1.9 copy-start.19
  253.4 17.0 %copy-start.3 = (bf16[512,512]{1,0:T(8,128)(2,1)S(1)}, bf16[512,512]{1,0:T(8,128)(2,1)}, u32[]{:S(2)}) copy-start(bf16[512,512]{1,0:T(8,128)(2,1)} %param.9) | copy-start | bytes 1572868
  258.6 25.0 %all-to-all-start.3 = ((bf16[8,512,128]{2,1,0:T(8,128)(2,1)}), bf16[8,512,128]{2,1,0:T(8,128)(2,1)}, u32[]{:S(2)}, u32[]{:S(2)}) async-start(bf16[8,512,128]{2,1,0:T(8,128)(2,1)} %bitcast.210), calls=%async_computation.3 | async-start | bytes 2097152 | tf_op jit(solution)/shard_map/all_to_all | solution.py:219
  270.4 15.5 %copy-start.24 = (f32[512]{0:T(512)S(1)}, f32[512]{0:T(512)}, u32[]{:S(2)}) copy-start(f32[512]{0:T(512)} %param.10) | copy-start | bytes 6148
  272.7 13.9 %copy-start.6 = (bf16[512,512]{1,0:T(8,128)(2,1)S(1)}, bf16[512,512]{1,0:T(8,128)(2,1)}, u32[]{:S(2)}) copy-start(bf16[512,512]{1,0:T(8,128)(2,1)} %param.13) | copy-start | bytes 1572868
  283.6 2.3 copy-start.20

commit v5 on v4

--- a/solution.py
+++ b/solution.py
@@ -176,13 +176,13 @@
         nblk, bsize, 2 * hwide
     )
     q_own = jnp.einsum("rd,hdc->hrc", hidden, w_q, preferred_element_type=f32).astype(bf16)
-    queries = head_exchange(q_own, "head").reshape(nblk, bsize, hwide)
-
     d_attn = jnp.einsum("rf,hef->hre", grad_y, w_out_heads, preferred_element_type=f32).astype(bf16)
-    d_group = head_exchange(d_attn, "head").reshape(nblk, bsize, hwide)
 
     send_ids = boundary_blocks[0].reshape(slots)
     outgoing = jnp.take(kv, send_ids, axis=0, mode="clip")
+    outgoing, q_own, d_attn = lax.optimization_barrier((outgoing, q_own, d_attn))
+    queries = head_exchange(q_own, "head").reshape(nblk, bsize, hwide)
+    d_group = head_exchange(d_attn, "head").reshape(nblk, bsize, hwide)
     pool = lax.all_to_all(
         outgoing.reshape(ndom, pair_slots * bsize, 2 * hwide),
         "dom",

time: 289 us -> 266 us (0.920)
  local copies, waits for them, and re-layouts: 60.6 us -> 38 us
    unnamed x113 -> x97, local copies, waits for them, and re-layouts: 38.1 us -> 22.2 us
    all_to_all x1, waiting for transfers between devices: 33 us -> 18.2 us  [local(): lax.all_to_all(outgoing.reshape(ndom, pair_slots * bsize, 2 * hwide), 'do...]
    ppermute x28, waiting for transfers between devices: 20.7 us -> 28.3 us  [head_exchange(): recv.append(lax.ppermute(rot[k], axis, perm))]
    all_to_all x1, waiting for transfers between devices: 0.01 us -> 6.55 us  [local(): lax.all_to_all(kv_own, 'head', split_axis=0, concat_axis=0, tiled=True)]
  transfers between devices with their start and end apart: 32 -> 32, of which waited for: 13 -> 16; matrix products, arithmetic and copies ran while one was open for 21% -> 14% of each run, Pallas kernels for 0% -> 0%
where the time goes in v5:
time: 266 us
  waiting for transfers between devices  89.6 us (34%)
  starting transfers between devices  79.7 us (30%)
  Pallas kernels  41.8 us (16%)
  local copies, waits for them, and re-layouts  38 us (14%)
  matrix products  10.1 us (4%)
  other arithmetic  5.2 us (2%)
    ppermute x28, starting transfers between devices, head_exchange(): recv.append(lax.ppermute(rot[k], axis, perm))  45.2 us
    pallas_call x1, Pallas kernels, fused_attention(): pl.pallas_call(kernel, out_shape=(jax.ShapeDtypeStruct((nq, bsize, depth)...  36.6 us
    ppermute x28, waiting for transfers between devices, head_exchange(): recv.append(lax.ppermute(rot[k], axis, perm))  28.3 us
    all_to_all x1, waiting for transfers between devices, local(): lax.all_to_all(slot_grads.reshape(ndom, pair_slots * 2 * hwide, bsize), '...  25.6 us
    unnamed x97, local copies, waits for them, and re-layouts  22.2 us
    all_to_all x1, waiting for transfers between devices, local(): lax.all_to_all(outgoing.reshape(ndom, pair_slots * bsize, 2 * hwide), 'do...  18.2 us
    all_to_all x1, waiting for transfers between devices, local(): lax.all_to_all(d_kv.reshape(nhead, rows, 2 * hwide), 'head', split_axis=0...  10.9 us
    all_to_all x1, starting transfers between devices, local(): lax.all_to_all(outgoing.reshape(ndom, pair_slots * bsize, 2 * hwide), 'do...  10.6 us
  transfers between devices with their start and end apart: 32, of which 16 were waited for; matrix products, arithmetic and copies ran while one was open for 14% of the time, Pallas kernels for 0%

profile of v5, /device:TPU:1, one launch (start us, length us, event | category | flops | bytes accessed | tf_op | source)
XLA Modules:
  0.0 265.5 jit_solution(14598012245749541512)
XLA Ops:
  0.6 1.3 fusion.14
  2.0 1.8 copy.26
  3.9 0.9 copy-done.7
  4.9 1.8 fusion.3
  6.7 6.7 %all-to-all-start = ((bf16[8,512,128]{2,1,0:T(8,128)(2,1)}), bf16[8,512,128]{2,1,0:T(8,128)(2,1)S(1)}, u32[]{:S(2)}, u32[]{:S(2)}) async-start(bf16[8,512,128]{2,1,0:T(8,128)(2,1)} %fusion.3), calls=%async_computation | async-start | bytes 2097152 | tf_op jit(solution)/shard_map/all_to_all | solution.py:175
  13.3 0.8 slice.141
  14.5 0.7 reshape.70.refs_0_
  15.4 1.2 gather_fusion.1
  17.1 0.7 copy.47
  17.8 1.8 fusion.24
  19.7 0.9 convert_bitcast_fusion
  20.5 1.3 fusion.7
  21.8 6.6 %all-to-all-done = bf16[8,512,128]{2,1,0:T(8,128)(2,1)S(1)} async-done(((bf16[8,512,128]{2,1,0:T(8,128)(2,1)}), bf16[8,512,128]{2,1,0:T(8,128)(2,1)S(1)}, u32[]{:S(2)}, u32[]{:S(2)}) %all-to-all-start) | async-done | bytes 1048608 | tf_op jit(solution)/shard_map/all_to_all | solution.py:175
  28.3 2.7 %gather_fusion = bf16[96,128,128]{2,1,0:T(8,128)(2,1)} fusion(bf16[32,128,128]{2,1,0:T(8,128)(2,1)S(1)} %bitcast.204, s32[1024]{0:T(1024)S(1)} %pad_clamp_fusion.1), kind=kCustom, calls=%fused_computation | custom fusion | bytes 6291840 | tf_op jit(solution)/shard_map/jit(_take)/gather | solution.py:182
  31.1 10.6 %all-to-all-start.1 = ((bf16[32,384,128]{2,1,0:T(8,128)(2,1)}), bf16[32,384,128]{2,1,0:T(8,128)(2,1)}, u32[]{:S(2)}, u32[]{:S(2)}) async-start(bf16[32,384,128]{2,1,0:T(8,128)(2,1)} %bitcast.206), calls=%async_computation.1 | async-start | bytes 6291456 | tf_op jit(solution)/shard_map/all_to_all | solution.py:186
  41.9 1.2 fusion.17
  43.1 1.4 collective-permute-start.13
  44.6 2.2 collective-permute-start.11
  46.8 1.4 collective-permute-start.10
  48.2 0.9 collective-permute-start.7
  49.1 0.7 slice_bitcast_fusion.21
  49.8 2.5 collective-permute-done.7
  52.3 3.4 %collective-permute-start.8 = (bf16[512,64]{0,1:T(8,128)(2,1)S(1)}, bf16[512,64]{0,1:T(8,128)(2,1)S(1)}, u32[]{:S(2)}, u32[]{:S(2)}) collective-permute-start(bf16[512,64]{0,1:T(8,128)(2,1)S(1)} %get-tuple-element.38), channel_id=1, source_target_pairs={{0,6},{1,7},{2,0},{3,1},{4,2},{5,3},{6,4},{7,5},{8,14},{9,15},{10,... | collective-permute-start | bytes 196616 | tf_op jit(solution)/shard_map/ppermute | solution.py:133
  55.6 1.3 collective-permute-done.8
  57.0 1.8 collective-permute-start.9
  58.8 3.8 %collective-permute-done.9 = bf16[512,64]{0,1:T(8,128)(2,1)S(1)} collective-permute-done((bf16[512,64]{0,1:T(8,128)(2,1)S(1)}, bf16[512,64]{0,1:T(8,128)(2,1)S(1)}, u32[]{:S(2)}, u32[]{:S(2)}) %collective-permute-start.9) | collective-permute-done | bytes 65568 | tf_op jit(solution)/shard_map/ppermute | solution.py:133
  63.6 4.4 %collective-permute-start.4 = (bf16[512,64]{0,1:T(8,128)(2,1)S(1)}, bf16[512,64]{0,1:T(8,128)(2,1)S(1)}, u32[]{:S(2)}, u32[]{:S(2)}) collective-permute-start(bf16[512,64]{0,1:T(8,128)(2,1)S(1)} %get-tuple-element.43), channel_id=1, source_target_pairs={{0,3},{1,4},{2,5},{3,6},{4,7},{5,0},{6,1},{7,2},{8,11},{9,12},{10,... | collective-permute-start | bytes 196616 | tf_op jit(solution)/shard_map/ppermute | solution.py:133
  68.7 3.6 %collective-permute-done = bf16[512,64]{0,1:T(8,128)(2,1)S(1)} collective-permute-done((bf16[512,64]{0,1:T(8,128)(2,1)S(1)}, bf16[512,64]{0,1:T(8,128)(2,1)S(1)}, u32[]{:S(2)}, u32[]{:S(2)}) %collective-permute-start) | collective-permute-done | bytes 65568 | tf_op jit(solution)/shard_map/ppermute | solution.py:133
  72.2 2.7 %collective-permute-start.1 = (bf16[512,64]{0,1:T(8,128)(2,1)S(1)}, bf16[512,64]{0,1:T(8,128)(2,1)S(1)}, u32[]{:S(2)}, u32[]{:S(2)}) collective-permute-start(bf16[512,64]{0,1:T(8,128)(2,1)S(1)} %get-tuple-element.46), channel_id=1, source_target_pairs={{0,6},{1,7},{2,0},{3,1},{4,2},{5,3},{6,4},{7,5},{8,14},{9,15},{10,... | collective-permute-start | bytes 196616 | tf_op jit(solution)/shard_map/ppermute | solution.py:133
  75.6 0.7 collective-permute-done.1
  76.3 2.7 %collective-permute-start.2 = (bf16[512,64]{0,1:T(8,128)(2,1)S(1)}, bf16[512,64]{0,1:T(8,128)(2,1)S(1)}, u32[]{:S(2)}, u32[]{:S(2)}) collective-permute-start(bf16[512,64]{0,1:T(8,128)(2,1)S(1)} %get-tuple-element.45), channel_id=1, source_target_pairs={{0,5},{1,6},{2,7},{3,0},{4,1},{5,2},{6,3},{7,4},{8,13},{9,14},{10,... | collective-permute-start | bytes 196616 | tf_op jit(solution)/shard_map/ppermute | solution.py:133
  79.7 2.2 collective-permute-done.2
  84.4 1.3 copy.31
  88.2 1.5 constant_dynamic-update-slice_fusion.4
  92.2 1.1 constant_dynamic-slice_fusion.1
  93.3 1.4 copy.30
  94.7 18.2 %all-to-all-done.1 = bf16[32,384,128]{2,1,0:T(8,128)(2,1)} async-done(((bf16[32,384,128]{2,1,0:T(8,128)(2,1)}), bf16[32,384,128]{2,1,0:T(8,128)(2,1)}, u32[]{:S(2)}, u32[]{:S(2)}) %all-to-all-start.1) | async-done | bytes 3145760 | tf_op jit(solution)/shard_map/all_to_all | solution.py:186
  112.8 36.6 %shard_map.104 = (bf16[32,128,64]{2,1,0:T(8,128)(2,1)}, bf16[32,128,64]{2,1,0:T(8,128)(2,1)}, f32[32,128,128]{2,1,0:T(8,128)}, bf16[96,128,128]{2,1,0:T(8,128)(2,1)}) custom-call(s32[128]{0:T(128)} %reshape.70.refs_0_, s32[128]{0:T(128)} %copy-done.10, bf16[32,128,64]{2,1,0:T(8,128)(2,1)} %bitcast.213, bf16[32,128,128]{2,1,0:T(8,128)(2,1)} %bitcast.205, ...), custom_call_target="tpu_custom_call" | custom-call | tf_op jit(solution)/shard_map/pallas_call | solution.py:79
  149.4 1.5 copy.32
  150.9 1.5 copy.34
  152.5 8.9 %all-to-all-start.2 = ((bf16[32,384,128]{2,1,0:T(8,128)(2,1)}), bf16[32,384,128]{2,1,0:T(8,128)(2,1)}, u32[]{:S(2)}, u32[]{:S(2)}) async-start(bf16[32,384,128]{2,1,0:T(8,128)(2,1)} %bitcast.214), calls=%async_computation.2 | async-start | bytes 6291456 | tf_op jit(solution)/shard_map/all_to_all | solution.py:211
  161.8 1.5 collective-permute-start.27
  163.7 1.8 collective-permute-start.25
  165.5 1.4 collective-permute-start.24
  166.9 1.0 collective-permute-start.21
  168.5 2.5 collective-permute-done.21
  171.0 3.4 %collective-permute-start.22 = (bf16[512,64]{0,1:T(8,128)(2,1)S(1)}, bf16[512,64]{0,1:T(8,128)(2,1)S(1)}, u32[]{:S(2)}, u32[]{:S(2)}) collective-permute-start(bf16[512,64]{0,1:T(8,128)(2,1)S(1)} %get-tuple-element.22), channel_id=1, source_target_pairs={{0,6},{1,7},{2,0},{3,1},{4,2},{5,3},{6,4},{7,5},{8,14},{9,15},{10,... | collective-permute-start | bytes 196616 | tf_op jit(solution)/shard_map/ppermute | solution.py:133
  174.4 1.3 collective-permute-done.22
  175.7 1.8 collective-permute-start.23
  177.5 3.8 %collective-permute-done.23 = bf16[512,64]{0,1:T(8,128)(2,1)S(1)} collective-permute-done((bf16[512,64]{0,1:T(8,128)(2,1)S(1)}, bf16[512,64]{0,1:T(8,128)(2,1)S(1)}, u32[]{:S(2)}, u32[]{:S(2)}) %collective-permute-start.23) | collective-permute-done | bytes 65568 | tf_op jit(solution)/shard_map/ppermute | solution.py:133
  181.9 1.0 collective-permute-start.19
  182.9 3.9 %collective-permute-start.18 = (bf16[512,64]{0,1:T(8,128)(2,1)S(1)}, bf16[512,64]{0,1:T(8,128)(2,1)S(1)}, u32[]{:S(2)}, u32[]{:S(2)}) collective-permute-start(bf16[512,64]{0,1:T(8,128)(2,1)S(1)} %get-tuple-element.27), channel_id=1, source_target_pairs={{0,3},{1,4},{2,5},{3,6},{4,7},{5,0},{6,1},{7,2},{8,11},{9,12},{10,... | collective-permute-start | bytes 196616 | tf_op jit(solution)/shard_map/ppermute | solution.py:133
  187.3 3.7 %collective-permute-done.14 = bf16[512,64]{0,1:T(8,128)(2,1)S(1)} collective-permute-done((bf16[512,64]{0,1:T(8,128)(2,1)S(1)}, bf16[512,64]{0,1:T(8,128)(2,1)S(1)}, u32[]{:S(2)}, u32[]{:S(2)}) %collective-permute-start.14) | collective-permute-done | bytes 65568 | tf_op jit(solution)/shard_map/ppermute | solution.py:133
  191.0 2.7 %collective-permute-start.15 = (bf16[512,64]{0,1:T(8,128)(2,1)S(1)}, bf16[512,64]{0,1:T(8,128)(2,1)S(1)}, u32[]{:S(2)}, u32[]{:S(2)}) collective-permute-start(bf16[512,64]{0,1:T(8,128)(2,1)S(1)} %get-tuple-element.30), channel_id=1, source_target_pairs={{0,6},{1,7},{2,0},{3,1},{4,2},{5,3},{6,4},{7,5},{8,14},{9,15},{10,... | collective-permute-start | bytes 196616 | tf_op jit(solution)/shard_map/ppermute | solution.py:133
  194.3 0.7 collective-permute-done.15
  195.0 2.7 %collective-permute-start.16 = (bf16[512,64]{0,1:T(8,128)(2,1)S(1)}, bf16[512,64]{0,1:T(8,128)(2,1)S(1)}, u32[]{:S(2)}, u32[]{:S(2)}) collective-permute-start(bf16[512,64]{0,1:T(8,128)(2,1)S(1)} %get-tuple-element.29), channel_id=1, source_target_pairs={{0,5},{1,6},{2,7},{3,0},{4,1},{5,2},{6,3},{7,4},{8,13},{9,14},{10,... | collective-permute-start | bytes 196616 | tf_op jit(solution)/shard_map/ppermute | solution.py:133
  198.4 2.2 collective-permute-done.16
  207.0 25.6 %all-to-all-done.2 = bf16[32,384,128]{2,1,0:T(8,128)(2,1)} async-done(((bf16[32,384,128]{2,1,0:T(8,128)(2,1)}), bf16[32,384,128]{2,1,0:T(8,128)(2,1)}, u32[]{:S(2)}, u32[]{:S(2)}) %all-to-all-start.2) | async-done | bytes 3145760 | tf_op jit(solution)/shard_map/all_to_all | solution.py:211
  232.6 5.2 %shard_map.105 = bf16[32,128,128]{2,1,0:T(8,128)(2,1)} custom-call(s32[96]{0:T(128)} %copy-done.9, f32[32,128,128]{2,1,0:T(8,128)} %get-tuple-element.14.acc_ref, bf16[96,128,128]{2,1,0:T(8,128)(2,1)} %bitcast.81.ret_ref), custom_call_target="tpu_custom_call" | custom-call | tf_op jit(solution)/shard_map/pallas_call | solution.py:115
  237.8 8.5 %all-to-all-start.3 = ((bf16[8,512,128]{2,1,0:T(8,128)(2,1)}), bf16[8,512,128]{2,1,0:T(8,128)(2,1)}, u32[]{:S(2)}, u32[]{:S(2)}) async-start(bf16[8,512,128]{2,1,0:T(8,128)(2,1)} %bitcast.210), calls=%async_computation.3 | async-start | bytes 2097152 | tf_op jit(solution)/shard_map/all_to_all | solution.py:219
  248.2 2.3 fusion.6
  250.5 10.9 %all-to-all-done.3 = bf16[8,512,128]{2,1,0:T(8,128)(2,1)} async-done(((bf16[8,512,128]{2,1,0:T(8,128)(2,1)}), bf16[8,512,128]{2,1,0:T(8,128)(2,1)}, u32[]{:S(2)}, u32[]{:S(2)}) %all-to-all-start.3) | async-done | bytes 1048608 | tf_op jit(solution)/shard_map/all_to_all | solution.py:219
  261.4 2.3 convolution_bitcast_fusion
  264.4 1.1 fusion.13
  (143 shorter events, 24.4 us)
Async XLA Ops:
  0.6 19.9 %copy-start = (bf16[512,512]{1,0:T(8,128)(2,1)S(1)}, bf16[512,512]{1,0:T(8,128)(2,1)}, u32[]{:S(2)}) copy-start(bf16[512,512]{1,0:T(8,128)(2,1)} %param.12) | copy-start | bytes 1572868
  1.9 2.9 %copy-start.2 = (bf16[512,512]{1,0:T(8,128)(2,1)S(1)}, bf16[512,512]{1,0:T(8,128)(2,1)}, u32[]{:S(2)}) copy-start(bf16[512,512]{1,0:T(8,128)(2,1)} %param.9) | copy-start | bytes 1572868
  1.9 2.9 %copy-start.15 = (f32[512]{0:T(512)S(1)}, f32[512]{0:T(512)}, u32[]{:S(2)}) copy-start(f32[512]{0:T(512)} %param.10) | copy-start | bytes 6148
  3.9 1.0 copy-start.7
  4.9 9.3 %copy-start.17 = (s32[32,1]{0,1:T(1,128)S(1)}, s32[32,1]{0,1:T(1,128)}, u32[]{:S(2)}) copy-start(s32[32,1]{0,1:T(1,128)} %param.17) | copy-start | bytes 388
  4.9 9.5 %copy-start.13 = (s32[32,4]{0,1:T(4,128)S(1)}, s32[32,4]{0,1:T(4,128)}, u32[]{:S(2)}) copy-start(s32[32,4]{0,1:T(4,128)} %param.14) | copy-start | bytes 1540
  4.9 10.3 %copy-start.14 = (s32[32,4]{0,1:T(4,128)S(1)}, s32[32,4]{0,1:T(4,128)}, u32[]{:S(2)}) copy-start(s32[32,4]{0,1:T(4,128)} %param.15) | copy-start | bytes 1540
  6.7 21.7 %all-to-all-start = ((bf16[8,512,128]{2,1,0:T(8,128)(2,1)}), bf16[8,512,128]{2,1,0:T(8,128)(2,1)S(1)}, u32[]{:S(2)}, u32[]{:S(2)}) async-start(bf16[8,512,128]{2,1,0:T(8,128)(2,1)} %fusion.3), calls=%async_computation | async-start | bytes 2097152 | tf_op jit(solution)/shard_map/all_to_all | solution.py:175
  13.3 3.4 %copy-start.16 = (s32[1,32,3]{1,0,2:T(1,128)S(1)}, s32[1,32,3]{1,0,2:T(1,128)}, u32[]{:S(2)}) copy-start(s32[1,32,3]{1,0,2:T(1,128)} %param.16) | copy-start | bytes 1156
  15.3 4.3 %copy-start.10 = (s32[128]{0:T(128)}, s32[128]{0:T(128)S(1)}, u32[]{:S(2)}) copy-start(s32[128]{0:T(128)S(1)} %reshape.71.refs_1_) | copy-start | bytes 1540
  16.9 14.1 %copy-start.9 = (s32[96]{0:T(128)}, s32[96]{0:T(128)S(1)}, u32[]{:S(2)}) copy-start(s32[96]{0:T(128)S(1)} %reshape.88.ids_ref) | copy-start | bytes 1156
  17.8 2.7 %copy-start.4 = (bf16[512,512]{1,0:T(8,128)(2,1)S(1)}, bf16[512,512]{1,0:T(8,128)(2,1)}, u32[]{:S(2)}) copy-start(bf16[512,512]{1,0:T(8,128)(2,1)} %param.13) | copy-start | bytes 1572868
  28.3 2.7 %copy-start.1 = (bf16[8,512,128]{2,1,0:T(8,128)(2,1)}, bf16[8,512,128]{2,1,0:T(8,128)(2,1)S(1)}, u32[]{:S(2)}) copy-start(bf16[8,512,128]{2,1,0:T(8,128)(2,1)S(1)} %all-to-all-done) | copy-start | bytes 3145732
  31.1 10.6 %copy-start.6 = (bf16[8,512,64]{1,2,0:T(8,128)(2,1)S(1)}, bf16[8,512,64]{1,2,0:T(8,128)(2,1)}, u32[]{:S(2)}) copy-start(bf16[8,512,64]{1,2,0:T(8,128)(2,1)} %convert_bitcast_fusion) | copy-start | bytes 1572868
  31.1 81.8 %all-to-all-start.1 = ((bf16[32,384,128]{2,1,0:T(8,128)(2,1)}), bf16[32,384,128]{2,1,0:T(8,128)(2,1)}, u32[]{:S(2)}, u32[]{:S(2)}) async-start(bf16[32,384,128]{2,1,0:T(8,128)(2,1)} %bitcast.206), calls=%async_computation.1 | async-start | bytes 6291456 | tf_op jit(solution)/shard_map/all_to_all | solution.py:186
  43.1 25.0 %collective-permute-start.13 = (bf16[512,64]{0,1:T(8,128)(2,1)S(1)}, bf16[512,64]{0,1:T(8,128)(2,1)S(1)}, u32[]{:S(2)}, u32[]{:S(2)}) collective-permute-start(bf16[512,64]{0,1:T(8,128)(2,1)S(1)} %get-tuple-element.32), channel_id=1, source_target_pairs={{0,1},{1,2},{2,3},{3,4},{4,5},{5,6},{6,7},{7,0},{8,9},{9,10},{10,1... | collective-permute-start | bytes 196616 | tf_op jit(solution)/shard_map/ppermute | solution.py:133
  44.6 23.4 %collective-permute-start.12 = (bf16[512,64]{0,1:T(8,128)(2,1)S(1)}, bf16[512,64]{0,1:T(8,128)(2,1)S(1)}, u32[]{:S(2)}, u32[]{:S(2)}) collective-permute-start(bf16[512,64]{0,1:T(8,128)(2,1)S(1)} %get-tuple-element.34), channel_id=1, source_target_pairs={{0,2},{1,3},{2,4},{3,5},{4,6},{5,7},{6,0},{7,1},{8,10},{9,11},{10,... | collective-permute-start | bytes 196616 | tf_op jit(solution)/shard_map/ppermute | solution.py:133
  44.6 19.0 %collective-permute-start.11 = (bf16[512,64]{0,1:T(8,128)(2,1)S(1)}, bf16[512,64]{0,1:T(8,128)(2,1)S(1)}, u32[]{:S(2)}, u32[]{:S(2)}) collective-permute-start(bf16[512,64]{0,1:T(8,128)(2,1)S(1)} %get-tuple-element.35), channel_id=1, source_target_pairs={{0,3},{1,4},{2,5},{3,6},{4,7},{5,0},{6,1},{7,2},{8,11},{9,12},{10,... | collective-permute-start | bytes 196616 | tf_op jit(solution)/shard_map/ppermute | solution.py:133
  46.8 16.4 %collective-permute-start.10 = (bf16[512,64]{0,1:T(8,128)(2,1)S(1)}, bf16[512,64]{0,1:T(8,128)(2,1)S(1)}, u32[]{:S(2)}, u32[]{:S(2)}) collective-permute-start(bf16[512,64]{0,1:T(8,128)(2,1)S(1)} %get-tuple-element.36), channel_id=1, source_target_pairs={{0,4},{1,5},{2,6},{3,7},{4,0},{5,1},{6,2},{7,3},{8,12},{9,13},{10,... | collective-permute-start | bytes 196616 | tf_op jit(solution)/shard_map/ppermute | solution.py:133
  48.2 4.1 %collective-permute-start.7 = (bf16[512,64]{0,1:T(8,128)(2,1)S(1)}, bf16[512,64]{0,1:T(8,128)(2,1)S(1)}, u32[]{:S(2)}, u32[]{:S(2)}) collective-permute-start(bf16[512,64]{0,1:T(8,128)(2,1)S(1)} %get-tuple-element.39), channel_id=1, source_target_pairs={{0,7},{1,0},{2,1},{3,2},{4,3},{5,4},{6,5},{7,6},{8,15},{9,8},{10,9... | collective-permute-start | bytes 196616 | tf_op jit(solution)/shard_map/ppermute | solution.py:133
  52.3 4.7 %collective-permute-start.8 = (bf16[512,64]{0,1:T(8,128)(2,1)S(1)}, bf16[512,64]{0,1:T(8,128)(2,1)S(1)}, u32[]{:S(2)}, u32[]{:S(2)}) collective-permute-start(bf16[512,64]{0,1:T(8,128)(2,1)S(1)} %get-tuple-element.38), channel_id=1, source_target_pairs={{0,6},{1,7},{2,0},{3,1},{4,2},{5,3},{6,4},{7,5},{8,14},{9,15},{10,... | collective-permute-start | bytes 196616 | tf_op jit(solution)/shard_map/ppermute | solution.py:133
  57.0 5.6 %collective-permute-start.9 = (bf16[512,64]{0,1:T(8,128)(2,1)S(1)}, bf16[512,64]{0,1:T(8,128)(2,1)S(1)}, u32[]{:S(2)}, u32[]{:S(2)}) collective-permute-start(bf16[512,64]{0,1:T(8,128)(2,1)S(1)} %get-tuple-element.37), channel_id=1, source_target_pairs={{0,5},{1,6},{2,7},{3,0},{4,1},{5,2},{6,3},{7,4},{8,13},{9,14},{10,... | collective-permute-start | bytes 196616 | tf_op jit(solution)/shard_map/ppermute | solution.py:133
  62.6 23.2 %collective-permute-start.6 = (bf16[512,64]{0,1:T(8,128)(2,1)}, bf16[512,64]{0,1:T(8,128)(2,1)S(1)}, u32[]{:S(2)}, u32[]{:S(2)}) collective-permute-start(bf16[512,64]{0,1:T(8,128)(2,1)} %get-tuple-element.40), channel_id=1, source_target_pairs={{0,1},{1,2},{2,3},{3,4},{4,5},{5,6},{6,7},{7,0},{8,9},{9,10},{10,1... | collective-permute-start | bytes 196616 | tf_op jit(solution)/shard_map/ppermute | solution.py:133
  63.1 20.6 %collective-permute-start.5 = (bf16[512,64]{0,1:T(8,128)(2,1)S(1)}, bf16[512,64]{0,1:T(8,128)(2,1)S(1)}, u32[]{:S(2)}, u32[]{:S(2)}) collective-permute-start(bf16[512,64]{0,1:T(8,128)(2,1)S(1)} %get-tuple-element.42), channel_id=1, source_target_pairs={{0,2},{1,3},{2,4},{3,5},{4,6},{5,7},{6,0},{7,1},{8,10},{9,11},{10,... | collective-permute-start | bytes 196616 | tf_op jit(solution)/shard_map/ppermute | solution.py:133
  63.6 19.5 %collective-permute-start.4 = (bf16[512,64]{0,1:T(8,128)(2,1)S(1)}, bf16[512,64]{0,1:T(8,128)(2,1)S(1)}, u32[]{:S(2)}, u32[]{:S(2)}) collective-permute-start(bf16[512,64]{0,1:T(8,128)(2,1)S(1)} %get-tuple-element.43), channel_id=1, source_target_pairs={{0,3},{1,4},{2,5},{3,6},{4,7},{5,0},{6,1},{7,2},{8,11},{9,12},{10,... | collective-permute-start | bytes 196616 | tf_op jit(solution)/shard_map/ppermute | solution.py:133
  68.0 14.5 %collective-permute-start.3 = (bf16[512,64]{0,1:T(8,128)(2,1)S(1)}, bf16[512,64]{0,1:T(8,128)(2,1)S(1)}, u32[]{:S(2)}, u32[]{:S(2)}) collective-permute-start(bf16[512,64]{0,1:T(8,128)(2,1)S(1)} %get-tuple-element.44), channel_id=1, source_target_pairs={{0,4},{1,5},{2,6},{3,7},{4,0},{5,1},{6,2},{7,3},{8,12},{9,13},{10,... | collective-permute-start | bytes 196616 | tf_op jit(solution)/shard_map/ppermute | solution.py:133
  68.1 4.1 %collective-permute-start = (bf16[512,64]{0,1:T(8,128)(2,1)S(1)}, bf16[512,64]{0,1:T(8,128)(2,1)S(1)}, u32[]{:S(2)}, u32[]{:S(2)}) collective-permute-start(bf16[512,64]{0,1:T(8,128)(2,1)S(1)} %get-tuple-element.47), channel_id=1, source_target_pairs={{0,7},{1,0},{2,1},{3,2},{4,3},{5,4},{6,5},{7,6},{8,15},{9,8},{10,9... | collective-permute-start | bytes 196616 | tf_op jit(solution)/shard_map/ppermute | solution.py:133
  72.2 4.1 %collective-permute-start.1 = (bf16[512,64]{0,1:T(8,128)(2,1)S(1)}, bf16[512,64]{0,1:T(8,128)(2,1)S(1)}, u32[]{:S(2)}, u32[]{:S(2)}) collective-permute-start(bf16[512,64]{0,1:T(8,128)(2,1)S(1)} %get-tuple-element.46), channel_id=1, source_target_pairs={{0,6},{1,7},{2,0},{3,1},{4,2},{5,3},{6,4},{7,5},{8,14},{9,15},{10,... | collective-permute-start | bytes 196616 | tf_op jit(solution)/shard_map/ppermute | solution.py:133
  76.3 5.6 %collective-permute-start.2 = (bf16[512,64]{0,1:T(8,128)(2,1)S(1)}, bf16[512,64]{0,1:T(8,128)(2,1)S(1)}, u32[]{:S(2)}, u32[]{:S(2)}) collective-permute-start(bf16[512,64]{0,1:T(8,128)(2,1)S(1)} %get-tuple-element.45), channel_id=1, source_target_pairs={{0,5},{1,6},{2,7},{3,0},{4,1},{5,2},{6,3},{7,4},{8,13},{9,14},{10,... | collective-permute-start | bytes 196616 | tf_op jit(solution)/shard_map/ppermute | solution.py:133
  81.9 1.9 copy-start.8
  152.5 80.1 %all-to-all-start.2 = ((bf16[32,384,128]{2,1,0:T(8,128)(2,1)}), bf16[32,384,128]{2,1,0:T(8,128)(2,1)}, u32[]{:S(2)}, u32[]{:S(2)}) async-start(bf16[32,384,128]{2,1,0:T(8,128)(2,1)} %bitcast.214), calls=%async_computation.2 | async-start | bytes 6291456 | tf_op jit(solution)/shard_map/all_to_all | solution.py:211
  161.8 25.0 %collective-permute-start.27 = (bf16[512,64]{0,1:T(8,128)(2,1)S(1)}, bf16[512,64]{0,1:T(8,128)(2,1)S(1)}, u32[]{:S(2)}, u32[]{:S(2)}) collective-permute-start(bf16[512,64]{0,1:T(8,128)(2,1)S(1)} %get-tuple-element.16), channel_id=1, source_target_pairs={{0,1},{1,2},{2,3},{3,4},{4,5},{5,6},{6,7},{7,0},{8,9},{9,10},{10,1... | collective-permute-start | bytes 196616 | tf_op jit(solution)/shard_map/ppermute | solution.py:133
  163.3 23.4 %collective-permute-start.26 = (bf16[512,64]{0,1:T(8,128)(2,1)S(1)}, bf16[512,64]{0,1:T(8,128)(2,1)S(1)}, u32[]{:S(2)}, u32[]{:S(2)}) collective-permute-start(bf16[512,64]{0,1:T(8,128)(2,1)S(1)} %get-tuple-element.18), channel_id=1, source_target_pairs={{0,2},{1,3},{2,4},{3,5},{4,6},{5,7},{6,0},{7,1},{8,10},{9,11},{10,... | collective-permute-start | bytes 196616 | tf_op jit(solution)/shard_map/ppermute | solution.py:133
  163.7 19.2 %collective-permute-start.25 = (bf16[512,64]{0,1:T(8,128)(2,1)S(1)}, bf16[512,64]{0,1:T(8,128)(2,1)S(1)}, u32[]{:S(2)}, u32[]{:S(2)}) collective-permute-start(bf16[512,64]{0,1:T(8,128)(2,1)S(1)} %get-tuple-element.19), channel_id=1, source_target_pairs={{0,3},{1,4},{2,5},{3,6},{4,7},{5,0},{6,1},{7,2},{8,11},{9,12},{10,... | collective-permute-start | bytes 196616 | tf_op jit(solution)/shard_map/ppermute | solution.py:133
  165.5 16.4 %collective-permute-start.24 = (bf16[512,64]{0,1:T(8,128)(2,1)S(1)}, bf16[512,64]{0,1:T(8,128)(2,1)S(1)}, u32[]{:S(2)}, u32[]{:S(2)}) collective-permute-start(bf16[512,64]{0,1:T(8,128)(2,1)S(1)} %get-tuple-element.20), channel_id=1, source_target_pairs={{0,4},{1,5},{2,6},{3,7},{4,0},{5,1},{6,2},{7,3},{8,12},{9,13},{10,... | collective-permute-start | bytes 196616 | tf_op jit(solution)/shard_map/ppermute | solution.py:133
  166.9 4.1 %collective-permute-start.21 = (bf16[512,64]{0,1:T(8,128)(2,1)S(1)}, bf16[512,64]{0,1:T(8,128)(2,1)S(1)}, u32[]{:S(2)}, u32[]{:S(2)}) collective-permute-start(bf16[512,64]{0,1:T(8,128)(2,1)S(1)} %get-tuple-element.23), channel_id=1, source_target_pairs={{0,7},{1,0},{2,1},{3,2},{4,3},{5,4},{6,5},{7,6},{8,15},{9,8},{10,9... | collective-permute-start | bytes 196616 | tf_op jit(solution)/shard_map/ppermute | solution.py:133
  171.0 4.7 %collective-permute-start.22 = (bf16[512,64]{0,1:T(8,128)(2,1)S(1)}, bf16[512,64]{0,1:T(8,128)(2,1)S(1)}, u32[]{:S(2)}, u32[]{:S(2)}) collective-permute-start(bf16[512,64]{0,1:T(8,128)(2,1)S(1)} %get-tuple-element.22), channel_id=1, source_target_pairs={{0,6},{1,7},{2,0},{3,1},{4,2},{5,3},{6,4},{7,5},{8,14},{9,15},{10,... | collective-permute-start | bytes 196616 | tf_op jit(solution)/shard_map/ppermute | solution.py:133
  175.7 5.6 %collective-permute-start.23 = (bf16[512,64]{0,1:T(8,128)(2,1)S(1)}, bf16[512,64]{0,1:T(8,128)(2,1)S(1)}, u32[]{:S(2)}, u32[]{:S(2)}) collective-permute-start(bf16[512,64]{0,1:T(8,128)(2,1)S(1)} %get-tuple-element.21), channel_id=1, source_target_pairs={{0,5},{1,6},{2,7},{3,0},{4,1},{5,2},{6,3},{7,4},{8,13},{9,14},{10,... | collective-permute-start | bytes 196616 | tf_op jit(solution)/shard_map/ppermute | solution.py:133
  181.3 21.8 %collective-permute-start.20 = (bf16[512,64]{0,1:T(8,128)(2,1)S(1)}, bf16[512,64]{0,1:T(8,128)(2,1)S(1)}, u32[]{:S(2)}, u32[]{:S(2)}) collective-permute-start(bf16[512,64]{0,1:T(8,128)(2,1)S(1)} %get-tuple-element.24), channel_id=1, source_target_pairs={{0,1},{1,2},{2,3},{3,4},{4,5},{5,6},{6,7},{7,0},{8,9},{9,10},{10,1... | collective-permute-start | bytes 196616 | tf_op jit(solution)/shard_map/ppermute | solution.py:133
  181.9 20.6 %collective-permute-start.19 = (bf16[512,64]{0,1:T(8,128)(2,1)S(1)}, bf16[512,64]{0,1:T(8,128)(2,1)S(1)}, u32[]{:S(2)}, u32[]{:S(2)}) collective-permute-start(bf16[512,64]{0,1:T(8,128)(2,1)S(1)} %get-tuple-element.26), channel_id=1, source_target_pairs={{0,2},{1,3},{2,4},{3,5},{4,6},{5,7},{6,0},{7,1},{8,10},{9,11},{10,... | collective-permute-start | bytes 196616 | tf_op jit(solution)/shard_map/ppermute | solution.py:133
  182.9 19.0 %collective-permute-start.18 = (bf16[512,64]{0,1:T(8,128)(2,1)S(1)}, bf16[512,64]{0,1:T(8,128)(2,1)S(1)}, u32[]{:S(2)}, u32[]{:S(2)}) collective-permute-start(bf16[512,64]{0,1:T(8,128)(2,1)S(1)} %get-tuple-element.27), channel_id=1, source_target_pairs={{0,3},{1,4},{2,5},{3,6},{4,7},{5,0},{6,1},{7,2},{8,11},{9,12},{10,... | collective-permute-start | bytes 196616 | tf_op jit(solution)/shard_map/ppermute | solution.py:133
  186.7 14.5 %collective-permute-start.17 = (bf16[512,64]{0,1:T(8,128)(2,1)S(1)}, bf16[512,64]{0,1:T(8,128)(2,1)S(1)}, u32[]{:S(2)}, u32[]{:S(2)}) collective-permute-start(bf16[512,64]{0,1:T(8,128)(2,1)S(1)} %get-tuple-element.28), channel_id=1, source_target_pairs={{0,4},{1,5},{2,6},{3,7},{4,0},{5,1},{6,2},{7,3},{8,12},{9,13},{10,... | collective-permute-start | bytes 196616 | tf_op jit(solution)/shard_map/ppermute | solution.py:133
  186.9 4.1 %collective-permute-start.14 = (bf16[512,64]{0,1:T(8,128)(2,1)S(1)}, bf16[512,64]{0,1:T(8,128)(2,1)S(1)}, u32[]{:S(2)}, u32[]{:S(2)}) collective-permute-start(bf16[512,64]{0,1:T(8,128)(2,1)S(1)} %get-tuple-element.31), channel_id=1, source_target_pairs={{0,7},{1,0},{2,1},{3,2},{4,3},{5,4},{6,5},{7,6},{8,15},{9,8},{10,9... | collective-permute-start | bytes 196616 | tf_op jit(solution)/shard_map/ppermute | solution.py:133
  191.0 4.1 %collective-permute-start.15 = (bf16[512,64]{0,1:T(8,128)(2,1)S(1)}, bf16[512,64]{0,1:T(8,128)(2,1)S(1)}, u32[]{:S(2)}, u32[]{:S(2)}) collective-permute-start(bf16[512,64]{0,1:T(8,128)(2,1)S(1)} %get-tuple-element.30), channel_id=1, source_target_pairs={{0,6},{1,7},{2,0},{3,1},{4,2},{5,3},{6,4},{7,5},{8,14},{9,15},{10,... | collective-permute-start | bytes 196616 | tf_op jit(solution)/shard_map/ppermute | solution.py:133
  195.0 5.6 %collective-permute-start.16 = (bf16[512,64]{0,1:T(8,128)(2,1)S(1)}, bf16[512,64]{0,1:T(8,128)(2,1)S(1)}, u32[]{:S(2)}, u32[]{:S(2)}) collective-permute-start(bf16[512,64]{0,1:T(8,128)(2,1)S(1)} %get-tuple-element.29), channel_id=1, source_target_pairs={{0,5},{1,6},{2,7},{3,0},{4,1},{5,2},{6,3},{7,4},{8,13},{9,14},{10,... | collective-permute-start | bytes 196616 | tf_op jit(solution)/shard_map/ppermute | solution.py:133
  204.4 1.9 copy-start.11
  232.6 15.5 %copy-start.3 = (bf16[512,512]{1,0:T(8,128)(2,1)S(1)}, bf16[512,512]{1,0:T(8,128)(2,1)}, u32[]{:S(2)}) copy-start(bf16[512,512]{1,0:T(8,128)(2,1)} %param.9) | copy-start | bytes 1572868
  237.8 23.6 %all-to-all-start.3 = ((bf16[8,512,128]{2,1,0:T(8,128)(2,1)}), bf16[8,512,128]{2,1,0:T(8,128)(2,1)}, u32[]{:S(2)}, u32[]{:S(2)}) async-start(bf16[8,512,128]{2,1,0:T(8,128)(2,1)} %bitcast.210), calls=%async_computation.3 | async-start | bytes 2097152 | tf_op jit(solution)/shard_map/all_to_all | solution.py:219
  250.5 13.9 %copy-start.5 = (bf16[512,512]{1,0:T(8,128)(2,1)S(1)}, bf16[512,512]{1,0:T(8,128)(2,1)}, u32[]{:S(2)}) copy-start(bf16[512,512]{1,0:T(8,128)(2,1)} %param.13) | copy-start | bytes 1572868
  261.4 2.3 copy-start.12

commit v6 on v5

--- a/solution.py
+++ b/solution.py
@@ -60,7 +60,7 @@
             slot_acc[ids_r[i]] = slot_acc[ids_r[i]] + part
         return carry
 
-    lax.fori_loop(0, nq, body, 0, unroll=2)
+    lax.fori_loop(0, nq, body, 0, unroll=4)
     slot_ref[...] = slot_acc[...].astype(bf16)
 
 
@@ -125,15 +125,13 @@
 def head_exchange(x, axis):
     n = x.shape[0]
     me = lax.axis_index(axis)
-    twice = jnp.concatenate([x, x], axis=0)
-    rot = lax.dynamic_slice_in_dim(twice, me, n, axis=0)
-    recv = [rot[0]]
+    out = x
     for k in range(1, n):
         perm = [(i, (i + k) % n) for i in range(n)]
-        recv.append(lax.ppermute(rot[k], axis, perm))
-    back = jnp.stack([recv[0]] + recv[1:][::-1], axis=0)
-    twice = jnp.concatenate([back, back], axis=0)
-    return lax.dynamic_slice_in_dim(twice, (n - me) % n, n, axis=0)
+        part = lax.dynamic_index_in_dim(x, (me + k) % n, 0, keepdims=True)
+        got = lax.ppermute(part, axis, perm)
+        out = lax.dynamic_update_index_in_dim(out, got, (me + n - k) % n, 0)
+    return out
 
 
 def local(

time: 266 us -> 265 us (level)
  waiting for transfers between devices: 89.6 us -> 114 us
  local copies, waits for them, and re-layouts: 38 us -> 21 us
  starting transfers between devices: 79.7 us -> 74.3 us
    ppermute x28, waiting for transfers between devices: 28.3 us -> 51 us  [head_exchange(): got = lax.ppermute(part, axis, perm)]
    unnamed x97 -> x41, local copies, waits for them, and re-layouts: 22.2 us -> 3.76 us
    all_to_all x1, waiting for transfers between devices: 25.6 us -> 37.5 us  [local(): lax.all_to_all(slot_grads.reshape(ndom, pair_slots * 2 * hwide, bsize), '...]
    all_to_all x1, waiting for transfers between devices: 10.9 us -> 0.01 us  [local(): lax.all_to_all(d_kv.reshape(nhead, rows, 2 * hwide), 'head', split_axis=0...]
    dynamic_update_slice x0 -> x28, local copies, waits for them, and re-layouts: none -> 7.12 us  [head_exchange(): out = lax.dynamic_update_index_in_dim(out, got, (me + n - k) % n, 0)]
    ppermute x28, starting transfers between devices: 45.2 us -> 39.8 us  [head_exchange(): got = lax.ppermute(part, axis, perm)]
    all_to_all x1, waiting for transfers between devices: 6.55 us -> 9.96 us  [local(): lax.all_to_all(kv_own, 'head', split_axis=0, concat_axis=0, tiled=True)]
    dynamic_slice x4 -> x6, local copies, waits for them, and re-layouts: 3.81 us -> 0.85 us  [head_exchange(): part = lax.dynamic_index_in_dim(x, (me + k) % n, 0, keepdims=True)]
  transfers between devices with their start and end apart: 32 -> 32, of which waited for: 16 -> 17; matrix products, arithmetic and copies ran while one was open for 14% -> 8% of each run, Pallas kernels for 0% -> 2%
where the time goes in v6:
time: 265 us; the launch traced here: 264 us
  waiting for transfers between devices  114 us (43%)
  starting transfers between devices  74.3 us (28%)
  Pallas kernels  40.8 us (15%)
  local copies, waits for them, and re-layouts  21 us (8%)
  matrix products  9.07 us (3%)
  other arithmetic  3.38 us (1%)
    ppermute x28, waiting for transfers between devices, head_exchange(): got = lax.ppermute(part, axis, perm)  51 us
    ppermute x28, starting transfers between devices, head_exchange(): got = lax.ppermute(part, axis, perm)  39.8 us
    all_to_all x1, waiting for transfers between devices, local(): lax.all_to_all(slot_grads.reshape(ndom, pair_slots * 2 * hwide, bsize), '...  37.5 us
    pallas_call x1, Pallas kernels, fused_attention(): pl.pallas_call(kernel, out_shape=(jax.ShapeDtypeStruct((nq, bsize, depth)...  35.6 us
    all_to_all x1, waiting for transfers between devices, local(): lax.all_to_all(outgoing.reshape(ndom, pair_slots * bsize, 2 * hwide), 'do...  15.8 us
    all_to_all x1, starting transfers between devices, local(): lax.all_to_all(outgoing.reshape(ndom, pair_slots * bsize, 2 * hwide), 'do...  10.6 us
    all_to_all x1, waiting for transfers between devices, local(): lax.all_to_all(kv_own, 'head', split_axis=0, concat_axis=0, tiled=True)  9.96 us
    all_to_all x1, starting transfers between devices, local(): lax.all_to_all(slot_grads.reshape(ndom, pair_slots * 2 * hwide, bsize), '...  8.8 us
  transfers between devices with their start and end apart: 32, of which 17 were waited for; matrix products, arithmetic and copies ran while one was open for 8% of the time, Pallas kernels for 2%

profile of v6, /device:TPU:1, one launch (start us, length us, event | category | flops | bytes accessed | tf_op | source)
XLA Modules:
  0.0 264.1 jit_solution(16253782434810113015)
XLA Ops:
  0.6 1.3 fusion.14
  2.0 1.8 copy.38
  3.9 0.9 copy-done.10
  4.9 1.8 fusion.3
  6.7 6.7 %all-to-all-start = ((bf16[8,512,128]{2,1,0:T(8,128)(2,1)}), bf16[8,512,128]{2,1,0:T(8,128)(2,1)S(1)}, u32[]{:S(2)}, u32[]{:S(2)}) async-start(bf16[8,512,128]{2,1,0:T(8,128)(2,1)} %fusion.3), calls=%async_computation | async-start | bytes 2097152 | tf_op jit(solution)/shard_map/all_to_all | solution.py:173
  13.3 0.8 slice.13
  14.4 1.8 fusion.18
  16.2 0.9 convert_bitcast_fusion
  17.1 1.3 fusion.7
  18.4 10.0 %all-to-all-done = bf16[8,512,128]{2,1,0:T(8,128)(2,1)S(1)} async-done(((bf16[8,512,128]{2,1,0:T(8,128)(2,1)}), bf16[8,512,128]{2,1,0:T(8,128)(2,1)S(1)}, u32[]{:S(2)}, u32[]{:S(2)}) %all-to-all-start) | async-done | bytes 1048608 | tf_op jit(solution)/shard_map/all_to_all | solution.py:173
  28.3 2.7 %gather_fusion = bf16[96,128,128]{2,1,0:T(8,128)(2,1)} fusion(bf16[32,128,128]{2,1,0:T(8,128)(2,1)S(1)} %bitcast.66, s32[1024]{0:T(1024)S(1)} %pad_clamp_fusion.1), kind=kCustom, calls=%fused_computation | custom fusion | bytes 6291840 | tf_op jit(solution)/shard_map/jit(_take)/gather | solution.py:180
  31.1 10.6 %all-to-all-start.1 = ((bf16[32,384,128]{2,1,0:T(8,128)(2,1)}), bf16[32,384,128]{2,1,0:T(8,128)(2,1)}, u32[]{:S(2)}, u32[]{:S(2)}) async-start(bf16[32,384,128]{2,1,0:T(8,128)(2,1)} %bitcast.68), calls=%async_computation.1 | async-start | bytes 6291456 | tf_op jit(solution)/shard_map/all_to_all | solution.py:184
  42.9 1.2 gather_fusion.1
  45.1 1.4 collective-permute-start.7
  46.6 1.3 collective-permute-done.7
  48.6 3.5 %collective-permute-start.6 = (bf16[1,512,64]{1,2,0:T(8,128)(2,1)S(1)}, bf16[1,512,64]{1,2,0:T(8,128)(2,1)}, u32[]{:S(2)}, u32[]{:S(2)}) collective-permute-start(bf16[1,512,64]{1,2,0:T(8,128)(2,1)S(1)} %get-tuple-element.37), channel_id=1, source_target_pairs={{0,7},{1,0},{2,1},{3,2},{4,3},{5,4},{6,5},{7,6},{8,15},{9,8},{10,9... | collective-permute-start | bytes 196616 | tf_op jit(solution)/shard_map/ppermute | solution.py:132
  52.1 2.4 collective-permute-start.5
  54.5 1.1 collective-permute-start.3
  55.6 2.4 collective-permute-start.9
  58.0 3.7 %collective-permute-done.9 = bf16[1,512,64]{1,2,0:T(8,128)(2,1)S(1)} collective-permute-done((bf16[1,512,64]{1,2,0:T(8,128)(2,1)S(1)}, bf16[1,512,64]{1,2,0:T(8,128)(2,1)S(1)}, u32[]{:S(2)}, u32[]{:S(2)}) %collective-permute-start.9) | collective-permute-done | bytes 65568 | tf_op jit(solution)/shard_map/ppermute | solution.py:132
  62.3 4.4 %collective-permute-done.10 = bf16[1,512,64]{1,2,0:T(8,128)(2,1)S(1)} collective-permute-done((bf16[1,512,64]{1,2,0:T(8,128)(2,1)S(1)}, bf16[1,512,64]{1,2,0:T(8,128)(2,1)S(1)}, u32[]{:S(2)}, u32[]{:S(2)}) %collective-permute-start.10) | collective-permute-done | bytes 65568 | tf_op jit(solution)/shard_map/ppermute | solution.py:132
  66.7 2.3 collective-permute-start.11
  69.0 3.3 %collective-permute-done.11 = bf16[1,512,64]{1,2,0:T(8,128)(2,1)S(1)} collective-permute-done((bf16[1,512,64]{1,2,0:T(8,128)(2,1)S(1)}, bf16[1,512,64]{1,2,0:T(8,128)(2,1)S(1)}, u32[]{:S(2)}, u32[]{:S(2)}) %collective-permute-start.11) | collective-permute-done | bytes 65568 | tf_op jit(solution)/shard_map/ppermute | solution.py:132
  72.3 1.3 collective-permute-start.12
  73.5 2.5 collective-permute-done.12
  76.1 1.0 collective-permute-start.13
  77.1 3.1 %collective-permute-done.13 = bf16[1,512,64]{1,2,0:T(8,128)(2,1)S(1)} collective-permute-done((bf16[1,512,64]{1,2,0:T(8,128)(2,1)S(1)}, bf16[1,512,64]{1,2,0:T(8,128)(2,1)S(1)}, u32[]{:S(2)}, u32[]{:S(2)}) %collective-permute-start.13) | collective-permute-done | bytes 65568 | tf_op jit(solution)/shard_map/ppermute | solution.py:132
  80.2 1.5 collective-permute-start.1
  81.7 1.3 copy.43
  83.0 3.2 %collective-permute-done.1 = bf16[1,512,64]{1,2,0:T(8,128)(2,1)} collective-permute-done((bf16[1,512,64]{1,2,0:T(8,128)(2,1)S(1)}, bf16[1,512,64]{1,2,0:T(8,128)(2,1)}, u32[]{:S(2)}, u32[]{:S(2)}) %collective-permute-start.1) | collective-permute-done | bytes 65568 | tf_op jit(solution)/shard_map/ppermute | solution.py:132
  86.2 0.8 constant_dynamic-update-slice_fusion.26
  87.0 5.2 %collective-permute-done.2 = bf16[1,512,64]{1,2,0:T(8,128)(2,1)S(1)} collective-permute-done((bf16[1,512,64]{1,2,0:T(8,128)(2,1)S(1)}, bf16[1,512,64]{1,2,0:T(8,128)(2,1)S(1)}, u32[]{:S(2)}, u32[]{:S(2)}) %collective-permute-start.2) | collective-permute-done | bytes 65568 | tf_op jit(solution)/shard_map/ppermute | solution.py:132
  92.2 0.9 constant_dynamic-update-slice_fusion.24
  93.1 0.8 constant_dynamic-update-slice_fusion.23
  93.9 0.8 constant_dynamic-update-slice_fusion.22
  94.8 0.8 constant_dynamic-update-slice_fusion.21
  95.6 1.4 copy.42
  97.0 15.8 %all-to-all-done.1 = bf16[32,384,128]{2,1,0:T(8,128)(2,1)} async-done(((bf16[32,384,128]{2,1,0:T(8,128)(2,1)}), bf16[32,384,128]{2,1,0:T(8,128)(2,1)}, u32[]{:S(2)}, u32[]{:S(2)}) %all-to-all-start.1) | async-done | bytes 3145760 | tf_op jit(solution)/shard_map/all_to_all | solution.py:184
  112.8 35.6 %shard_map.104 = (bf16[32,128,64]{2,1,0:T(8,128)(2,1)}, bf16[32,128,64]{2,1,0:T(8,128)(2,1)}, f32[32,128,128]{2,1,0:T(8,128)}, bf16[96,128,128]{2,1,0:T(8,128)(2,1)}) custom-call(s32[128]{0:T(128)} %reshape.70.refs_0_, s32[128]{0:T(128)} %copy-done.12, bf16[32,128,64]{2,1,0:T(8,128)(2,1)} %bitcast.75, bf16[32,128,128]{2,1,0:T(8,128)(2,1)} %bitcast.67, ...), custom_call_target="tpu_custom_call" | custom-call | tf_op jit(solution)/shard_map/pallas_call | solution.py:79
  148.4 8.8 %all-to-all-start.2 = ((bf16[32,384,128]{2,1,0:T(8,128)(2,1)}), bf16[32,384,128]{2,1,0:T(8,128)(2,1)}, u32[]{:S(2)}, u32[]{:S(2)}) async-start(bf16[32,384,128]{2,1,0:T(8,128)(2,1)} %bitcast.76), calls=%async_computation.2 | async-start | bytes 6291456 | tf_op jit(solution)/shard_map/all_to_all | solution.py:209
  157.2 1.5 copy.45
  158.8 1.5 copy.53
  160.4 1.3 collective-permute-start.27
  161.7 0.9 collective-permute-start.26
  163.3 1.9 collective-permute-start.24
  165.2 1.5 collective-permute-start.21
  166.7 0.7 constant_dynamic-slice_fusion.7
  167.4 0.9 collective-permute-done.21
  168.4 2.5 collective-permute-start.14
  170.9 1.3 collective-permute-done.14
  172.6 4.6 %collective-permute-done.22 = bf16[1,512,64]{1,2,0:T(8,128)(2,1)S(1)} collective-permute-done((bf16[1,512,64]{1,2,0:T(8,128)(2,1)S(1)}, bf16[1,512,64]{1,2,0:T(8,128)(2,1)S(1)}, u32[]{:S(2)}, u32[]{:S(2)}) %collective-permute-start.22) | collective-permute-done | bytes 65568 | tf_op jit(solution)/shard_map/ppermute | solution.py:132
  177.2 2.3 collective-permute-start.23
  179.5 3.7 %collective-permute-done.23 = bf16[1,512,64]{1,2,0:T(8,128)(2,1)S(1)} collective-permute-done((bf16[1,512,64]{1,2,0:T(8,128)(2,1)S(1)}, bf16[1,512,64]{1,2,0:T(8,128)(2,1)S(1)}, u32[]{:S(2)}, u32[]{:S(2)}) %collective-permute-start.23) | collective-permute-done | bytes 65568 | tf_op jit(solution)/shard_map/ppermute | solution.py:132
  183.2 3.6 %collective-permute-start.20 = (bf16[1,512,64]{1,2,0:T(8,128)(2,1)S(1)}, bf16[1,512,64]{1,2,0:T(8,128)(2,1)S(1)}, u32[]{:S(2)}, u32[]{:S(2)}) collective-permute-start(bf16[1,512,64]{1,2,0:T(8,128)(2,1)S(1)} %get-tuple-element.23), channel_id=1, source_target_pairs={{0,7},{1,0},{2,1},{3,2},{4,3},{5,4},{6,5},{7,6},{8,15},{9,8},{10,9... | collective-permute-start | bytes 196616 | tf_op jit(solution)/shard_map/ppermute | solution.py:132
  187.0 1.2 collective-permute-start.18
  188.2 2.4 collective-permute-start.17
  190.9 37.5 %all-to-all-done.2 = bf16[32,384,128]{2,1,0:T(8,128)(2,1)} async-done(((bf16[32,384,128]{2,1,0:T(8,128)(2,1)}), bf16[32,384,128]{2,1,0:T(8,128)(2,1)}, u32[]{:S(2)}, u32[]{:S(2)}) %all-to-all-start.2) | async-done | bytes 3145760 | tf_op jit(solution)/shard_map/all_to_all | solution.py:209
  228.5 5.2 %shard_map.105 = bf16[32,128,128]{2,1,0:T(8,128)(2,1)} custom-call(s32[96]{0:T(128)} %copy-done.11, f32[32,128,128]{2,1,0:T(8,128)} %get-tuple-element.14.acc_ref, bf16[96,128,128]{2,1,0:T(8,128)(2,1)} %bitcast.25.ret_ref), custom_call_target="tpu_custom_call" | custom-call | tf_op jit(solution)/shard_map/pallas_call | solution.py:115
  233.7 8.5 %all-to-all-start.3 = ((bf16[8,512,128]{2,1,0:T(8,128)(2,1)}), bf16[8,512,128]{2,1,0:T(8,128)(2,1)}, u32[]{:S(2)}, u32[]{:S(2)}) async-start(bf16[8,512,128]{2,1,0:T(8,128)(2,1)} %bitcast.72), calls=%async_computation.3 | async-start | bytes 2097152 | tf_op jit(solution)/shard_map/all_to_all | solution.py:217
  242.2 3.2 %collective-permute-start.16 = (bf16[1,512,64]{1,2,0:T(8,128)(2,1)}, bf16[1,512,64]{1,2,0:T(8,128)(2,1)S(1)}, u32[]{:S(2)}, u32[]{:S(2)}) collective-permute-start(bf16[1,512,64]{1,2,0:T(8,128)(2,1)} %get-tuple-element.27), channel_id=1, source_target_pairs={{0,3},{1,4},{2,5},{3,6},{4,7},{5,0},{6,1},{7,2},{8,11},{9,12},{10,... | collective-permute-start | bytes 196616 | tf_op jit(solution)/shard_map/ppermute | solution.py:132
  245.3 13.3 %collective-permute-done.16 = bf16[1,512,64]{1,2,0:T(8,128)(2,1)S(1)} collective-permute-done((bf16[1,512,64]{1,2,0:T(8,128)(2,1)}, bf16[1,512,64]{1,2,0:T(8,128)(2,1)S(1)}, u32[]{:S(2)}, u32[]{:S(2)}) %collective-permute-start.16) | collective-permute-done | bytes 65568 | tf_op jit(solution)/shard_map/ppermute | solution.py:132
  258.7 1.3 fusion.6
  260.0 2.3 convolution_bitcast_fusion
  263.0 1.1 fusion.13
  (106 shorter events, 6.3 us)
Async XLA Ops:
  0.6 16.5 %copy-start = (bf16[512,512]{1,0:T(8,128)(2,1)S(1)}, bf16[512,512]{1,0:T(8,128)(2,1)}, u32[]{:S(2)}) copy-start(bf16[512,512]{1,0:T(8,128)(2,1)} %param.12) | copy-start | bytes 1572868
  1.9 2.9 %copy-start.2 = (bf16[512,512]{1,0:T(8,128)(2,1)S(1)}, bf16[512,512]{1,0:T(8,128)(2,1)}, u32[]{:S(2)}) copy-start(bf16[512,512]{1,0:T(8,128)(2,1)} %param.9) | copy-start | bytes 1572868
  1.9 2.9 %copy-start.15 = (f32[512]{0:T(512)S(1)}, f32[512]{0:T(512)}, u32[]{:S(2)}) copy-start(f32[512]{0:T(512)} %param.10) | copy-start | bytes 6148
  3.9 1.0 copy-start.10
  3.9 10.2 %copy-start.16 = (s32[1,32,3]{1,0,2:T(1,128)S(1)}, s32[1,32,3]{1,0,2:T(1,128)}, u32[]{:S(2)}) copy-start(s32[1,32,3]{1,0,2:T(1,128)} %param.16) | copy-start | bytes 1156
  6.7 21.7 %all-to-all-start = ((bf16[8,512,128]{2,1,0:T(8,128)(2,1)}), bf16[8,512,128]{2,1,0:T(8,128)(2,1)S(1)}, u32[]{:S(2)}, u32[]{:S(2)}) async-start(bf16[8,512,128]{2,1,0:T(8,128)(2,1)} %fusion.3), calls=%async_computation | async-start | bytes 2097152 | tf_op jit(solution)/shard_map/all_to_all | solution.py:173
  14.3 16.7 %copy-start.11 = (s32[96]{0:T(128)}, s32[96]{0:T(128)S(1)}, u32[]{:S(2)}) copy-start(s32[96]{0:T(128)S(1)} %reshape.88.ids_ref) | copy-start | bytes 1156
  14.3 2.7 %copy-start.6 = (bf16[512,512]{1,0:T(8,128)(2,1)S(1)}, bf16[512,512]{1,0:T(8,128)(2,1)}, u32[]{:S(2)}) copy-start(bf16[512,512]{1,0:T(8,128)(2,1)} %param.13) | copy-start | bytes 1572868
  28.3 2.7 %copy-start.1 = (bf16[8,512,128]{2,1,0:T(8,128)(2,1)}, bf16[8,512,128]{2,1,0:T(8,128)(2,1)S(1)}, u32[]{:S(2)}) copy-start(bf16[8,512,128]{2,1,0:T(8,128)(2,1)S(1)} %all-to-all-done) | copy-start | bytes 3145732
  31.0 10.7 %copy-start.17 = (s32[32,1]{0,1:T(1,128)S(1)}, s32[32,1]{0,1:T(1,128)}, u32[]{:S(2)}) copy-start(s32[32,1]{0,1:T(1,128)} %param.17) | copy-start | bytes 388
  31.0 10.9 %copy-start.13 = (s32[32,4]{0,1:T(4,128)S(1)}, s32[32,4]{0,1:T(4,128)}, u32[]{:S(2)}) copy-start(s32[32,4]{0,1:T(4,128)} %param.14) | copy-start | bytes 1540
  31.0 11.6 %copy-start.14 = (s32[32,4]{0,1:T(4,128)S(1)}, s32[32,4]{0,1:T(4,128)}, u32[]{:S(2)}) copy-start(s32[32,4]{0,1:T(4,128)} %param.15) | copy-start | bytes 1540
  31.1 81.8 %all-to-all-start.1 = ((bf16[32,384,128]{2,1,0:T(8,128)(2,1)}), bf16[32,384,128]{2,1,0:T(8,128)(2,1)}, u32[]{:S(2)}, u32[]{:S(2)}) async-start(bf16[32,384,128]{2,1,0:T(8,128)(2,1)} %bitcast.68), calls=%async_computation.1 | async-start | bytes 6291456 | tf_op jit(solution)/shard_map/all_to_all | solution.py:184
  41.6 3.5 %copy-start.5 = (bf16[8,512,64]{1,2,0:T(8,128)(2,1)S(1)}, bf16[8,512,64]{1,2,0:T(8,128)(2,1)}, u32[]{:S(2)}) copy-start(bf16[8,512,64]{1,2,0:T(8,128)(2,1)} %fusion.7) | copy-start | bytes 1572868
  41.6 4.9 %copy-start.4 = (bf16[8,512,64]{1,2,0:T(8,128)(2,1)S(1)}, bf16[8,512,64]{1,2,0:T(8,128)(2,1)}, u32[]{:S(2)}) copy-start(bf16[8,512,64]{1,2,0:T(8,128)(2,1)} %convert_bitcast_fusion) | copy-start | bytes 1572868
  42.9 5.7 %copy-start.12 = (s32[128]{0:T(128)}, s32[128]{0:T(128)S(1)}, u32[]{:S(2)}) copy-start(s32[128]{0:T(128)S(1)} %reshape.71.refs_1_) | copy-start | bytes 1540
  45.1 2.8 %collective-permute-start.7 = (bf16[1,512,64]{1,2,0:T(8,128)(2,1)S(1)}, bf16[1,512,64]{1,2,0:T(8,128)(2,1)S(1)}, u32[]{:S(2)}, u32[]{:S(2)}) collective-permute-start(bf16[1,512,64]{1,2,0:T(8,128)(2,1)S(1)} %constant_dynamic-slice_fusion.20), channel_id=1, source_target_pairs={{0,1},{1,2},{2,3},{3,4},{4,5},{5,6},{6,7},{7,0},{8,9},{9,10},{10,1... | collective-permute-start | bytes 196616 | tf_op jit(solution)/shard_map/ppermute | solution.py:132
  46.6 1.9 collective-permute-start
  47.9 7.6 %collective-permute-start.8 = (bf16[1,512,64]{1,2,0:T(8,128)(2,1)S(1)}, bf16[1,512,64]{1,2,0:T(8,128)(2,1)S(1)}, u32[]{:S(2)}, u32[]{:S(2)}) collective-permute-start(bf16[1,512,64]{1,2,0:T(8,128)(2,1)S(1)} %get-tuple-element.35), channel_id=1, source_target_pairs={{0,2},{1,3},{2,4},{3,5},{4,6},{5,7},{6,0},{7,1},{8,10},{9,11},{10,... | collective-permute-start | bytes 196616 | tf_op jit(solution)/shard_map/ppermute | solution.py:132
  48.6 46.2 %collective-permute-start.6 = (bf16[1,512,64]{1,2,0:T(8,128)(2,1)S(1)}, bf16[1,512,64]{1,2,0:T(8,128)(2,1)}, u32[]{:S(2)}, u32[]{:S(2)}) collective-permute-start(bf16[1,512,64]{1,2,0:T(8,128)(2,1)S(1)} %get-tuple-element.37), channel_id=1, source_target_pairs={{0,7},{1,0},{2,1},{3,2},{4,3},{5,4},{6,5},{7,6},{8,15},{9,8},{10,9... | collective-permute-start | bytes 196616 | tf_op jit(solution)/shard_map/ppermute | solution.py:132
  52.1 41.8 %collective-permute-start.5 = (bf16[1,512,64]{1,2,0:T(8,128)(2,1)S(1)}, bf16[1,512,64]{1,2,0:T(8,128)(2,1)}, u32[]{:S(2)}, u32[]{:S(2)}) collective-permute-start(bf16[1,512,64]{1,2,0:T(8,128)(2,1)S(1)} %get-tuple-element.38), channel_id=1, source_target_pairs={{0,6},{1,7},{2,0},{3,1},{4,2},{5,3},{6,4},{7,5},{8,14},{9,15},{10,... | collective-permute-start | bytes 196616 | tf_op jit(solution)/shard_map/ppermute | solution.py:132
  54.5 38.6 %collective-permute-start.4 = (bf16[1,512,64]{1,2,0:T(8,128)(2,1)S(1)}, bf16[1,512,64]{1,2,0:T(8,128)(2,1)}, u32[]{:S(2)}, u32[]{:S(2)}) collective-permute-start(bf16[1,512,64]{1,2,0:T(8,128)(2,1)S(1)} %get-tuple-element.39), channel_id=1, source_target_pairs={{0,5},{1,6},{2,7},{3,0},{4,1},{5,2},{6,3},{7,4},{8,13},{9,14},{10,... | collective-permute-start | bytes 196616 | tf_op jit(solution)/shard_map/ppermute | solution.py:132
  54.5 37.7 %collective-permute-start.3 = (bf16[1,512,64]{1,2,0:T(8,128)(2,1)S(1)}, bf16[1,512,64]{1,2,0:T(8,128)(2,1)}, u32[]{:S(2)}, u32[]{:S(2)}) collective-permute-start(bf16[1,512,64]{1,2,0:T(8,128)(2,1)S(1)} %get-tuple-element.40), channel_id=1, source_target_pairs={{0,4},{1,5},{2,6},{3,7},{4,0},{5,1},{6,2},{7,3},{8,12},{9,13},{10,... | collective-permute-start | bytes 196616 | tf_op jit(solution)/shard_map/ppermute | solution.py:132
  55.6 6.1 %collective-permute-start.9 = (bf16[1,512,64]{1,2,0:T(8,128)(2,1)S(1)}, bf16[1,512,64]{1,2,0:T(8,128)(2,1)S(1)}, u32[]{:S(2)}, u32[]{:S(2)}) collective-permute-start(bf16[1,512,64]{1,2,0:T(8,128)(2,1)S(1)} %get-tuple-element.34), channel_id=1, source_target_pairs={{0,3},{1,4},{2,5},{3,6},{4,7},{5,0},{6,1},{7,2},{8,11},{9,12},{10,... | collective-permute-start | bytes 196616 | tf_op jit(solution)/shard_map/ppermute | solution.py:132
  61.7 5.0 %collective-permute-start.10 = (bf16[1,512,64]{1,2,0:T(8,128)(2,1)S(1)}, bf16[1,512,64]{1,2,0:T(8,128)(2,1)S(1)}, u32[]{:S(2)}, u32[]{:S(2)}) collective-permute-start(bf16[1,512,64]{1,2,0:T(8,128)(2,1)S(1)} %get-tuple-element.33), channel_id=1, source_target_pairs={{0,4},{1,5},{2,6},{3,7},{4,0},{5,1},{6,2},{7,3},{8,12},{9,13},{10,... | collective-permute-start | bytes 196616 | tf_op jit(solution)/shard_map/ppermute | solution.py:132
  66.7 5.6 %collective-permute-start.11 = (bf16[1,512,64]{1,2,0:T(8,128)(2,1)S(1)}, bf16[1,512,64]{1,2,0:T(8,128)(2,1)S(1)}, u32[]{:S(2)}, u32[]{:S(2)}) collective-permute-start(bf16[1,512,64]{1,2,0:T(8,128)(2,1)S(1)} %get-tuple-element.32), channel_id=1, source_target_pairs={{0,5},{1,6},{2,7},{3,0},{4,1},{5,2},{6,3},{7,4},{8,13},{9,14},{10,... | collective-permute-start | bytes 196616 | tf_op jit(solution)/shard_map/ppermute | solution.py:132
  72.3 3.8 %collective-permute-start.12 = (bf16[1,512,64]{1,2,0:T(8,128)(2,1)S(1)}, bf16[1,512,64]{1,2,0:T(8,128)(2,1)S(1)}, u32[]{:S(2)}, u32[]{:S(2)}) collective-permute-start(bf16[1,512,64]{1,2,0:T(8,128)(2,1)S(1)} %get-tuple-element.31), channel_id=1, source_target_pairs={{0,6},{1,7},{2,0},{3,1},{4,2},{5,3},{6,4},{7,5},{8,14},{9,15},{10,... | collective-permute-start | bytes 196616 | tf_op jit(solution)/shard_map/ppermute | solution.py:132
  76.1 4.1 %collective-permute-start.13 = (bf16[1,512,64]{1,2,0:T(8,128)(2,1)S(1)}, bf16[1,512,64]{1,2,0:T(8,128)(2,1)S(1)}, u32[]{:S(2)}, u32[]{:S(2)}) collective-permute-start(bf16[1,512,64]{1,2,0:T(8,128)(2,1)S(1)} %get-tuple-element.30), channel_id=1, source_target_pairs={{0,7},{1,0},{2,1},{3,2},{4,3},{5,4},{6,5},{7,6},{8,15},{9,8},{10,9... | collective-permute-start | bytes 196616 | tf_op jit(solution)/shard_map/ppermute | solution.py:132
  80.2 6.0 %collective-permute-start.1 = (bf16[1,512,64]{1,2,0:T(8,128)(2,1)S(1)}, bf16[1,512,64]{1,2,0:T(8,128)(2,1)}, u32[]{:S(2)}, u32[]{:S(2)}) collective-permute-start(bf16[1,512,64]{1,2,0:T(8,128)(2,1)S(1)} %get-tuple-element.42), channel_id=1, source_target_pairs={{0,2},{1,3},{2,4},{3,5},{4,6},{5,7},{6,0},{7,1},{8,10},{9,11},{10,... | collective-permute-start | bytes 196616 | tf_op jit(solution)/shard_map/ppermute | solution.py:132
  86.2 6.0 %collective-permute-start.2 = (bf16[1,512,64]{1,2,0:T(8,128)(2,1)S(1)}, bf16[1,512,64]{1,2,0:T(8,128)(2,1)S(1)}, u32[]{:S(2)}, u32[]{:S(2)}) collective-permute-start(bf16[1,512,64]{1,2,0:T(8,128)(2,1)S(1)} %get-tuple-element.41), channel_id=1, source_target_pairs={{0,3},{1,4},{2,5},{3,6},{4,7},{5,0},{6,1},{7,2},{8,11},{9,12},{10,... | collective-permute-start | bytes 196616 | tf_op jit(solution)/shard_map/ppermute | solution.py:132
  148.4 80.0 %all-to-all-start.2 = ((bf16[32,384,128]{2,1,0:T(8,128)(2,1)}), bf16[32,384,128]{2,1,0:T(8,128)(2,1)}, u32[]{:S(2)}, u32[]{:S(2)}) async-start(bf16[32,384,128]{2,1,0:T(8,128)(2,1)} %bitcast.76), calls=%async_computation.2 | async-start | bytes 6291456 | tf_op jit(solution)/shard_map/all_to_all | solution.py:209
  160.4 30.2 %collective-permute-start.27 = (bf16[1,512,64]{1,2,0:T(8,128)(2,1)S(1)}, bf16[1,512,64]{1,2,0:T(8,128)(2,1)S(1)}, u32[]{:S(2)}, u32[]{:S(2)}) collective-permute-start(bf16[1,512,64]{1,2,0:T(8,128)(2,1)S(1)} %get-tuple-element.16), channel_id=1, source_target_pairs={{0,7},{1,0},{2,1},{3,2},{4,3},{5,4},{6,5},{7,6},{8,15},{9,8},{10,9... | collective-permute-start | bytes 196616 | tf_op jit(solution)/shard_map/ppermute | solution.py:132
  161.7 26.5 %collective-permute-start.26 = (bf16[1,512,64]{1,2,0:T(8,128)(2,1)S(1)}, bf16[1,512,64]{1,2,0:T(8,128)(2,1)S(1)}, u32[]{:S(2)}, u32[]{:S(2)}) collective-permute-start(bf16[1,512,64]{1,2,0:T(8,128)(2,1)S(1)} %get-tuple-element.17), channel_id=1, source_target_pairs={{0,6},{1,7},{2,0},{3,1},{4,2},{5,3},{6,4},{7,5},{8,14},{9,15},{10,... | collective-permute-start | bytes 196616 | tf_op jit(solution)/shard_map/ppermute | solution.py:132
  162.6 24.3 %collective-permute-start.25 = (bf16[1,512,64]{1,2,0:T(8,128)(2,1)S(1)}, bf16[1,512,64]{1,2,0:T(8,128)(2,1)S(1)}, u32[]{:S(2)}, u32[]{:S(2)}) collective-permute-start(bf16[1,512,64]{1,2,0:T(8,128)(2,1)S(1)} %get-tuple-element.18), channel_id=1, source_target_pairs={{0,5},{1,6},{2,7},{3,0},{4,1},{5,2},{6,3},{7,4},{8,13},{9,14},{10,... | collective-permute-start | bytes 196616 | tf_op jit(solution)/shard_map/ppermute | solution.py:132
  163.3 23.5 %collective-permute-start.24 = (bf16[1,512,64]{1,2,0:T(8,128)(2,1)S(1)}, bf16[1,512,64]{1,2,0:T(8,128)(2,1)S(1)}, u32[]{:S(2)}, u32[]{:S(2)}) collective-permute-start(bf16[1,512,64]{1,2,0:T(8,128)(2,1)S(1)} %get-tuple-element.19), channel_id=1, source_target_pairs={{0,4},{1,5},{2,6},{3,7},{4,0},{5,1},{6,2},{7,3},{8,12},{9,13},{10,... | collective-permute-start | bytes 196616 | tf_op jit(solution)/shard_map/ppermute | solution.py:132
  165.2 3.1 %collective-permute-start.21 = (bf16[1,512,64]{1,2,0:T(8,128)(2,1)S(1)}, bf16[1,512,64]{1,2,0:T(8,128)(2,1)S(1)}, u32[]{:S(2)}, u32[]{:S(2)}) collective-permute-start(bf16[1,512,64]{1,2,0:T(8,128)(2,1)S(1)} %get-tuple-element.22), channel_id=1, source_target_pairs={{0,1},{1,2},{2,3},{3,4},{4,5},{5,6},{6,7},{7,0},{8,9},{9,10},{10,1... | collective-permute-start | bytes 196616 | tf_op jit(solution)/shard_map/ppermute | solution.py:132
  168.4 3.8 %collective-permute-start.14 = (bf16[1,512,64]{1,2,0:T(8,128)(2,1)S(1)}, bf16[1,512,64]{1,2,0:T(8,128)(2,1)S(1)}, u32[]{:S(2)}, u32[]{:S(2)}) collective-permute-start(bf16[1,512,64]{1,2,0:T(8,128)(2,1)S(1)} %get-tuple-element.29), channel_id=1, source_target_pairs={{0,1},{1,2},{2,3},{3,4},{4,5},{5,6},{6,7},{7,0},{8,9},{9,10},{10,1... | collective-permute-start | bytes 196616 | tf_op jit(solution)/shard_map/ppermute | solution.py:132
  172.2 5.0 %collective-permute-start.22 = (bf16[1,512,64]{1,2,0:T(8,128)(2,1)S(1)}, bf16[1,512,64]{1,2,0:T(8,128)(2,1)S(1)}, u32[]{:S(2)}, u32[]{:S(2)}) collective-permute-start(bf16[1,512,64]{1,2,0:T(8,128)(2,1)S(1)} %get-tuple-element.21), channel_id=1, source_target_pairs={{0,2},{1,3},{2,4},{3,5},{4,6},{5,7},{6,0},{7,1},{8,10},{9,11},{10,... | collective-permute-start | bytes 196616 | tf_op jit(solution)/shard_map/ppermute | solution.py:132
  177.2 6.0 %collective-permute-start.23 = (bf16[1,512,64]{1,2,0:T(8,128)(2,1)S(1)}, bf16[1,512,64]{1,2,0:T(8,128)(2,1)S(1)}, u32[]{:S(2)}, u32[]{:S(2)}) collective-permute-start(bf16[1,512,64]{1,2,0:T(8,128)(2,1)S(1)} %get-tuple-element.20), channel_id=1, source_target_pairs={{0,3},{1,4},{2,5},{3,6},{4,7},{5,0},{6,1},{7,2},{8,11},{9,12},{10,... | collective-permute-start | bytes 196616 | tf_op jit(solution)/shard_map/ppermute | solution.py:132
  183.2 75.5 %collective-permute-start.20 = (bf16[1,512,64]{1,2,0:T(8,128)(2,1)S(1)}, bf16[1,512,64]{1,2,0:T(8,128)(2,1)S(1)}, u32[]{:S(2)}, u32[]{:S(2)}) collective-permute-start(bf16[1,512,64]{1,2,0:T(8,128)(2,1)S(1)} %get-tuple-element.23), channel_id=1, source_target_pairs={{0,7},{1,0},{2,1},{3,2},{4,3},{5,4},{6,5},{7,6},{8,15},{9,8},{10,9... | collective-permute-start | bytes 196616 | tf_op jit(solution)/shard_map/ppermute | solution.py:132
  186.8 71.8 %collective-permute-start.19 = (bf16[1,512,64]{1,2,0:T(8,128)(2,1)}, bf16[1,512,64]{1,2,0:T(8,128)(2,1)S(1)}, u32[]{:S(2)}, u32[]{:S(2)}) collective-permute-start(bf16[1,512,64]{1,2,0:T(8,128)(2,1)} %get-tuple-element.24), channel_id=1, source_target_pairs={{0,6},{1,7},{2,0},{3,1},{4,2},{5,3},{6,4},{7,5},{8,14},{9,15},{10,... | collective-permute-start | bytes 196616 | tf_op jit(solution)/shard_map/ppermute | solution.py:132
  187.0 71.7 %collective-permute-start.18 = (bf16[1,512,64]{1,2,0:T(8,128)(2,1)}, bf16[1,512,64]{1,2,0:T(8,128)(2,1)S(1)}, u32[]{:S(2)}, u32[]{:S(2)}) collective-permute-start(bf16[1,512,64]{1,2,0:T(8,128)(2,1)} %get-tuple-element.25), channel_id=1, source_target_pairs={{0,5},{1,6},{2,7},{3,0},{4,1},{5,2},{6,3},{7,4},{8,13},{9,14},{10,... | collective-permute-start | bytes 196616 | tf_op jit(solution)/shard_map/ppermute | solution.py:132
  188.2 70.4 %collective-permute-start.17 = (bf16[1,512,64]{1,2,0:T(8,128)(2,1)}, bf16[1,512,64]{1,2,0:T(8,128)(2,1)S(1)}, u32[]{:S(2)}, u32[]{:S(2)}) collective-permute-start(bf16[1,512,64]{1,2,0:T(8,128)(2,1)} %get-tuple-element.26), channel_id=1, source_target_pairs={{0,4},{1,5},{2,6},{3,7},{4,0},{5,1},{6,2},{7,3},{8,12},{9,13},{10,... | collective-permute-start | bytes 196616 | tf_op jit(solution)/shard_map/ppermute | solution.py:132
  190.6 51.6 %collective-permute-start.15 = (bf16[1,512,64]{1,2,0:T(8,128)(2,1)}, bf16[1,512,64]{1,2,0:T(8,128)(2,1)S(1)}, u32[]{:S(2)}, u32[]{:S(2)}) collective-permute-start(bf16[1,512,64]{1,2,0:T(8,128)(2,1)} %get-tuple-element.28), channel_id=1, source_target_pairs={{0,2},{1,3},{2,4},{3,5},{4,6},{5,7},{6,0},{7,1},{8,10},{9,11},{10,... | collective-permute-start | bytes 196616 | tf_op jit(solution)/shard_map/ppermute | solution.py:132
  190.9 37.5 %copy-start.8 = (bf16[8,512,64]{1,2,0:T(8,128)(2,1)}, bf16[8,512,64]{1,2,0:T(8,128)(2,1)S(1)}, u32[]{:S(2)}) copy-start(bf16[8,512,64]{1,2,0:T(8,128)(2,1)S(1)} %constant_dynamic-update-slice_fusion) | copy-start | bytes 1572868
  228.5 30.3 %copy-start.3 = (bf16[512,512]{1,0:T(8,128)(2,1)S(1)}, bf16[512,512]{1,0:T(8,128)(2,1)}, u32[]{:S(2)}) copy-start(bf16[512,512]{1,0:T(8,128)(2,1)} %param.9) | copy-start | bytes 1572868
  233.7 26.3 %all-to-all-start.3 = ((bf16[8,512,128]{2,1,0:T(8,128)(2,1)}), bf16[8,512,128]{2,1,0:T(8,128)(2,1)}, u32[]{:S(2)}, u32[]{:S(2)}) async-start(bf16[8,512,128]{2,1,0:T(8,128)(2,1)} %bitcast.72), calls=%async_computation.3 | async-start | bytes 2097152 | tf_op jit(solution)/shard_map/all_to_all | solution.py:217
  242.2 16.4 %collective-permute-start.16 = (bf16[1,512,64]{1,2,0:T(8,128)(2,1)}, bf16[1,512,64]{1,2,0:T(8,128)(2,1)S(1)}, u32[]{:S(2)}, u32[]{:S(2)}) collective-permute-start(bf16[1,512,64]{1,2,0:T(8,128)(2,1)} %get-tuple-element.27), channel_id=1, source_target_pairs={{0,3},{1,4},{2,5},{3,6},{4,7},{5,0},{6,1},{7,2},{8,11},{9,12},{10,... | collective-permute-start | bytes 196616 | tf_op jit(solution)/shard_map/ppermute | solution.py:132
  260.0 3.0 %copy-start.7 = (bf16[512,512]{1,0:T(8,128)(2,1)S(1)}, bf16[512,512]{1,0:T(8,128)(2,1)}, u32[]{:S(2)}) copy-start(bf16[512,512]{1,0:T(8,128)(2,1)} %param.13) | copy-start | bytes 1572868
  260.0 2.3 copy-start.9

commit v7 on v6

--- a/solution.py
+++ b/solution.py
@@ -11,30 +11,42 @@
 EPS = 1e-05
 
 
-def attention_kernel(
-    lk_ref, rk_ref, q_ref, kv_ref, do_ref, pool_ref, bias_ref, o_ref, dq_ref, acc_ref, slot_ref, slot_acc,
-    *, near, far, bsize, depth, scale
+def load_blocks(kv_ref, pool_ref, ids_l, ids_r, cols):
+    return jnp.concatenate(
+        [kv_ref[i, :, cols] for i in ids_l] + [pool_ref[i, :, cols] for i in ids_r], axis=0
+    )
+
+
+def column_to_row(col):
+    n = col.shape[0]
+    return jnp.broadcast_to(col, (n, n)).T[0:1, :]
+
+
+def row_to_column(row):
+    n = row.shape[1]
+    return jnp.broadcast_to(row, (n, n)).T[:, 0:1]
+
+
+def remote_kernel(
+    lk_ref, rk_ref, q_ref, kv_ref, do_ref, pool_ref, bias_ref, o_ref, dq_ref, stats_ref,
+    slot_ref, slot_acc, *, near, far, bsize, depth, scale
 ):
     f32 = jnp.float32
     bf16 = jnp.bfloat16
     nq = q_ref.shape[0]
-    acc_ref[...] = jnp.zeros(acc_ref.shape, f32)
     slot_acc[...] = jnp.zeros(slot_acc.shape, f32)
     kcols = pl.ds(0, depth)
     vcols = pl.ds(depth, depth)
     nt = (((1,), (1,)), ((), ()))
+    split = near * bsize
 
     def body(b, carry):
         q = q_ref[b]
         do = do_ref[b]
         ids_l = [lk_ref[b * near + i] for i in range(near)]
         ids_r = [rk_ref[b * far + i] for i in range(far)]
-        keys = jnp.concatenate(
-            [kv_ref[i, :, kcols] for i in ids_l] + [pool_ref[i, :, kcols] for i in ids_r], axis=0
-        )
-        vals = jnp.concatenate(
-            [kv_ref[i, :, vcols] for i in ids_l] + [pool_ref[i, :, vcols] for i in ids_r], axis=0
-        )
+        keys = load_blocks(kv_ref, pool_ref, ids_l, ids_r, kcols)
+        vals = load_blocks(kv_ref, pool_ref, ids_l, ids_r, vcols)
         q_s = q * scale
         do_s = do * scale
         s = lax.dot_general(q_s, keys, nt, preferred_element_type=f32)
@@ -42,26 +54,71 @@
         top = jnp.max(s, axis=1, keepdims=True)
         expo = jnp.exp(s - top)
         total = jnp.sum(expo, axis=1, keepdims=True)
-        w = (expo * (1.0 / total)).astype(bf16)
+        rtot = 1.0 / total
+        w = (expo * rtot).astype(bf16)
         o = jnp.dot(w, vals, preferred_element_type=f32).astype(bf16)
         o_ref[b] = o
         delta = jnp.sum(do_s.astype(f32) * o.astype(f32), axis=1, keepdims=True)
+        stats_ref[b] = jnp.concatenate(
+            [column_to_row(top), column_to_row(rtot), column_to_row(delta)], axis=0
+        )
+        keys_r = keys[split:]
+        vals_r = vals[split:]
+        w_r = w[:, split:]
+        dw = lax.dot_general(do_s, vals_r, nt, preferred_element_type=f32)
+        ds = (w_r.astype(f32) * (dw - delta)).astype(bf16)
+        dq_ref[b] = jnp.dot(ds, keys_r, preferred_element_type=f32)
+        dk_t = jnp.dot(q.T, ds, preferred_element_type=f32)
+        dv_t = jnp.dot(do.T, w_r, preferred_element_type=f32)
+        dkv_t = jnp.concatenate([dk_t, dv_t], axis=0)
+        for i in range(far):
+            part = dkv_t[:, i * bsize:(i + 1) * bsize]
+            slot_acc[ids_r[i]] = slot_acc[ids_r[i]] + part
+        return carry
+
+    lax.fori_loop(0, nq, body, 0, unroll=4)
+    slot_ref[...] = slot_acc[...].astype(bf16)
+
+
+def local_kernel(
+    lk_ref, q_ref, kv_ref, do_ref, stats_ref, dqr_ref, dq_ref, acc_ref,
+    *, near, bsize, depth, scale
+):
+    f32 = jnp.float32
+    bf16 = jnp.bfloat16
+    nq = q_ref.shape[0]
+    acc_ref[...] = jnp.zeros(acc_ref.shape, f32)
+    kcols = pl.ds(0, depth)
+    vcols = pl.ds(depth, depth)
+    nt = (((1,), (1,)), ((), ()))
+
+    def body(b, carry):
+        q = q_ref[b]
+        do = do_ref[b]
+        ids_l = [lk_ref[b * near + i] for i in range(near)]
+        keys = jnp.concatenate([kv_ref[i, :, kcols] for i in ids_l], axis=0)
+        vals = jnp.concatenate([kv_ref[i, :, vcols] for i in ids_l], axis=0)
+        q_s = q * scale
+        do_s = do * scale
+        stats = stats_ref[b]
+        top = row_to_column(stats[0:1, :])
+        rtot = row_to_column(stats[1:2, :])
+        delta = row_to_column(stats[2:3, :])
+        s = lax.dot_general(q_s, keys, nt, preferred_element_type=f32)
+        w = (jnp.exp(s - top) * rtot).astype(bf16)
         dw = lax.dot_general(do_s, vals, nt, preferred_element_type=f32)
         ds = (w.astype(f32) * (dw - delta)).astype(bf16)
-        dq_ref[b] = jnp.dot(ds, keys, preferred_element_type=f32).astype(bf16)
+        dq = dqr_ref[b] + jnp.dot(ds, keys, preferred_element_type=f32)
+        dq_ref[b] = dq.astype(bf16)
         dk_t = jnp.dot(q.T, ds, preferred_element_type=f32)
         dv_t = jnp.dot(do.T, w, preferred_element_type=f32)
         dkv_t = jnp.concatenate([dk_t, dv_t], axis=0)
         for i in range(near):
             part = dkv_t[:, i * bsize:(i + 1) * bsize]
             acc_ref[ids_l[i]] = acc_ref[ids_l[i]] + part
-        for i in range(far):
-            part = dkv_t[:, (near + i) * bsize:(near + i + 1) * bsize]
-            slot_acc[ids_r[i]] = slot_acc[ids_r[i]] + part
         return carry
 
     lax.fori_loop(0, nq, body, 0, unroll=4)
-    slot_ref[...] = slot_acc[...].astype(bf16)
 
 
 def fused_attention(local_ids, remote_ids, q, kv, d_out, pool, bias, scale):
@@ -72,23 +129,34 @@
     f32 = jnp.float32
     smem = pl.BlockSpec(memory_space=pltpu.SMEM)
     vmem = pl.BlockSpec(memory_space=pltpu.VMEM)
-    kernel = lambda *refs: attention_kernel(
-        *refs, near=near, far=far, bsize=bsize, depth=depth, scale=scale
-    )
     kv_t = (2 * depth, bsize)
-    return pl.pallas_call(
-        kernel,
+    params = pltpu.CompilerParams(vmem_limit_bytes=60 * 1024 * 1024)
+    o, dq_r, stats, slot = pl.pallas_call(
+        lambda *refs: remote_kernel(
+            *refs, near=near, far=far, bsize=bsize, depth=depth, scale=scale
+        ),
         out_shape=(
             jax.ShapeDtypeStruct((nq, bsize, depth), jnp.bfloat16),
-            jax.ShapeDtypeStruct((nq, bsize, depth), jnp.bfloat16),
-            jax.ShapeDtypeStruct((nq,) + kv_t, f32),
+            jax.ShapeDtypeStruct((nq, bsize, depth), f32),
+            jax.ShapeDtypeStruct((nq, 3, bsize), f32),
             jax.ShapeDtypeStruct((npool,) + kv_t, jnp.bfloat16),
         ),
         in_specs=[smem, smem] + [vmem] * 5,
         out_specs=(vmem, vmem, vmem, vmem),
         scratch_shapes=[pltpu.VMEM((npool,) + kv_t, f32)],
-        compiler_params=pltpu.CompilerParams(vmem_limit_bytes=60 * 1024 * 1024),
+        compiler_params=params,
     )(local_ids, remote_ids, q, kv, d_out, pool, bias)
+    dq, acc = pl.pallas_call(
+        lambda *refs: local_kernel(*refs, near=near, bsize=bsize, depth=depth, scale=scale),
+        out_shape=(
+            jax.ShapeDtypeStruct((nq, bsize, depth), jnp.bfloat16),
+            jax.ShapeDtypeStruct((nq,) + kv_t, f32),
+        ),
+        in_specs=[smem] + [vmem] * 5,
+        out_specs=(vmem, vmem),
+        compiler_params=params,
+    )(local_ids, q, kv, d_out, stats, dq_r)
+    return o, dq, acc, slot
 
 
 def finish_kernel(ids_ref, acc_ref, ret_ref, out_ref, total_ref):

time: 265 us -> 261 us (0.985)
  waiting for transfers between devices: 114 us -> 98.3 us
  Pallas kernels: 40.8 us -> 53 us
    all_to_all x1, waiting for transfers between devices: 37.5 us -> 22.1 us  [local(): lax.all_to_all(slot_grads.reshape(ndom, pair_slots * 2 * hwide, bsize), '...]
    pallas_call x1 -> x2, Pallas kernels: 35.6 us -> 47.8 us  [the longest x1 32.3 us: fused_attention(): pl.pallas_call(lambda *refs: remote_kernel(*refs, near=near, far=far, bsi...]
  transfers between devices with their start and end apart: 32 -> 32, of which waited for: 17 -> 17; matrix products, arithmetic and copies ran while one was open for 8% -> 8% of each run, Pallas kernels for 2% -> 8%
where the time goes in v7:
time: 261 us
  waiting for transfers between devices  98.3 us (38%)
  starting transfers between devices  74.7 us (29%)
  Pallas kernels  53 us (20%)
  local copies, waits for them, and re-layouts  21 us (8%)
  matrix products  9.09 us (3%)
  other arithmetic  3.38 us (1%)
    ppermute x28, waiting for transfers between devices, head_exchange(): got = lax.ppermute(part, axis, perm)  50.4 us
    ppermute x28, starting transfers between devices, head_exchange(): got = lax.ppermute(part, axis, perm)  40.4 us
    pallas_call x1, Pallas kernels, fused_attention(): pl.pallas_call(lambda *refs: remote_kernel(*refs, near=near, far=far, bsi...  32.3 us
    all_to_all x1, waiting for transfers between devices, local(): lax.all_to_all(slot_grads.reshape(ndom, pair_slots * 2 * hwide, bsize), '...  22.1 us
    all_to_all x1, waiting for transfers between devices, local(): lax.all_to_all(outgoing.reshape(ndom, pair_slots * bsize, 2 * hwide), 'do...  15.8 us
    pallas_call x1, Pallas kernels, fused_attention(): pl.pallas_call(lambda *refs: local_kernel(*refs, near=near, bsize=bsize,...  15.5 us
    all_to_all x1, starting transfers between devices, local(): lax.all_to_all(outgoing.reshape(ndom, pair_slots * bsize, 2 * hwide), 'do...  10.6 us
    all_to_all x1, waiting for transfers between devices, local(): lax.all_to_all(kv_own, 'head', split_axis=0, concat_axis=0, tiled=True)  9.96 us
  transfers between devices with their start and end apart: 32, of which 17 were waited for; matrix products, arithmetic and copies ran while one was open for 8% of the time, Pallas kernels for 8%

profile of v7, /device:TPU:1, one launch (start us, length us, event | category | flops | bytes accessed | tf_op | source)
XLA Modules:
  0.0 260.7 jit_solution(14499389611404820872)
XLA Ops:
  0.6 1.3 fusion.14
  2.0 1.8 copy.38
  3.9 0.9 copy-done.10
  4.9 1.8 fusion.3
  6.7 6.7 %all-to-all-start = ((bf16[8,512,128]{2,1,0:T(8,128)(2,1)}), bf16[8,512,128]{2,1,0:T(8,128)(2,1)S(1)}, u32[]{:S(2)}, u32[]{:S(2)}) async-start(bf16[8,512,128]{2,1,0:T(8,128)(2,1)} %fusion.3), calls=%async_computation | async-start | bytes 2097152 | tf_op jit(solution)/shard_map/all_to_all | solution.py:241
  13.3 0.8 slice.13
  14.4 1.8 fusion.18
  16.2 0.9 convert_bitcast_fusion
  17.1 1.3 fusion.7
  18.4 10.0 %all-to-all-done = bf16[8,512,128]{2,1,0:T(8,128)(2,1)S(1)} async-done(((bf16[8,512,128]{2,1,0:T(8,128)(2,1)}), bf16[8,512,128]{2,1,0:T(8,128)(2,1)S(1)}, u32[]{:S(2)}, u32[]{:S(2)}) %all-to-all-start) | async-done | bytes 1048608 | tf_op jit(solution)/shard_map/all_to_all | solution.py:241
  28.3 2.7 %gather_fusion = bf16[96,128,128]{2,1,0:T(8,128)(2,1)} fusion(bf16[32,128,128]{2,1,0:T(8,128)(2,1)S(1)} %bitcast.66, s32[1024]{0:T(1024)S(1)} %pad_clamp_fusion.1), kind=kCustom, calls=%fused_computation | custom fusion | bytes 6291840 | tf_op jit(solution)/shard_map/jit(_take)/gather | solution.py:248
  31.1 10.6 %all-to-all-start.1 = ((bf16[32,384,128]{2,1,0:T(8,128)(2,1)}), bf16[32,384,128]{2,1,0:T(8,128)(2,1)}, u32[]{:S(2)}, u32[]{:S(2)}) async-start(bf16[32,384,128]{2,1,0:T(8,128)(2,1)} %bitcast.69), calls=%async_computation.1 | async-start | bytes 6291456 | tf_op jit(solution)/shard_map/all_to_all | solution.py:252
  43.0 1.2 gather_fusion.1
  45.2 1.4 collective-permute-start.7
  46.7 1.3 collective-permute-done.7
  48.7 3.5 %collective-permute-start.6 = (bf16[1,512,64]{1,2,0:T(8,128)(2,1)S(1)}, bf16[1,512,64]{1,2,0:T(8,128)(2,1)}, u32[]{:S(2)}, u32[]{:S(2)}) collective-permute-start(bf16[1,512,64]{1,2,0:T(8,128)(2,1)S(1)} %get-tuple-element.41), channel_id=1, source_target_pairs={{0,7},{1,0},{2,1},{3,2},{4,3},{5,4},{6,5},{7,6},{8,15},{9,8},{10,9... | collective-permute-start | bytes 196616 | tf_op jit(solution)/shard_map/ppermute | solution.py:200
  52.1 2.4 collective-permute-start.5
  54.6 1.1 collective-permute-start.3
  55.7 2.4 collective-permute-start.9
  58.1 3.7 %collective-permute-done.9 = bf16[1,512,64]{1,2,0:T(8,128)(2,1)S(1)} collective-permute-done((bf16[1,512,64]{1,2,0:T(8,128)(2,1)S(1)}, bf16[1,512,64]{1,2,0:T(8,128)(2,1)S(1)}, u32[]{:S(2)}, u32[]{:S(2)}) %collective-permute-start.9) | collective-permute-done | bytes 65568 | tf_op jit(solution)/shard_map/ppermute | solution.py:200
  62.4 4.4 %collective-permute-done.10 = bf16[1,512,64]{1,2,0:T(8,128)(2,1)S(1)} collective-permute-done((bf16[1,512,64]{1,2,0:T(8,128)(2,1)S(1)}, bf16[1,512,64]{1,2,0:T(8,128)(2,1)S(1)}, u32[]{:S(2)}, u32[]{:S(2)}) %collective-permute-start.10) | collective-permute-done | bytes 65568 | tf_op jit(solution)/shard_map/ppermute | solution.py:200
  66.7 2.3 collective-permute-start.11
  69.0 3.3 %collective-permute-done.11 = bf16[1,512,64]{1,2,0:T(8,128)(2,1)S(1)} collective-permute-done((bf16[1,512,64]{1,2,0:T(8,128)(2,1)S(1)}, bf16[1,512,64]{1,2,0:T(8,128)(2,1)S(1)}, u32[]{:S(2)}, u32[]{:S(2)}) %collective-permute-start.11) | collective-permute-done | bytes 65568 | tf_op jit(solution)/shard_map/ppermute | solution.py:200
  72.3 1.3 collective-permute-start.12
  73.6 2.5 collective-permute-done.12
  76.2 1.0 collective-permute-start.13
  77.2 3.1 %collective-permute-done.13 = bf16[1,512,64]{1,2,0:T(8,128)(2,1)S(1)} collective-permute-done((bf16[1,512,64]{1,2,0:T(8,128)(2,1)S(1)}, bf16[1,512,64]{1,2,0:T(8,128)(2,1)S(1)}, u32[]{:S(2)}, u32[]{:S(2)}) %collective-permute-start.13) | collective-permute-done | bytes 65568 | tf_op jit(solution)/shard_map/ppermute | solution.py:200
  80.3 1.5 collective-permute-start.1
  81.7 1.3 copy.43
  83.1 3.2 %collective-permute-done.1 = bf16[1,512,64]{1,2,0:T(8,128)(2,1)} collective-permute-done((bf16[1,512,64]{1,2,0:T(8,128)(2,1)S(1)}, bf16[1,512,64]{1,2,0:T(8,128)(2,1)}, u32[]{:S(2)}, u32[]{:S(2)}) %collective-permute-start.1) | collective-permute-done | bytes 65568 | tf_op jit(solution)/shard_map/ppermute | solution.py:200
  86.3 0.8 constant_dynamic-update-slice_fusion.26
  87.1 5.2 %collective-permute-done.2 = bf16[1,512,64]{1,2,0:T(8,128)(2,1)S(1)} collective-permute-done((bf16[1,512,64]{1,2,0:T(8,128)(2,1)S(1)}, bf16[1,512,64]{1,2,0:T(8,128)(2,1)S(1)}, u32[]{:S(2)}, u32[]{:S(2)}) %collective-permute-start.2) | collective-permute-done | bytes 65568 | tf_op jit(solution)/shard_map/ppermute | solution.py:200
  92.3 0.9 constant_dynamic-update-slice_fusion.24
  93.1 0.8 constant_dynamic-update-slice_fusion.23
  94.0 0.8 constant_dynamic-update-slice_fusion.22
  94.8 0.8 constant_dynamic-update-slice_fusion.21
  95.7 1.3 copy.42
  97.0 15.8 %all-to-all-done.1 = bf16[32,384,128]{2,1,0:T(8,128)(2,1)} async-done(((bf16[32,384,128]{2,1,0:T(8,128)(2,1)}), bf16[32,384,128]{2,1,0:T(8,128)(2,1)}, u32[]{:S(2)}, u32[]{:S(2)}) %all-to-all-start.1) | async-done | bytes 3145760 | tf_op jit(solution)/shard_map/all_to_all | solution.py:252
  112.8 32.3 %shard_map.104 = (bf16[32,128,64]{2,1,0:T(8,128)(2,1)}, f32[32,128,64]{2,1,0:T(8,128)}, f32[32,3,128]{2,1,0:T(4,128)}, bf16[96,128,128]{2,1,0:T(8,128)(2,1)}) custom-call(s32[128]{0:T(128)} %reshape.70.refs_0_, s32[128]{0:T(128)} %copy-done.12, bf16[32,128,64]{2,1,0:T(8,128)(2,1)} %bitcast.72, bf16[32,128,128]{2,1,0:T(8,128)(2,1)} %bitcast.67, ...), custom_call_target="tpu_custom_call" | custom-call | tf_op jit(solution)/shard_map/pallas_call | solution.py:134
  145.1 8.7 %all-to-all-start.2 = ((bf16[32,384,128]{2,1,0:T(8,128)(2,1)}), bf16[32,384,128]{2,1,0:T(8,128)(2,1)}, u32[]{:S(2)}, u32[]{:S(2)}) async-start(bf16[32,384,128]{2,1,0:T(8,128)(2,1)} %bitcast.79), calls=%async_computation.2 | async-start | bytes 6291456 | tf_op jit(solution)/shard_map/all_to_all | solution.py:277
  153.8 1.5 copy.45
  155.4 15.5 %shard_map.105 = (bf16[32,128,64]{2,1,0:T(8,128)(2,1)}, f32[32,128,128]{2,1,0:T(8,128)}) custom-call(s32[128]{0:T(128)} %reshape.70.refs_0_, bf16[32,128,64]{2,1,0:T(8,128)(2,1)} %bitcast.73, bf16[32,128,128]{2,1,0:T(8,128)(2,1)} %bitcast.68, bf16[32,128,64]{2,1,0:T(8,128)(2,1)} %bitcast.71, f32[32,3,128]{2,1,0:T(4,128)} %get-tuple-element.15.refs_4_, ...), custom_call_target="tpu_custom_call" | custom-call | tf_op jit(solution)/shard_map/pallas_call | solution.py:149
  170.9 1.5 copy.53
  172.5 1.4 collective-permute-start.27
  173.9 0.8 collective-permute-start.26
  175.5 1.9 collective-permute-start.24
  177.5 1.5 collective-permute-start.21
  179.7 0.8 collective-permute-done.21
  180.5 2.5 collective-permute-start.14
  183.0 1.3 collective-permute-done.14
  185.0 4.4 %collective-permute-done.22 = bf16[1,512,64]{1,2,0:T(8,128)(2,1)S(1)} collective-permute-done((bf16[1,512,64]{1,2,0:T(8,128)(2,1)S(1)}, bf16[1,512,64]{1,2,0:T(8,128)(2,1)S(1)}, u32[]{:S(2)}, u32[]{:S(2)}) %collective-permute-start.22) | collective-permute-done | bytes 65568 | tf_op jit(solution)/shard_map/ppermute | solution.py:200
  189.4 2.5 collective-permute-start.23
  191.9 3.5 %collective-permute-done.23 = bf16[1,512,64]{1,2,0:T(8,128)(2,1)S(1)} collective-permute-done((bf16[1,512,64]{1,2,0:T(8,128)(2,1)S(1)}, bf16[1,512,64]{1,2,0:T(8,128)(2,1)S(1)}, u32[]{:S(2)}, u32[]{:S(2)}) %collective-permute-start.23) | collective-permute-done | bytes 65568 | tf_op jit(solution)/shard_map/ppermute | solution.py:200
  195.5 3.6 %collective-permute-start.20 = (bf16[1,512,64]{1,2,0:T(8,128)(2,1)S(1)}, bf16[1,512,64]{1,2,0:T(8,128)(2,1)S(1)}, u32[]{:S(2)}, u32[]{:S(2)}) collective-permute-start(bf16[1,512,64]{1,2,0:T(8,128)(2,1)S(1)} %get-tuple-element.27), channel_id=1, source_target_pairs={{0,7},{1,0},{2,1},{3,2},{4,3},{5,4},{6,5},{7,6},{8,15},{9,8},{10,9... | collective-permute-start | bytes 196616 | tf_op jit(solution)/shard_map/ppermute | solution.py:200
  199.2 1.2 collective-permute-start.18
  200.4 2.4 collective-permute-start.17
  203.1 22.1 %all-to-all-done.2 = bf16[32,384,128]{2,1,0:T(8,128)(2,1)} async-done(((bf16[32,384,128]{2,1,0:T(8,128)(2,1)}), bf16[32,384,128]{2,1,0:T(8,128)(2,1)}, u32[]{:S(2)}, u32[]{:S(2)}) %all-to-all-start.2) | async-done | bytes 3145760 | tf_op jit(solution)/shard_map/all_to_all | solution.py:277
  225.2 5.2 %shard_map.106 = bf16[32,128,128]{2,1,0:T(8,128)(2,1)} custom-call(s32[96]{0:T(128)} %copy-done.11, f32[32,128,128]{2,1,0:T(8,128)} %get-tuple-element.18.acc_ref, bf16[96,128,128]{2,1,0:T(8,128)(2,1)} %bitcast.25.ret_ref), custom_call_target="tpu_custom_call" | custom-call | tf_op jit(solution)/shard_map/pallas_call | solution.py:183
  230.4 8.3 %all-to-all-start.3 = ((bf16[8,512,128]{2,1,0:T(8,128)(2,1)}), bf16[8,512,128]{2,1,0:T(8,128)(2,1)}, u32[]{:S(2)}, u32[]{:S(2)}) async-start(bf16[8,512,128]{2,1,0:T(8,128)(2,1)} %bitcast.77), calls=%async_computation.3 | async-start | bytes 2097152 | tf_op jit(solution)/shard_map/all_to_all | solution.py:285
  238.7 3.2 %collective-permute-start.16 = (bf16[1,512,64]{1,2,0:T(8,128)(2,1)}, bf16[1,512,64]{1,2,0:T(8,128)(2,1)S(1)}, u32[]{:S(2)}, u32[]{:S(2)}) collective-permute-start(bf16[1,512,64]{1,2,0:T(8,128)(2,1)} %get-tuple-element.31), channel_id=1, source_target_pairs={{0,3},{1,4},{2,5},{3,6},{4,7},{5,0},{6,1},{7,2},{8,11},{9,12},{10,... | collective-permute-start | bytes 196616 | tf_op jit(solution)/shard_map/ppermute | solution.py:200
  241.9 13.3 %collective-permute-done.16 = bf16[1,512,64]{1,2,0:T(8,128)(2,1)S(1)} collective-permute-done((bf16[1,512,64]{1,2,0:T(8,128)(2,1)}, bf16[1,512,64]{1,2,0:T(8,128)(2,1)S(1)}, u32[]{:S(2)}, u32[]{:S(2)}) %collective-permute-start.16) | collective-permute-done | bytes 65568 | tf_op jit(solution)/shard_map/ppermute | solution.py:200
  255.3 1.3 fusion.6
  256.6 2.3 convolution_bitcast_fusion
  259.6 1.1 fusion.13
  (107 shorter events, 7.4 us)
Async XLA Ops:
  0.6 16.5 %copy-start = (bf16[512,512]{1,0:T(8,128)(2,1)S(1)}, bf16[512,512]{1,0:T(8,128)(2,1)}, u32[]{:S(2)}) copy-start(bf16[512,512]{1,0:T(8,128)(2,1)} %param.12) | copy-start | bytes 1572868
  1.9 2.9 %copy-start.2 = (bf16[512,512]{1,0:T(8,128)(2,1)S(1)}, bf16[512,512]{1,0:T(8,128)(2,1)}, u32[]{:S(2)}) copy-start(bf16[512,512]{1,0:T(8,128)(2,1)} %param.9) | copy-start | bytes 1572868
  1.9 2.9 %copy-start.15 = (f32[512]{0:T(512)S(1)}, f32[512]{0:T(512)}, u32[]{:S(2)}) copy-start(f32[512]{0:T(512)} %param.10) | copy-start | bytes 6148
  3.9 1.0 copy-start.10
  3.9 10.2 %copy-start.16 = (s32[1,32,3]{1,0,2:T(1,128)S(1)}, s32[1,32,3]{1,0,2:T(1,128)}, u32[]{:S(2)}) copy-start(s32[1,32,3]{1,0,2:T(1,128)} %param.16) | copy-start | bytes 1156
  6.7 21.7 %all-to-all-start = ((bf16[8,512,128]{2,1,0:T(8,128)(2,1)}), bf16[8,512,128]{2,1,0:T(8,128)(2,1)S(1)}, u32[]{:S(2)}, u32[]{:S(2)}) async-start(bf16[8,512,128]{2,1,0:T(8,128)(2,1)} %fusion.3), calls=%async_computation | async-start | bytes 2097152 | tf_op jit(solution)/shard_map/all_to_all | solution.py:241
  14.3 16.7 %copy-start.11 = (s32[96]{0:T(128)}, s32[96]{0:T(128)S(1)}, u32[]{:S(2)}) copy-start(s32[96]{0:T(128)S(1)} %reshape.88.ids_ref) | copy-start | bytes 1156
  14.4 2.7 %copy-start.6 = (bf16[512,512]{1,0:T(8,128)(2,1)S(1)}, bf16[512,512]{1,0:T(8,128)(2,1)}, u32[]{:S(2)}) copy-start(bf16[512,512]{1,0:T(8,128)(2,1)} %param.13) | copy-start | bytes 1572868
  28.3 2.7 %copy-start.1 = (bf16[8,512,128]{2,1,0:T(8,128)(2,1)}, bf16[8,512,128]{2,1,0:T(8,128)(2,1)S(1)}, u32[]{:S(2)}) copy-start(bf16[8,512,128]{2,1,0:T(8,128)(2,1)S(1)} %all-to-all-done) | copy-start | bytes 3145732
  31.1 10.7 %copy-start.17 = (s32[32,1]{0,1:T(1,128)S(1)}, s32[32,1]{0,1:T(1,128)}, u32[]{:S(2)}) copy-start(s32[32,1]{0,1:T(1,128)} %param.17) | copy-start | bytes 388
  31.1 10.9 %copy-start.13 = (s32[32,4]{0,1:T(4,128)S(1)}, s32[32,4]{0,1:T(4,128)}, u32[]{:S(2)}) copy-start(s32[32,4]{0,1:T(4,128)} %param.14) | copy-start | bytes 1540
  31.1 11.7 %copy-start.14 = (s32[32,4]{0,1:T(4,128)S(1)}, s32[32,4]{0,1:T(4,128)}, u32[]{:S(2)}) copy-start(s32[32,4]{0,1:T(4,128)} %param.15) | copy-start | bytes 1540
  31.1 81.8 %all-to-all-start.1 = ((bf16[32,384,128]{2,1,0:T(8,128)(2,1)}), bf16[32,384,128]{2,1,0:T(8,128)(2,1)}, u32[]{:S(2)}, u32[]{:S(2)}) async-start(bf16[32,384,128]{2,1,0:T(8,128)(2,1)} %bitcast.69), calls=%async_computation.1 | async-start | bytes 6291456 | tf_op jit(solution)/shard_map/all_to_all | solution.py:252
  41.6 3.6 %copy-start.5 = (bf16[8,512,64]{1,2,0:T(8,128)(2,1)S(1)}, bf16[8,512,64]{1,2,0:T(8,128)(2,1)}, u32[]{:S(2)}) copy-start(bf16[8,512,64]{1,2,0:T(8,128)(2,1)} %fusion.7) | copy-start | bytes 1572868
  41.7 5.0 %copy-start.4 = (bf16[8,512,64]{1,2,0:T(8,128)(2,1)S(1)}, bf16[8,512,64]{1,2,0:T(8,128)(2,1)}, u32[]{:S(2)}) copy-start(bf16[8,512,64]{1,2,0:T(8,128)(2,1)} %convert_bitcast_fusion) | copy-start | bytes 1572868
  42.9 5.7 %copy-start.12 = (s32[128]{0:T(128)}, s32[128]{0:T(128)S(1)}, u32[]{:S(2)}) copy-start(s32[128]{0:T(128)S(1)} %reshape.71.refs_1_) | copy-start | bytes 1540
  45.2 2.8 %collective-permute-start.7 = (bf16[1,512,64]{1,2,0:T(8,128)(2,1)S(1)}, bf16[1,512,64]{1,2,0:T(8,128)(2,1)S(1)}, u32[]{:S(2)}, u32[]{:S(2)}) collective-permute-start(bf16[1,512,64]{1,2,0:T(8,128)(2,1)S(1)} %constant_dynamic-slice_fusion.20), channel_id=1, source_target_pairs={{0,1},{1,2},{2,3},{3,4},{4,5},{5,6},{6,7},{7,0},{8,9},{9,10},{10,1... | collective-permute-start | bytes 196616 | tf_op jit(solution)/shard_map/ppermute | solution.py:200
  46.7 1.9 collective-permute-start
  48.0 7.6 %collective-permute-start.8 = (bf16[1,512,64]{1,2,0:T(8,128)(2,1)S(1)}, bf16[1,512,64]{1,2,0:T(8,128)(2,1)S(1)}, u32[]{:S(2)}, u32[]{:S(2)}) collective-permute-start(bf16[1,512,64]{1,2,0:T(8,128)(2,1)S(1)} %get-tuple-element.39), channel_id=1, source_target_pairs={{0,2},{1,3},{2,4},{3,5},{4,6},{5,7},{6,0},{7,1},{8,10},{9,11},{10,... | collective-permute-start | bytes 196616 | tf_op jit(solution)/shard_map/ppermute | solution.py:200
  48.7 46.2 %collective-permute-start.6 = (bf16[1,512,64]{1,2,0:T(8,128)(2,1)S(1)}, bf16[1,512,64]{1,2,0:T(8,128)(2,1)}, u32[]{:S(2)}, u32[]{:S(2)}) collective-permute-start(bf16[1,512,64]{1,2,0:T(8,128)(2,1)S(1)} %get-tuple-element.41), channel_id=1, source_target_pairs={{0,7},{1,0},{2,1},{3,2},{4,3},{5,4},{6,5},{7,6},{8,15},{9,8},{10,9... | collective-permute-start | bytes 196616 | tf_op jit(solution)/shard_map/ppermute | solution.py:200
  52.1 41.8 %collective-permute-start.5 = (bf16[1,512,64]{1,2,0:T(8,128)(2,1)S(1)}, bf16[1,512,64]{1,2,0:T(8,128)(2,1)}, u32[]{:S(2)}, u32[]{:S(2)}) collective-permute-start(bf16[1,512,64]{1,2,0:T(8,128)(2,1)S(1)} %get-tuple-element.42), channel_id=1, source_target_pairs={{0,6},{1,7},{2,0},{3,1},{4,2},{5,3},{6,4},{7,5},{8,14},{9,15},{10,... | collective-permute-start | bytes 196616 | tf_op jit(solution)/shard_map/ppermute | solution.py:200
  54.5 38.6 %collective-permute-start.4 = (bf16[1,512,64]{1,2,0:T(8,128)(2,1)S(1)}, bf16[1,512,64]{1,2,0:T(8,128)(2,1)}, u32[]{:S(2)}, u32[]{:S(2)}) collective-permute-start(bf16[1,512,64]{1,2,0:T(8,128)(2,1)S(1)} %get-tuple-element.43), channel_id=1, source_target_pairs={{0,5},{1,6},{2,7},{3,0},{4,1},{5,2},{6,3},{7,4},{8,13},{9,14},{10,... | collective-permute-start | bytes 196616 | tf_op jit(solution)/shard_map/ppermute | solution.py:200
  54.6 37.7 %collective-permute-start.3 = (bf16[1,512,64]{1,2,0:T(8,128)(2,1)S(1)}, bf16[1,512,64]{1,2,0:T(8,128)(2,1)}, u32[]{:S(2)}, u32[]{:S(2)}) collective-permute-start(bf16[1,512,64]{1,2,0:T(8,128)(2,1)S(1)} %get-tuple-element.44), channel_id=1, source_target_pairs={{0,4},{1,5},{2,6},{3,7},{4,0},{5,1},{6,2},{7,3},{8,12},{9,13},{10,... | collective-permute-start | bytes 196616 | tf_op jit(solution)/shard_map/ppermute | solution.py:200
  55.7 6.1 %collective-permute-start.9 = (bf16[1,512,64]{1,2,0:T(8,128)(2,1)S(1)}, bf16[1,512,64]{1,2,0:T(8,128)(2,1)S(1)}, u32[]{:S(2)}, u32[]{:S(2)}) collective-permute-start(bf16[1,512,64]{1,2,0:T(8,128)(2,1)S(1)} %get-tuple-element.38), channel_id=1, source_target_pairs={{0,3},{1,4},{2,5},{3,6},{4,7},{5,0},{6,1},{7,2},{8,11},{9,12},{10,... | collective-permute-start | bytes 196616 | tf_op jit(solution)/shard_map/ppermute | solution.py:200
  61.7 5.0 %collective-permute-start.10 = (bf16[1,512,64]{1,2,0:T(8,128)(2,1)S(1)}, bf16[1,512,64]{1,2,0:T(8,128)(2,1)S(1)}, u32[]{:S(2)}, u32[]{:S(2)}) collective-permute-start(bf16[1,512,64]{1,2,0:T(8,128)(2,1)S(1)} %get-tuple-element.37), channel_id=1, source_target_pairs={{0,4},{1,5},{2,6},{3,7},{4,0},{5,1},{6,2},{7,3},{8,12},{9,13},{10,... | collective-permute-start | bytes 196616 | tf_op jit(solution)/shard_map/ppermute | solution.py:200
  66.7 5.6 %collective-permute-start.11 = (bf16[1,512,64]{1,2,0:T(8,128)(2,1)S(1)}, bf16[1,512,64]{1,2,0:T(8,128)(2,1)S(1)}, u32[]{:S(2)}, u32[]{:S(2)}) collective-permute-start(bf16[1,512,64]{1,2,0:T(8,128)(2,1)S(1)} %get-tuple-element.36), channel_id=1, source_target_pairs={{0,5},{1,6},{2,7},{3,0},{4,1},{5,2},{6,3},{7,4},{8,13},{9,14},{10,... | collective-permute-start | bytes 196616 | tf_op jit(solution)/shard_map/ppermute | solution.py:200
  72.3 3.8 %collective-permute-start.12 = (bf16[1,512,64]{1,2,0:T(8,128)(2,1)S(1)}, bf16[1,512,64]{1,2,0:T(8,128)(2,1)S(1)}, u32[]{:S(2)}, u32[]{:S(2)}) collective-permute-start(bf16[1,512,64]{1,2,0:T(8,128)(2,1)S(1)} %get-tuple-element.35), channel_id=1, source_target_pairs={{0,6},{1,7},{2,0},{3,1},{4,2},{5,3},{6,4},{7,5},{8,14},{9,15},{10,... | collective-permute-start | bytes 196616 | tf_op jit(solution)/shard_map/ppermute | solution.py:200
  76.2 4.1 %collective-permute-start.13 = (bf16[1,512,64]{1,2,0:T(8,128)(2,1)S(1)}, bf16[1,512,64]{1,2,0:T(8,128)(2,1)S(1)}, u32[]{:S(2)}, u32[]{:S(2)}) collective-permute-start(bf16[1,512,64]{1,2,0:T(8,128)(2,1)S(1)} %get-tuple-element.34), channel_id=1, source_target_pairs={{0,7},{1,0},{2,1},{3,2},{4,3},{5,4},{6,5},{7,6},{8,15},{9,8},{10,9... | collective-permute-start | bytes 196616 | tf_op jit(solution)/shard_map/ppermute | solution.py:200
  80.3 6.0 %collective-permute-start.1 = (bf16[1,512,64]{1,2,0:T(8,128)(2,1)S(1)}, bf16[1,512,64]{1,2,0:T(8,128)(2,1)}, u32[]{:S(2)}, u32[]{:S(2)}) collective-permute-start(bf16[1,512,64]{1,2,0:T(8,128)(2,1)S(1)} %get-tuple-element.46), channel_id=1, source_target_pairs={{0,2},{1,3},{2,4},{3,5},{4,6},{5,7},{6,0},{7,1},{8,10},{9,11},{10,... | collective-permute-start | bytes 196616 | tf_op jit(solution)/shard_map/ppermute | solution.py:200
  86.3 6.0 %collective-permute-start.2 = (bf16[1,512,64]{1,2,0:T(8,128)(2,1)S(1)}, bf16[1,512,64]{1,2,0:T(8,128)(2,1)S(1)}, u32[]{:S(2)}, u32[]{:S(2)}) collective-permute-start(bf16[1,512,64]{1,2,0:T(8,128)(2,1)S(1)} %get-tuple-element.45), channel_id=1, source_target_pairs={{0,3},{1,4},{2,5},{3,6},{4,7},{5,0},{6,1},{7,2},{8,11},{9,12},{10,... | collective-permute-start | bytes 196616 | tf_op jit(solution)/shard_map/ppermute | solution.py:200
  145.1 80.1 %all-to-all-start.2 = ((bf16[32,384,128]{2,1,0:T(8,128)(2,1)}), bf16[32,384,128]{2,1,0:T(8,128)(2,1)}, u32[]{:S(2)}, u32[]{:S(2)}) async-start(bf16[32,384,128]{2,1,0:T(8,128)(2,1)} %bitcast.79), calls=%async_computation.2 | async-start | bytes 6291456 | tf_op jit(solution)/shard_map/all_to_all | solution.py:277
  172.5 30.2 %collective-permute-start.27 = (bf16[1,512,64]{1,2,0:T(8,128)(2,1)S(1)}, bf16[1,512,64]{1,2,0:T(8,128)(2,1)S(1)}, u32[]{:S(2)}, u32[]{:S(2)}) collective-permute-start(bf16[1,512,64]{1,2,0:T(8,128)(2,1)S(1)} %get-tuple-element.20), channel_id=1, source_target_pairs={{0,7},{1,0},{2,1},{3,2},{4,3},{5,4},{6,5},{7,6},{8,15},{9,8},{10,9... | collective-permute-start | bytes 196616 | tf_op jit(solution)/shard_map/ppermute | solution.py:200
  173.9 26.4 %collective-permute-start.26 = (bf16[1,512,64]{1,2,0:T(8,128)(2,1)S(1)}, bf16[1,512,64]{1,2,0:T(8,128)(2,1)S(1)}, u32[]{:S(2)}, u32[]{:S(2)}) collective-permute-start(bf16[1,512,64]{1,2,0:T(8,128)(2,1)S(1)} %get-tuple-element.21), channel_id=1, source_target_pairs={{0,6},{1,7},{2,0},{3,1},{4,2},{5,3},{6,4},{7,5},{8,14},{9,15},{10,... | collective-permute-start | bytes 196616 | tf_op jit(solution)/shard_map/ppermute | solution.py:200
  174.8 24.4 %collective-permute-start.25 = (bf16[1,512,64]{1,2,0:T(8,128)(2,1)S(1)}, bf16[1,512,64]{1,2,0:T(8,128)(2,1)S(1)}, u32[]{:S(2)}, u32[]{:S(2)}) collective-permute-start(bf16[1,512,64]{1,2,0:T(8,128)(2,1)S(1)} %get-tuple-element.22), channel_id=1, source_target_pairs={{0,5},{1,6},{2,7},{3,0},{4,1},{5,2},{6,3},{7,4},{8,13},{9,14},{10,... | collective-permute-start | bytes 196616 | tf_op jit(solution)/shard_map/ppermute | solution.py:200
  175.5 23.5 %collective-permute-start.24 = (bf16[1,512,64]{1,2,0:T(8,128)(2,1)S(1)}, bf16[1,512,64]{1,2,0:T(8,128)(2,1)S(1)}, u32[]{:S(2)}, u32[]{:S(2)}) collective-permute-start(bf16[1,512,64]{1,2,0:T(8,128)(2,1)S(1)} %get-tuple-element.23), channel_id=1, source_target_pairs={{0,4},{1,5},{2,6},{3,7},{4,0},{5,1},{6,2},{7,3},{8,12},{9,13},{10,... | collective-permute-start | bytes 196616 | tf_op jit(solution)/shard_map/ppermute | solution.py:200
  177.5 3.0 %collective-permute-start.21 = (bf16[1,512,64]{1,2,0:T(8,128)(2,1)S(1)}, bf16[1,512,64]{1,2,0:T(8,128)(2,1)S(1)}, u32[]{:S(2)}, u32[]{:S(2)}) collective-permute-start(bf16[1,512,64]{1,2,0:T(8,128)(2,1)S(1)} %get-tuple-element.26), channel_id=1, source_target_pairs={{0,1},{1,2},{2,3},{3,4},{4,5},{5,6},{6,7},{7,0},{8,9},{9,10},{10,1... | collective-permute-start | bytes 196616 | tf_op jit(solution)/shard_map/ppermute | solution.py:200
  180.5 3.8 %collective-permute-start.14 = (bf16[1,512,64]{1,2,0:T(8,128)(2,1)S(1)}, bf16[1,512,64]{1,2,0:T(8,128)(2,1)S(1)}, u32[]{:S(2)}, u32[]{:S(2)}) collective-permute-start(bf16[1,512,64]{1,2,0:T(8,128)(2,1)S(1)} %get-tuple-element.33), channel_id=1, source_target_pairs={{0,1},{1,2},{2,3},{3,4},{4,5},{5,6},{6,7},{7,0},{8,9},{9,10},{10,1... | collective-permute-start | bytes 196616 | tf_op jit(solution)/shard_map/ppermute | solution.py:200
  184.3 5.1 %collective-permute-start.22 = (bf16[1,512,64]{1,2,0:T(8,128)(2,1)S(1)}, bf16[1,512,64]{1,2,0:T(8,128)(2,1)S(1)}, u32[]{:S(2)}, u32[]{:S(2)}) collective-permute-start(bf16[1,512,64]{1,2,0:T(8,128)(2,1)S(1)} %get-tuple-element.25), channel_id=1, source_target_pairs={{0,2},{1,3},{2,4},{3,5},{4,6},{5,7},{6,0},{7,1},{8,10},{9,11},{10,... | collective-permute-start | bytes 196616 | tf_op jit(solution)/shard_map/ppermute | solution.py:200
  189.4 6.0 %collective-permute-start.23 = (bf16[1,512,64]{1,2,0:T(8,128)(2,1)S(1)}, bf16[1,512,64]{1,2,0:T(8,128)(2,1)S(1)}, u32[]{:S(2)}, u32[]{:S(2)}) collective-permute-start(bf16[1,512,64]{1,2,0:T(8,128)(2,1)S(1)} %get-tuple-element.24), channel_id=1, source_target_pairs={{0,3},{1,4},{2,5},{3,6},{4,7},{5,0},{6,1},{7,2},{8,11},{9,12},{10,... | collective-permute-start | bytes 196616 | tf_op jit(solution)/shard_map/ppermute | solution.py:200
  195.5 59.8 %collective-permute-start.20 = (bf16[1,512,64]{1,2,0:T(8,128)(2,1)S(1)}, bf16[1,512,64]{1,2,0:T(8,128)(2,1)S(1)}, u32[]{:S(2)}, u32[]{:S(2)}) collective-permute-start(bf16[1,512,64]{1,2,0:T(8,128)(2,1)S(1)} %get-tuple-element.27), channel_id=1, source_target_pairs={{0,7},{1,0},{2,1},{3,2},{4,3},{5,4},{6,5},{7,6},{8,15},{9,8},{10,9... | collective-permute-start | bytes 196616 | tf_op jit(solution)/shard_map/ppermute | solution.py:200
  199.1 56.2 %collective-permute-start.19 = (bf16[1,512,64]{1,2,0:T(8,128)(2,1)}, bf16[1,512,64]{1,2,0:T(8,128)(2,1)S(1)}, u32[]{:S(2)}, u32[]{:S(2)}) collective-permute-start(bf16[1,512,64]{1,2,0:T(8,128)(2,1)} %get-tuple-element.28), channel_id=1, source_target_pairs={{0,6},{1,7},{2,0},{3,1},{4,2},{5,3},{6,4},{7,5},{8,14},{9,15},{10,... | collective-permute-start | bytes 196616 | tf_op jit(solution)/shard_map/ppermute | solution.py:200
  199.2 56.0 %collective-permute-start.18 = (bf16[1,512,64]{1,2,0:T(8,128)(2,1)}, bf16[1,512,64]{1,2,0:T(8,128)(2,1)S(1)}, u32[]{:S(2)}, u32[]{:S(2)}) collective-permute-start(bf16[1,512,64]{1,2,0:T(8,128)(2,1)} %get-tuple-element.29), channel_id=1, source_target_pairs={{0,5},{1,6},{2,7},{3,0},{4,1},{5,2},{6,3},{7,4},{8,13},{9,14},{10,... | collective-permute-start | bytes 196616 | tf_op jit(solution)/shard_map/ppermute | solution.py:200
  200.4 54.8 %collective-permute-start.17 = (bf16[1,512,64]{1,2,0:T(8,128)(2,1)}, bf16[1,512,64]{1,2,0:T(8,128)(2,1)S(1)}, u32[]{:S(2)}, u32[]{:S(2)}) collective-permute-start(bf16[1,512,64]{1,2,0:T(8,128)(2,1)} %get-tuple-element.30), channel_id=1, source_target_pairs={{0,4},{1,5},{2,6},{3,7},{4,0},{5,1},{6,2},{7,3},{8,12},{9,13},{10,... | collective-permute-start | bytes 196616 | tf_op jit(solution)/shard_map/ppermute | solution.py:200
  202.8 35.9 %collective-permute-start.15 = (bf16[1,512,64]{1,2,0:T(8,128)(2,1)}, bf16[1,512,64]{1,2,0:T(8,128)(2,1)S(1)}, u32[]{:S(2)}, u32[]{:S(2)}) collective-permute-start(bf16[1,512,64]{1,2,0:T(8,128)(2,1)} %get-tuple-element.32), channel_id=1, source_target_pairs={{0,2},{1,3},{2,4},{3,5},{4,6},{5,7},{6,0},{7,1},{8,10},{9,11},{10,... | collective-permute-start | bytes 196616 | tf_op jit(solution)/shard_map/ppermute | solution.py:200
  203.1 22.1 %copy-start.8 = (bf16[8,512,64]{1,2,0:T(8,128)(2,1)}, bf16[8,512,64]{1,2,0:T(8,128)(2,1)S(1)}, u32[]{:S(2)}) copy-start(bf16[8,512,64]{1,2,0:T(8,128)(2,1)S(1)} %constant_dynamic-update-slice_fusion) | copy-start | bytes 1572868
  225.2 30.1 %copy-start.3 = (bf16[512,512]{1,0:T(8,128)(2,1)S(1)}, bf16[512,512]{1,0:T(8,128)(2,1)}, u32[]{:S(2)}) copy-start(bf16[512,512]{1,0:T(8,128)(2,1)} %param.9) | copy-start | bytes 1572868
  230.4 26.2 %all-to-all-start.3 = ((bf16[8,512,128]{2,1,0:T(8,128)(2,1)}), bf16[8,512,128]{2,1,0:T(8,128)(2,1)}, u32[]{:S(2)}, u32[]{:S(2)}) async-start(bf16[8,512,128]{2,1,0:T(8,128)(2,1)} %bitcast.77), calls=%async_computation.3 | async-start | bytes 2097152 | tf_op jit(solution)/shard_map/all_to_all | solution.py:285
  238.7 16.4 %collective-permute-start.16 = (bf16[1,512,64]{1,2,0:T(8,128)(2,1)}, bf16[1,512,64]{1,2,0:T(8,128)(2,1)S(1)}, u32[]{:S(2)}, u32[]{:S(2)}) collective-permute-start(bf16[1,512,64]{1,2,0:T(8,128)(2,1)} %get-tuple-element.31), channel_id=1, source_target_pairs={{0,3},{1,4},{2,5},{3,6},{4,7},{5,0},{6,1},{7,2},{8,11},{9,12},{10,... | collective-permute-start | bytes 196616 | tf_op jit(solution)/shard_map/ppermute | solution.py:200
  256.6 3.0 %copy-start.7 = (bf16[512,512]{1,0:T(8,128)(2,1)S(1)}, bf16[512,512]{1,0:T(8,128)(2,1)}, u32[]{:S(2)}) copy-start(bf16[512,512]{1,0:T(8,128)(2,1)} %param.13) | copy-start | bytes 1572868
  256.6 2.3 copy-start.9

commit v8 on v7

--- a/solution.py
+++ b/solution.py
@@ -15,16 +15,6 @@
     return jnp.concatenate(
         [kv_ref[i, :, cols] for i in ids_l] + [pool_ref[i, :, cols] for i in ids_r], axis=0
     )
-
-
-def column_to_row(col):
-    n = col.shape[0]
-    return jnp.broadcast_to(col, (n, n)).T[0:1, :]
-
-
-def row_to_column(row):
-    n = row.shape[1]
-    return jnp.broadcast_to(row, (n, n)).T[:, 0:1]
 
 
 def remote_kernel(
@@ -59,9 +49,7 @@
         o = jnp.dot(w, vals, preferred_element_type=f32).astype(bf16)
         o_ref[b] = o
         delta = jnp.sum(do_s.astype(f32) * o.astype(f32), axis=1, keepdims=True)
-        stats_ref[b] = jnp.concatenate(
-            [column_to_row(top), column_to_row(rtot), column_to_row(delta)], axis=0
-        )
+        stats_ref[b] = jnp.concatenate([top, rtot, delta], axis=1)
         keys_r = keys[split:]
         vals_r = vals[split:]
         w_r = w[:, split:]
@@ -101,9 +89,9 @@
         q_s = q * scale
         do_s = do * scale
         stats = stats_ref[b]
-        top = row_to_column(stats[0:1, :])
-        rtot = row_to_column(stats[1:2, :])
-        delta = row_to_column(stats[2:3, :])
+        top = stats[:, 0:1]
+        rtot = stats[:, 1:2]
+        delta = stats[:, 2:3]
         s = lax.dot_general(q_s, keys, nt, preferred_element_type=f32)
         w = (jnp.exp(s - top) * rtot).astype(bf16)
         dw = lax.dot_general(do_s, vals, nt, preferred_element_type=f32)
@@ -138,7 +126,7 @@
         out_shape=(
             jax.ShapeDtypeStruct((nq, bsize, depth), jnp.bfloat16),
             jax.ShapeDtypeStruct((nq, bsize, depth), f32),
-            jax.ShapeDtypeStruct((nq, 3, bsize), f32),
+            jax.ShapeDtypeStruct((nq, bsize, 3), f32),
             jax.ShapeDtypeStruct((npool,) + kv_t, jnp.bfloat16),
         ),
         in_specs=[smem, smem] + [vmem] * 5,

time: 261 us -> 262 us (level)
  no operation moved by 1% of the time
where the time goes in v8:
time: 262 us; the launch traced here: 261 us
  waiting for transfers between devices  98.2 us (37%)
  starting transfers between devices  74.9 us (29%)
  Pallas kernels  53.3 us (20%)
  local copies, waits for them, and re-layouts  21.4 us (8%)
  matrix products  9.05 us (3%)
  other arithmetic  3.38 us (1%)
    ppermute x28, waiting for transfers between devices, head_exchange(): got = lax.ppermute(part, axis, perm)  50.6 us
    ppermute x28, starting transfers between devices, head_exchange(): got = lax.ppermute(part, axis, perm)  40.1 us
    pallas_call x1, Pallas kernels, fused_attention(): pl.pallas_call(lambda *refs: remote_kernel(*refs, near=near, far=far, bsi...  32.3 us
    all_to_all x1, waiting for transfers between devices, local(): lax.all_to_all(slot_grads.reshape(ndom, pair_slots * 2 * hwide, bsize), '...  21.7 us
    all_to_all x1, waiting for transfers between devices, local(): lax.all_to_all(outgoing.reshape(ndom, pair_slots * bsize, 2 * hwide), 'do...  15.9 us
    pallas_call x1, Pallas kernels, fused_attention(): pl.pallas_call(lambda *refs: local_kernel(*refs, near=near, bsize=bsize,...  15.8 us
    all_to_all x1, starting transfers between devices, local(): lax.all_to_all(outgoing.reshape(ndom, pair_slots * bsize, 2 * hwide), 'do...  10.6 us
    all_to_all x1, waiting for transfers between devices, local(): lax.all_to_all(kv_own, 'head', split_axis=0, concat_axis=0, tiled=True)  9.95 us
  transfers between devices with their start and end apart: 32, of which 17 were waited for; matrix products, arithmetic and copies ran while one was open for 8% of the time, Pallas kernels for 8%

profile of v8, /device:TPU:1, one launch (start us, length us, event | category | flops | bytes accessed | tf_op | source)
XLA Modules:
  0.0 261.3 jit_solution(17473075830679992181)
XLA Ops:
  0.6 1.3 fusion.14
  1.9 1.7 copy.38
  3.9 1.0 copy-done.10
  4.8 1.8 fusion.3
  6.6 6.8 %all-to-all-start = ((bf16[8,512,128]{2,1,0:T(8,128)(2,1)}), bf16[8,512,128]{2,1,0:T(8,128)(2,1)S(1)}, u32[]{:S(2)}, u32[]{:S(2)}) async-start(bf16[8,512,128]{2,1,0:T(8,128)(2,1)} %fusion.3), calls=%async_computation | async-start | bytes 2097152 | tf_op jit(solution)/shard_map/all_to_all | solution.py:229
  13.4 0.8 slice.13
  14.5 1.8 fusion.18
  16.3 0.9 convert_bitcast_fusion
  17.2 1.3 fusion.7
  18.5 10.0 %all-to-all-done = bf16[8,512,128]{2,1,0:T(8,128)(2,1)S(1)} async-done(((bf16[8,512,128]{2,1,0:T(8,128)(2,1)}), bf16[8,512,128]{2,1,0:T(8,128)(2,1)S(1)}, u32[]{:S(2)}, u32[]{:S(2)}) %all-to-all-start) | async-done | bytes 1048608 | tf_op jit(solution)/shard_map/all_to_all | solution.py:229
  28.4 2.7 %gather_fusion = bf16[96,128,128]{2,1,0:T(8,128)(2,1)} fusion(bf16[32,128,128]{2,1,0:T(8,128)(2,1)S(1)} %bitcast.66, s32[1024]{0:T(1024)S(1)} %pad_clamp_fusion.1), kind=kCustom, calls=%fused_computation | custom fusion | bytes 6291840 | tf_op jit(solution)/shard_map/jit(_take)/gather | solution.py:236
  31.2 10.6 %all-to-all-start.1 = ((bf16[32,384,128]{2,1,0:T(8,128)(2,1)}), bf16[32,384,128]{2,1,0:T(8,128)(2,1)}, u32[]{:S(2)}, u32[]{:S(2)}) async-start(bf16[32,384,128]{2,1,0:T(8,128)(2,1)} %bitcast.69), calls=%async_computation.1 | async-start | bytes 6291456 | tf_op jit(solution)/shard_map/all_to_all | solution.py:240
  43.0 1.2 gather_fusion.1
  45.3 1.4 collective-permute-start.7
  46.8 1.3 collective-permute-done.7
  48.7 3.5 %collective-permute-start.6 = (bf16[1,512,64]{1,2,0:T(8,128)(2,1)S(1)}, bf16[1,512,64]{1,2,0:T(8,128)(2,1)}, u32[]{:S(2)}, u32[]{:S(2)}) collective-permute-start(bf16[1,512,64]{1,2,0:T(8,128)(2,1)S(1)} %get-tuple-element.41), channel_id=1, source_target_pairs={{0,7},{1,0},{2,1},{3,2},{4,3},{5,4},{6,5},{7,6},{8,15},{9,8},{10,9... | collective-permute-start | bytes 196616 | tf_op jit(solution)/shard_map/ppermute | solution.py:188
  52.2 2.4 collective-permute-start.5
  54.6 1.1 collective-permute-start.3
  55.7 2.4 collective-permute-start.9
  58.1 3.7 %collective-permute-done.9 = bf16[1,512,64]{1,2,0:T(8,128)(2,1)S(1)} collective-permute-done((bf16[1,512,64]{1,2,0:T(8,128)(2,1)S(1)}, bf16[1,512,64]{1,2,0:T(8,128)(2,1)S(1)}, u32[]{:S(2)}, u32[]{:S(2)}) %collective-permute-start.9) | collective-permute-done | bytes 65568 | tf_op jit(solution)/shard_map/ppermute | solution.py:188
  62.4 4.4 %collective-permute-done.10 = bf16[1,512,64]{1,2,0:T(8,128)(2,1)S(1)} collective-permute-done((bf16[1,512,64]{1,2,0:T(8,128)(2,1)S(1)}, bf16[1,512,64]{1,2,0:T(8,128)(2,1)S(1)}, u32[]{:S(2)}, u32[]{:S(2)}) %collective-permute-start.10) | collective-permute-done | bytes 65568 | tf_op jit(solution)/shard_map/ppermute | solution.py:188
  66.8 2.3 collective-permute-start.11
  69.1 3.3 %collective-permute-done.11 = bf16[1,512,64]{1,2,0:T(8,128)(2,1)S(1)} collective-permute-done((bf16[1,512,64]{1,2,0:T(8,128)(2,1)S(1)}, bf16[1,512,64]{1,2,0:T(8,128)(2,1)S(1)}, u32[]{:S(2)}, u32[]{:S(2)}) %collective-permute-start.11) | collective-permute-done | bytes 65568 | tf_op jit(solution)/shard_map/ppermute | solution.py:188
  72.4 1.3 collective-permute-start.12
  73.7 2.5 collective-permute-done.12
  76.2 1.0 collective-permute-start.13
  77.2 3.1 %collective-permute-done.13 = bf16[1,512,64]{1,2,0:T(8,128)(2,1)S(1)} collective-permute-done((bf16[1,512,64]{1,2,0:T(8,128)(2,1)S(1)}, bf16[1,512,64]{1,2,0:T(8,128)(2,1)S(1)}, u32[]{:S(2)}, u32[]{:S(2)}) %collective-permute-start.13) | collective-permute-done | bytes 65568 | tf_op jit(solution)/shard_map/ppermute | solution.py:188
  80.3 1.5 collective-permute-start.1
  81.8 1.3 copy.43
  83.1 3.2 %collective-permute-done.1 = bf16[1,512,64]{1,2,0:T(8,128)(2,1)} collective-permute-done((bf16[1,512,64]{1,2,0:T(8,128)(2,1)S(1)}, bf16[1,512,64]{1,2,0:T(8,128)(2,1)}, u32[]{:S(2)}, u32[]{:S(2)}) %collective-permute-start.1) | collective-permute-done | bytes 65568 | tf_op jit(solution)/shard_map/ppermute | solution.py:188
  86.3 0.8 constant_dynamic-update-slice_fusion.26
  87.1 5.2 %collective-permute-done.2 = bf16[1,512,64]{1,2,0:T(8,128)(2,1)S(1)} collective-permute-done((bf16[1,512,64]{1,2,0:T(8,128)(2,1)S(1)}, bf16[1,512,64]{1,2,0:T(8,128)(2,1)S(1)}, u32[]{:S(2)}, u32[]{:S(2)}) %collective-permute-start.2) | collective-permute-done | bytes 65568 | tf_op jit(solution)/shard_map/ppermute | solution.py:188
  92.3 0.9 constant_dynamic-update-slice_fusion.24
  93.2 0.8 constant_dynamic-update-slice_fusion.23
  94.0 0.8 constant_dynamic-update-slice_fusion.22
  94.9 0.8 constant_dynamic-update-slice_fusion.21
  95.7 1.3 copy.42
  97.1 15.9 %all-to-all-done.1 = bf16[32,384,128]{2,1,0:T(8,128)(2,1)} async-done(((bf16[32,384,128]{2,1,0:T(8,128)(2,1)}), bf16[32,384,128]{2,1,0:T(8,128)(2,1)}, u32[]{:S(2)}, u32[]{:S(2)}) %all-to-all-start.1) | async-done | bytes 3145760 | tf_op jit(solution)/shard_map/all_to_all | solution.py:240
  112.9 32.3 %shard_map.104 = (bf16[32,128,64]{2,1,0:T(8,128)(2,1)}, f32[32,128,64]{2,1,0:T(8,128)}, f32[32,128,3]{2,1,0:T(8,128)}, bf16[96,128,128]{2,1,0:T(8,128)(2,1)}) custom-call(s32[128]{0:T(128)} %reshape.70.refs_0_, s32[128]{0:T(128)} %copy-done.12, bf16[32,128,64]{2,1,0:T(8,128)(2,1)} %bitcast.72, bf16[32,128,128]{2,1,0:T(8,128)(2,1)} %bitcast.67, ...), custom_call_target="tpu_custom_call" | custom-call | tf_op jit(solution)/shard_map/pallas_call | solution.py:122
  145.2 8.8 %all-to-all-start.2 = ((bf16[32,384,128]{2,1,0:T(8,128)(2,1)}), bf16[32,384,128]{2,1,0:T(8,128)(2,1)}, u32[]{:S(2)}, u32[]{:S(2)}) async-start(bf16[32,384,128]{2,1,0:T(8,128)(2,1)} %bitcast.79), calls=%async_computation.2 | async-start | bytes 6291456 | tf_op jit(solution)/shard_map/all_to_all | solution.py:265
  154.0 1.5 copy.45
  155.5 15.8 %shard_map.105 = (bf16[32,128,64]{2,1,0:T(8,128)(2,1)}, f32[32,128,128]{2,1,0:T(8,128)}) custom-call(s32[128]{0:T(128)} %reshape.70.refs_0_, bf16[32,128,64]{2,1,0:T(8,128)(2,1)} %bitcast.73, bf16[32,128,128]{2,1,0:T(8,128)(2,1)} %bitcast.68, bf16[32,128,64]{2,1,0:T(8,128)(2,1)} %bitcast.71, f32[32,128,3]{2,1,0:T(8,128)} %get-tuple-element.15.refs_4_, ...), custom_call_target="tpu_custom_call" | custom-call | tf_op jit(solution)/shard_map/pallas_call | solution.py:137
  171.4 1.5 copy.53
  173.0 1.4 collective-permute-start.27
  174.3 0.9 collective-permute-start.26
  175.9 1.9 collective-permute-start.24
  177.8 1.5 collective-permute-start.21
  180.0 0.9 collective-permute-done.21
  180.9 2.5 collective-permute-start.14
  183.4 1.3 collective-permute-done.14
  185.2 4.5 %collective-permute-done.22 = bf16[1,512,64]{1,2,0:T(8,128)(2,1)S(1)} collective-permute-done((bf16[1,512,64]{1,2,0:T(8,128)(2,1)S(1)}, bf16[1,512,64]{1,2,0:T(8,128)(2,1)S(1)}, u32[]{:S(2)}, u32[]{:S(2)}) %collective-permute-start.22) | collective-permute-done | bytes 65568 | tf_op jit(solution)/shard_map/ppermute | solution.py:188
  189.7 2.5 collective-permute-start.23
  192.2 3.6 %collective-permute-done.23 = bf16[1,512,64]{1,2,0:T(8,128)(2,1)S(1)} collective-permute-done((bf16[1,512,64]{1,2,0:T(8,128)(2,1)S(1)}, bf16[1,512,64]{1,2,0:T(8,128)(2,1)S(1)}, u32[]{:S(2)}, u32[]{:S(2)}) %collective-permute-start.23) | collective-permute-done | bytes 65568 | tf_op jit(solution)/shard_map/ppermute | solution.py:188
  195.8 3.6 %collective-permute-start.20 = (bf16[1,512,64]{1,2,0:T(8,128)(2,1)S(1)}, bf16[1,512,64]{1,2,0:T(8,128)(2,1)S(1)}, u32[]{:S(2)}, u32[]{:S(2)}) collective-permute-start(bf16[1,512,64]{1,2,0:T(8,128)(2,1)S(1)} %get-tuple-element.27), channel_id=1, source_target_pairs={{0,7},{1,0},{2,1},{3,2},{4,3},{5,4},{6,5},{7,6},{8,15},{9,8},{10,9... | collective-permute-start | bytes 196616 | tf_op jit(solution)/shard_map/ppermute | solution.py:188
  199.5 1.2 collective-permute-start.18
  200.7 2.4 collective-permute-start.17
  203.4 21.7 %all-to-all-done.2 = bf16[32,384,128]{2,1,0:T(8,128)(2,1)} async-done(((bf16[32,384,128]{2,1,0:T(8,128)(2,1)}), bf16[32,384,128]{2,1,0:T(8,128)(2,1)}, u32[]{:S(2)}, u32[]{:S(2)}) %all-to-all-start.2) | async-done | bytes 3145760 | tf_op jit(solution)/shard_map/all_to_all | solution.py:265
  225.2 5.2 %shard_map.106 = bf16[32,128,128]{2,1,0:T(8,128)(2,1)} custom-call(s32[96]{0:T(128)} %copy-done.11, f32[32,128,128]{2,1,0:T(8,128)} %get-tuple-element.18.acc_ref, bf16[96,128,128]{2,1,0:T(8,128)(2,1)} %bitcast.25.ret_ref), custom_call_target="tpu_custom_call" | custom-call | tf_op jit(solution)/shard_map/pallas_call | solution.py:171
  230.3 8.6 %all-to-all-start.3 = ((bf16[8,512,128]{2,1,0:T(8,128)(2,1)}), bf16[8,512,128]{2,1,0:T(8,128)(2,1)}, u32[]{:S(2)}, u32[]{:S(2)}) async-start(bf16[8,512,128]{2,1,0:T(8,128)(2,1)} %bitcast.77), calls=%async_computation.3 | async-start | bytes 2097152 | tf_op jit(solution)/shard_map/all_to_all | solution.py:273
  239.0 3.2 %collective-permute-start.16 = (bf16[1,512,64]{1,2,0:T(8,128)(2,1)}, bf16[1,512,64]{1,2,0:T(8,128)(2,1)S(1)}, u32[]{:S(2)}, u32[]{:S(2)}) collective-permute-start(bf16[1,512,64]{1,2,0:T(8,128)(2,1)} %get-tuple-element.31), channel_id=1, source_target_pairs={{0,3},{1,4},{2,5},{3,6},{4,7},{5,0},{6,1},{7,2},{8,11},{9,12},{10,... | collective-permute-start | bytes 196616 | tf_op jit(solution)/shard_map/ppermute | solution.py:188
  242.2 13.3 %collective-permute-done.16 = bf16[1,512,64]{1,2,0:T(8,128)(2,1)S(1)} collective-permute-done((bf16[1,512,64]{1,2,0:T(8,128)(2,1)}, bf16[1,512,64]{1,2,0:T(8,128)(2,1)S(1)}, u32[]{:S(2)}, u32[]{:S(2)}) %collective-permute-start.16) | collective-permute-done | bytes 65568 | tf_op jit(solution)/shard_map/ppermute | solution.py:188
  255.6 1.3 fusion.6
  256.8 2.3 convolution_bitcast_fusion
  260.2 1.1 fusion.13
  (107 shorter events, 7.5 us)
Async XLA Ops:
  0.6 16.6 %copy-start = (bf16[512,512]{1,0:T(8,128)(2,1)S(1)}, bf16[512,512]{1,0:T(8,128)(2,1)}, u32[]{:S(2)}) copy-start(bf16[512,512]{1,0:T(8,128)(2,1)} %param.12) | copy-start | bytes 1572868
  3.7 1.2 copy-start.2
  3.7 1.2 copy-start.15
  3.9 1.0 copy-start.10
  6.6 7.6 %copy-start.16 = (s32[1,32,3]{1,0,2:T(1,128)S(1)}, s32[1,32,3]{1,0,2:T(1,128)}, u32[]{:S(2)}) copy-start(s32[1,32,3]{1,0,2:T(1,128)} %param.16) | copy-start | bytes 1156
  6.6 21.8 %all-to-all-start = ((bf16[8,512,128]{2,1,0:T(8,128)(2,1)}), bf16[8,512,128]{2,1,0:T(8,128)(2,1)S(1)}, u32[]{:S(2)}, u32[]{:S(2)}) async-start(bf16[8,512,128]{2,1,0:T(8,128)(2,1)} %fusion.3), calls=%async_computation | async-start | bytes 2097152 | tf_op jit(solution)/shard_map/all_to_all | solution.py:229
  14.4 4.0 %copy-start.11 = (s32[96]{0:T(128)}, s32[96]{0:T(128)S(1)}, u32[]{:S(2)}) copy-start(s32[96]{0:T(128)S(1)} %reshape.88.ids_ref) | copy-start | bytes 1156
  14.5 2.7 %copy-start.6 = (bf16[512,512]{1,0:T(8,128)(2,1)S(1)}, bf16[512,512]{1,0:T(8,128)(2,1)}, u32[]{:S(2)}) copy-start(bf16[512,512]{1,0:T(8,128)(2,1)} %param.13) | copy-start | bytes 1572868
  28.4 2.7 %copy-start.1 = (bf16[8,512,128]{2,1,0:T(8,128)(2,1)}, bf16[8,512,128]{2,1,0:T(8,128)(2,1)S(1)}, u32[]{:S(2)}) copy-start(bf16[8,512,128]{2,1,0:T(8,128)(2,1)S(1)} %all-to-all-done) | copy-start | bytes 3145732
  31.2 10.7 %copy-start.17 = (s32[32,1]{0,1:T(1,128)S(1)}, s32[32,1]{0,1:T(1,128)}, u32[]{:S(2)}) copy-start(s32[32,1]{0,1:T(1,128)} %param.17) | copy-start | bytes 388
  31.2 10.9 %copy-start.13 = (s32[32,4]{0,1:T(4,128)S(1)}, s32[32,4]{0,1:T(4,128)}, u32[]{:S(2)}) copy-start(s32[32,4]{0,1:T(4,128)} %param.14) | copy-start | bytes 1540
  31.2 11.6 %copy-start.14 = (s32[32,4]{0,1:T(4,128)S(1)}, s32[32,4]{0,1:T(4,128)}, u32[]{:S(2)}) copy-start(s32[32,4]{0,1:T(4,128)} %param.15) | copy-start | bytes 1540
  31.2 81.8 %all-to-all-start.1 = ((bf16[32,384,128]{2,1,0:T(8,128)(2,1)}), bf16[32,384,128]{2,1,0:T(8,128)(2,1)}, u32[]{:S(2)}, u32[]{:S(2)}) async-start(bf16[32,384,128]{2,1,0:T(8,128)(2,1)} %bitcast.69), calls=%async_computation.1 | async-start | bytes 6291456 | tf_op jit(solution)/shard_map/all_to_all | solution.py:240
  43.0 1.3 copy-start.12
  43.0 2.3 copy-start.5
  43.0 3.7 %copy-start.4 = (bf16[8,512,64]{1,2,0:T(8,128)(2,1)S(1)}, bf16[8,512,64]{1,2,0:T(8,128)(2,1)}, u32[]{:S(2)}) copy-start(bf16[8,512,64]{1,2,0:T(8,128)(2,1)} %convert_bitcast_fusion) | copy-start | bytes 1572868
  45.3 2.8 %collective-permute-start.7 = (bf16[1,512,64]{1,2,0:T(8,128)(2,1)S(1)}, bf16[1,512,64]{1,2,0:T(8,128)(2,1)S(1)}, u32[]{:S(2)}, u32[]{:S(2)}) collective-permute-start(bf16[1,512,64]{1,2,0:T(8,128)(2,1)S(1)} %constant_dynamic-slice_fusion.20), channel_id=1, source_target_pairs={{0,1},{1,2},{2,3},{3,4},{4,5},{5,6},{6,7},{7,0},{8,9},{9,10},{10,1... | collective-permute-start | bytes 196616 | tf_op jit(solution)/shard_map/ppermute | solution.py:188
  46.7 1.9 collective-permute-start
  48.1 7.6 %collective-permute-start.8 = (bf16[1,512,64]{1,2,0:T(8,128)(2,1)S(1)}, bf16[1,512,64]{1,2,0:T(8,128)(2,1)S(1)}, u32[]{:S(2)}, u32[]{:S(2)}) collective-permute-start(bf16[1,512,64]{1,2,0:T(8,128)(2,1)S(1)} %get-tuple-element.39), channel_id=1, source_target_pairs={{0,2},{1,3},{2,4},{3,5},{4,6},{5,7},{6,0},{7,1},{8,10},{9,11},{10,... | collective-permute-start | bytes 196616 | tf_op jit(solution)/shard_map/ppermute | solution.py:188
  48.7 46.2 %collective-permute-start.6 = (bf16[1,512,64]{1,2,0:T(8,128)(2,1)S(1)}, bf16[1,512,64]{1,2,0:T(8,128)(2,1)}, u32[]{:S(2)}, u32[]{:S(2)}) collective-permute-start(bf16[1,512,64]{1,2,0:T(8,128)(2,1)S(1)} %get-tuple-element.41), channel_id=1, source_target_pairs={{0,7},{1,0},{2,1},{3,2},{4,3},{5,4},{6,5},{7,6},{8,15},{9,8},{10,9... | collective-permute-start | bytes 196616 | tf_op jit(solution)/shard_map/ppermute | solution.py:188
  52.2 41.8 %collective-permute-start.5 = (bf16[1,512,64]{1,2,0:T(8,128)(2,1)S(1)}, bf16[1,512,64]{1,2,0:T(8,128)(2,1)}, u32[]{:S(2)}, u32[]{:S(2)}) collective-permute-start(bf16[1,512,64]{1,2,0:T(8,128)(2,1)S(1)} %get-tuple-element.42), channel_id=1, source_target_pairs={{0,6},{1,7},{2,0},{3,1},{4,2},{5,3},{6,4},{7,5},{8,14},{9,15},{10,... | collective-permute-start | bytes 196616 | tf_op jit(solution)/shard_map/ppermute | solution.py:188
  54.6 38.6 %collective-permute-start.4 = (bf16[1,512,64]{1,2,0:T(8,128)(2,1)S(1)}, bf16[1,512,64]{1,2,0:T(8,128)(2,1)}, u32[]{:S(2)}, u32[]{:S(2)}) collective-permute-start(bf16[1,512,64]{1,2,0:T(8,128)(2,1)S(1)} %get-tuple-element.43), channel_id=1, source_target_pairs={{0,5},{1,6},{2,7},{3,0},{4,1},{5,2},{6,3},{7,4},{8,13},{9,14},{10,... | collective-permute-start | bytes 196616 | tf_op jit(solution)/shard_map/ppermute | solution.py:188
  54.6 37.7 %collective-permute-start.3 = (bf16[1,512,64]{1,2,0:T(8,128)(2,1)S(1)}, bf16[1,512,64]{1,2,0:T(8,128)(2,1)}, u32[]{:S(2)}, u32[]{:S(2)}) collective-permute-start(bf16[1,512,64]{1,2,0:T(8,128)(2,1)S(1)} %get-tuple-element.44), channel_id=1, source_target_pairs={{0,4},{1,5},{2,6},{3,7},{4,0},{5,1},{6,2},{7,3},{8,12},{9,13},{10,... | collective-permute-start | bytes 196616 | tf_op jit(solution)/shard_map/ppermute | solution.py:188
  55.7 6.1 %collective-permute-start.9 = (bf16[1,512,64]{1,2,0:T(8,128)(2,1)S(1)}, bf16[1,512,64]{1,2,0:T(8,128)(2,1)S(1)}, u32[]{:S(2)}, u32[]{:S(2)}) collective-permute-start(bf16[1,512,64]{1,2,0:T(8,128)(2,1)S(1)} %get-tuple-element.38), channel_id=1, source_target_pairs={{0,3},{1,4},{2,5},{3,6},{4,7},{5,0},{6,1},{7,2},{8,11},{9,12},{10,... | collective-permute-start | bytes 196616 | tf_op jit(solution)/shard_map/ppermute | solution.py:188
  61.8 5.0 %collective-permute-start.10 = (bf16[1,512,64]{1,2,0:T(8,128)(2,1)S(1)}, bf16[1,512,64]{1,2,0:T(8,128)(2,1)S(1)}, u32[]{:S(2)}, u32[]{:S(2)}) collective-permute-start(bf16[1,512,64]{1,2,0:T(8,128)(2,1)S(1)} %get-tuple-element.37), channel_id=1, source_target_pairs={{0,4},{1,5},{2,6},{3,7},{4,0},{5,1},{6,2},{7,3},{8,12},{9,13},{10,... | collective-permute-start | bytes 196616 | tf_op jit(solution)/shard_map/ppermute | solution.py:188
  66.8 5.6 %collective-permute-start.11 = (bf16[1,512,64]{1,2,0:T(8,128)(2,1)S(1)}, bf16[1,512,64]{1,2,0:T(8,128)(2,1)S(1)}, u32[]{:S(2)}, u32[]{:S(2)}) collective-permute-start(bf16[1,512,64]{1,2,0:T(8,128)(2,1)S(1)} %get-tuple-element.36), channel_id=1, source_target_pairs={{0,5},{1,6},{2,7},{3,0},{4,1},{5,2},{6,3},{7,4},{8,13},{9,14},{10,... | collective-permute-start | bytes 196616 | tf_op jit(solution)/shard_map/ppermute | solution.py:188
  72.4 3.8 %collective-permute-start.12 = (bf16[1,512,64]{1,2,0:T(8,128)(2,1)S(1)}, bf16[1,512,64]{1,2,0:T(8,128)(2,1)S(1)}, u32[]{:S(2)}, u32[]{:S(2)}) collective-permute-start(bf16[1,512,64]{1,2,0:T(8,128)(2,1)S(1)} %get-tuple-element.35), channel_id=1, source_target_pairs={{0,6},{1,7},{2,0},{3,1},{4,2},{5,3},{6,4},{7,5},{8,14},{9,15},{10,... | collective-permute-start | bytes 196616 | tf_op jit(solution)/shard_map/ppermute | solution.py:188
  76.2 4.1 %collective-permute-start.13 = (bf16[1,512,64]{1,2,0:T(8,128)(2,1)S(1)}, bf16[1,512,64]{1,2,0:T(8,128)(2,1)S(1)}, u32[]{:S(2)}, u32[]{:S(2)}) collective-permute-start(bf16[1,512,64]{1,2,0:T(8,128)(2,1)S(1)} %get-tuple-element.34), channel_id=1, source_target_pairs={{0,7},{1,0},{2,1},{3,2},{4,3},{5,4},{6,5},{7,6},{8,15},{9,8},{10,9... | collective-permute-start | bytes 196616 | tf_op jit(solution)/shard_map/ppermute | solution.py:188
  80.3 6.0 %collective-permute-start.1 = (bf16[1,512,64]{1,2,0:T(8,128)(2,1)S(1)}, bf16[1,512,64]{1,2,0:T(8,128)(2,1)}, u32[]{:S(2)}, u32[]{:S(2)}) collective-permute-start(bf16[1,512,64]{1,2,0:T(8,128)(2,1)S(1)} %get-tuple-element.46), channel_id=1, source_target_pairs={{0,2},{1,3},{2,4},{3,5},{4,6},{5,7},{6,0},{7,1},{8,10},{9,11},{10,... | collective-permute-start | bytes 196616 | tf_op jit(solution)/shard_map/ppermute | solution.py:188
  86.3 6.0 %collective-permute-start.2 = (bf16[1,512,64]{1,2,0:T(8,128)(2,1)S(1)}, bf16[1,512,64]{1,2,0:T(8,128)(2,1)S(1)}, u32[]{:S(2)}, u32[]{:S(2)}) collective-permute-start(bf16[1,512,64]{1,2,0:T(8,128)(2,1)S(1)} %get-tuple-element.45), channel_id=1, source_target_pairs={{0,3},{1,4},{2,5},{3,6},{4,7},{5,0},{6,1},{7,2},{8,11},{9,12},{10,... | collective-permute-start | bytes 196616 | tf_op jit(solution)/shard_map/ppermute | solution.py:188
  145.2 80.0 %all-to-all-start.2 = ((bf16[32,384,128]{2,1,0:T(8,128)(2,1)}), bf16[32,384,128]{2,1,0:T(8,128)(2,1)}, u32[]{:S(2)}, u32[]{:S(2)}) async-start(bf16[32,384,128]{2,1,0:T(8,128)(2,1)} %bitcast.79), calls=%async_computation.2 | async-start | bytes 6291456 | tf_op jit(solution)/shard_map/all_to_all | solution.py:265
  173.0 30.1 %collective-permute-start.27 = (bf16[1,512,64]{1,2,0:T(8,128)(2,1)S(1)}, bf16[1,512,64]{1,2,0:T(8,128)(2,1)S(1)}, u32[]{:S(2)}, u32[]{:S(2)}) collective-permute-start(bf16[1,512,64]{1,2,0:T(8,128)(2,1)S(1)} %get-tuple-element.20), channel_id=1, source_target_pairs={{0,7},{1,0},{2,1},{3,2},{4,3},{5,4},{6,5},{7,6},{8,15},{9,8},{10,9... | collective-permute-start | bytes 196616 | tf_op jit(solution)/shard_map/ppermute | solution.py:188
  174.3 26.4 %collective-permute-start.26 = (bf16[1,512,64]{1,2,0:T(8,128)(2,1)S(1)}, bf16[1,512,64]{1,2,0:T(8,128)(2,1)S(1)}, u32[]{:S(2)}, u32[]{:S(2)}) collective-permute-start(bf16[1,512,64]{1,2,0:T(8,128)(2,1)S(1)} %get-tuple-element.21), channel_id=1, source_target_pairs={{0,6},{1,7},{2,0},{3,1},{4,2},{5,3},{6,4},{7,5},{8,14},{9,15},{10,... | collective-permute-start | bytes 196616 | tf_op jit(solution)/shard_map/ppermute | solution.py:188
  175.2 24.3 %collective-permute-start.25 = (bf16[1,512,64]{1,2,0:T(8,128)(2,1)S(1)}, bf16[1,512,64]{1,2,0:T(8,128)(2,1)S(1)}, u32[]{:S(2)}, u32[]{:S(2)}) collective-permute-start(bf16[1,512,64]{1,2,0:T(8,128)(2,1)S(1)} %get-tuple-element.22), channel_id=1, source_target_pairs={{0,5},{1,6},{2,7},{3,0},{4,1},{5,2},{6,3},{7,4},{8,13},{9,14},{10,... | collective-permute-start | bytes 196616 | tf_op jit(solution)/shard_map/ppermute | solution.py:188
  175.9 23.4 %collective-permute-start.24 = (bf16[1,512,64]{1,2,0:T(8,128)(2,1)S(1)}, bf16[1,512,64]{1,2,0:T(8,128)(2,1)S(1)}, u32[]{:S(2)}, u32[]{:S(2)}) collective-permute-start(bf16[1,512,64]{1,2,0:T(8,128)(2,1)S(1)} %get-tuple-element.23), channel_id=1, source_target_pairs={{0,4},{1,5},{2,6},{3,7},{4,0},{5,1},{6,2},{7,3},{8,12},{9,13},{10,... | collective-permute-start | bytes 196616 | tf_op jit(solution)/shard_map/ppermute | solution.py:188
  177.8 3.1 %collective-permute-start.21 = (bf16[1,512,64]{1,2,0:T(8,128)(2,1)S(1)}, bf16[1,512,64]{1,2,0:T(8,128)(2,1)S(1)}, u32[]{:S(2)}, u32[]{:S(2)}) collective-permute-start(bf16[1,512,64]{1,2,0:T(8,128)(2,1)S(1)} %get-tuple-element.26), channel_id=1, source_target_pairs={{0,1},{1,2},{2,3},{3,4},{4,5},{5,6},{6,7},{7,0},{8,9},{9,10},{10,1... | collective-permute-start | bytes 196616 | tf_op jit(solution)/shard_map/ppermute | solution.py:188
  180.9 3.8 %collective-permute-start.14 = (bf16[1,512,64]{1,2,0:T(8,128)(2,1)S(1)}, bf16[1,512,64]{1,2,0:T(8,128)(2,1)S(1)}, u32[]{:S(2)}, u32[]{:S(2)}) collective-permute-start(bf16[1,512,64]{1,2,0:T(8,128)(2,1)S(1)} %get-tuple-element.33), channel_id=1, source_target_pairs={{0,1},{1,2},{2,3},{3,4},{4,5},{5,6},{6,7},{7,0},{8,9},{9,10},{10,1... | collective-permute-start | bytes 196616 | tf_op jit(solution)/shard_map/ppermute | solution.py:188
  184.8 5.0 %collective-permute-start.22 = (bf16[1,512,64]{1,2,0:T(8,128)(2,1)S(1)}, bf16[1,512,64]{1,2,0:T(8,128)(2,1)S(1)}, u32[]{:S(2)}, u32[]{:S(2)}) collective-permute-start(bf16[1,512,64]{1,2,0:T(8,128)(2,1)S(1)} %get-tuple-element.25), channel_id=1, source_target_pairs={{0,2},{1,3},{2,4},{3,5},{4,6},{5,7},{6,0},{7,1},{8,10},{9,11},{10,... | collective-permute-start | bytes 196616 | tf_op jit(solution)/shard_map/ppermute | solution.py:188
  189.7 6.0 %collective-permute-start.23 = (bf16[1,512,64]{1,2,0:T(8,128)(2,1)S(1)}, bf16[1,512,64]{1,2,0:T(8,128)(2,1)S(1)}, u32[]{:S(2)}, u32[]{:S(2)}) collective-permute-start(bf16[1,512,64]{1,2,0:T(8,128)(2,1)S(1)} %get-tuple-element.24), channel_id=1, source_target_pairs={{0,3},{1,4},{2,5},{3,6},{4,7},{5,0},{6,1},{7,2},{8,11},{9,12},{10,... | collective-permute-start | bytes 196616 | tf_op jit(solution)/shard_map/ppermute | solution.py:188
  195.8 59.8 %collective-permute-start.20 = (bf16[1,512,64]{1,2,0:T(8,128)(2,1)S(1)}, bf16[1,512,64]{1,2,0:T(8,128)(2,1)S(1)}, u32[]{:S(2)}, u32[]{:S(2)}) collective-permute-start(bf16[1,512,64]{1,2,0:T(8,128)(2,1)S(1)} %get-tuple-element.27), channel_id=1, source_target_pairs={{0,7},{1,0},{2,1},{3,2},{4,3},{5,4},{6,5},{7,6},{8,15},{9,8},{10,9... | collective-permute-start | bytes 196616 | tf_op jit(solution)/shard_map/ppermute | solution.py:188
  199.4 56.1 %collective-permute-start.19 = (bf16[1,512,64]{1,2,0:T(8,128)(2,1)}, bf16[1,512,64]{1,2,0:T(8,128)(2,1)S(1)}, u32[]{:S(2)}, u32[]{:S(2)}) collective-permute-start(bf16[1,512,64]{1,2,0:T(8,128)(2,1)} %get-tuple-element.28), channel_id=1, source_target_pairs={{0,6},{1,7},{2,0},{3,1},{4,2},{5,3},{6,4},{7,5},{8,14},{9,15},{10,... | collective-permute-start | bytes 196616 | tf_op jit(solution)/shard_map/ppermute | solution.py:188
  199.5 56.0 %collective-permute-start.18 = (bf16[1,512,64]{1,2,0:T(8,128)(2,1)}, bf16[1,512,64]{1,2,0:T(8,128)(2,1)S(1)}, u32[]{:S(2)}, u32[]{:S(2)}) collective-permute-start(bf16[1,512,64]{1,2,0:T(8,128)(2,1)} %get-tuple-element.29), channel_id=1, source_target_pairs={{0,5},{1,6},{2,7},{3,0},{4,1},{5,2},{6,3},{7,4},{8,13},{9,14},{10,... | collective-permute-start | bytes 196616 | tf_op jit(solution)/shard_map/ppermute | solution.py:188
  200.7 54.7 %collective-permute-start.17 = (bf16[1,512,64]{1,2,0:T(8,128)(2,1)}, bf16[1,512,64]{1,2,0:T(8,128)(2,1)S(1)}, u32[]{:S(2)}, u32[]{:S(2)}) collective-permute-start(bf16[1,512,64]{1,2,0:T(8,128)(2,1)} %get-tuple-element.30), channel_id=1, source_target_pairs={{0,4},{1,5},{2,6},{3,7},{4,0},{5,1},{6,2},{7,3},{8,12},{9,13},{10,... | collective-permute-start | bytes 196616 | tf_op jit(solution)/shard_map/ppermute | solution.py:188
  203.1 35.9 %collective-permute-start.15 = (bf16[1,512,64]{1,2,0:T(8,128)(2,1)}, bf16[1,512,64]{1,2,0:T(8,128)(2,1)S(1)}, u32[]{:S(2)}, u32[]{:S(2)}) collective-permute-start(bf16[1,512,64]{1,2,0:T(8,128)(2,1)} %get-tuple-element.32), channel_id=1, source_target_pairs={{0,2},{1,3},{2,4},{3,5},{4,6},{5,7},{6,0},{7,1},{8,10},{9,11},{10,... | collective-permute-start | bytes 196616 | tf_op jit(solution)/shard_map/ppermute | solution.py:188
  203.4 21.8 %copy-start.8 = (bf16[8,512,64]{1,2,0:T(8,128)(2,1)}, bf16[8,512,64]{1,2,0:T(8,128)(2,1)S(1)}, u32[]{:S(2)}) copy-start(bf16[8,512,64]{1,2,0:T(8,128)(2,1)S(1)} %constant_dynamic-update-slice_fusion) | copy-start | bytes 1572868
  230.3 25.2 %copy-start.3 = (bf16[512,512]{1,0:T(8,128)(2,1)S(1)}, bf16[512,512]{1,0:T(8,128)(2,1)}, u32[]{:S(2)}) copy-start(bf16[512,512]{1,0:T(8,128)(2,1)} %param.9) | copy-start | bytes 1572868
  230.3 26.5 %all-to-all-start.3 = ((bf16[8,512,128]{2,1,0:T(8,128)(2,1)}), bf16[8,512,128]{2,1,0:T(8,128)(2,1)}, u32[]{:S(2)}, u32[]{:S(2)}) async-start(bf16[8,512,128]{2,1,0:T(8,128)(2,1)} %bitcast.77), calls=%async_computation.3 | async-start | bytes 2097152 | tf_op jit(solution)/shard_map/all_to_all | solution.py:273
  239.0 16.4 %collective-permute-start.16 = (bf16[1,512,64]{1,2,0:T(8,128)(2,1)}, bf16[1,512,64]{1,2,0:T(8,128)(2,1)S(1)}, u32[]{:S(2)}, u32[]{:S(2)}) collective-permute-start(bf16[1,512,64]{1,2,0:T(8,128)(2,1)} %get-tuple-element.31), channel_id=1, source_target_pairs={{0,3},{1,4},{2,5},{3,6},{4,7},{5,0},{6,1},{7,2},{8,11},{9,12},{10,... | collective-permute-start | bytes 196616 | tf_op jit(solution)/shard_map/ppermute | solution.py:188
  256.8 2.3 copy-start.9
  259.1 1.0 copy-start.7

commit v9 on v7

--- a/solution.py
+++ b/solution.py
@@ -76,7 +76,7 @@
             slot_acc[ids_r[i]] = slot_acc[ids_r[i]] + part
         return carry
 
-    lax.fori_loop(0, nq, body, 0, unroll=4)
+    lax.fori_loop(0, nq, body, 0, unroll=8)
     slot_ref[...] = slot_acc[...].astype(bf16)
 
 
@@ -233,9 +233,13 @@
     inv = lax.rsqrt(jnp.mean(xf * xf, axis=1, keepdims=True) + EPS)
     normed = xf * inv
     hidden = (normed * norm_gain).astype(bf16)
-    w_split = w_qkv.reshape(width, 3, nhead, hwide).transpose(2, 0, 1, 3)
-    w_q = w_split[:, :, 0]
-    w_kv = w_split[:, :, 1:].reshape(nhead, width, 2 * hwide)
+    w_q = w_qkv[:, :width].reshape(width, nhead, hwide).transpose(1, 0, 2)
+    w_kv = (
+        w_qkv[:, width:]
+        .reshape(width, 2, nhead, hwide)
+        .transpose(2, 0, 1, 3)
+        .reshape(nhead, width, 2 * hwide)
+    )
     w_out_heads = w_out.reshape(nhead, hwide, width)
     kv_own = jnp.einsum("rd,hdc->hrc", hidden, w_kv, preferred_element_type=f32).astype(bf16)
     kv = lax.all_to_all(kv_own, "head", split_axis=0, concat_axis=0, tiled=True).reshape(

time: 261 us -> 258 us (0.989)
  waiting for transfers between devices: 98.3 us -> 105 us
  local copies, waits for them, and re-layouts: 21 us -> 15.3 us
  starting transfers between devices: 74.7 us -> 71.5 us
    ppermute x28, waiting for transfers between devices: 50.4 us -> 20 us  [head_exchange(): got = lax.ppermute(part, axis, perm)]
    all_to_all x1, waiting for transfers between devices: 15.8 us -> 40.7 us  [local(): lax.all_to_all(outgoing.reshape(ndom, pair_slots * bsize, 2 * hwide), 'do...]
    all_to_all x1, waiting for transfers between devices: 22.1 us -> 32.9 us  [local(): lax.all_to_all(slot_grads.reshape(ndom, pair_slots * 2 * hwide, bsize), '...]
    dynamic_update_slice x28, local copies, waits for them, and re-layouts: 7.05 us -> 2.88 us  [head_exchange(): out = lax.dynamic_update_index_in_dim(out, got, (me + n - k) % n, 0)]
    ppermute x28, starting transfers between devices: 40.4 us -> 36.8 us  [head_exchange(): got = lax.ppermute(part, axis, perm)]
  transfers between devices with their start and end apart: 32 -> 32, of which waited for: 17 -> 9; matrix products, arithmetic and copies ran while one was open for 8% -> 6% of each run, Pallas kernels for 8% -> 8%
where the time goes in v9:
time: 258 us
  waiting for transfers between devices  105 us (41%)
  starting transfers between devices  71.5 us (28%)
  Pallas kernels  52.8 us (20%)
  local copies, waits for them, and re-layouts  15.3 us (6%)
  matrix products  8.82 us (3%)
  other arithmetic  2.64 us (1%)
    all_to_all x1, waiting for transfers between devices, local(): lax.all_to_all(outgoing.reshape(ndom, pair_slots * bsize, 2 * hwide), 'do...  40.7 us
    ppermute x28, starting transfers between devices, head_exchange(): got = lax.ppermute(part, axis, perm)  36.8 us
    all_to_all x1, waiting for transfers between devices, local(): lax.all_to_all(slot_grads.reshape(ndom, pair_slots * 2 * hwide, bsize), '...  32.9 us
    pallas_call x1, Pallas kernels, fused_attention(): pl.pallas_call(lambda *refs: remote_kernel(*refs, near=near, far=far, bsi...  32.1 us
    ppermute x28, waiting for transfers between devices, head_exchange(): got = lax.ppermute(part, axis, perm)  20 us
    pallas_call x1, Pallas kernels, fused_attention(): pl.pallas_call(lambda *refs: local_kernel(*refs, near=near, bsize=bsize,...  15.6 us
    all_to_all x1, waiting for transfers between devices, local(): lax.all_to_all(kv_own, 'head', split_axis=0, concat_axis=0, tiled=True)  11.5 us
    all_to_all x1, starting transfers between devices, local(): lax.all_to_all(outgoing.reshape(ndom, pair_slots * bsize, 2 * hwide), 'do...  10.6 us
  transfers between devices with their start and end apart: 32, of which 9 were waited for; matrix products, arithmetic and copies ran while one was open for 6% of the time, Pallas kernels for 8%

profile of v9, /device:TPU:1, one launch (start us, length us, event | category | flops | bytes accessed | tf_op | source)
XLA Modules:
  0.0 257.7 jit_solution(16425128378813650162)
XLA Ops:
  0.7 1.3 fusion.14
  2.0 0.2 slice-done
  2.2 0.5 copy.70
  2.8 1.0 copy-done.5
  3.8 1.8 fusion.3
  5.6 6.7 %all-to-all-start = ((bf16[8,512,128]{2,1,0:T(8,128)(2,1)}), bf16[8,512,128]{2,1,0:T(8,128)(2,1)S(1)}, u32[]{:S(2)}, u32[]{:S(2)}) async-start(bf16[8,512,128]{2,1,0:T(8,128)(2,1)} %fusion.3), calls=%async_computation | async-start | bytes 2097152 | tf_op jit(solution)/shard_map/all_to_all | solution.py:245
  12.3 0.1 reshape.92.ids_ref
  12.5 1.6 fusion.17
  14.2 1.5 fusion.7
  15.7 11.5 %all-to-all-done = bf16[8,512,128]{2,1,0:T(8,128)(2,1)S(1)} async-done(((bf16[8,512,128]{2,1,0:T(8,128)(2,1)}), bf16[8,512,128]{2,1,0:T(8,128)(2,1)S(1)}, u32[]{:S(2)}, u32[]{:S(2)}) %all-to-all-start) | async-done | bytes 1048608 | tf_op jit(solution)/shard_map/all_to_all | solution.py:245
  27.2 2.7 %gather_fusion = bf16[96,128,128]{2,1,0:T(8,128)(2,1)} fusion(bf16[32,128,128]{2,1,0:T(8,128)(2,1)S(1)} %bitcast.64, s32[1024]{0:T(1024)S(1)} %pad_clamp_fusion.1), kind=kCustom, calls=%fused_computation | custom fusion | bytes 6291840 | tf_op jit(solution)/shard_map/jit(_take)/gather | solution.py:252
  30.0 10.6 %all-to-all-start.1 = ((bf16[32,384,128]{2,1,0:T(8,128)(2,1)}), bf16[32,384,128]{2,1,0:T(8,128)(2,1)}, u32[]{:S(2)}, u32[]{:S(2)}) async-start(bf16[32,384,128]{2,1,0:T(8,128)(2,1)} %bitcast.67), calls=%async_computation.1 | async-start | bytes 6291456 | tf_op jit(solution)/shard_map/all_to_all | solution.py:256
  40.7 0.1 reshape.74.refs_1_
  40.9 0.1 lt.237
  41.1 1.2 gather_fusion.1
  42.6 0.7 copy.73
  43.4 0.6 reshape.73.refs_0_
  44.0 1.4 collective-permute-start.7
  45.5 1.3 collective-permute-done.7
  46.9 4.4 %collective-permute-start.9 = (bf16[1,512,64]{1,2,0:T(8,128)(2,1)S(1)}, bf16[1,512,64]{1,2,0:T(8,128)(2,1)S(1)}, u32[]{:S(2)}, u32[]{:S(2)}) collective-permute-start(bf16[1,512,64]{1,2,0:T(8,128)(2,1)S(1)} %get-tuple-element.38), channel_id=1, source_target_pairs={{0,3},{1,4},{2,5},{3,6},{4,7},{5,0},{6,1},{7,2},{8,11},{9,12},{10,... | collective-permute-start | bytes 196616 | tf_op jit(solution)/shard_map/ppermute | solution.py:200
  51.3 1.9 collective-permute-start.10
  53.3 2.9 %collective-permute-start.12 = (bf16[1,512,64]{1,2,0:T(8,128)(2,1)S(1)}, bf16[1,512,64]{1,2,0:T(8,128)(2,1)S(1)}, u32[]{:S(2)}, u32[]{:S(2)}) collective-permute-start(bf16[1,512,64]{1,2,0:T(8,128)(2,1)S(1)} %get-tuple-element.35), channel_id=1, source_target_pairs={{0,6},{1,7},{2,0},{3,1},{4,2},{5,3},{6,4},{7,5},{8,14},{9,15},{10,... | collective-permute-start | bytes 196616 | tf_op jit(solution)/shard_map/ppermute | solution.py:200
  56.2 1.5 collective-permute-start.13
  57.7 0.4 collective-permute-done.9
  58.1 2.0 collective-permute-start.2
  60.1 1.4 collective-permute-start.3
  61.5 1.1 collective-permute-start.4
  62.6 1.6 collective-permute-start.5
  64.2 1.3 copy.44
  65.6 1.6 collective-permute-start.6
  67.3 0.4 collective-permute-done.5
  67.7 2.0 collective-permute-done.6
  69.7 1.3 copy.43
  71.0 40.7 %all-to-all-done.1 = bf16[32,384,128]{2,1,0:T(8,128)(2,1)} async-done(((bf16[32,384,128]{2,1,0:T(8,128)(2,1)}), bf16[32,384,128]{2,1,0:T(8,128)(2,1)}, u32[]{:S(2)}, u32[]{:S(2)}) %all-to-all-start.1) | async-done | bytes 3145760 | tf_op jit(solution)/shard_map/all_to_all | solution.py:256
  111.7 32.1 %shard_map.104 = (bf16[32,128,64]{2,1,0:T(8,128)(2,1)}, f32[32,128,64]{2,1,0:T(8,128)}, f32[32,3,128]{2,1,0:T(4,128)}, bf16[96,128,128]{2,1,0:T(8,128)(2,1)}) custom-call(s32[128]{0:T(128)} %reshape.73.refs_0_, s32[128]{0:T(128)} %copy-done.9, bf16[32,128,64]{2,1,0:T(8,128)(2,1)} %bitcast.70, bf16[32,128,128]{2,1,0:T(8,128)(2,1)} %bitcast.65, ...), custom_call_target="tpu_custom_call" | custom-call | tf_op jit(solution)/shard_map/pallas_call | solution.py:134
  143.8 8.9 %all-to-all-start.2 = ((bf16[32,384,128]{2,1,0:T(8,128)(2,1)}), bf16[32,384,128]{2,1,0:T(8,128)(2,1)}, u32[]{:S(2)}, u32[]{:S(2)}) async-start(bf16[32,384,128]{2,1,0:T(8,128)(2,1)} %bitcast.75), calls=%async_computation.2 | async-start | bytes 6291456 | tf_op jit(solution)/shard_map/all_to_all | solution.py:281
  152.8 1.0 copy.42
  153.8 15.6 %shard_map.105 = (bf16[32,128,64]{2,1,0:T(8,128)(2,1)}, f32[32,128,128]{2,1,0:T(8,128)}) custom-call(s32[128]{0:T(128)} %reshape.73.refs_0_, bf16[32,128,64]{2,1,0:T(8,128)(2,1)} %bitcast.71, bf16[32,128,128]{2,1,0:T(8,128)(2,1)} %bitcast.66, bf16[32,128,64]{2,1,0:T(8,128)(2,1)} %bitcast.69, f32[32,3,128]{2,1,0:T(4,128)} %get-tuple-element.15.refs_4_, ...), custom_call_target="tpu_custom_call" | custom-call | tf_op jit(solution)/shard_map/pallas_call | solution.py:149
  169.4 1.5 copy.54
  170.9 0.8 constant_dynamic-slice_fusion
  171.7 1.5 collective-permute-start.21
  173.2 0.3 collective-permute-start.22
  173.6 1.7 collective-permute-start.23
  175.3 1.5 collective-permute-start.24
  176.8 2.6 %collective-permute-start.25 = (bf16[1,512,64]{1,2,0:T(8,128)(2,1)}, bf16[1,512,64]{1,2,0:T(8,128)(2,1)S(1)}, u32[]{:S(2)}, u32[]{:S(2)}) collective-permute-start(bf16[1,512,64]{1,2,0:T(8,128)(2,1)} %get-tuple-element.22), channel_id=1, source_target_pairs={{0,5},{1,6},{2,7},{3,0},{4,1},{5,2},{6,3},{7,4},{8,13},{9,14},{10,... | collective-permute-start | bytes 196616 | tf_op jit(solution)/shard_map/ppermute | solution.py:200
  179.4 0.3 copy.46
  179.8 0.7 constant_dynamic-slice_fusion.7
  180.5 0.3 collective-permute-start.14
  180.8 1.3 collective-permute-done.14
  182.2 1.5 collective-permute-start.26
  183.7 1.0 collective-permute-start.27
  184.7 1.8 collective-permute-start.15
  186.5 0.7 collective-permute-start.16
  187.3 2.6 %collective-permute-start.17 = (bf16[1,512,64]{1,2,0:T(8,128)(2,1)}, bf16[1,512,64]{1,2,0:T(8,128)(2,1)S(1)}, u32[]{:S(2)}, u32[]{:S(2)}) collective-permute-start(bf16[1,512,64]{1,2,0:T(8,128)(2,1)} %get-tuple-element.30), channel_id=1, source_target_pairs={{0,4},{1,5},{2,6},{3,7},{4,0},{5,1},{6,2},{7,3},{8,12},{9,13},{10,... | collective-permute-start | bytes 196616 | tf_op jit(solution)/shard_map/ppermute | solution.py:200
  190.0 1.0 collective-permute-start.19
  191.1 32.9 %all-to-all-done.2 = bf16[32,384,128]{2,1,0:T(8,128)(2,1)} async-done(((bf16[32,384,128]{2,1,0:T(8,128)(2,1)}), bf16[32,384,128]{2,1,0:T(8,128)(2,1)}, u32[]{:S(2)}, u32[]{:S(2)}) %all-to-all-start.2) | async-done | bytes 3145760 | tf_op jit(solution)/shard_map/all_to_all | solution.py:281
  224.0 5.1 %shard_map.106 = bf16[32,128,128]{2,1,0:T(8,128)(2,1)} custom-call(s32[96]{0:T(128)} %copy-done.8, f32[32,128,128]{2,1,0:T(8,128)} %get-tuple-element.18.acc_ref, bf16[96,128,128]{2,1,0:T(8,128)(2,1)} %bitcast.26.ret_ref), custom_call_target="tpu_custom_call" | custom-call | tf_op jit(solution)/shard_map/pallas_call | solution.py:183
  229.1 8.6 %all-to-all-start.3 = ((bf16[8,512,128]{2,1,0:T(8,128)(2,1)}), bf16[8,512,128]{2,1,0:T(8,128)(2,1)}, u32[]{:S(2)}, u32[]{:S(2)}) async-start(bf16[8,512,128]{2,1,0:T(8,128)(2,1)} %bitcast.72), calls=%async_computation.3 | async-start | bytes 2097152 | tf_op jit(solution)/shard_map/all_to_all | solution.py:289
  237.7 0.2 collective-permute-start.20
  238.0 14.6 %collective-permute-done.20 = bf16[1,512,64]{1,2,0:T(8,128)(2,1)S(1)} collective-permute-done((bf16[1,512,64]{1,2,0:T(8,128)(2,1)S(1)}, bf16[1,512,64]{1,2,0:T(8,128)(2,1)S(1)}, u32[]{:S(2)}, u32[]{:S(2)}) %collective-permute-start.20) | collective-permute-done | bytes 65568 | tf_op jit(solution)/shard_map/ppermute | solution.py:200
  252.6 1.3 fusion.6
  253.9 2.0 convolution_bitcast_fusion
  255.9 0.6 fusion.9
  256.5 1.1 fusion.13
  (104 shorter events, 1.4 us)
Async XLA Ops:
  0.6 13.5 %copy-start = (bf16[512,512]{1,0:T(8,128)(2,1)S(1)}, bf16[512,512]{1,0:T(8,128)(2,1)}, u32[]{:S(2)}) copy-start(bf16[512,512]{1,0:T(8,128)(2,1)} %param.12) | copy-start | bytes 1572868
  0.6 1.5 slice-start
  2.0 1.8 copy-start.2
  2.0 1.8 copy-start.12
  2.7 9.5 %copy-start.13 = (s32[1,32,3]{1,0,2:T(1,128)S(1)}, s32[1,32,3]{1,0,2:T(1,128)}, u32[]{:S(2)}) copy-start(s32[1,32,3]{1,0,2:T(1,128)} %param.16) | copy-start | bytes 1156
  2.8 1.0 copy-start.5
  5.6 21.7 %all-to-all-start = ((bf16[8,512,128]{2,1,0:T(8,128)(2,1)}), bf16[8,512,128]{2,1,0:T(8,128)(2,1)S(1)}, u32[]{:S(2)}, u32[]{:S(2)}) async-start(bf16[8,512,128]{2,1,0:T(8,128)(2,1)} %fusion.3), calls=%async_computation | async-start | bytes 2097152 | tf_op jit(solution)/shard_map/all_to_all | solution.py:245
  12.4 17.5 %copy-start.8 = (s32[96]{0:T(128)}, s32[96]{0:T(128)S(1)}, u32[]{:S(2)}) copy-start(s32[96]{0:T(128)S(1)} %reshape.92.ids_ref) | copy-start | bytes 1156
  27.2 2.7 %copy-start.1 = (bf16[8,512,128]{2,1,0:T(8,128)(2,1)}, bf16[8,512,128]{2,1,0:T(8,128)(2,1)S(1)}, u32[]{:S(2)}) copy-start(bf16[8,512,128]{2,1,0:T(8,128)(2,1)S(1)} %all-to-all-done) | copy-start | bytes 3145732
  30.0 10.7 %copy-start.10 = (s32[32,4]{0,1:T(4,128)S(1)}, s32[32,4]{0,1:T(4,128)}, u32[]{:S(2)}) copy-start(s32[32,4]{0,1:T(4,128)} %param.15) | copy-start | bytes 1540
  30.0 10.9 %copy-start.14 = (s32[32,1]{0,1:T(1,128)S(1)}, s32[32,1]{0,1:T(1,128)}, u32[]{:S(2)}) copy-start(s32[32,1]{0,1:T(1,128)} %param.17) | copy-start | bytes 388
  30.0 81.8 %all-to-all-start.1 = ((bf16[32,384,128]{2,1,0:T(8,128)(2,1)}), bf16[32,384,128]{2,1,0:T(8,128)(2,1)}, u32[]{:S(2)}, u32[]{:S(2)}) async-start(bf16[32,384,128]{2,1,0:T(8,128)(2,1)} %bitcast.67), calls=%async_computation.1 | async-start | bytes 6291456 | tf_op jit(solution)/shard_map/all_to_all | solution.py:256
  40.5 2.8 %copy-start.11 = (s32[32,4]{0,1:T(4,128)S(1)}, s32[32,4]{0,1:T(4,128)}, u32[]{:S(2)}) copy-start(s32[32,4]{0,1:T(4,128)} %param.14) | copy-start | bytes 1540
  40.8 15.3 %copy-start.9 = (s32[128]{0:T(128)}, s32[128]{0:T(128)S(1)}, u32[]{:S(2)}) copy-start(s32[128]{0:T(128)S(1)} %reshape.74.refs_1_) | copy-start | bytes 1540
  44.0 2.8 %collective-permute-start.7 = (bf16[1,512,64]{1,2,0:T(8,128)(2,1)S(1)}, bf16[1,512,64]{1,2,0:T(8,128)(2,1)S(1)}, u32[]{:S(2)}, u32[]{:S(2)}) collective-permute-start(bf16[1,512,64]{1,2,0:T(8,128)(2,1)S(1)} %constant_dynamic-slice_fusion.20), channel_id=1, source_target_pairs={{0,1},{1,2},{2,3},{3,4},{4,5},{5,6},{6,7},{7,0},{8,9},{9,10},{10,1... | collective-permute-start | bytes 196616 | tf_op jit(solution)/shard_map/ppermute | solution.py:200
  45.5 7.8 %collective-permute-start = (bf16[1,512,64]{1,2,0:T(8,128)(2,1)S(1)}, bf16[1,512,64]{1,2,0:T(8,128)(2,1)S(1)}, u32[]{:S(2)}, u32[]{:S(2)}) collective-permute-start(bf16[1,512,64]{1,2,0:T(8,128)(2,1)S(1)} %constant_dynamic-slice_fusion.27), channel_id=1, source_target_pairs={{0,1},{1,2},{2,3},{3,4},{4,5},{5,6},{6,7},{7,0},{8,9},{9,10},{10,1... | collective-permute-start | bytes 196616 | tf_op jit(solution)/shard_map/ppermute | solution.py:200
  46.8 9.4 %collective-permute-start.8 = (bf16[1,512,64]{1,2,0:T(8,128)(2,1)S(1)}, bf16[1,512,64]{1,2,0:T(8,128)(2,1)S(1)}, u32[]{:S(2)}, u32[]{:S(2)}) collective-permute-start(bf16[1,512,64]{1,2,0:T(8,128)(2,1)S(1)} %get-tuple-element.39), channel_id=1, source_target_pairs={{0,2},{1,3},{2,4},{3,5},{4,6},{5,7},{6,0},{7,1},{8,10},{9,11},{10,... | collective-permute-start | bytes 196616 | tf_op jit(solution)/shard_map/ppermute | solution.py:200
  46.9 11.2 %collective-permute-start.9 = (bf16[1,512,64]{1,2,0:T(8,128)(2,1)S(1)}, bf16[1,512,64]{1,2,0:T(8,128)(2,1)S(1)}, u32[]{:S(2)}, u32[]{:S(2)}) collective-permute-start(bf16[1,512,64]{1,2,0:T(8,128)(2,1)S(1)} %get-tuple-element.38), channel_id=1, source_target_pairs={{0,3},{1,4},{2,5},{3,6},{4,7},{5,0},{6,1},{7,2},{8,11},{9,12},{10,... | collective-permute-start | bytes 196616 | tf_op jit(solution)/shard_map/ppermute | solution.py:200
  51.3 6.8 %collective-permute-start.10 = (bf16[1,512,64]{1,2,0:T(8,128)(2,1)S(1)}, bf16[1,512,64]{1,2,0:T(8,128)(2,1)S(1)}, u32[]{:S(2)}, u32[]{:S(2)}) collective-permute-start(bf16[1,512,64]{1,2,0:T(8,128)(2,1)S(1)} %get-tuple-element.37), channel_id=1, source_target_pairs={{0,4},{1,5},{2,6},{3,7},{4,0},{5,1},{6,2},{7,3},{8,12},{9,13},{10,... | collective-permute-start | bytes 196616 | tf_op jit(solution)/shard_map/ppermute | solution.py:200
  53.2 6.9 %collective-permute-start.11 = (bf16[1,512,64]{1,2,0:T(8,128)(2,1)S(1)}, bf16[1,512,64]{1,2,0:T(8,128)(2,1)S(1)}, u32[]{:S(2)}, u32[]{:S(2)}) collective-permute-start(bf16[1,512,64]{1,2,0:T(8,128)(2,1)S(1)} %get-tuple-element.36), channel_id=1, source_target_pairs={{0,5},{1,6},{2,7},{3,0},{4,1},{5,2},{6,3},{7,4},{8,13},{9,14},{10,... | collective-permute-start | bytes 196616 | tf_op jit(solution)/shard_map/ppermute | solution.py:200
  53.3 8.3 %collective-permute-start.12 = (bf16[1,512,64]{1,2,0:T(8,128)(2,1)S(1)}, bf16[1,512,64]{1,2,0:T(8,128)(2,1)S(1)}, u32[]{:S(2)}, u32[]{:S(2)}) collective-permute-start(bf16[1,512,64]{1,2,0:T(8,128)(2,1)S(1)} %get-tuple-element.35), channel_id=1, source_target_pairs={{0,6},{1,7},{2,0},{3,1},{4,2},{5,3},{6,4},{7,5},{8,14},{9,15},{10,... | collective-permute-start | bytes 196616 | tf_op jit(solution)/shard_map/ppermute | solution.py:200
  56.2 6.4 %collective-permute-start.13 = (bf16[1,512,64]{1,2,0:T(8,128)(2,1)S(1)}, bf16[1,512,64]{1,2,0:T(8,128)(2,1)S(1)}, u32[]{:S(2)}, u32[]{:S(2)}) collective-permute-start(bf16[1,512,64]{1,2,0:T(8,128)(2,1)S(1)} %get-tuple-element.34), channel_id=1, source_target_pairs={{0,7},{1,0},{2,1},{3,2},{4,3},{5,4},{6,5},{7,6},{8,15},{9,8},{10,9... | collective-permute-start | bytes 196616 | tf_op jit(solution)/shard_map/ppermute | solution.py:200
  58.1 7.5 %collective-permute-start.1 = (bf16[1,512,64]{1,2,0:T(8,128)(2,1)S(1)}, bf16[1,512,64]{1,2,0:T(8,128)(2,1)S(1)}, u32[]{:S(2)}, u32[]{:S(2)}) collective-permute-start(bf16[1,512,64]{1,2,0:T(8,128)(2,1)S(1)} %get-tuple-element.46), channel_id=1, source_target_pairs={{0,2},{1,3},{2,4},{3,5},{4,6},{5,7},{6,0},{7,1},{8,10},{9,11},{10,... | collective-permute-start | bytes 196616 | tf_op jit(solution)/shard_map/ppermute | solution.py:200
  58.1 9.1 %collective-permute-start.2 = (bf16[1,512,64]{1,2,0:T(8,128)(2,1)S(1)}, bf16[1,512,64]{1,2,0:T(8,128)(2,1)S(1)}, u32[]{:S(2)}, u32[]{:S(2)}) collective-permute-start(bf16[1,512,64]{1,2,0:T(8,128)(2,1)S(1)} %get-tuple-element.45), channel_id=1, source_target_pairs={{0,3},{1,4},{2,5},{3,6},{4,7},{5,0},{6,1},{7,2},{8,11},{9,12},{10,... | collective-permute-start | bytes 196616 | tf_op jit(solution)/shard_map/ppermute | solution.py:200
  60.1 7.1 %collective-permute-start.3 = (bf16[1,512,64]{1,2,0:T(8,128)(2,1)S(1)}, bf16[1,512,64]{1,2,0:T(8,128)(2,1)S(1)}, u32[]{:S(2)}, u32[]{:S(2)}) collective-permute-start(bf16[1,512,64]{1,2,0:T(8,128)(2,1)S(1)} %get-tuple-element.44), channel_id=1, source_target_pairs={{0,4},{1,5},{2,6},{3,7},{4,0},{5,1},{6,2},{7,3},{8,12},{9,13},{10,... | collective-permute-start | bytes 196616 | tf_op jit(solution)/shard_map/ppermute | solution.py:200
  61.5 5.7 %collective-permute-start.4 = (bf16[1,512,64]{1,2,0:T(8,128)(2,1)S(1)}, bf16[1,512,64]{1,2,0:T(8,128)(2,1)S(1)}, u32[]{:S(2)}, u32[]{:S(2)}) collective-permute-start(bf16[1,512,64]{1,2,0:T(8,128)(2,1)S(1)} %get-tuple-element.43), channel_id=1, source_target_pairs={{0,5},{1,6},{2,7},{3,0},{4,1},{5,2},{6,3},{7,4},{8,13},{9,14},{10,... | collective-permute-start | bytes 196616 | tf_op jit(solution)/shard_map/ppermute | solution.py:200
  62.6 5.1 %collective-permute-start.5 = (bf16[1,512,64]{1,2,0:T(8,128)(2,1)S(1)}, bf16[1,512,64]{1,2,0:T(8,128)(2,1)S(1)}, u32[]{:S(2)}, u32[]{:S(2)}) collective-permute-start(bf16[1,512,64]{1,2,0:T(8,128)(2,1)S(1)} %get-tuple-element.42), channel_id=1, source_target_pairs={{0,6},{1,7},{2,0},{3,1},{4,2},{5,3},{6,4},{7,5},{8,14},{9,15},{10,... | collective-permute-start | bytes 196616 | tf_op jit(solution)/shard_map/ppermute | solution.py:200
  65.6 4.1 %collective-permute-start.6 = (bf16[1,512,64]{1,2,0:T(8,128)(2,1)S(1)}, bf16[1,512,64]{1,2,0:T(8,128)(2,1)S(1)}, u32[]{:S(2)}, u32[]{:S(2)}) collective-permute-start(bf16[1,512,64]{1,2,0:T(8,128)(2,1)S(1)} %get-tuple-element.41), channel_id=1, source_target_pairs={{0,7},{1,0},{2,1},{3,2},{4,3},{5,4},{6,5},{7,6},{8,15},{9,8},{10,9... | collective-permute-start | bytes 196616 | tf_op jit(solution)/shard_map/ppermute | solution.py:200
  143.8 8.9 %slice-start.1 = ((bf16[512,1536]{1,0:T(8,128)(2,1)}), bf16[512,512]{1,0:T(8,128)(2,1)S(1)}, s32[]{:S(2)}) async-start(bf16[512,1536]{1,0:T(8,128)(2,1)} %param.11), calls=%async_computation.5 | async-start | bytes 1048576 | tf_op jit(solution)/shard_map/slice | solution.py:236
  143.8 80.2 %all-to-all-start.2 = ((bf16[32,384,128]{2,1,0:T(8,128)(2,1)}), bf16[32,384,128]{2,1,0:T(8,128)(2,1)}, u32[]{:S(2)}, u32[]{:S(2)}) async-start(bf16[32,384,128]{2,1,0:T(8,128)(2,1)} %bitcast.75), calls=%async_computation.2 | async-start | bytes 6291456 | tf_op jit(solution)/shard_map/all_to_all | solution.py:281
  153.8 25.7 %copy-start.4 = (bf16[32,128,64]{2,1,0:T(8,128)(2,1)S(1)}, bf16[32,128,64]{2,1,0:T(8,128)(2,1)}, u32[]{:S(2)}) copy-start(bf16[32,128,64]{2,1,0:T(8,128)(2,1)} %get-tuple-element.14) | copy-start | bytes 1572868
  171.7 8.8 %collective-permute-start.21 = (bf16[1,512,64]{1,2,0:T(8,128)(2,1)}, bf16[1,512,64]{1,2,0:T(8,128)(2,1)S(1)}, u32[]{:S(2)}, u32[]{:S(2)}) collective-permute-start(bf16[1,512,64]{1,2,0:T(8,128)(2,1)} %get-tuple-element.26), channel_id=1, source_target_pairs={{0,1},{1,2},{2,3},{3,4},{4,5},{5,6},{6,7},{7,0},{8,9},{9,10},{10,1... | collective-permute-start | bytes 196616 | tf_op jit(solution)/shard_map/ppermute | solution.py:200
  173.2 10.4 %collective-permute-start.22 = (bf16[1,512,64]{1,2,0:T(8,128)(2,1)}, bf16[1,512,64]{1,2,0:T(8,128)(2,1)S(1)}, u32[]{:S(2)}, u32[]{:S(2)}) collective-permute-start(bf16[1,512,64]{1,2,0:T(8,128)(2,1)} %get-tuple-element.25), channel_id=1, source_target_pairs={{0,2},{1,3},{2,4},{3,5},{4,6},{5,7},{6,0},{7,1},{8,10},{9,11},{10,... | collective-permute-start | bytes 196616 | tf_op jit(solution)/shard_map/ppermute | solution.py:200
  173.6 11.1 %collective-permute-start.23 = (bf16[1,512,64]{1,2,0:T(8,128)(2,1)}, bf16[1,512,64]{1,2,0:T(8,128)(2,1)S(1)}, u32[]{:S(2)}, u32[]{:S(2)}) collective-permute-start(bf16[1,512,64]{1,2,0:T(8,128)(2,1)} %get-tuple-element.24), channel_id=1, source_target_pairs={{0,3},{1,4},{2,5},{3,6},{4,7},{5,0},{6,1},{7,2},{8,11},{9,12},{10,... | collective-permute-start | bytes 196616 | tf_op jit(solution)/shard_map/ppermute | solution.py:200
  175.3 11.2 %collective-permute-start.24 = (bf16[1,512,64]{1,2,0:T(8,128)(2,1)}, bf16[1,512,64]{1,2,0:T(8,128)(2,1)S(1)}, u32[]{:S(2)}, u32[]{:S(2)}) collective-permute-start(bf16[1,512,64]{1,2,0:T(8,128)(2,1)} %get-tuple-element.23), channel_id=1, source_target_pairs={{0,4},{1,5},{2,6},{3,7},{4,0},{5,1},{6,2},{7,3},{8,12},{9,13},{10,... | collective-permute-start | bytes 196616 | tf_op jit(solution)/shard_map/ppermute | solution.py:200
  176.8 10.4 %collective-permute-start.25 = (bf16[1,512,64]{1,2,0:T(8,128)(2,1)}, bf16[1,512,64]{1,2,0:T(8,128)(2,1)S(1)}, u32[]{:S(2)}, u32[]{:S(2)}) collective-permute-start(bf16[1,512,64]{1,2,0:T(8,128)(2,1)} %get-tuple-element.22), channel_id=1, source_target_pairs={{0,5},{1,6},{2,7},{3,0},{4,1},{5,2},{6,3},{7,4},{8,13},{9,14},{10,... | collective-permute-start | bytes 196616 | tf_op jit(solution)/shard_map/ppermute | solution.py:200
  180.5 1.6 collective-permute-start.14
  182.2 7.7 %collective-permute-start.26 = (bf16[1,512,64]{1,2,0:T(8,128)(2,1)}, bf16[1,512,64]{1,2,0:T(8,128)(2,1)S(1)}, u32[]{:S(2)}, u32[]{:S(2)}) collective-permute-start(bf16[1,512,64]{1,2,0:T(8,128)(2,1)} %get-tuple-element.21), channel_id=1, source_target_pairs={{0,6},{1,7},{2,0},{3,1},{4,2},{5,3},{6,4},{7,5},{8,14},{9,15},{10,... | collective-permute-start | bytes 196616 | tf_op jit(solution)/shard_map/ppermute | solution.py:200
  183.7 6.4 %collective-permute-start.27 = (bf16[1,512,64]{1,2,0:T(8,128)(2,1)}, bf16[1,512,64]{1,2,0:T(8,128)(2,1)S(1)}, u32[]{:S(2)}, u32[]{:S(2)}) collective-permute-start(bf16[1,512,64]{1,2,0:T(8,128)(2,1)} %get-tuple-element.20), channel_id=1, source_target_pairs={{0,7},{1,0},{2,1},{3,2},{4,3},{5,4},{6,5},{7,6},{8,15},{9,8},{10,9... | collective-permute-start | bytes 196616 | tf_op jit(solution)/shard_map/ppermute | solution.py:200
  184.7 53.0 %collective-permute-start.15 = (bf16[1,512,64]{1,2,0:T(8,128)(2,1)}, bf16[1,512,64]{1,2,0:T(8,128)(2,1)S(1)}, u32[]{:S(2)}, u32[]{:S(2)}) collective-permute-start(bf16[1,512,64]{1,2,0:T(8,128)(2,1)} %get-tuple-element.32), channel_id=1, source_target_pairs={{0,2},{1,3},{2,4},{3,5},{4,6},{5,7},{6,0},{7,1},{8,10},{9,11},{10,... | collective-permute-start | bytes 196616 | tf_op jit(solution)/shard_map/ppermute | solution.py:200
  186.5 51.4 %collective-permute-start.16 = (bf16[1,512,64]{1,2,0:T(8,128)(2,1)}, bf16[1,512,64]{1,2,0:T(8,128)(2,1)S(1)}, u32[]{:S(2)}, u32[]{:S(2)}) collective-permute-start(bf16[1,512,64]{1,2,0:T(8,128)(2,1)} %get-tuple-element.31), channel_id=1, source_target_pairs={{0,3},{1,4},{2,5},{3,6},{4,7},{5,0},{6,1},{7,2},{8,11},{9,12},{10,... | collective-permute-start | bytes 196616 | tf_op jit(solution)/shard_map/ppermute | solution.py:200
  187.3 50.7 %collective-permute-start.17 = (bf16[1,512,64]{1,2,0:T(8,128)(2,1)}, bf16[1,512,64]{1,2,0:T(8,128)(2,1)S(1)}, u32[]{:S(2)}, u32[]{:S(2)}) collective-permute-start(bf16[1,512,64]{1,2,0:T(8,128)(2,1)} %get-tuple-element.30), channel_id=1, source_target_pairs={{0,4},{1,5},{2,6},{3,7},{4,0},{5,1},{6,2},{7,3},{8,12},{9,13},{10,... | collective-permute-start | bytes 196616 | tf_op jit(solution)/shard_map/ppermute | solution.py:200
  189.9 48.0 %collective-permute-start.18 = (bf16[1,512,64]{1,2,0:T(8,128)(2,1)}, bf16[1,512,64]{1,2,0:T(8,128)(2,1)S(1)}, u32[]{:S(2)}, u32[]{:S(2)}) collective-permute-start(bf16[1,512,64]{1,2,0:T(8,128)(2,1)} %get-tuple-element.29), channel_id=1, source_target_pairs={{0,5},{1,6},{2,7},{3,0},{4,1},{5,2},{6,3},{7,4},{8,13},{9,14},{10,... | collective-permute-start | bytes 196616 | tf_op jit(solution)/shard_map/ppermute | solution.py:200
  190.0 48.0 %collective-permute-start.19 = (bf16[1,512,64]{1,2,0:T(8,128)(2,1)}, bf16[1,512,64]{1,2,0:T(8,128)(2,1)S(1)}, u32[]{:S(2)}, u32[]{:S(2)}) collective-permute-start(bf16[1,512,64]{1,2,0:T(8,128)(2,1)} %get-tuple-element.28), channel_id=1, source_target_pairs={{0,6},{1,7},{2,0},{3,1},{4,2},{5,3},{6,4},{7,5},{8,14},{9,15},{10,... | collective-permute-start | bytes 196616 | tf_op jit(solution)/shard_map/ppermute | solution.py:200
  229.1 24.7 %copy-start.6 = (bf16[8,512,2,64]{1,3,2,0:T(8,128)(2,1)S(1)}, bf16[8,512,2,64]{1,3,2,0:T(8,128)(2,1)}, u32[]{:S(2)}) copy-start(bf16[8,512,2,64]{1,3,2,0:T(8,128)(2,1)} %copy-done.5) | copy-start | bytes 3145732
  229.1 24.7 %all-to-all-start.3 = ((bf16[8,512,128]{2,1,0:T(8,128)(2,1)}), bf16[8,512,128]{2,1,0:T(8,128)(2,1)}, u32[]{:S(2)}, u32[]{:S(2)}) async-start(bf16[8,512,128]{2,1,0:T(8,128)(2,1)} %bitcast.72), calls=%async_computation.3 | async-start | bytes 2097152 | tf_op jit(solution)/shard_map/all_to_all | solution.py:289
  237.7 14.9 %collective-permute-start.20 = (bf16[1,512,64]{1,2,0:T(8,128)(2,1)S(1)}, bf16[1,512,64]{1,2,0:T(8,128)(2,1)S(1)}, u32[]{:S(2)}, u32[]{:S(2)}) collective-permute-start(bf16[1,512,64]{1,2,0:T(8,128)(2,1)S(1)} %get-tuple-element.27), channel_id=1, source_target_pairs={{0,7},{1,0},{2,1},{3,2},{4,3},{5,4},{6,5},{7,6},{8,15},{9,8},{10,9... | collective-permute-start | bytes 196616 | tf_op jit(solution)/shard_map/ppermute | solution.py:200
  253.9 2.7 %copy-start.3 = (bf16[512,512]{1,0:T(8,128)(2,1)S(1)}, bf16[512,512]{1,0:T(8,128)(2,1)}, u32[]{:S(2)}) copy-start(bf16[512,512]{1,0:T(8,128)(2,1)} %param.13) | copy-start | bytes 1572868
  253.9 2.0 copy-start.7

commit v10 on v9

--- a/solution.py
+++ b/solution.py
@@ -34,17 +34,23 @@
     f32 = jnp.float32
     bf16 = jnp.bfloat16
     nq = q_ref.shape[0]
-    slot_acc[...] = jnp.zeros(slot_acc.shape, f32)
+    step = pl.program_id(0)
+
+    @pl.when(step == 0)
+    def _():
+        slot_acc[...] = jnp.zeros(slot_acc.shape, f32)
+
     kcols = pl.ds(0, depth)
     vcols = pl.ds(depth, depth)
     nt = (((1,), (1,)), ((), ()))
     split = near * bsize
 
     def body(b, carry):
+        g = step * nq + b
         q = q_ref[b]
         do = do_ref[b]
-        ids_l = [lk_ref[b * near + i] for i in range(near)]
-        ids_r = [rk_ref[b * far + i] for i in range(far)]
+        ids_l = [lk_ref[g * near + i] for i in range(near)]
+        ids_r = [rk_ref[g * far + i] for i in range(far)]
         keys = load_blocks(kv_ref, pool_ref, ids_l, ids_r, kcols)
         vals = load_blocks(kv_ref, pool_ref, ids_l, ids_r, vcols)
         q_s = q * scale
@@ -76,8 +82,11 @@
             slot_acc[ids_r[i]] = slot_acc[ids_r[i]] + part
         return carry
 
-    lax.fori_loop(0, nq, body, 0, unroll=8)
-    slot_ref[...] = slot_acc[...].astype(bf16)
+    lax.fori_loop(0, nq, body, 0, unroll=4)
+
+    @pl.when(step == pl.num_programs(0) - 1)
+    def _():
+        slot_ref[...] = slot_acc[...].astype(bf16)
 
 
 def local_kernel(
@@ -131,20 +140,32 @@
     vmem = pl.BlockSpec(memory_space=pltpu.VMEM)
     kv_t = (2 * depth, bsize)
     params = pltpu.CompilerParams(vmem_limit_bytes=60 * 1024 * 1024)
+    per_step = 8
+    blk = lambda *shape: pl.BlockSpec((per_step,) + shape, lambda i: (i,) + (0,) * len(shape))
+    whole = lambda a: pl.BlockSpec(a.shape, lambda i: (0,) * a.ndim)
     o, dq_r, stats, slot = pl.pallas_call(
         lambda *refs: remote_kernel(
             *refs, near=near, far=far, bsize=bsize, depth=depth, scale=scale
         ),
+        grid=(nq // per_step,),
         out_shape=(
             jax.ShapeDtypeStruct((nq, bsize, depth), jnp.bfloat16),
             jax.ShapeDtypeStruct((nq, bsize, depth), f32),
             jax.ShapeDtypeStruct((nq, 3, bsize), f32),
             jax.ShapeDtypeStruct((npool,) + kv_t, jnp.bfloat16),
         ),
-        in_specs=[smem, smem] + [vmem] * 5,
-        out_specs=(vmem, vmem, vmem, vmem),
+        in_specs=[
+            smem, smem, blk(bsize, depth), whole(kv), blk(bsize, depth), whole(pool),
+            pl.BlockSpec((per_step, bias.shape[1]), lambda i: (i, 0)),
+        ],
+        out_specs=(
+            blk(bsize, depth), blk(bsize, depth), blk(3, bsize),
+            pl.BlockSpec((npool,) + kv_t, lambda i: (0, 0, 0)),
+        ),
         scratch_shapes=[pltpu.VMEM((npool,) + kv_t, f32)],
-        compiler_params=params,
+        compiler_params=pltpu.CompilerParams(
+            dimension_semantics=("arbitrary",), vmem_limit_bytes=60 * 1024 * 1024
+        ),
     )(local_ids, remote_ids, q, kv, d_out, pool, bias)
     dq, acc = pl.pallas_call(
         lambda *refs: local_kernel(*refs, near=near, bsize=bsize, depth=depth, scale=scale),

time: 258 us -> 258 us (level)
  no operation moved by 1% of the time
where the time goes in v10:
time: 258 us
  waiting for transfers between devices  105 us (41%)
  starting transfers between devices  71.8 us (28%)
  Pallas kernels  52.8 us (20%)
  local copies, waits for them, and re-layouts  15.3 us (6%)
  matrix products  8.81 us (3%)
  other arithmetic  2.64 us (1%)
    all_to_all x1, waiting for transfers between devices, local(): lax.all_to_all(outgoing.reshape(ndom, pair_slots * bsize, 2 * hwide), 'do...  40.7 us
    ppermute x28, starting transfers between devices, head_exchange(): got = lax.ppermute(part, axis, perm)  37 us
    all_to_all x1, waiting for transfers between devices, local(): lax.all_to_all(slot_grads.reshape(ndom, pair_slots * 2 * hwide, bsize), '...  32.7 us
    pallas_call x1, Pallas kernels, fused_attention(): pl.pallas_call(lambda *refs: remote_kernel(*refs, near=near, far=far, bsi...  32.1 us
    ppermute x28, waiting for transfers between devices, head_exchange(): got = lax.ppermute(part, axis, perm)  20 us
    pallas_call x1, Pallas kernels, fused_attention(): pl.pallas_call(lambda *refs: local_kernel(*refs, near=near, bsize=bsize,...  15.6 us
    all_to_all x1, waiting for transfers between devices, local(): lax.all_to_all(kv_own, 'head', split_axis=0, concat_axis=0, tiled=True)  11.5 us
    all_to_all x1, starting transfers between devices, local(): lax.all_to_all(outgoing.reshape(ndom, pair_slots * bsize, 2 * hwide), 'do...  10.6 us
  transfers between devices with their start and end apart: 32, of which 9 were waited for; matrix products, arithmetic and copies ran while one was open for 6% of the time, Pallas kernels for 8%

profile of v10, /device:TPU:1, one launch (start us, length us, event | category | flops | bytes accessed | tf_op | source)
XLA Modules:
  0.0 257.7 jit_solution(14156562006376435661)
XLA Ops:
  0.7 1.3 fusion.14
  2.0 0.2 slice-done
  2.2 0.5 copy.70
  2.8 1.0 copy-done.5
  3.8 1.8 fusion.3
  5.6 6.7 %all-to-all-start = ((bf16[8,512,128]{2,1,0:T(8,128)(2,1)}), bf16[8,512,128]{2,1,0:T(8,128)(2,1)S(1)}, u32[]{:S(2)}, u32[]{:S(2)}) async-start(bf16[8,512,128]{2,1,0:T(8,128)(2,1)} %fusion.3), calls=%async_computation | async-start | bytes 2097152 | tf_op jit(solution)/shard_map/all_to_all | solution.py:266
  12.3 0.1 reshape.92.ids_ref
  12.5 1.6 fusion.17
  14.2 1.5 fusion.7
  15.7 11.5 %all-to-all-done = bf16[8,512,128]{2,1,0:T(8,128)(2,1)S(1)} async-done(((bf16[8,512,128]{2,1,0:T(8,128)(2,1)}), bf16[8,512,128]{2,1,0:T(8,128)(2,1)S(1)}, u32[]{:S(2)}, u32[]{:S(2)}) %all-to-all-start) | async-done | bytes 1048608 | tf_op jit(solution)/shard_map/all_to_all | solution.py:266
  27.2 2.7 %gather_fusion = bf16[96,128,128]{2,1,0:T(8,128)(2,1)} fusion(bf16[32,128,128]{2,1,0:T(8,128)(2,1)S(1)} %bitcast.64, s32[1024]{0:T(1024)S(1)} %pad_clamp_fusion.1), kind=kCustom, calls=%fused_computation | custom fusion | bytes 6291840 | tf_op jit(solution)/shard_map/jit(_take)/gather | solution.py:273
  30.0 10.6 %all-to-all-start.1 = ((bf16[32,384,128]{2,1,0:T(8,128)(2,1)}), bf16[32,384,128]{2,1,0:T(8,128)(2,1)}, u32[]{:S(2)}, u32[]{:S(2)}) async-start(bf16[32,384,128]{2,1,0:T(8,128)(2,1)} %bitcast.67), calls=%async_computation.1 | async-start | bytes 6291456 | tf_op jit(solution)/shard_map/all_to_all | solution.py:277
  40.7 0.1 reshape.74.refs_1_
  40.9 0.1 lt.237
  41.1 1.2 gather_fusion.1
  42.6 0.7 copy.73
  43.4 0.6 reshape.73.refs_0_
  44.0 1.4 collective-permute-start.7
  45.5 1.3 collective-permute-done.7
  46.9 4.4 %collective-permute-start.9 = (bf16[1,512,64]{1,2,0:T(8,128)(2,1)S(1)}, bf16[1,512,64]{1,2,0:T(8,128)(2,1)S(1)}, u32[]{:S(2)}, u32[]{:S(2)}) collective-permute-start(bf16[1,512,64]{1,2,0:T(8,128)(2,1)S(1)} %get-tuple-element.38), channel_id=1, source_target_pairs={{0,3},{1,4},{2,5},{3,6},{4,7},{5,0},{6,1},{7,2},{8,11},{9,12},{10,... | collective-permute-start | bytes 196616 | tf_op jit(solution)/shard_map/ppermute | solution.py:221
  51.3 1.9 collective-permute-start.10
  53.3 2.9 %collective-permute-start.12 = (bf16[1,512,64]{1,2,0:T(8,128)(2,1)S(1)}, bf16[1,512,64]{1,2,0:T(8,128)(2,1)S(1)}, u32[]{:S(2)}, u32[]{:S(2)}) collective-permute-start(bf16[1,512,64]{1,2,0:T(8,128)(2,1)S(1)} %get-tuple-element.35), channel_id=1, source_target_pairs={{0,6},{1,7},{2,0},{3,1},{4,2},{5,3},{6,4},{7,5},{8,14},{9,15},{10,... | collective-permute-start | bytes 196616 | tf_op jit(solution)/shard_map/ppermute | solution.py:221
  56.2 1.5 collective-permute-start.13
  57.7 0.4 collective-permute-done.9
  58.1 2.0 collective-permute-start.2
  60.1 1.4 collective-permute-start.3
  61.5 1.1 collective-permute-start.4
  62.6 1.6 collective-permute-start.5
  64.2 1.3 copy.44
  65.6 1.6 collective-permute-start.6
  67.3 0.4 collective-permute-done.5
  67.7 2.0 collective-permute-done.6
  69.7 1.3 copy.43
  71.0 40.7 %all-to-all-done.1 = bf16[32,384,128]{2,1,0:T(8,128)(2,1)} async-done(((bf16[32,384,128]{2,1,0:T(8,128)(2,1)}), bf16[32,384,128]{2,1,0:T(8,128)(2,1)}, u32[]{:S(2)}, u32[]{:S(2)}) %all-to-all-start.1) | async-done | bytes 3145760 | tf_op jit(solution)/shard_map/all_to_all | solution.py:277
  111.7 32.1 %shard_map.104 = (bf16[32,128,64]{2,1,0:T(8,128)(2,1)}, f32[32,128,64]{2,1,0:T(8,128)}, f32[32,3,128]{2,1,0:T(4,128)}, bf16[96,128,128]{2,1,0:T(8,128)(2,1)}) custom-call(s32[128]{0:T(128)} %reshape.73.refs_0_, s32[128]{0:T(128)} %copy-done.9, bf16[32,128,64]{2,1,0:T(8,128)(2,1)} %bitcast.70, bf16[32,128,128]{2,1,0:T(8,128)(2,1)} %bitcast.65, ...), custom_call_target="tpu_custom_call" | custom-call | tf_op jit(solution)/shard_map/pallas_call | solution.py:146
  143.8 8.9 %all-to-all-start.2 = ((bf16[32,384,128]{2,1,0:T(8,128)(2,1)}), bf16[32,384,128]{2,1,0:T(8,128)(2,1)}, u32[]{:S(2)}, u32[]{:S(2)}) async-start(bf16[32,384,128]{2,1,0:T(8,128)(2,1)} %bitcast.75), calls=%async_computation.2 | async-start | bytes 6291456 | tf_op jit(solution)/shard_map/all_to_all | solution.py:302
  152.8 1.0 copy.42
  153.8 15.6 %shard_map.105 = (bf16[32,128,64]{2,1,0:T(8,128)(2,1)}, f32[32,128,128]{2,1,0:T(8,128)}) custom-call(s32[128]{0:T(128)} %reshape.73.refs_0_, bf16[32,128,64]{2,1,0:T(8,128)(2,1)} %bitcast.71, bf16[32,128,128]{2,1,0:T(8,128)(2,1)} %bitcast.66, bf16[32,128,64]{2,1,0:T(8,128)(2,1)} %bitcast.69, f32[32,3,128]{2,1,0:T(4,128)} %get-tuple-element.15.refs_4_, ...), custom_call_target="tpu_custom_call" | custom-call | tf_op jit(solution)/shard_map/pallas_call | solution.py:170
  169.4 1.5 copy.54
  170.9 0.8 constant_dynamic-slice_fusion
  171.7 1.5 collective-permute-start.21
  173.2 0.4 collective-permute-start.22
  173.6 1.7 collective-permute-start.23
  175.3 1.5 collective-permute-start.24
  176.8 2.6 %collective-permute-start.25 = (bf16[1,512,64]{1,2,0:T(8,128)(2,1)}, bf16[1,512,64]{1,2,0:T(8,128)(2,1)S(1)}, u32[]{:S(2)}, u32[]{:S(2)}) collective-permute-start(bf16[1,512,64]{1,2,0:T(8,128)(2,1)} %get-tuple-element.22), channel_id=1, source_target_pairs={{0,5},{1,6},{2,7},{3,0},{4,1},{5,2},{6,3},{7,4},{8,13},{9,14},{10,... | collective-permute-start | bytes 196616 | tf_op jit(solution)/shard_map/ppermute | solution.py:221
  179.5 0.3 copy.46
  179.8 0.7 constant_dynamic-slice_fusion.7
  180.5 0.3 collective-permute-start.14
  180.8 1.3 collective-permute-done.14
  182.2 1.5 collective-permute-start.26
  183.7 1.0 collective-permute-start.27
  184.7 1.8 collective-permute-start.15
  186.6 0.7 collective-permute-start.16
  187.3 2.8 %collective-permute-start.17 = (bf16[1,512,64]{1,2,0:T(8,128)(2,1)}, bf16[1,512,64]{1,2,0:T(8,128)(2,1)S(1)}, u32[]{:S(2)}, u32[]{:S(2)}) collective-permute-start(bf16[1,512,64]{1,2,0:T(8,128)(2,1)} %get-tuple-element.30), channel_id=1, source_target_pairs={{0,4},{1,5},{2,6},{3,7},{4,0},{5,1},{6,2},{7,3},{8,12},{9,13},{10,... | collective-permute-start | bytes 196616 | tf_op jit(solution)/shard_map/ppermute | solution.py:221
  190.3 1.0 collective-permute-start.19
  191.3 32.7 %all-to-all-done.2 = bf16[32,384,128]{2,1,0:T(8,128)(2,1)} async-done(((bf16[32,384,128]{2,1,0:T(8,128)(2,1)}), bf16[32,384,128]{2,1,0:T(8,128)(2,1)}, u32[]{:S(2)}, u32[]{:S(2)}) %all-to-all-start.2) | async-done | bytes 3145760 | tf_op jit(solution)/shard_map/all_to_all | solution.py:302
  224.0 5.1 %shard_map.106 = bf16[32,128,128]{2,1,0:T(8,128)(2,1)} custom-call(s32[96]{0:T(128)} %copy-done.8, f32[32,128,128]{2,1,0:T(8,128)} %get-tuple-element.18.acc_ref, bf16[96,128,128]{2,1,0:T(8,128)(2,1)} %bitcast.26.ret_ref), custom_call_target="tpu_custom_call" | custom-call | tf_op jit(solution)/shard_map/pallas_call | solution.py:204
  229.1 8.6 %all-to-all-start.3 = ((bf16[8,512,128]{2,1,0:T(8,128)(2,1)}), bf16[8,512,128]{2,1,0:T(8,128)(2,1)}, u32[]{:S(2)}, u32[]{:S(2)}) async-start(bf16[8,512,128]{2,1,0:T(8,128)(2,1)} %bitcast.72), calls=%async_computation.3 | async-start | bytes 2097152 | tf_op jit(solution)/shard_map/all_to_all | solution.py:310
  237.7 0.2 collective-permute-start.20
  238.0 14.6 %collective-permute-done.20 = bf16[1,512,64]{1,2,0:T(8,128)(2,1)S(1)} collective-permute-done((bf16[1,512,64]{1,2,0:T(8,128)(2,1)S(1)}, bf16[1,512,64]{1,2,0:T(8,128)(2,1)S(1)}, u32[]{:S(2)}, u32[]{:S(2)}) %collective-permute-start.20) | collective-permute-done | bytes 65568 | tf_op jit(solution)/shard_map/ppermute | solution.py:221
  252.6 1.3 fusion.6
  253.9 2.0 convolution_bitcast_fusion
  255.9 0.6 fusion.9
  256.5 1.1 fusion.13
  (104 shorter events, 1.4 us)
Async XLA Ops:
  0.6 13.5 %copy-start = (bf16[512,512]{1,0:T(8,128)(2,1)S(1)}, bf16[512,512]{1,0:T(8,128)(2,1)}, u32[]{:S(2)}) copy-start(bf16[512,512]{1,0:T(8,128)(2,1)} %param.12) | copy-start | bytes 1572868
  0.6 1.5 slice-start
  2.0 1.8 copy-start.2
  2.0 1.8 copy-start.12
  2.7 9.5 %copy-start.13 = (s32[1,32,3]{1,0,2:T(1,128)S(1)}, s32[1,32,3]{1,0,2:T(1,128)}, u32[]{:S(2)}) copy-start(s32[1,32,3]{1,0,2:T(1,128)} %param.16) | copy-start | bytes 1156
  2.8 1.0 copy-start.5
  5.6 21.7 %all-to-all-start = ((bf16[8,512,128]{2,1,0:T(8,128)(2,1)}), bf16[8,512,128]{2,1,0:T(8,128)(2,1)S(1)}, u32[]{:S(2)}, u32[]{:S(2)}) async-start(bf16[8,512,128]{2,1,0:T(8,128)(2,1)} %fusion.3), calls=%async_computation | async-start | bytes 2097152 | tf_op jit(solution)/shard_map/all_to_all | solution.py:266
  12.4 17.5 %copy-start.8 = (s32[96]{0:T(128)}, s32[96]{0:T(128)S(1)}, u32[]{:S(2)}) copy-start(s32[96]{0:T(128)S(1)} %reshape.92.ids_ref) | copy-start | bytes 1156
  27.2 2.7 %copy-start.1 = (bf16[8,512,128]{2,1,0:T(8,128)(2,1)}, bf16[8,512,128]{2,1,0:T(8,128)(2,1)S(1)}, u32[]{:S(2)}) copy-start(bf16[8,512,128]{2,1,0:T(8,128)(2,1)S(1)} %all-to-all-done) | copy-start | bytes 3145732
  30.0 10.7 %copy-start.10 = (s32[32,4]{0,1:T(4,128)S(1)}, s32[32,4]{0,1:T(4,128)}, u32[]{:S(2)}) copy-start(s32[32,4]{0,1:T(4,128)} %param.15) | copy-start | bytes 1540
  30.0 10.9 %copy-start.14 = (s32[32,1]{0,1:T(1,128)S(1)}, s32[32,1]{0,1:T(1,128)}, u32[]{:S(2)}) copy-start(s32[32,1]{0,1:T(1,128)} %param.17) | copy-start | bytes 388
  30.0 81.8 %all-to-all-start.1 = ((bf16[32,384,128]{2,1,0:T(8,128)(2,1)}), bf16[32,384,128]{2,1,0:T(8,128)(2,1)}, u32[]{:S(2)}, u32[]{:S(2)}) async-start(bf16[32,384,128]{2,1,0:T(8,128)(2,1)} %bitcast.67), calls=%async_computation.1 | async-start | bytes 6291456 | tf_op jit(solution)/shard_map/all_to_all | solution.py:277
  40.5 2.8 %copy-start.11 = (s32[32,4]{0,1:T(4,128)S(1)}, s32[32,4]{0,1:T(4,128)}, u32[]{:S(2)}) copy-start(s32[32,4]{0,1:T(4,128)} %param.14) | copy-start | bytes 1540
  40.8 15.3 %copy-start.9 = (s32[128]{0:T(128)}, s32[128]{0:T(128)S(1)}, u32[]{:S(2)}) copy-start(s32[128]{0:T(128)S(1)} %reshape.74.refs_1_) | copy-start | bytes 1540
  44.0 2.8 %collective-permute-start.7 = (bf16[1,512,64]{1,2,0:T(8,128)(2,1)S(1)}, bf16[1,512,64]{1,2,0:T(8,128)(2,1)S(1)}, u32[]{:S(2)}, u32[]{:S(2)}) collective-permute-start(bf16[1,512,64]{1,2,0:T(8,128)(2,1)S(1)} %constant_dynamic-slice_fusion.20), channel_id=1, source_target_pairs={{0,1},{1,2},{2,3},{3,4},{4,5},{5,6},{6,7},{7,0},{8,9},{9,10},{10,1... | collective-permute-start | bytes 196616 | tf_op jit(solution)/shard_map/ppermute | solution.py:221
  45.5 7.8 %collective-permute-start = (bf16[1,512,64]{1,2,0:T(8,128)(2,1)S(1)}, bf16[1,512,64]{1,2,0:T(8,128)(2,1)S(1)}, u32[]{:S(2)}, u32[]{:S(2)}) collective-permute-start(bf16[1,512,64]{1,2,0:T(8,128)(2,1)S(1)} %constant_dynamic-slice_fusion.27), channel_id=1, source_target_pairs={{0,1},{1,2},{2,3},{3,4},{4,5},{5,6},{6,7},{7,0},{8,9},{9,10},{10,1... | collective-permute-start | bytes 196616 | tf_op jit(solution)/shard_map/ppermute | solution.py:221
  46.8 9.4 %collective-permute-start.8 = (bf16[1,512,64]{1,2,0:T(8,128)(2,1)S(1)}, bf16[1,512,64]{1,2,0:T(8,128)(2,1)S(1)}, u32[]{:S(2)}, u32[]{:S(2)}) collective-permute-start(bf16[1,512,64]{1,2,0:T(8,128)(2,1)S(1)} %get-tuple-element.39), channel_id=1, source_target_pairs={{0,2},{1,3},{2,4},{3,5},{4,6},{5,7},{6,0},{7,1},{8,10},{9,11},{10,... | collective-permute-start | bytes 196616 | tf_op jit(solution)/shard_map/ppermute | solution.py:221
  46.9 11.2 %collective-permute-start.9 = (bf16[1,512,64]{1,2,0:T(8,128)(2,1)S(1)}, bf16[1,512,64]{1,2,0:T(8,128)(2,1)S(1)}, u32[]{:S(2)}, u32[]{:S(2)}) collective-permute-start(bf16[1,512,64]{1,2,0:T(8,128)(2,1)S(1)} %get-tuple-element.38), channel_id=1, source_target_pairs={{0,3},{1,4},{2,5},{3,6},{4,7},{5,0},{6,1},{7,2},{8,11},{9,12},{10,... | collective-permute-start | bytes 196616 | tf_op jit(solution)/shard_map/ppermute | solution.py:221
  51.3 6.8 %collective-permute-start.10 = (bf16[1,512,64]{1,2,0:T(8,128)(2,1)S(1)}, bf16[1,512,64]{1,2,0:T(8,128)(2,1)S(1)}, u32[]{:S(2)}, u32[]{:S(2)}) collective-permute-start(bf16[1,512,64]{1,2,0:T(8,128)(2,1)S(1)} %get-tuple-element.37), channel_id=1, source_target_pairs={{0,4},{1,5},{2,6},{3,7},{4,0},{5,1},{6,2},{7,3},{8,12},{9,13},{10,... | collective-permute-start | bytes 196616 | tf_op jit(solution)/shard_map/ppermute | solution.py:221
  53.2 6.9 %collective-permute-start.11 = (bf16[1,512,64]{1,2,0:T(8,128)(2,1)S(1)}, bf16[1,512,64]{1,2,0:T(8,128)(2,1)S(1)}, u32[]{:S(2)}, u32[]{:S(2)}) collective-permute-start(bf16[1,512,64]{1,2,0:T(8,128)(2,1)S(1)} %get-tuple-element.36), channel_id=1, source_target_pairs={{0,5},{1,6},{2,7},{3,0},{4,1},{5,2},{6,3},{7,4},{8,13},{9,14},{10,... | collective-permute-start | bytes 196616 | tf_op jit(solution)/shard_map/ppermute | solution.py:221
  53.3 8.3 %collective-permute-start.12 = (bf16[1,512,64]{1,2,0:T(8,128)(2,1)S(1)}, bf16[1,512,64]{1,2,0:T(8,128)(2,1)S(1)}, u32[]{:S(2)}, u32[]{:S(2)}) collective-permute-start(bf16[1,512,64]{1,2,0:T(8,128)(2,1)S(1)} %get-tuple-element.35), channel_id=1, source_target_pairs={{0,6},{1,7},{2,0},{3,1},{4,2},{5,3},{6,4},{7,5},{8,14},{9,15},{10,... | collective-permute-start | bytes 196616 | tf_op jit(solution)/shard_map/ppermute | solution.py:221
  56.2 6.4 %collective-permute-start.13 = (bf16[1,512,64]{1,2,0:T(8,128)(2,1)S(1)}, bf16[1,512,64]{1,2,0:T(8,128)(2,1)S(1)}, u32[]{:S(2)}, u32[]{:S(2)}) collective-permute-start(bf16[1,512,64]{1,2,0:T(8,128)(2,1)S(1)} %get-tuple-element.34), channel_id=1, source_target_pairs={{0,7},{1,0},{2,1},{3,2},{4,3},{5,4},{6,5},{7,6},{8,15},{9,8},{10,9... | collective-permute-start | bytes 196616 | tf_op jit(solution)/shard_map/ppermute | solution.py:221
  58.1 7.5 %collective-permute-start.1 = (bf16[1,512,64]{1,2,0:T(8,128)(2,1)S(1)}, bf16[1,512,64]{1,2,0:T(8,128)(2,1)S(1)}, u32[]{:S(2)}, u32[]{:S(2)}) collective-permute-start(bf16[1,512,64]{1,2,0:T(8,128)(2,1)S(1)} %get-tuple-element.46), channel_id=1, source_target_pairs={{0,2},{1,3},{2,4},{3,5},{4,6},{5,7},{6,0},{7,1},{8,10},{9,11},{10,... | collective-permute-start | bytes 196616 | tf_op jit(solution)/shard_map/ppermute | solution.py:221
  58.1 9.1 %collective-permute-start.2 = (bf16[1,512,64]{1,2,0:T(8,128)(2,1)S(1)}, bf16[1,512,64]{1,2,0:T(8,128)(2,1)S(1)}, u32[]{:S(2)}, u32[]{:S(2)}) collective-permute-start(bf16[1,512,64]{1,2,0:T(8,128)(2,1)S(1)} %get-tuple-element.45), channel_id=1, source_target_pairs={{0,3},{1,4},{2,5},{3,6},{4,7},{5,0},{6,1},{7,2},{8,11},{9,12},{10,... | collective-permute-start | bytes 196616 | tf_op jit(solution)/shard_map/ppermute | solution.py:221
  60.1 7.1 %collective-permute-start.3 = (bf16[1,512,64]{1,2,0:T(8,128)(2,1)S(1)}, bf16[1,512,64]{1,2,0:T(8,128)(2,1)S(1)}, u32[]{:S(2)}, u32[]{:S(2)}) collective-permute-start(bf16[1,512,64]{1,2,0:T(8,128)(2,1)S(1)} %get-tuple-element.44), channel_id=1, source_target_pairs={{0,4},{1,5},{2,6},{3,7},{4,0},{5,1},{6,2},{7,3},{8,12},{9,13},{10,... | collective-permute-start | bytes 196616 | tf_op jit(solution)/shard_map/ppermute | solution.py:221
  61.5 5.7 %collective-permute-start.4 = (bf16[1,512,64]{1,2,0:T(8,128)(2,1)S(1)}, bf16[1,512,64]{1,2,0:T(8,128)(2,1)S(1)}, u32[]{:S(2)}, u32[]{:S(2)}) collective-permute-start(bf16[1,512,64]{1,2,0:T(8,128)(2,1)S(1)} %get-tuple-element.43), channel_id=1, source_target_pairs={{0,5},{1,6},{2,7},{3,0},{4,1},{5,2},{6,3},{7,4},{8,13},{9,14},{10,... | collective-permute-start | bytes 196616 | tf_op jit(solution)/shard_map/ppermute | solution.py:221
  62.6 5.1 %collective-permute-start.5 = (bf16[1,512,64]{1,2,0:T(8,128)(2,1)S(1)}, bf16[1,512,64]{1,2,0:T(8,128)(2,1)S(1)}, u32[]{:S(2)}, u32[]{:S(2)}) collective-permute-start(bf16[1,512,64]{1,2,0:T(8,128)(2,1)S(1)} %get-tuple-element.42), channel_id=1, source_target_pairs={{0,6},{1,7},{2,0},{3,1},{4,2},{5,3},{6,4},{7,5},{8,14},{9,15},{10,... | collective-permute-start | bytes 196616 | tf_op jit(solution)/shard_map/ppermute | solution.py:221
  65.6 4.1 %collective-permute-start.6 = (bf16[1,512,64]{1,2,0:T(8,128)(2,1)S(1)}, bf16[1,512,64]{1,2,0:T(8,128)(2,1)S(1)}, u32[]{:S(2)}, u32[]{:S(2)}) collective-permute-start(bf16[1,512,64]{1,2,0:T(8,128)(2,1)S(1)} %get-tuple-element.41), channel_id=1, source_target_pairs={{0,7},{1,0},{2,1},{3,2},{4,3},{5,4},{6,5},{7,6},{8,15},{9,8},{10,9... | collective-permute-start | bytes 196616 | tf_op jit(solution)/shard_map/ppermute | solution.py:221
  143.8 9.0 %slice-start.1 = ((bf16[512,1536]{1,0:T(8,128)(2,1)}), bf16[512,512]{1,0:T(8,128)(2,1)S(1)}, s32[]{:S(2)}) async-start(bf16[512,1536]{1,0:T(8,128)(2,1)} %param.11), calls=%async_computation.5 | async-start | bytes 1048576 | tf_op jit(solution)/shard_map/slice | solution.py:257
  143.8 80.2 %all-to-all-start.2 = ((bf16[32,384,128]{2,1,0:T(8,128)(2,1)}), bf16[32,384,128]{2,1,0:T(8,128)(2,1)}, u32[]{:S(2)}, u32[]{:S(2)}) async-start(bf16[32,384,128]{2,1,0:T(8,128)(2,1)} %bitcast.75), calls=%async_computation.2 | async-start | bytes 6291456 | tf_op jit(solution)/shard_map/all_to_all | solution.py:302
  153.8 25.7 %copy-start.4 = (bf16[32,128,64]{2,1,0:T(8,128)(2,1)S(1)}, bf16[32,128,64]{2,1,0:T(8,128)(2,1)}, u32[]{:S(2)}) copy-start(bf16[32,128,64]{2,1,0:T(8,128)(2,1)} %get-tuple-element.14) | copy-start | bytes 1572868
  171.7 8.8 %collective-permute-start.21 = (bf16[1,512,64]{1,2,0:T(8,128)(2,1)}, bf16[1,512,64]{1,2,0:T(8,128)(2,1)S(1)}, u32[]{:S(2)}, u32[]{:S(2)}) collective-permute-start(bf16[1,512,64]{1,2,0:T(8,128)(2,1)} %get-tuple-element.26), channel_id=1, source_target_pairs={{0,1},{1,2},{2,3},{3,4},{4,5},{5,6},{6,7},{7,0},{8,9},{9,10},{10,1... | collective-permute-start | bytes 196616 | tf_op jit(solution)/shard_map/ppermute | solution.py:221
  173.2 10.4 %collective-permute-start.22 = (bf16[1,512,64]{1,2,0:T(8,128)(2,1)}, bf16[1,512,64]{1,2,0:T(8,128)(2,1)S(1)}, u32[]{:S(2)}, u32[]{:S(2)}) collective-permute-start(bf16[1,512,64]{1,2,0:T(8,128)(2,1)} %get-tuple-element.25), channel_id=1, source_target_pairs={{0,2},{1,3},{2,4},{3,5},{4,6},{5,7},{6,0},{7,1},{8,10},{9,11},{10,... | collective-permute-start | bytes 196616 | tf_op jit(solution)/shard_map/ppermute | solution.py:221
  173.6 11.1 %collective-permute-start.23 = (bf16[1,512,64]{1,2,0:T(8,128)(2,1)}, bf16[1,512,64]{1,2,0:T(8,128)(2,1)S(1)}, u32[]{:S(2)}, u32[]{:S(2)}) collective-permute-start(bf16[1,512,64]{1,2,0:T(8,128)(2,1)} %get-tuple-element.24), channel_id=1, source_target_pairs={{0,3},{1,4},{2,5},{3,6},{4,7},{5,0},{6,1},{7,2},{8,11},{9,12},{10,... | collective-permute-start | bytes 196616 | tf_op jit(solution)/shard_map/ppermute | solution.py:221
  175.3 11.2 %collective-permute-start.24 = (bf16[1,512,64]{1,2,0:T(8,128)(2,1)}, bf16[1,512,64]{1,2,0:T(8,128)(2,1)S(1)}, u32[]{:S(2)}, u32[]{:S(2)}) collective-permute-start(bf16[1,512,64]{1,2,0:T(8,128)(2,1)} %get-tuple-element.23), channel_id=1, source_target_pairs={{0,4},{1,5},{2,6},{3,7},{4,0},{5,1},{6,2},{7,3},{8,12},{9,13},{10,... | collective-permute-start | bytes 196616 | tf_op jit(solution)/shard_map/ppermute | solution.py:221
  176.8 10.4 %collective-permute-start.25 = (bf16[1,512,64]{1,2,0:T(8,128)(2,1)}, bf16[1,512,64]{1,2,0:T(8,128)(2,1)S(1)}, u32[]{:S(2)}, u32[]{:S(2)}) collective-permute-start(bf16[1,512,64]{1,2,0:T(8,128)(2,1)} %get-tuple-element.22), channel_id=1, source_target_pairs={{0,5},{1,6},{2,7},{3,0},{4,1},{5,2},{6,3},{7,4},{8,13},{9,14},{10,... | collective-permute-start | bytes 196616 | tf_op jit(solution)/shard_map/ppermute | solution.py:221
  180.5 1.6 collective-permute-start.14
  182.2 8.0 %collective-permute-start.26 = (bf16[1,512,64]{1,2,0:T(8,128)(2,1)}, bf16[1,512,64]{1,2,0:T(8,128)(2,1)S(1)}, u32[]{:S(2)}, u32[]{:S(2)}) collective-permute-start(bf16[1,512,64]{1,2,0:T(8,128)(2,1)} %get-tuple-element.21), channel_id=1, source_target_pairs={{0,6},{1,7},{2,0},{3,1},{4,2},{5,3},{6,4},{7,5},{8,14},{9,15},{10,... | collective-permute-start | bytes 196616 | tf_op jit(solution)/shard_map/ppermute | solution.py:221
  183.7 6.6 %collective-permute-start.27 = (bf16[1,512,64]{1,2,0:T(8,128)(2,1)}, bf16[1,512,64]{1,2,0:T(8,128)(2,1)S(1)}, u32[]{:S(2)}, u32[]{:S(2)}) collective-permute-start(bf16[1,512,64]{1,2,0:T(8,128)(2,1)} %get-tuple-element.20), channel_id=1, source_target_pairs={{0,7},{1,0},{2,1},{3,2},{4,3},{5,4},{6,5},{7,6},{8,15},{9,8},{10,9... | collective-permute-start | bytes 196616 | tf_op jit(solution)/shard_map/ppermute | solution.py:221
  184.7 53.0 %collective-permute-start.15 = (bf16[1,512,64]{1,2,0:T(8,128)(2,1)}, bf16[1,512,64]{1,2,0:T(8,128)(2,1)S(1)}, u32[]{:S(2)}, u32[]{:S(2)}) collective-permute-start(bf16[1,512,64]{1,2,0:T(8,128)(2,1)} %get-tuple-element.32), channel_id=1, source_target_pairs={{0,2},{1,3},{2,4},{3,5},{4,6},{5,7},{6,0},{7,1},{8,10},{9,11},{10,... | collective-permute-start | bytes 196616 | tf_op jit(solution)/shard_map/ppermute | solution.py:221
  186.6 51.3 %collective-permute-start.16 = (bf16[1,512,64]{1,2,0:T(8,128)(2,1)}, bf16[1,512,64]{1,2,0:T(8,128)(2,1)S(1)}, u32[]{:S(2)}, u32[]{:S(2)}) collective-permute-start(bf16[1,512,64]{1,2,0:T(8,128)(2,1)} %get-tuple-element.31), channel_id=1, source_target_pairs={{0,3},{1,4},{2,5},{3,6},{4,7},{5,0},{6,1},{7,2},{8,11},{9,12},{10,... | collective-permute-start | bytes 196616 | tf_op jit(solution)/shard_map/ppermute | solution.py:221
  187.3 50.7 %collective-permute-start.17 = (bf16[1,512,64]{1,2,0:T(8,128)(2,1)}, bf16[1,512,64]{1,2,0:T(8,128)(2,1)S(1)}, u32[]{:S(2)}, u32[]{:S(2)}) collective-permute-start(bf16[1,512,64]{1,2,0:T(8,128)(2,1)} %get-tuple-element.30), channel_id=1, source_target_pairs={{0,4},{1,5},{2,6},{3,7},{4,0},{5,1},{6,2},{7,3},{8,12},{9,13},{10,... | collective-permute-start | bytes 196616 | tf_op jit(solution)/shard_map/ppermute | solution.py:221
  190.1 47.8 %collective-permute-start.18 = (bf16[1,512,64]{1,2,0:T(8,128)(2,1)}, bf16[1,512,64]{1,2,0:T(8,128)(2,1)S(1)}, u32[]{:S(2)}, u32[]{:S(2)}) collective-permute-start(bf16[1,512,64]{1,2,0:T(8,128)(2,1)} %get-tuple-element.29), channel_id=1, source_target_pairs={{0,5},{1,6},{2,7},{3,0},{4,1},{5,2},{6,3},{7,4},{8,13},{9,14},{10,... | collective-permute-start | bytes 196616 | tf_op jit(solution)/shard_map/ppermute | solution.py:221
  190.3 47.7 %collective-permute-start.19 = (bf16[1,512,64]{1,2,0:T(8,128)(2,1)}, bf16[1,512,64]{1,2,0:T(8,128)(2,1)S(1)}, u32[]{:S(2)}, u32[]{:S(2)}) collective-permute-start(bf16[1,512,64]{1,2,0:T(8,128)(2,1)} %get-tuple-element.28), channel_id=1, source_target_pairs={{0,6},{1,7},{2,0},{3,1},{4,2},{5,3},{6,4},{7,5},{8,14},{9,15},{10,... | collective-permute-start | bytes 196616 | tf_op jit(solution)/shard_map/ppermute | solution.py:221
  229.1 24.7 %copy-start.6 = (bf16[8,512,2,64]{1,3,2,0:T(8,128)(2,1)S(1)}, bf16[8,512,2,64]{1,3,2,0:T(8,128)(2,1)}, u32[]{:S(2)}) copy-start(bf16[8,512,2,64]{1,3,2,0:T(8,128)(2,1)} %copy-done.5) | copy-start | bytes 3145732
  229.1 24.7 %all-to-all-start.3 = ((bf16[8,512,128]{2,1,0:T(8,128)(2,1)}), bf16[8,512,128]{2,1,0:T(8,128)(2,1)}, u32[]{:S(2)}, u32[]{:S(2)}) async-start(bf16[8,512,128]{2,1,0:T(8,128)(2,1)} %bitcast.72), calls=%async_computation.3 | async-start | bytes 2097152 | tf_op jit(solution)/shard_map/all_to_all | solution.py:310
  237.7 14.9 %collective-permute-start.20 = (bf16[1,512,64]{1,2,0:T(8,128)(2,1)S(1)}, bf16[1,512,64]{1,2,0:T(8,128)(2,1)S(1)}, u32[]{:S(2)}, u32[]{:S(2)}) collective-permute-start(bf16[1,512,64]{1,2,0:T(8,128)(2,1)S(1)} %get-tuple-element.27), channel_id=1, source_target_pairs={{0,7},{1,0},{2,1},{3,2},{4,3},{5,4},{6,5},{7,6},{8,15},{9,8},{10,9... | collective-permute-start | bytes 196616 | tf_op jit(solution)/shard_map/ppermute | solution.py:221
  253.9 2.7 %copy-start.3 = (bf16[512,512]{1,0:T(8,128)(2,1)S(1)}, bf16[512,512]{1,0:T(8,128)(2,1)}, u32[]{:S(2)}) copy-start(bf16[512,512]{1,0:T(8,128)(2,1)} %param.13) | copy-start | bytes 1572868
  253.9 2.0 copy-start.7

commit v11 on v10

--- a/solution.py
+++ b/solution.py
@@ -181,33 +181,48 @@
 
 
 def finish_kernel(ids_ref, acc_ref, ret_ref, out_ref, total_ref):
-    total_ref[...] = acc_ref[...]
+    step = pl.program_id(0)
+    chunk = ret_ref.shape[0]
+
+    @pl.when(step == 0)
+    def _():
+        total_ref[...] = acc_ref[...]
 
     def add_slot(j, carry):
-        i = ids_ref[j]
+        i = ids_ref[step * chunk + j]
         total_ref[i] = total_ref[i] + ret_ref[j].astype(jnp.float32)
         return carry
 
-    lax.fori_loop(0, ret_ref.shape[0], add_slot, 0, unroll=8)
+    lax.fori_loop(0, chunk, add_slot, 0, unroll=8)
 
     def emit(b, carry):
         out_ref[b] = total_ref[b].T.astype(jnp.bfloat16)
         return carry
 
-    lax.fori_loop(0, acc_ref.shape[0], emit, 0, unroll=4)
+    @pl.when(step == pl.num_programs(0) - 1)
+    def _():
+        lax.fori_loop(0, acc_ref.shape[0], emit, 0, unroll=4)
 
 
 def finish_grads(send_ids, acc, returned):
     nq, kvw, bsize = acc.shape
+    steps = 4
+    chunk = returned.shape[0] // steps
     smem = pl.BlockSpec(memory_space=pltpu.SMEM)
-    vmem = pl.BlockSpec(memory_space=pltpu.VMEM)
     return pl.pallas_call(
         finish_kernel,
+        grid=(steps,),
         out_shape=jax.ShapeDtypeStruct((nq, bsize, kvw), jnp.bfloat16),
-        in_specs=[smem, vmem, vmem],
-        out_specs=vmem,
+        in_specs=[
+            smem,
+            pl.BlockSpec(acc.shape, lambda i: (0, 0, 0)),
+            pl.BlockSpec((chunk,) + returned.shape[1:], lambda i: (i, 0, 0)),
+        ],
+        out_specs=pl.BlockSpec((nq, bsize, kvw), lambda i: (0, 0, 0)),
         scratch_shapes=[pltpu.VMEM(acc.shape, jnp.float32)],
-        compiler_params=pltpu.CompilerParams(vmem_limit_bytes=60 * 1024 * 1024),
+        compiler_params=pltpu.CompilerParams(
+            dimension_semantics=("arbitrary",), vmem_limit_bytes=60 * 1024 * 1024
+        ),
     )(send_ids, acc, returned)
 
 

time: 258 us -> 259 us (level)
  no operation moved by 1% of the time
where the time goes in v11:
time: 259 us; the launch traced here: 258 us
  waiting for transfers between devices  105 us (41%)
  starting transfers between devices  71.8 us (28%)
  Pallas kernels  53.3 us (21%)
  local copies, waits for them, and re-layouts  15.3 us (6%)
  matrix products  8.81 us (3%)
  other arithmetic  2.64 us (1%)
    all_to_all x1, waiting for transfers between devices, local(): lax.all_to_all(outgoing.reshape(ndom, pair_slots * bsize, 2 * hwide), 'do...  40.7 us
    ppermute x28, starting transfers between devices, head_exchange(): got = lax.ppermute(part, axis, perm)  37 us
    all_to_all x1, waiting for transfers between devices, local(): lax.all_to_all(slot_grads.reshape(ndom, pair_slots * 2 * hwide, bsize), '...  32.7 us
    pallas_call x1, Pallas kernels, fused_attention(): pl.pallas_call(lambda *refs: remote_kernel(*refs, near=near, far=far, bsi...  32.1 us
    ppermute x28, waiting for transfers between devices, head_exchange(): got = lax.ppermute(part, axis, perm)  20 us
    pallas_call x1, Pallas kernels, fused_attention(): pl.pallas_call(lambda *refs: local_kernel(*refs, near=near, bsize=bsize,...  15.6 us
    all_to_all x1, waiting for transfers between devices, local(): lax.all_to_all(kv_own, 'head', split_axis=0, concat_axis=0, tiled=True)  11.5 us
    all_to_all x1, starting transfers between devices, local(): lax.all_to_all(outgoing.reshape(ndom, pair_slots * bsize, 2 * hwide), 'do...  10.6 us
  transfers between devices with their start and end apart: 32, of which 9 were waited for; matrix products, arithmetic and copies ran while one was open for 6% of the time, Pallas kernels for 8%

profile of v11, /device:TPU:1, one launch (start us, length us, event | category | flops | bytes accessed | tf_op | source)
XLA Modules:
  0.0 258.1 jit_solution(920948639461837378)
XLA Ops:
  0.7 1.3 fusion.14
  2.0 0.2 slice-done
  2.2 0.5 copy.70
  2.8 1.0 copy-done.5
  3.8 1.8 fusion.3
  5.6 6.7 %all-to-all-start = ((bf16[8,512,128]{2,1,0:T(8,128)(2,1)}), bf16[8,512,128]{2,1,0:T(8,128)(2,1)S(1)}, u32[]{:S(2)}, u32[]{:S(2)}) async-start(bf16[8,512,128]{2,1,0:T(8,128)(2,1)} %fusion.3), calls=%async_computation | async-start | bytes 2097152 | tf_op jit(solution)/shard_map/all_to_all | solution.py:281
  12.3 0.1 reshape.92.ids_ref
  12.5 1.6 fusion.17
  14.2 1.5 fusion.7
  15.7 11.5 %all-to-all-done = bf16[8,512,128]{2,1,0:T(8,128)(2,1)S(1)} async-done(((bf16[8,512,128]{2,1,0:T(8,128)(2,1)}), bf16[8,512,128]{2,1,0:T(8,128)(2,1)S(1)}, u32[]{:S(2)}, u32[]{:S(2)}) %all-to-all-start) | async-done | bytes 1048608 | tf_op jit(solution)/shard_map/all_to_all | solution.py:281
  27.2 2.7 %gather_fusion = bf16[96,128,128]{2,1,0:T(8,128)(2,1)} fusion(bf16[32,128,128]{2,1,0:T(8,128)(2,1)S(1)} %bitcast.64, s32[1024]{0:T(1024)S(1)} %pad_clamp_fusion.1), kind=kCustom, calls=%fused_computation | custom fusion | bytes 6291840 | tf_op jit(solution)/shard_map/jit(_take)/gather | solution.py:288
  30.0 10.6 %all-to-all-start.1 = ((bf16[32,384,128]{2,1,0:T(8,128)(2,1)}), bf16[32,384,128]{2,1,0:T(8,128)(2,1)}, u32[]{:S(2)}, u32[]{:S(2)}) async-start(bf16[32,384,128]{2,1,0:T(8,128)(2,1)} %bitcast.67), calls=%async_computation.1 | async-start | bytes 6291456 | tf_op jit(solution)/shard_map/all_to_all | solution.py:292
  40.7 0.1 reshape.74.refs_1_
  40.9 0.1 lt.237
  41.1 1.2 gather_fusion.1
  42.6 0.7 copy.73
  43.4 0.6 reshape.73.refs_0_
  44.0 1.4 collective-permute-start.7
  45.5 1.3 collective-permute-done.7
  46.9 4.4 %collective-permute-start.9 = (bf16[1,512,64]{1,2,0:T(8,128)(2,1)S(1)}, bf16[1,512,64]{1,2,0:T(8,128)(2,1)S(1)}, u32[]{:S(2)}, u32[]{:S(2)}) collective-permute-start(bf16[1,512,64]{1,2,0:T(8,128)(2,1)S(1)} %get-tuple-element.38), channel_id=1, source_target_pairs={{0,3},{1,4},{2,5},{3,6},{4,7},{5,0},{6,1},{7,2},{8,11},{9,12},{10,... | collective-permute-start | bytes 196616 | tf_op jit(solution)/shard_map/ppermute | solution.py:236
  51.3 1.9 collective-permute-start.10
  53.3 2.9 %collective-permute-start.12 = (bf16[1,512,64]{1,2,0:T(8,128)(2,1)S(1)}, bf16[1,512,64]{1,2,0:T(8,128)(2,1)S(1)}, u32[]{:S(2)}, u32[]{:S(2)}) collective-permute-start(bf16[1,512,64]{1,2,0:T(8,128)(2,1)S(1)} %get-tuple-element.35), channel_id=1, source_target_pairs={{0,6},{1,7},{2,0},{3,1},{4,2},{5,3},{6,4},{7,5},{8,14},{9,15},{10,... | collective-permute-start | bytes 196616 | tf_op jit(solution)/shard_map/ppermute | solution.py:236
  56.2 1.5 collective-permute-start.13
  57.7 0.4 collective-permute-done.9
  58.1 2.0 collective-permute-start.2
  60.1 1.4 collective-permute-start.3
  61.5 1.1 collective-permute-start.4
  62.6 1.6 collective-permute-start.5
  64.2 1.3 copy.44
  65.6 1.6 collective-permute-start.6
  67.3 0.4 collective-permute-done.5
  67.7 2.0 collective-permute-done.6
  69.7 1.3 copy.43
  71.0 40.7 %all-to-all-done.1 = bf16[32,384,128]{2,1,0:T(8,128)(2,1)} async-done(((bf16[32,384,128]{2,1,0:T(8,128)(2,1)}), bf16[32,384,128]{2,1,0:T(8,128)(2,1)}, u32[]{:S(2)}, u32[]{:S(2)}) %all-to-all-start.1) | async-done | bytes 3145760 | tf_op jit(solution)/shard_map/all_to_all | solution.py:292
  111.7 32.1 %shard_map.104 = (bf16[32,128,64]{2,1,0:T(8,128)(2,1)}, f32[32,128,64]{2,1,0:T(8,128)}, f32[32,3,128]{2,1,0:T(4,128)}, bf16[96,128,128]{2,1,0:T(8,128)(2,1)}) custom-call(s32[128]{0:T(128)} %reshape.73.refs_0_, s32[128]{0:T(128)} %copy-done.9, bf16[32,128,64]{2,1,0:T(8,128)(2,1)} %bitcast.70, bf16[32,128,128]{2,1,0:T(8,128)(2,1)} %bitcast.65, ...), custom_call_target="tpu_custom_call" | custom-call | tf_op jit(solution)/shard_map/pallas_call | solution.py:146
  143.8 8.9 %all-to-all-start.2 = ((bf16[32,384,128]{2,1,0:T(8,128)(2,1)}), bf16[32,384,128]{2,1,0:T(8,128)(2,1)}, u32[]{:S(2)}, u32[]{:S(2)}) async-start(bf16[32,384,128]{2,1,0:T(8,128)(2,1)} %bitcast.75), calls=%async_computation.2 | async-start | bytes 6291456 | tf_op jit(solution)/shard_map/all_to_all | solution.py:317
  152.8 1.0 copy.42
  153.8 15.6 %shard_map.105 = (bf16[32,128,64]{2,1,0:T(8,128)(2,1)}, f32[32,128,128]{2,1,0:T(8,128)}) custom-call(s32[128]{0:T(128)} %reshape.73.refs_0_, bf16[32,128,64]{2,1,0:T(8,128)(2,1)} %bitcast.71, bf16[32,128,128]{2,1,0:T(8,128)(2,1)} %bitcast.66, bf16[32,128,64]{2,1,0:T(8,128)(2,1)} %bitcast.69, f32[32,3,128]{2,1,0:T(4,128)} %get-tuple-element.15.refs_4_, ...), custom_call_target="tpu_custom_call" | custom-call | tf_op jit(solution)/shard_map/pallas_call | solution.py:170
  169.4 1.5 copy.54
  170.9 0.8 constant_dynamic-slice_fusion
  171.7 1.5 collective-permute-start.21
  173.2 0.4 collective-permute-start.22
  173.6 1.7 collective-permute-start.23
  175.3 1.5 collective-permute-start.24
  176.8 2.6 %collective-permute-start.25 = (bf16[1,512,64]{1,2,0:T(8,128)(2,1)}, bf16[1,512,64]{1,2,0:T(8,128)(2,1)S(1)}, u32[]{:S(2)}, u32[]{:S(2)}) collective-permute-start(bf16[1,512,64]{1,2,0:T(8,128)(2,1)} %get-tuple-element.22), channel_id=1, source_target_pairs={{0,5},{1,6},{2,7},{3,0},{4,1},{5,2},{6,3},{7,4},{8,13},{9,14},{10,... | collective-permute-start | bytes 196616 | tf_op jit(solution)/shard_map/ppermute | solution.py:236
  179.5 0.3 copy.46
  179.8 0.7 constant_dynamic-slice_fusion.7
  180.5 0.3 collective-permute-start.14
  180.8 1.3 collective-permute-done.14
  182.2 1.5 collective-permute-start.26
  183.7 1.0 collective-permute-start.27
  184.7 1.8 collective-permute-start.15
  186.6 0.7 collective-permute-start.16
  187.3 2.8 %collective-permute-start.17 = (bf16[1,512,64]{1,2,0:T(8,128)(2,1)}, bf16[1,512,64]{1,2,0:T(8,128)(2,1)S(1)}, u32[]{:S(2)}, u32[]{:S(2)}) collective-permute-start(bf16[1,512,64]{1,2,0:T(8,128)(2,1)} %get-tuple-element.30), channel_id=1, source_target_pairs={{0,4},{1,5},{2,6},{3,7},{4,0},{5,1},{6,2},{7,3},{8,12},{9,13},{10,... | collective-permute-start | bytes 196616 | tf_op jit(solution)/shard_map/ppermute | solution.py:236
  190.3 1.0 collective-permute-start.19
  191.3 32.7 %all-to-all-done.2 = bf16[32,384,128]{2,1,0:T(8,128)(2,1)} async-done(((bf16[32,384,128]{2,1,0:T(8,128)(2,1)}), bf16[32,384,128]{2,1,0:T(8,128)(2,1)}, u32[]{:S(2)}, u32[]{:S(2)}) %all-to-all-start.2) | async-done | bytes 3145760 | tf_op jit(solution)/shard_map/all_to_all | solution.py:317
  224.0 5.6 %shard_map.106 = bf16[32,128,128]{2,1,0:T(8,128)(2,1)} custom-call(s32[96]{0:T(128)} %copy-done.8, f32[32,128,128]{2,1,0:T(8,128)} %get-tuple-element.18.acc_ref, bf16[96,128,128]{2,1,0:T(8,128)(2,1)} %bitcast.26.ret_ref), custom_call_target="tpu_custom_call" | custom-call | tf_op jit(solution)/shard_map/pallas_call | solution.py:212
  229.6 8.6 %all-to-all-start.3 = ((bf16[8,512,128]{2,1,0:T(8,128)(2,1)}), bf16[8,512,128]{2,1,0:T(8,128)(2,1)}, u32[]{:S(2)}, u32[]{:S(2)}) async-start(bf16[8,512,128]{2,1,0:T(8,128)(2,1)} %bitcast.72), calls=%async_computation.3 | async-start | bytes 2097152 | tf_op jit(solution)/shard_map/all_to_all | solution.py:325
  238.2 0.2 collective-permute-start.20
  238.5 14.6 %collective-permute-done.20 = bf16[1,512,64]{1,2,0:T(8,128)(2,1)S(1)} collective-permute-done((bf16[1,512,64]{1,2,0:T(8,128)(2,1)S(1)}, bf16[1,512,64]{1,2,0:T(8,128)(2,1)S(1)}, u32[]{:S(2)}, u32[]{:S(2)}) %collective-permute-start.20) | collective-permute-done | bytes 65568 | tf_op jit(solution)/shard_map/ppermute | solution.py:236
  253.1 1.3 fusion.6
  254.3 2.0 convolution_bitcast_fusion
  256.4 0.6 fusion.9
  257.0 1.1 fusion.13
  (104 shorter events, 1.4 us)
Async XLA Ops:
  0.6 13.5 %copy-start = (bf16[512,512]{1,0:T(8,128)(2,1)S(1)}, bf16[512,512]{1,0:T(8,128)(2,1)}, u32[]{:S(2)}) copy-start(bf16[512,512]{1,0:T(8,128)(2,1)} %param.12) | copy-start | bytes 1572868
  0.6 1.5 slice-start
  2.0 1.8 copy-start.2
  2.0 1.8 copy-start.12
  2.7 9.5 %copy-start.13 = (s32[1,32,3]{1,0,2:T(1,128)S(1)}, s32[1,32,3]{1,0,2:T(1,128)}, u32[]{:S(2)}) copy-start(s32[1,32,3]{1,0,2:T(1,128)} %param.16) | copy-start | bytes 1156
  2.8 1.0 copy-start.5
  5.6 21.7 %all-to-all-start = ((bf16[8,512,128]{2,1,0:T(8,128)(2,1)}), bf16[8,512,128]{2,1,0:T(8,128)(2,1)S(1)}, u32[]{:S(2)}, u32[]{:S(2)}) async-start(bf16[8,512,128]{2,1,0:T(8,128)(2,1)} %fusion.3), calls=%async_computation | async-start | bytes 2097152 | tf_op jit(solution)/shard_map/all_to_all | solution.py:281
  12.4 17.5 %copy-start.8 = (s32[96]{0:T(128)}, s32[96]{0:T(128)S(1)}, u32[]{:S(2)}) copy-start(s32[96]{0:T(128)S(1)} %reshape.92.ids_ref) | copy-start | bytes 1156
  27.2 2.7 %copy-start.1 = (bf16[8,512,128]{2,1,0:T(8,128)(2,1)}, bf16[8,512,128]{2,1,0:T(8,128)(2,1)S(1)}, u32[]{:S(2)}) copy-start(bf16[8,512,128]{2,1,0:T(8,128)(2,1)S(1)} %all-to-all-done) | copy-start | bytes 3145732
  30.0 10.7 %copy-start.10 = (s32[32,4]{0,1:T(4,128)S(1)}, s32[32,4]{0,1:T(4,128)}, u32[]{:S(2)}) copy-start(s32[32,4]{0,1:T(4,128)} %param.15) | copy-start | bytes 1540
  30.0 10.9 %copy-start.14 = (s32[32,1]{0,1:T(1,128)S(1)}, s32[32,1]{0,1:T(1,128)}, u32[]{:S(2)}) copy-start(s32[32,1]{0,1:T(1,128)} %param.17) | copy-start | bytes 388
  30.0 81.8 %all-to-all-start.1 = ((bf16[32,384,128]{2,1,0:T(8,128)(2,1)}), bf16[32,384,128]{2,1,0:T(8,128)(2,1)}, u32[]{:S(2)}, u32[]{:S(2)}) async-start(bf16[32,384,128]{2,1,0:T(8,128)(2,1)} %bitcast.67), calls=%async_computation.1 | async-start | bytes 6291456 | tf_op jit(solution)/shard_map/all_to_all | solution.py:292
  40.5 2.8 %copy-start.11 = (s32[32,4]{0,1:T(4,128)S(1)}, s32[32,4]{0,1:T(4,128)}, u32[]{:S(2)}) copy-start(s32[32,4]{0,1:T(4,128)} %param.14) | copy-start | bytes 1540
  40.8 15.3 %copy-start.9 = (s32[128]{0:T(128)}, s32[128]{0:T(128)S(1)}, u32[]{:S(2)}) copy-start(s32[128]{0:T(128)S(1)} %reshape.74.refs_1_) | copy-start | bytes 1540
  44.0 2.8 %collective-permute-start.7 = (bf16[1,512,64]{1,2,0:T(8,128)(2,1)S(1)}, bf16[1,512,64]{1,2,0:T(8,128)(2,1)S(1)}, u32[]{:S(2)}, u32[]{:S(2)}) collective-permute-start(bf16[1,512,64]{1,2,0:T(8,128)(2,1)S(1)} %constant_dynamic-slice_fusion.20), channel_id=1, source_target_pairs={{0,1},{1,2},{2,3},{3,4},{4,5},{5,6},{6,7},{7,0},{8,9},{9,10},{10,1... | collective-permute-start | bytes 196616 | tf_op jit(solution)/shard_map/ppermute | solution.py:236
  45.5 7.8 %collective-permute-start = (bf16[1,512,64]{1,2,0:T(8,128)(2,1)S(1)}, bf16[1,512,64]{1,2,0:T(8,128)(2,1)S(1)}, u32[]{:S(2)}, u32[]{:S(2)}) collective-permute-start(bf16[1,512,64]{1,2,0:T(8,128)(2,1)S(1)} %constant_dynamic-slice_fusion.27), channel_id=1, source_target_pairs={{0,1},{1,2},{2,3},{3,4},{4,5},{5,6},{6,7},{7,0},{8,9},{9,10},{10,1... | collective-permute-start | bytes 196616 | tf_op jit(solution)/shard_map/ppermute | solution.py:236
  46.8 9.4 %collective-permute-start.8 = (bf16[1,512,64]{1,2,0:T(8,128)(2,1)S(1)}, bf16[1,512,64]{1,2,0:T(8,128)(2,1)S(1)}, u32[]{:S(2)}, u32[]{:S(2)}) collective-permute-start(bf16[1,512,64]{1,2,0:T(8,128)(2,1)S(1)} %get-tuple-element.39), channel_id=1, source_target_pairs={{0,2},{1,3},{2,4},{3,5},{4,6},{5,7},{6,0},{7,1},{8,10},{9,11},{10,... | collective-permute-start | bytes 196616 | tf_op jit(solution)/shard_map/ppermute | solution.py:236
  46.9 11.2 %collective-permute-start.9 = (bf16[1,512,64]{1,2,0:T(8,128)(2,1)S(1)}, bf16[1,512,64]{1,2,0:T(8,128)(2,1)S(1)}, u32[]{:S(2)}, u32[]{:S(2)}) collective-permute-start(bf16[1,512,64]{1,2,0:T(8,128)(2,1)S(1)} %get-tuple-element.38), channel_id=1, source_target_pairs={{0,3},{1,4},{2,5},{3,6},{4,7},{5,0},{6,1},{7,2},{8,11},{9,12},{10,... | collective-permute-start | bytes 196616 | tf_op jit(solution)/shard_map/ppermute | solution.py:236
  51.3 6.8 %collective-permute-start.10 = (bf16[1,512,64]{1,2,0:T(8,128)(2,1)S(1)}, bf16[1,512,64]{1,2,0:T(8,128)(2,1)S(1)}, u32[]{:S(2)}, u32[]{:S(2)}) collective-permute-start(bf16[1,512,64]{1,2,0:T(8,128)(2,1)S(1)} %get-tuple-element.37), channel_id=1, source_target_pairs={{0,4},{1,5},{2,6},{3,7},{4,0},{5,1},{6,2},{7,3},{8,12},{9,13},{10,... | collective-permute-start | bytes 196616 | tf_op jit(solution)/shard_map/ppermute | solution.py:236
  53.2 6.9 %collective-permute-start.11 = (bf16[1,512,64]{1,2,0:T(8,128)(2,1)S(1)}, bf16[1,512,64]{1,2,0:T(8,128)(2,1)S(1)}, u32[]{:S(2)}, u32[]{:S(2)}) collective-permute-start(bf16[1,512,64]{1,2,0:T(8,128)(2,1)S(1)} %get-tuple-element.36), channel_id=1, source_target_pairs={{0,5},{1,6},{2,7},{3,0},{4,1},{5,2},{6,3},{7,4},{8,13},{9,14},{10,... | collective-permute-start | bytes 196616 | tf_op jit(solution)/shard_map/ppermute | solution.py:236
  53.3 8.3 %collective-permute-start.12 = (bf16[1,512,64]{1,2,0:T(8,128)(2,1)S(1)}, bf16[1,512,64]{1,2,0:T(8,128)(2,1)S(1)}, u32[]{:S(2)}, u32[]{:S(2)}) collective-permute-start(bf16[1,512,64]{1,2,0:T(8,128)(2,1)S(1)} %get-tuple-element.35), channel_id=1, source_target_pairs={{0,6},{1,7},{2,0},{3,1},{4,2},{5,3},{6,4},{7,5},{8,14},{9,15},{10,... | collective-permute-start | bytes 196616 | tf_op jit(solution)/shard_map/ppermute | solution.py:236
  56.2 6.4 %collective-permute-start.13 = (bf16[1,512,64]{1,2,0:T(8,128)(2,1)S(1)}, bf16[1,512,64]{1,2,0:T(8,128)(2,1)S(1)}, u32[]{:S(2)}, u32[]{:S(2)}) collective-permute-start(bf16[1,512,64]{1,2,0:T(8,128)(2,1)S(1)} %get-tuple-element.34), channel_id=1, source_target_pairs={{0,7},{1,0},{2,1},{3,2},{4,3},{5,4},{6,5},{7,6},{8,15},{9,8},{10,9... | collective-permute-start | bytes 196616 | tf_op jit(solution)/shard_map/ppermute | solution.py:236
  58.1 7.5 %collective-permute-start.1 = (bf16[1,512,64]{1,2,0:T(8,128)(2,1)S(1)}, bf16[1,512,64]{1,2,0:T(8,128)(2,1)S(1)}, u32[]{:S(2)}, u32[]{:S(2)}) collective-permute-start(bf16[1,512,64]{1,2,0:T(8,128)(2,1)S(1)} %get-tuple-element.46), channel_id=1, source_target_pairs={{0,2},{1,3},{2,4},{3,5},{4,6},{5,7},{6,0},{7,1},{8,10},{9,11},{10,... | collective-permute-start | bytes 196616 | tf_op jit(solution)/shard_map/ppermute | solution.py:236
  58.1 9.1 %collective-permute-start.2 = (bf16[1,512,64]{1,2,0:T(8,128)(2,1)S(1)}, bf16[1,512,64]{1,2,0:T(8,128)(2,1)S(1)}, u32[]{:S(2)}, u32[]{:S(2)}) collective-permute-start(bf16[1,512,64]{1,2,0:T(8,128)(2,1)S(1)} %get-tuple-element.45), channel_id=1, source_target_pairs={{0,3},{1,4},{2,5},{3,6},{4,7},{5,0},{6,1},{7,2},{8,11},{9,12},{10,... | collective-permute-start | bytes 196616 | tf_op jit(solution)/shard_map/ppermute | solution.py:236
  60.1 7.1 %collective-permute-start.3 = (bf16[1,512,64]{1,2,0:T(8,128)(2,1)S(1)}, bf16[1,512,64]{1,2,0:T(8,128)(2,1)S(1)}, u32[]{:S(2)}, u32[]{:S(2)}) collective-permute-start(bf16[1,512,64]{1,2,0:T(8,128)(2,1)S(1)} %get-tuple-element.44), channel_id=1, source_target_pairs={{0,4},{1,5},{2,6},{3,7},{4,0},{5,1},{6,2},{7,3},{8,12},{9,13},{10,... | collective-permute-start | bytes 196616 | tf_op jit(solution)/shard_map/ppermute | solution.py:236
  61.5 5.7 %collective-permute-start.4 = (bf16[1,512,64]{1,2,0:T(8,128)(2,1)S(1)}, bf16[1,512,64]{1,2,0:T(8,128)(2,1)S(1)}, u32[]{:S(2)}, u32[]{:S(2)}) collective-permute-start(bf16[1,512,64]{1,2,0:T(8,128)(2,1)S(1)} %get-tuple-element.43), channel_id=1, source_target_pairs={{0,5},{1,6},{2,7},{3,0},{4,1},{5,2},{6,3},{7,4},{8,13},{9,14},{10,... | collective-permute-start | bytes 196616 | tf_op jit(solution)/shard_map/ppermute | solution.py:236
  62.6 5.1 %collective-permute-start.5 = (bf16[1,512,64]{1,2,0:T(8,128)(2,1)S(1)}, bf16[1,512,64]{1,2,0:T(8,128)(2,1)S(1)}, u32[]{:S(2)}, u32[]{:S(2)}) collective-permute-start(bf16[1,512,64]{1,2,0:T(8,128)(2,1)S(1)} %get-tuple-element.42), channel_id=1, source_target_pairs={{0,6},{1,7},{2,0},{3,1},{4,2},{5,3},{6,4},{7,5},{8,14},{9,15},{10,... | collective-permute-start | bytes 196616 | tf_op jit(solution)/shard_map/ppermute | solution.py:236
  65.6 4.1 %collective-permute-start.6 = (bf16[1,512,64]{1,2,0:T(8,128)(2,1)S(1)}, bf16[1,512,64]{1,2,0:T(8,128)(2,1)S(1)}, u32[]{:S(2)}, u32[]{:S(2)}) collective-permute-start(bf16[1,512,64]{1,2,0:T(8,128)(2,1)S(1)} %get-tuple-element.41), channel_id=1, source_target_pairs={{0,7},{1,0},{2,1},{3,2},{4,3},{5,4},{6,5},{7,6},{8,15},{9,8},{10,9... | collective-permute-start | bytes 196616 | tf_op jit(solution)/shard_map/ppermute | solution.py:236
  143.8 9.0 %slice-start.1 = ((bf16[512,1536]{1,0:T(8,128)(2,1)}), bf16[512,512]{1,0:T(8,128)(2,1)S(1)}, s32[]{:S(2)}) async-start(bf16[512,1536]{1,0:T(8,128)(2,1)} %param.11), calls=%async_computation.5 | async-start | bytes 1048576 | tf_op jit(solution)/shard_map/slice | solution.py:272
  143.8 80.2 %all-to-all-start.2 = ((bf16[32,384,128]{2,1,0:T(8,128)(2,1)}), bf16[32,384,128]{2,1,0:T(8,128)(2,1)}, u32[]{:S(2)}, u32[]{:S(2)}) async-start(bf16[32,384,128]{2,1,0:T(8,128)(2,1)} %bitcast.75), calls=%async_computation.2 | async-start | bytes 6291456 | tf_op jit(solution)/shard_map/all_to_all | solution.py:317
  153.8 25.7 %copy-start.4 = (bf16[32,128,64]{2,1,0:T(8,128)(2,1)S(1)}, bf16[32,128,64]{2,1,0:T(8,128)(2,1)}, u32[]{:S(2)}) copy-start(bf16[32,128,64]{2,1,0:T(8,128)(2,1)} %get-tuple-element.14) | copy-start | bytes 1572868
  171.7 8.8 %collective-permute-start.21 = (bf16[1,512,64]{1,2,0:T(8,128)(2,1)}, bf16[1,512,64]{1,2,0:T(8,128)(2,1)S(1)}, u32[]{:S(2)}, u32[]{:S(2)}) collective-permute-start(bf16[1,512,64]{1,2,0:T(8,128)(2,1)} %get-tuple-element.26), channel_id=1, source_target_pairs={{0,1},{1,2},{2,3},{3,4},{4,5},{5,6},{6,7},{7,0},{8,9},{9,10},{10,1... | collective-permute-start | bytes 196616 | tf_op jit(solution)/shard_map/ppermute | solution.py:236
  173.2 10.4 %collective-permute-start.22 = (bf16[1,512,64]{1,2,0:T(8,128)(2,1)}, bf16[1,512,64]{1,2,0:T(8,128)(2,1)S(1)}, u32[]{:S(2)}, u32[]{:S(2)}) collective-permute-start(bf16[1,512,64]{1,2,0:T(8,128)(2,1)} %get-tuple-element.25), channel_id=1, source_target_pairs={{0,2},{1,3},{2,4},{3,5},{4,6},{5,7},{6,0},{7,1},{8,10},{9,11},{10,... | collective-permute-start | bytes 196616 | tf_op jit(solution)/shard_map/ppermute | solution.py:236
  173.6 11.1 %collective-permute-start.23 = (bf16[1,512,64]{1,2,0:T(8,128)(2,1)}, bf16[1,512,64]{1,2,0:T(8,128)(2,1)S(1)}, u32[]{:S(2)}, u32[]{:S(2)}) collective-permute-start(bf16[1,512,64]{1,2,0:T(8,128)(2,1)} %get-tuple-element.24), channel_id=1, source_target_pairs={{0,3},{1,4},{2,5},{3,6},{4,7},{5,0},{6,1},{7,2},{8,11},{9,12},{10,... | collective-permute-start | bytes 196616 | tf_op jit(solution)/shard_map/ppermute | solution.py:236
  175.3 11.2 %collective-permute-start.24 = (bf16[1,512,64]{1,2,0:T(8,128)(2,1)}, bf16[1,512,64]{1,2,0:T(8,128)(2,1)S(1)}, u32[]{:S(2)}, u32[]{:S(2)}) collective-permute-start(bf16[1,512,64]{1,2,0:T(8,128)(2,1)} %get-tuple-element.23), channel_id=1, source_target_pairs={{0,4},{1,5},{2,6},{3,7},{4,0},{5,1},{6,2},{7,3},{8,12},{9,13},{10,... | collective-permute-start | bytes 196616 | tf_op jit(solution)/shard_map/ppermute | solution.py:236
  176.8 10.4 %collective-permute-start.25 = (bf16[1,512,64]{1,2,0:T(8,128)(2,1)}, bf16[1,512,64]{1,2,0:T(8,128)(2,1)S(1)}, u32[]{:S(2)}, u32[]{:S(2)}) collective-permute-start(bf16[1,512,64]{1,2,0:T(8,128)(2,1)} %get-tuple-element.22), channel_id=1, source_target_pairs={{0,5},{1,6},{2,7},{3,0},{4,1},{5,2},{6,3},{7,4},{8,13},{9,14},{10,... | collective-permute-start | bytes 196616 | tf_op jit(solution)/shard_map/ppermute | solution.py:236
  180.5 1.6 collective-permute-start.14
  182.2 8.0 %collective-permute-start.26 = (bf16[1,512,64]{1,2,0:T(8,128)(2,1)}, bf16[1,512,64]{1,2,0:T(8,128)(2,1)S(1)}, u32[]{:S(2)}, u32[]{:S(2)}) collective-permute-start(bf16[1,512,64]{1,2,0:T(8,128)(2,1)} %get-tuple-element.21), channel_id=1, source_target_pairs={{0,6},{1,7},{2,0},{3,1},{4,2},{5,3},{6,4},{7,5},{8,14},{9,15},{10,... | collective-permute-start | bytes 196616 | tf_op jit(solution)/shard_map/ppermute | solution.py:236
  183.7 6.6 %collective-permute-start.27 = (bf16[1,512,64]{1,2,0:T(8,128)(2,1)}, bf16[1,512,64]{1,2,0:T(8,128)(2,1)S(1)}, u32[]{:S(2)}, u32[]{:S(2)}) collective-permute-start(bf16[1,512,64]{1,2,0:T(8,128)(2,1)} %get-tuple-element.20), channel_id=1, source_target_pairs={{0,7},{1,0},{2,1},{3,2},{4,3},{5,4},{6,5},{7,6},{8,15},{9,8},{10,9... | collective-permute-start | bytes 196616 | tf_op jit(solution)/shard_map/ppermute | solution.py:236
  184.7 53.5 %collective-permute-start.15 = (bf16[1,512,64]{1,2,0:T(8,128)(2,1)}, bf16[1,512,64]{1,2,0:T(8,128)(2,1)S(1)}, u32[]{:S(2)}, u32[]{:S(2)}) collective-permute-start(bf16[1,512,64]{1,2,0:T(8,128)(2,1)} %get-tuple-element.32), channel_id=1, source_target_pairs={{0,2},{1,3},{2,4},{3,5},{4,6},{5,7},{6,0},{7,1},{8,10},{9,11},{10,... | collective-permute-start | bytes 196616 | tf_op jit(solution)/shard_map/ppermute | solution.py:236
  186.6 51.8 %collective-permute-start.16 = (bf16[1,512,64]{1,2,0:T(8,128)(2,1)}, bf16[1,512,64]{1,2,0:T(8,128)(2,1)S(1)}, u32[]{:S(2)}, u32[]{:S(2)}) collective-permute-start(bf16[1,512,64]{1,2,0:T(8,128)(2,1)} %get-tuple-element.31), channel_id=1, source_target_pairs={{0,3},{1,4},{2,5},{3,6},{4,7},{5,0},{6,1},{7,2},{8,11},{9,12},{10,... | collective-permute-start | bytes 196616 | tf_op jit(solution)/shard_map/ppermute | solution.py:236
  187.3 51.1 %collective-permute-start.17 = (bf16[1,512,64]{1,2,0:T(8,128)(2,1)}, bf16[1,512,64]{1,2,0:T(8,128)(2,1)S(1)}, u32[]{:S(2)}, u32[]{:S(2)}) collective-permute-start(bf16[1,512,64]{1,2,0:T(8,128)(2,1)} %get-tuple-element.30), channel_id=1, source_target_pairs={{0,4},{1,5},{2,6},{3,7},{4,0},{5,1},{6,2},{7,3},{8,12},{9,13},{10,... | collective-permute-start | bytes 196616 | tf_op jit(solution)/shard_map/ppermute | solution.py:236
  190.1 48.3 %collective-permute-start.18 = (bf16[1,512,64]{1,2,0:T(8,128)(2,1)}, bf16[1,512,64]{1,2,0:T(8,128)(2,1)S(1)}, u32[]{:S(2)}, u32[]{:S(2)}) collective-permute-start(bf16[1,512,64]{1,2,0:T(8,128)(2,1)} %get-tuple-element.29), channel_id=1, source_target_pairs={{0,5},{1,6},{2,7},{3,0},{4,1},{5,2},{6,3},{7,4},{8,13},{9,14},{10,... | collective-permute-start | bytes 196616 | tf_op jit(solution)/shard_map/ppermute | solution.py:236
  190.3 48.2 %collective-permute-start.19 = (bf16[1,512,64]{1,2,0:T(8,128)(2,1)}, bf16[1,512,64]{1,2,0:T(8,128)(2,1)S(1)}, u32[]{:S(2)}, u32[]{:S(2)}) collective-permute-start(bf16[1,512,64]{1,2,0:T(8,128)(2,1)} %get-tuple-element.28), channel_id=1, source_target_pairs={{0,6},{1,7},{2,0},{3,1},{4,2},{5,3},{6,4},{7,5},{8,14},{9,15},{10,... | collective-permute-start | bytes 196616 | tf_op jit(solution)/shard_map/ppermute | solution.py:236
  229.6 24.7 %copy-start.6 = (bf16[8,512,2,64]{1,3,2,0:T(8,128)(2,1)S(1)}, bf16[8,512,2,64]{1,3,2,0:T(8,128)(2,1)}, u32[]{:S(2)}) copy-start(bf16[8,512,2,64]{1,3,2,0:T(8,128)(2,1)} %copy-done.5) | copy-start | bytes 3145732
  229.6 24.7 %all-to-all-start.3 = ((bf16[8,512,128]{2,1,0:T(8,128)(2,1)}), bf16[8,512,128]{2,1,0:T(8,128)(2,1)}, u32[]{:S(2)}, u32[]{:S(2)}) async-start(bf16[8,512,128]{2,1,0:T(8,128)(2,1)} %bitcast.72), calls=%async_computation.3 | async-start | bytes 2097152 | tf_op jit(solution)/shard_map/all_to_all | solution.py:325
  238.2 14.9 %collective-permute-start.20 = (bf16[1,512,64]{1,2,0:T(8,128)(2,1)S(1)}, bf16[1,512,64]{1,2,0:T(8,128)(2,1)S(1)}, u32[]{:S(2)}, u32[]{:S(2)}) collective-permute-start(bf16[1,512,64]{1,2,0:T(8,128)(2,1)S(1)} %get-tuple-element.27), channel_id=1, source_target_pairs={{0,7},{1,0},{2,1},{3,2},{4,3},{5,4},{6,5},{7,6},{8,15},{9,8},{10,9... | collective-permute-start | bytes 196616 | tf_op jit(solution)/shard_map/ppermute | solution.py:236
  254.3 2.7 %copy-start.3 = (bf16[512,512]{1,0:T(8,128)(2,1)S(1)}, bf16[512,512]{1,0:T(8,128)(2,1)}, u32[]{:S(2)}) copy-start(bf16[512,512]{1,0:T(8,128)(2,1)} %param.13) | copy-start | bytes 1572868
  254.3 2.0 copy-start.7

commit v12 on v10

--- a/solution.py
+++ b/solution.py
@@ -188,13 +188,13 @@
         total_ref[i] = total_ref[i] + ret_ref[j].astype(jnp.float32)
         return carry
 
-    lax.fori_loop(0, ret_ref.shape[0], add_slot, 0, unroll=8)
+    lax.fori_loop(0, ret_ref.shape[0], add_slot, 0, unroll=16)
 
     def emit(b, carry):
         out_ref[b] = total_ref[b].T.astype(jnp.bfloat16)
         return carry
 
-    lax.fori_loop(0, acc_ref.shape[0], emit, 0, unroll=4)
+    lax.fori_loop(0, acc_ref.shape[0], emit, 0, unroll=8)
 
 
 def finish_grads(send_ids, acc, returned):

time: 258 us -> 258 us (level)
  no operation moved by 1% of the time
where the time goes in v12:
time: 258 us; the launch traced here: 257 us
  waiting for transfers between devices  105 us (41%)
  starting transfers between devices  71.8 us (28%)
  Pallas kernels  52.5 us (20%)
  local copies, waits for them, and re-layouts  15.3 us (6%)
  matrix products  8.81 us (3%)
  other arithmetic  2.64 us (1%)
    all_to_all x1, waiting for transfers between devices, local(): lax.all_to_all(outgoing.reshape(ndom, pair_slots * bsize, 2 * hwide), 'do...  40.7 us
    ppermute x28, starting transfers between devices, head_exchange(): got = lax.ppermute(part, axis, perm)  37 us
    all_to_all x1, waiting for transfers between devices, local(): lax.all_to_all(slot_grads.reshape(ndom, pair_slots * 2 * hwide, bsize), '...  32.7 us
    pallas_call x1, Pallas kernels, fused_attention(): pl.pallas_call(lambda *refs: remote_kernel(*refs, near=near, far=far, bsi...  32.1 us
    ppermute x28, waiting for transfers between devices, head_exchange(): got = lax.ppermute(part, axis, perm)  20 us
    pallas_call x1, Pallas kernels, fused_attention(): pl.pallas_call(lambda *refs: local_kernel(*refs, near=near, bsize=bsize,...  15.6 us
    all_to_all x1, waiting for transfers between devices, local(): lax.all_to_all(kv_own, 'head', split_axis=0, concat_axis=0, tiled=True)  11.5 us
    all_to_all x1, starting transfers between devices, local(): lax.all_to_all(outgoing.reshape(ndom, pair_slots * bsize, 2 * hwide), 'do...  10.6 us
  transfers between devices with their start and end apart: 32, of which 9 were waited for; matrix products, arithmetic and copies ran while one was open for 6% of the time, Pallas kernels for 8%

profile of v12, /device:TPU:1, one launch (start us, length us, event | category | flops | bytes accessed | tf_op | source)
XLA Modules:
  0.0 257.4 jit_solution(11467894478474886670)
XLA Ops:
  0.7 1.3 fusion.14
  2.0 0.2 slice-done
  2.2 0.5 copy.70
  2.8 1.0 copy-done.5
  3.8 1.8 fusion.3
  5.6 6.7 %all-to-all-start = ((bf16[8,512,128]{2,1,0:T(8,128)(2,1)}), bf16[8,512,128]{2,1,0:T(8,128)(2,1)S(1)}, u32[]{:S(2)}, u32[]{:S(2)}) async-start(bf16[8,512,128]{2,1,0:T(8,128)(2,1)} %fusion.3), calls=%async_computation | async-start | bytes 2097152 | tf_op jit(solution)/shard_map/all_to_all | solution.py:266
  12.3 0.1 reshape.92.ids_ref
  12.5 1.6 fusion.17
  14.2 1.5 fusion.7
  15.7 11.5 %all-to-all-done = bf16[8,512,128]{2,1,0:T(8,128)(2,1)S(1)} async-done(((bf16[8,512,128]{2,1,0:T(8,128)(2,1)}), bf16[8,512,128]{2,1,0:T(8,128)(2,1)S(1)}, u32[]{:S(2)}, u32[]{:S(2)}) %all-to-all-start) | async-done | bytes 1048608 | tf_op jit(solution)/shard_map/all_to_all | solution.py:266
  27.2 2.7 %gather_fusion = bf16[96,128,128]{2,1,0:T(8,128)(2,1)} fusion(bf16[32,128,128]{2,1,0:T(8,128)(2,1)S(1)} %bitcast.64, s32[1024]{0:T(1024)S(1)} %pad_clamp_fusion.1), kind=kCustom, calls=%fused_computation | custom fusion | bytes 6291840 | tf_op jit(solution)/shard_map/jit(_take)/gather | solution.py:273
  30.0 10.6 %all-to-all-start.1 = ((bf16[32,384,128]{2,1,0:T(8,128)(2,1)}), bf16[32,384,128]{2,1,0:T(8,128)(2,1)}, u32[]{:S(2)}, u32[]{:S(2)}) async-start(bf16[32,384,128]{2,1,0:T(8,128)(2,1)} %bitcast.67), calls=%async_computation.1 | async-start | bytes 6291456 | tf_op jit(solution)/shard_map/all_to_all | solution.py:277
  40.7 0.1 reshape.74.refs_1_
  40.9 0.1 lt.237
  41.1 1.2 gather_fusion.1
  42.6 0.7 copy.73
  43.4 0.6 reshape.73.refs_0_
  44.0 1.4 collective-permute-start.7
  45.5 1.3 collective-permute-done.7
  46.9 4.4 %collective-permute-start.9 = (bf16[1,512,64]{1,2,0:T(8,128)(2,1)S(1)}, bf16[1,512,64]{1,2,0:T(8,128)(2,1)S(1)}, u32[]{:S(2)}, u32[]{:S(2)}) collective-permute-start(bf16[1,512,64]{1,2,0:T(8,128)(2,1)S(1)} %get-tuple-element.38), channel_id=1, source_target_pairs={{0,3},{1,4},{2,5},{3,6},{4,7},{5,0},{6,1},{7,2},{8,11},{9,12},{10,... | collective-permute-start | bytes 196616 | tf_op jit(solution)/shard_map/ppermute | solution.py:221
  51.3 1.9 collective-permute-start.10
  53.3 2.9 %collective-permute-start.12 = (bf16[1,512,64]{1,2,0:T(8,128)(2,1)S(1)}, bf16[1,512,64]{1,2,0:T(8,128)(2,1)S(1)}, u32[]{:S(2)}, u32[]{:S(2)}) collective-permute-start(bf16[1,512,64]{1,2,0:T(8,128)(2,1)S(1)} %get-tuple-element.35), channel_id=1, source_target_pairs={{0,6},{1,7},{2,0},{3,1},{4,2},{5,3},{6,4},{7,5},{8,14},{9,15},{10,... | collective-permute-start | bytes 196616 | tf_op jit(solution)/shard_map/ppermute | solution.py:221
  56.2 1.5 collective-permute-start.13
  57.7 0.4 collective-permute-done.9
  58.1 2.0 collective-permute-start.2
  60.1 1.4 collective-permute-start.3
  61.5 1.1 collective-permute-start.4
  62.6 1.6 collective-permute-start.5
  64.2 1.3 copy.44
  65.6 1.6 collective-permute-start.6
  67.3 0.4 collective-permute-done.5
  67.7 2.0 collective-permute-done.6
  69.7 1.3 copy.43
  71.0 40.7 %all-to-all-done.1 = bf16[32,384,128]{2,1,0:T(8,128)(2,1)} async-done(((bf16[32,384,128]{2,1,0:T(8,128)(2,1)}), bf16[32,384,128]{2,1,0:T(8,128)(2,1)}, u32[]{:S(2)}, u32[]{:S(2)}) %all-to-all-start.1) | async-done | bytes 3145760 | tf_op jit(solution)/shard_map/all_to_all | solution.py:277
  111.7 32.1 %shard_map.104 = (bf16[32,128,64]{2,1,0:T(8,128)(2,1)}, f32[32,128,64]{2,1,0:T(8,128)}, f32[32,3,128]{2,1,0:T(4,128)}, bf16[96,128,128]{2,1,0:T(8,128)(2,1)}) custom-call(s32[128]{0:T(128)} %reshape.73.refs_0_, s32[128]{0:T(128)} %copy-done.9, bf16[32,128,64]{2,1,0:T(8,128)(2,1)} %bitcast.70, bf16[32,128,128]{2,1,0:T(8,128)(2,1)} %bitcast.65, ...), custom_call_target="tpu_custom_call" | custom-call | tf_op jit(solution)/shard_map/pallas_call | solution.py:146
  143.8 8.9 %all-to-all-start.2 = ((bf16[32,384,128]{2,1,0:T(8,128)(2,1)}), bf16[32,384,128]{2,1,0:T(8,128)(2,1)}, u32[]{:S(2)}, u32[]{:S(2)}) async-start(bf16[32,384,128]{2,1,0:T(8,128)(2,1)} %bitcast.75), calls=%async_computation.2 | async-start | bytes 6291456 | tf_op jit(solution)/shard_map/all_to_all | solution.py:302
  152.8 1.0 copy.42
  153.8 15.6 %shard_map.105 = (bf16[32,128,64]{2,1,0:T(8,128)(2,1)}, f32[32,128,128]{2,1,0:T(8,128)}) custom-call(s32[128]{0:T(128)} %reshape.73.refs_0_, bf16[32,128,64]{2,1,0:T(8,128)(2,1)} %bitcast.71, bf16[32,128,128]{2,1,0:T(8,128)(2,1)} %bitcast.66, bf16[32,128,64]{2,1,0:T(8,128)(2,1)} %bitcast.69, f32[32,3,128]{2,1,0:T(4,128)} %get-tuple-element.15.refs_4_, ...), custom_call_target="tpu_custom_call" | custom-call | tf_op jit(solution)/shard_map/pallas_call | solution.py:170
  169.4 1.5 copy.54
  170.9 0.8 constant_dynamic-slice_fusion
  171.7 1.5 collective-permute-start.21
  173.2 0.4 collective-permute-start.22
  173.6 1.7 collective-permute-start.23
  175.3 1.5 collective-permute-start.24
  176.8 2.6 %collective-permute-start.25 = (bf16[1,512,64]{1,2,0:T(8,128)(2,1)}, bf16[1,512,64]{1,2,0:T(8,128)(2,1)S(1)}, u32[]{:S(2)}, u32[]{:S(2)}) collective-permute-start(bf16[1,512,64]{1,2,0:T(8,128)(2,1)} %get-tuple-element.22), channel_id=1, source_target_pairs={{0,5},{1,6},{2,7},{3,0},{4,1},{5,2},{6,3},{7,4},{8,13},{9,14},{10,... | collective-permute-start | bytes 196616 | tf_op jit(solution)/shard_map/ppermute | solution.py:221
  179.5 0.3 copy.46
  179.8 0.7 constant_dynamic-slice_fusion.7
  180.5 0.3 collective-permute-start.14
  180.8 1.3 collective-permute-done.14
  182.2 1.5 collective-permute-start.26
  183.7 1.0 collective-permute-start.27
  184.7 1.8 collective-permute-start.15
  186.6 0.7 collective-permute-start.16
  187.3 2.8 %collective-permute-start.17 = (bf16[1,512,64]{1,2,0:T(8,128)(2,1)}, bf16[1,512,64]{1,2,0:T(8,128)(2,1)S(1)}, u32[]{:S(2)}, u32[]{:S(2)}) collective-permute-start(bf16[1,512,64]{1,2,0:T(8,128)(2,1)} %get-tuple-element.30), channel_id=1, source_target_pairs={{0,4},{1,5},{2,6},{3,7},{4,0},{5,1},{6,2},{7,3},{8,12},{9,13},{10,... | collective-permute-start | bytes 196616 | tf_op jit(solution)/shard_map/ppermute | solution.py:221
  190.3 1.0 collective-permute-start.19
  191.3 32.7 %all-to-all-done.2 = bf16[32,384,128]{2,1,0:T(8,128)(2,1)} async-done(((bf16[32,384,128]{2,1,0:T(8,128)(2,1)}), bf16[32,384,128]{2,1,0:T(8,128)(2,1)}, u32[]{:S(2)}, u32[]{:S(2)}) %all-to-all-start.2) | async-done | bytes 3145760 | tf_op jit(solution)/shard_map/all_to_all | solution.py:302
  224.0 4.9 %shard_map.106 = bf16[32,128,128]{2,1,0:T(8,128)(2,1)} custom-call(s32[96]{0:T(128)} %copy-done.8, f32[32,128,128]{2,1,0:T(8,128)} %get-tuple-element.18.acc_ref, bf16[96,128,128]{2,1,0:T(8,128)(2,1)} %bitcast.26.ret_ref), custom_call_target="tpu_custom_call" | custom-call | tf_op jit(solution)/shard_map/pallas_call | solution.py:204
  228.9 8.6 %all-to-all-start.3 = ((bf16[8,512,128]{2,1,0:T(8,128)(2,1)}), bf16[8,512,128]{2,1,0:T(8,128)(2,1)}, u32[]{:S(2)}, u32[]{:S(2)}) async-start(bf16[8,512,128]{2,1,0:T(8,128)(2,1)} %bitcast.72), calls=%async_computation.3 | async-start | bytes 2097152 | tf_op jit(solution)/shard_map/all_to_all | solution.py:310
  237.5 0.2 collective-permute-start.20
  237.7 14.6 %collective-permute-done.20 = bf16[1,512,64]{1,2,0:T(8,128)(2,1)S(1)} collective-permute-done((bf16[1,512,64]{1,2,0:T(8,128)(2,1)S(1)}, bf16[1,512,64]{1,2,0:T(8,128)(2,1)S(1)}, u32[]{:S(2)}, u32[]{:S(2)}) %collective-permute-start.20) | collective-permute-done | bytes 65568 | tf_op jit(solution)/shard_map/ppermute | solution.py:221
  252.3 1.3 fusion.6
  253.6 2.0 convolution_bitcast_fusion
  255.6 0.6 fusion.9
  256.2 1.1 fusion.13
  (104 shorter events, 1.4 us)
Async XLA Ops:
  0.6 13.5 %copy-start = (bf16[512,512]{1,0:T(8,128)(2,1)S(1)}, bf16[512,512]{1,0:T(8,128)(2,1)}, u32[]{:S(2)}) copy-start(bf16[512,512]{1,0:T(8,128)(2,1)} %param.12) | copy-start | bytes 1572868
  0.6 1.5 slice-start
  2.0 1.8 copy-start.2
  2.0 1.8 copy-start.12
  2.7 9.5 %copy-start.13 = (s32[1,32,3]{1,0,2:T(1,128)S(1)}, s32[1,32,3]{1,0,2:T(1,128)}, u32[]{:S(2)}) copy-start(s32[1,32,3]{1,0,2:T(1,128)} %param.16) | copy-start | bytes 1156
  2.8 1.0 copy-start.5
  5.6 21.7 %all-to-all-start = ((bf16[8,512,128]{2,1,0:T(8,128)(2,1)}), bf16[8,512,128]{2,1,0:T(8,128)(2,1)S(1)}, u32[]{:S(2)}, u32[]{:S(2)}) async-start(bf16[8,512,128]{2,1,0:T(8,128)(2,1)} %fusion.3), calls=%async_computation | async-start | bytes 2097152 | tf_op jit(solution)/shard_map/all_to_all | solution.py:266
  12.4 17.5 %copy-start.8 = (s32[96]{0:T(128)}, s32[96]{0:T(128)S(1)}, u32[]{:S(2)}) copy-start(s32[96]{0:T(128)S(1)} %reshape.92.ids_ref) | copy-start | bytes 1156
  27.2 2.7 %copy-start.1 = (bf16[8,512,128]{2,1,0:T(8,128)(2,1)}, bf16[8,512,128]{2,1,0:T(8,128)(2,1)S(1)}, u32[]{:S(2)}) copy-start(bf16[8,512,128]{2,1,0:T(8,128)(2,1)S(1)} %all-to-all-done) | copy-start | bytes 3145732
  30.0 10.7 %copy-start.10 = (s32[32,4]{0,1:T(4,128)S(1)}, s32[32,4]{0,1:T(4,128)}, u32[]{:S(2)}) copy-start(s32[32,4]{0,1:T(4,128)} %param.15) | copy-start | bytes 1540
  30.0 10.9 %copy-start.14 = (s32[32,1]{0,1:T(1,128)S(1)}, s32[32,1]{0,1:T(1,128)}, u32[]{:S(2)}) copy-start(s32[32,1]{0,1:T(1,128)} %param.17) | copy-start | bytes 388
  30.0 81.8 %all-to-all-start.1 = ((bf16[32,384,128]{2,1,0:T(8,128)(2,1)}), bf16[32,384,128]{2,1,0:T(8,128)(2,1)}, u32[]{:S(2)}, u32[]{:S(2)}) async-start(bf16[32,384,128]{2,1,0:T(8,128)(2,1)} %bitcast.67), calls=%async_computation.1 | async-start | bytes 6291456 | tf_op jit(solution)/shard_map/all_to_all | solution.py:277
  40.5 2.8 %copy-start.11 = (s32[32,4]{0,1:T(4,128)S(1)}, s32[32,4]{0,1:T(4,128)}, u32[]{:S(2)}) copy-start(s32[32,4]{0,1:T(4,128)} %param.14) | copy-start | bytes 1540
  40.8 15.3 %copy-start.9 = (s32[128]{0:T(128)}, s32[128]{0:T(128)S(1)}, u32[]{:S(2)}) copy-start(s32[128]{0:T(128)S(1)} %reshape.74.refs_1_) | copy-start | bytes 1540
  44.0 2.8 %collective-permute-start.7 = (bf16[1,512,64]{1,2,0:T(8,128)(2,1)S(1)}, bf16[1,512,64]{1,2,0:T(8,128)(2,1)S(1)}, u32[]{:S(2)}, u32[]{:S(2)}) collective-permute-start(bf16[1,512,64]{1,2,0:T(8,128)(2,1)S(1)} %constant_dynamic-slice_fusion.20), channel_id=1, source_target_pairs={{0,1},{1,2},{2,3},{3,4},{4,5},{5,6},{6,7},{7,0},{8,9},{9,10},{10,1... | collective-permute-start | bytes 196616 | tf_op jit(solution)/shard_map/ppermute | solution.py:221
  45.5 7.8 %collective-permute-start = (bf16[1,512,64]{1,2,0:T(8,128)(2,1)S(1)}, bf16[1,512,64]{1,2,0:T(8,128)(2,1)S(1)}, u32[]{:S(2)}, u32[]{:S(2)}) collective-permute-start(bf16[1,512,64]{1,2,0:T(8,128)(2,1)S(1)} %constant_dynamic-slice_fusion.27), channel_id=1, source_target_pairs={{0,1},{1,2},{2,3},{3,4},{4,5},{5,6},{6,7},{7,0},{8,9},{9,10},{10,1... | collective-permute-start | bytes 196616 | tf_op jit(solution)/shard_map/ppermute | solution.py:221
  46.8 9.4 %collective-permute-start.8 = (bf16[1,512,64]{1,2,0:T(8,128)(2,1)S(1)}, bf16[1,512,64]{1,2,0:T(8,128)(2,1)S(1)}, u32[]{:S(2)}, u32[]{:S(2)}) collective-permute-start(bf16[1,512,64]{1,2,0:T(8,128)(2,1)S(1)} %get-tuple-element.39), channel_id=1, source_target_pairs={{0,2},{1,3},{2,4},{3,5},{4,6},{5,7},{6,0},{7,1},{8,10},{9,11},{10,... | collective-permute-start | bytes 196616 | tf_op jit(solution)/shard_map/ppermute | solution.py:221
  46.9 11.2 %collective-permute-start.9 = (bf16[1,512,64]{1,2,0:T(8,128)(2,1)S(1)}, bf16[1,512,64]{1,2,0:T(8,128)(2,1)S(1)}, u32[]{:S(2)}, u32[]{:S(2)}) collective-permute-start(bf16[1,512,64]{1,2,0:T(8,128)(2,1)S(1)} %get-tuple-element.38), channel_id=1, source_target_pairs={{0,3},{1,4},{2,5},{3,6},{4,7},{5,0},{6,1},{7,2},{8,11},{9,12},{10,... | collective-permute-start | bytes 196616 | tf_op jit(solution)/shard_map/ppermute | solution.py:221
  51.3 6.8 %collective-permute-start.10 = (bf16[1,512,64]{1,2,0:T(8,128)(2,1)S(1)}, bf16[1,512,64]{1,2,0:T(8,128)(2,1)S(1)}, u32[]{:S(2)}, u32[]{:S(2)}) collective-permute-start(bf16[1,512,64]{1,2,0:T(8,128)(2,1)S(1)} %get-tuple-element.37), channel_id=1, source_target_pairs={{0,4},{1,5},{2,6},{3,7},{4,0},{5,1},{6,2},{7,3},{8,12},{9,13},{10,... | collective-permute-start | bytes 196616 | tf_op jit(solution)/shard_map/ppermute | solution.py:221
  53.2 6.9 %collective-permute-start.11 = (bf16[1,512,64]{1,2,0:T(8,128)(2,1)S(1)}, bf16[1,512,64]{1,2,0:T(8,128)(2,1)S(1)}, u32[]{:S(2)}, u32[]{:S(2)}) collective-permute-start(bf16[1,512,64]{1,2,0:T(8,128)(2,1)S(1)} %get-tuple-element.36), channel_id=1, source_target_pairs={{0,5},{1,6},{2,7},{3,0},{4,1},{5,2},{6,3},{7,4},{8,13},{9,14},{10,... | collective-permute-start | bytes 196616 | tf_op jit(solution)/shard_map/ppermute | solution.py:221
  53.3 8.3 %collective-permute-start.12 = (bf16[1,512,64]{1,2,0:T(8,128)(2,1)S(1)}, bf16[1,512,64]{1,2,0:T(8,128)(2,1)S(1)}, u32[]{:S(2)}, u32[]{:S(2)}) collective-permute-start(bf16[1,512,64]{1,2,0:T(8,128)(2,1)S(1)} %get-tuple-element.35), channel_id=1, source_target_pairs={{0,6},{1,7},{2,0},{3,1},{4,2},{5,3},{6,4},{7,5},{8,14},{9,15},{10,... | collective-permute-start | bytes 196616 | tf_op jit(solution)/shard_map/ppermute | solution.py:221
  56.2 6.4 %collective-permute-start.13 = (bf16[1,512,64]{1,2,0:T(8,128)(2,1)S(1)}, bf16[1,512,64]{1,2,0:T(8,128)(2,1)S(1)}, u32[]{:S(2)}, u32[]{:S(2)}) collective-permute-start(bf16[1,512,64]{1,2,0:T(8,128)(2,1)S(1)} %get-tuple-element.34), channel_id=1, source_target_pairs={{0,7},{1,0},{2,1},{3,2},{4,3},{5,4},{6,5},{7,6},{8,15},{9,8},{10,9... | collective-permute-start | bytes 196616 | tf_op jit(solution)/shard_map/ppermute | solution.py:221
  58.1 7.5 %collective-permute-start.1 = (bf16[1,512,64]{1,2,0:T(8,128)(2,1)S(1)}, bf16[1,512,64]{1,2,0:T(8,128)(2,1)S(1)}, u32[]{:S(2)}, u32[]{:S(2)}) collective-permute-start(bf16[1,512,64]{1,2,0:T(8,128)(2,1)S(1)} %get-tuple-element.46), channel_id=1, source_target_pairs={{0,2},{1,3},{2,4},{3,5},{4,6},{5,7},{6,0},{7,1},{8,10},{9,11},{10,... | collective-permute-start | bytes 196616 | tf_op jit(solution)/shard_map/ppermute | solution.py:221
  58.1 9.1 %collective-permute-start.2 = (bf16[1,512,64]{1,2,0:T(8,128)(2,1)S(1)}, bf16[1,512,64]{1,2,0:T(8,128)(2,1)S(1)}, u32[]{:S(2)}, u32[]{:S(2)}) collective-permute-start(bf16[1,512,64]{1,2,0:T(8,128)(2,1)S(1)} %get-tuple-element.45), channel_id=1, source_target_pairs={{0,3},{1,4},{2,5},{3,6},{4,7},{5,0},{6,1},{7,2},{8,11},{9,12},{10,... | collective-permute-start | bytes 196616 | tf_op jit(solution)/shard_map/ppermute | solution.py:221
  60.1 7.1 %collective-permute-start.3 = (bf16[1,512,64]{1,2,0:T(8,128)(2,1)S(1)}, bf16[1,512,64]{1,2,0:T(8,128)(2,1)S(1)}, u32[]{:S(2)}, u32[]{:S(2)}) collective-permute-start(bf16[1,512,64]{1,2,0:T(8,128)(2,1)S(1)} %get-tuple-element.44), channel_id=1, source_target_pairs={{0,4},{1,5},{2,6},{3,7},{4,0},{5,1},{6,2},{7,3},{8,12},{9,13},{10,... | collective-permute-start | bytes 196616 | tf_op jit(solution)/shard_map/ppermute | solution.py:221
  61.5 5.7 %collective-permute-start.4 = (bf16[1,512,64]{1,2,0:T(8,128)(2,1)S(1)}, bf16[1,512,64]{1,2,0:T(8,128)(2,1)S(1)}, u32[]{:S(2)}, u32[]{:S(2)}) collective-permute-start(bf16[1,512,64]{1,2,0:T(8,128)(2,1)S(1)} %get-tuple-element.43), channel_id=1, source_target_pairs={{0,5},{1,6},{2,7},{3,0},{4,1},{5,2},{6,3},{7,4},{8,13},{9,14},{10,... | collective-permute-start | bytes 196616 | tf_op jit(solution)/shard_map/ppermute | solution.py:221
  62.6 5.1 %collective-permute-start.5 = (bf16[1,512,64]{1,2,0:T(8,128)(2,1)S(1)}, bf16[1,512,64]{1,2,0:T(8,128)(2,1)S(1)}, u32[]{:S(2)}, u32[]{:S(2)}) collective-permute-start(bf16[1,512,64]{1,2,0:T(8,128)(2,1)S(1)} %get-tuple-element.42), channel_id=1, source_target_pairs={{0,6},{1,7},{2,0},{3,1},{4,2},{5,3},{6,4},{7,5},{8,14},{9,15},{10,... | collective-permute-start | bytes 196616 | tf_op jit(solution)/shard_map/ppermute | solution.py:221
  65.6 4.1 %collective-permute-start.6 = (bf16[1,512,64]{1,2,0:T(8,128)(2,1)S(1)}, bf16[1,512,64]{1,2,0:T(8,128)(2,1)S(1)}, u32[]{:S(2)}, u32[]{:S(2)}) collective-permute-start(bf16[1,512,64]{1,2,0:T(8,128)(2,1)S(1)} %get-tuple-element.41), channel_id=1, source_target_pairs={{0,7},{1,0},{2,1},{3,2},{4,3},{5,4},{6,5},{7,6},{8,15},{9,8},{10,9... | collective-permute-start | bytes 196616 | tf_op jit(solution)/shard_map/ppermute | solution.py:221
  143.8 9.0 %slice-start.1 = ((bf16[512,1536]{1,0:T(8,128)(2,1)}), bf16[512,512]{1,0:T(8,128)(2,1)S(1)}, s32[]{:S(2)}) async-start(bf16[512,1536]{1,0:T(8,128)(2,1)} %param.11), calls=%async_computation.5 | async-start | bytes 1048576 | tf_op jit(solution)/shard_map/slice | solution.py:257
  143.8 80.2 %all-to-all-start.2 = ((bf16[32,384,128]{2,1,0:T(8,128)(2,1)}), bf16[32,384,128]{2,1,0:T(8,128)(2,1)}, u32[]{:S(2)}, u32[]{:S(2)}) async-start(bf16[32,384,128]{2,1,0:T(8,128)(2,1)} %bitcast.75), calls=%async_computation.2 | async-start | bytes 6291456 | tf_op jit(solution)/shard_map/all_to_all | solution.py:302
  153.8 25.7 %copy-start.4 = (bf16[32,128,64]{2,1,0:T(8,128)(2,1)S(1)}, bf16[32,128,64]{2,1,0:T(8,128)(2,1)}, u32[]{:S(2)}) copy-start(bf16[32,128,64]{2,1,0:T(8,128)(2,1)} %get-tuple-element.14) | copy-start | bytes 1572868
  171.7 8.8 %collective-permute-start.21 = (bf16[1,512,64]{1,2,0:T(8,128)(2,1)}, bf16[1,512,64]{1,2,0:T(8,128)(2,1)S(1)}, u32[]{:S(2)}, u32[]{:S(2)}) collective-permute-start(bf16[1,512,64]{1,2,0:T(8,128)(2,1)} %get-tuple-element.26), channel_id=1, source_target_pairs={{0,1},{1,2},{2,3},{3,4},{4,5},{5,6},{6,7},{7,0},{8,9},{9,10},{10,1... | collective-permute-start | bytes 196616 | tf_op jit(solution)/shard_map/ppermute | solution.py:221
  173.2 10.4 %collective-permute-start.22 = (bf16[1,512,64]{1,2,0:T(8,128)(2,1)}, bf16[1,512,64]{1,2,0:T(8,128)(2,1)S(1)}, u32[]{:S(2)}, u32[]{:S(2)}) collective-permute-start(bf16[1,512,64]{1,2,0:T(8,128)(2,1)} %get-tuple-element.25), channel_id=1, source_target_pairs={{0,2},{1,3},{2,4},{3,5},{4,6},{5,7},{6,0},{7,1},{8,10},{9,11},{10,... | collective-permute-start | bytes 196616 | tf_op jit(solution)/shard_map/ppermute | solution.py:221
  173.6 11.1 %collective-permute-start.23 = (bf16[1,512,64]{1,2,0:T(8,128)(2,1)}, bf16[1,512,64]{1,2,0:T(8,128)(2,1)S(1)}, u32[]{:S(2)}, u32[]{:S(2)}) collective-permute-start(bf16[1,512,64]{1,2,0:T(8,128)(2,1)} %get-tuple-element.24), channel_id=1, source_target_pairs={{0,3},{1,4},{2,5},{3,6},{4,7},{5,0},{6,1},{7,2},{8,11},{9,12},{10,... | collective-permute-start | bytes 196616 | tf_op jit(solution)/shard_map/ppermute | solution.py:221
  175.3 11.2 %collective-permute-start.24 = (bf16[1,512,64]{1,2,0:T(8,128)(2,1)}, bf16[1,512,64]{1,2,0:T(8,128)(2,1)S(1)}, u32[]{:S(2)}, u32[]{:S(2)}) collective-permute-start(bf16[1,512,64]{1,2,0:T(8,128)(2,1)} %get-tuple-element.23), channel_id=1, source_target_pairs={{0,4},{1,5},{2,6},{3,7},{4,0},{5,1},{6,2},{7,3},{8,12},{9,13},{10,... | collective-permute-start | bytes 196616 | tf_op jit(solution)/shard_map/ppermute | solution.py:221
  176.8 10.4 %collective-permute-start.25 = (bf16[1,512,64]{1,2,0:T(8,128)(2,1)}, bf16[1,512,64]{1,2,0:T(8,128)(2,1)S(1)}, u32[]{:S(2)}, u32[]{:S(2)}) collective-permute-start(bf16[1,512,64]{1,2,0:T(8,128)(2,1)} %get-tuple-element.22), channel_id=1, source_target_pairs={{0,5},{1,6},{2,7},{3,0},{4,1},{5,2},{6,3},{7,4},{8,13},{9,14},{10,... | collective-permute-start | bytes 196616 | tf_op jit(solution)/shard_map/ppermute | solution.py:221
  180.5 1.6 collective-permute-start.14
  182.2 8.0 %collective-permute-start.26 = (bf16[1,512,64]{1,2,0:T(8,128)(2,1)}, bf16[1,512,64]{1,2,0:T(8,128)(2,1)S(1)}, u32[]{:S(2)}, u32[]{:S(2)}) collective-permute-start(bf16[1,512,64]{1,2,0:T(8,128)(2,1)} %get-tuple-element.21), channel_id=1, source_target_pairs={{0,6},{1,7},{2,0},{3,1},{4,2},{5,3},{6,4},{7,5},{8,14},{9,15},{10,... | collective-permute-start | bytes 196616 | tf_op jit(solution)/shard_map/ppermute | solution.py:221
  183.7 6.6 %collective-permute-start.27 = (bf16[1,512,64]{1,2,0:T(8,128)(2,1)}, bf16[1,512,64]{1,2,0:T(8,128)(2,1)S(1)}, u32[]{:S(2)}, u32[]{:S(2)}) collective-permute-start(bf16[1,512,64]{1,2,0:T(8,128)(2,1)} %get-tuple-element.20), channel_id=1, source_target_pairs={{0,7},{1,0},{2,1},{3,2},{4,3},{5,4},{6,5},{7,6},{8,15},{9,8},{10,9... | collective-permute-start | bytes 196616 | tf_op jit(solution)/shard_map/ppermute | solution.py:221
  184.7 52.7 %collective-permute-start.15 = (bf16[1,512,64]{1,2,0:T(8,128)(2,1)}, bf16[1,512,64]{1,2,0:T(8,128)(2,1)S(1)}, u32[]{:S(2)}, u32[]{:S(2)}) collective-permute-start(bf16[1,512,64]{1,2,0:T(8,128)(2,1)} %get-tuple-element.32), channel_id=1, source_target_pairs={{0,2},{1,3},{2,4},{3,5},{4,6},{5,7},{6,0},{7,1},{8,10},{9,11},{10,... | collective-permute-start | bytes 196616 | tf_op jit(solution)/shard_map/ppermute | solution.py:221
  186.6 51.1 %collective-permute-start.16 = (bf16[1,512,64]{1,2,0:T(8,128)(2,1)}, bf16[1,512,64]{1,2,0:T(8,128)(2,1)S(1)}, u32[]{:S(2)}, u32[]{:S(2)}) collective-permute-start(bf16[1,512,64]{1,2,0:T(8,128)(2,1)} %get-tuple-element.31), channel_id=1, source_target_pairs={{0,3},{1,4},{2,5},{3,6},{4,7},{5,0},{6,1},{7,2},{8,11},{9,12},{10,... | collective-permute-start | bytes 196616 | tf_op jit(solution)/shard_map/ppermute | solution.py:221
  187.3 50.4 %collective-permute-start.17 = (bf16[1,512,64]{1,2,0:T(8,128)(2,1)}, bf16[1,512,64]{1,2,0:T(8,128)(2,1)S(1)}, u32[]{:S(2)}, u32[]{:S(2)}) collective-permute-start(bf16[1,512,64]{1,2,0:T(8,128)(2,1)} %get-tuple-element.30), channel_id=1, source_target_pairs={{0,4},{1,5},{2,6},{3,7},{4,0},{5,1},{6,2},{7,3},{8,12},{9,13},{10,... | collective-permute-start | bytes 196616 | tf_op jit(solution)/shard_map/ppermute | solution.py:221
  190.1 47.5 %collective-permute-start.18 = (bf16[1,512,64]{1,2,0:T(8,128)(2,1)}, bf16[1,512,64]{1,2,0:T(8,128)(2,1)S(1)}, u32[]{:S(2)}, u32[]{:S(2)}) collective-permute-start(bf16[1,512,64]{1,2,0:T(8,128)(2,1)} %get-tuple-element.29), channel_id=1, source_target_pairs={{0,5},{1,6},{2,7},{3,0},{4,1},{5,2},{6,3},{7,4},{8,13},{9,14},{10,... | collective-permute-start | bytes 196616 | tf_op jit(solution)/shard_map/ppermute | solution.py:221
  190.3 47.4 %collective-permute-start.19 = (bf16[1,512,64]{1,2,0:T(8,128)(2,1)}, bf16[1,512,64]{1,2,0:T(8,128)(2,1)S(1)}, u32[]{:S(2)}, u32[]{:S(2)}) collective-permute-start(bf16[1,512,64]{1,2,0:T(8,128)(2,1)} %get-tuple-element.28), channel_id=1, source_target_pairs={{0,6},{1,7},{2,0},{3,1},{4,2},{5,3},{6,4},{7,5},{8,14},{9,15},{10,... | collective-permute-start | bytes 196616 | tf_op jit(solution)/shard_map/ppermute | solution.py:221
  228.9 24.7 %copy-start.6 = (bf16[8,512,2,64]{1,3,2,0:T(8,128)(2,1)S(1)}, bf16[8,512,2,64]{1,3,2,0:T(8,128)(2,1)}, u32[]{:S(2)}) copy-start(bf16[8,512,2,64]{1,3,2,0:T(8,128)(2,1)} %copy-done.5) | copy-start | bytes 3145732
  228.9 24.7 %all-to-all-start.3 = ((bf16[8,512,128]{2,1,0:T(8,128)(2,1)}), bf16[8,512,128]{2,1,0:T(8,128)(2,1)}, u32[]{:S(2)}, u32[]{:S(2)}) async-start(bf16[8,512,128]{2,1,0:T(8,128)(2,1)} %bitcast.72), calls=%async_computation.3 | async-start | bytes 2097152 | tf_op jit(solution)/shard_map/all_to_all | solution.py:310
  237.5 14.9 %collective-permute-start.20 = (bf16[1,512,64]{1,2,0:T(8,128)(2,1)S(1)}, bf16[1,512,64]{1,2,0:T(8,128)(2,1)S(1)}, u32[]{:S(2)}, u32[]{:S(2)}) collective-permute-start(bf16[1,512,64]{1,2,0:T(8,128)(2,1)S(1)} %get-tuple-element.27), channel_id=1, source_target_pairs={{0,7},{1,0},{2,1},{3,2},{4,3},{5,4},{6,5},{7,6},{8,15},{9,8},{10,9... | collective-permute-start | bytes 196616 | tf_op jit(solution)/shard_map/ppermute | solution.py:221
  253.6 2.7 %copy-start.3 = (bf16[512,512]{1,0:T(8,128)(2,1)S(1)}, bf16[512,512]{1,0:T(8,128)(2,1)}, u32[]{:S(2)}) copy-start(bf16[512,512]{1,0:T(8,128)(2,1)} %param.13) | copy-start | bytes 1572868
  253.6 2.0 copy-start.7
